TPU v7x, 32 devices: a whole 2x2x4 slice. The times are simulated.
32 devices in a mesh: groups: 2 (over x), inst: 2 (over core), section: 8 (over z, y).
Axes of the slice: x: 2, y: 2, z: 4, core: 2. Of those that a mesh axis runs over, the one named last changes fastest.
Arguments:
- tokens: bfloat16 [4, 4, 8, 8192], P(('groups', 'inst')), parts along dimension 0, may hold values from -8 to 8
- kv_pool: bfloat16 [4, 8, 16, 2, 8, 128, 128], P(('groups', 'inst'), 'section'), parts along dimension 0, may hold values from -7.125 to 7.125
- page_table: int32 [4, 8, 2], P(('groups', 'inst')), parts along dimension 0, may hold values from 0 to 15, as said below
- lengths: int32 [4, 8], P(('groups', 'inst')), parts along dimension 0, may hold values from 1 to 256, 1280 in all within a row
- migrate_ids: int32 [4, 2], P(('groups', 'inst')), parts along dimension 0, may hold values from 0 to 7, as said below
- norm_gain: float32 [8, 8192], P('section'), may hold values from 0.5 to 1.5
- out_scale: float32 [8, 8192], P('section'), may hold values from 0.5 to 3
Outputs:
- section_rows: bfloat16 [4, 8, 4, 8, 8192], P(('groups', 'inst'), 'section'), parts along dimension 0
- arrived: bfloat16 [4, 8, 2, 2, 2, 8, 128, 128], P(('groups', 'inst'), 'section'), parts along dimension 0
There are 2 independent parts, one for each index of `groups`. A program takes and returns all parts, laid end to end along the dimension named above; an argument that names none is the same for every part. Nothing has to cross between parts.
Inputs may be any that keep to these rules, and one draw needn't show every extreme that they name: `page_table`: each instance's table names each of its 16 pages exactly once. `migrate_ids`: the 2 requests of one instance are different.
All inputs are finite; a program needn't handle non-finite values.
Results may differ from a plain program's by a relative error of at most 0.0091.
Values may be sent and summed in bfloat16 or wider, within the bound.
No kernel may reach another device: no remote copies, remote signals or barrier semaphores. Data moves between devices by JAX's collectives and lax.ppermute only.
A program may use at most 128 MiB of HBM per device.

v0:
```python
import math

import jax
import jax.numpy as jnp
from jax import lax
from jax.sharding import PartitionSpec as P

CHUNKS = 4


def partner(block, axis, stride):
    count = lax.axis_size(axis)
    route = []
    for low in range(count):
        high = low | 1 << stride
        if high != low and high < count:
            route += [(low, high), (high, low)]
    return lax.ppermute(block, axis, route)


def passed_along(array, axis, by):
    peers = lax.axis_size(axis)
    pairs = [(i, i + by) for i in range(peers) if 0 <= i + by < peers]
    return lax.ppermute(array, axis, pairs)


def layer(rows, keys, values, lens, gain, scale):
    steps, reqs, width = rows.shape
    pages = keys.shape[1]
    kv_heads = keys.shape[2]
    page_len = keys.shape[3]
    head = keys.shape[4]
    group = width // (kv_heads * head)
    wide = rows.astype(jnp.float32)
    normed = wide * lax.rsqrt(jnp.mean(wide * wide, axis=-1, keepdims=True) + 1e-05) * gain
    heads = normed.reshape(steps, reqs, kv_heads, group, head)
    query = jnp.transpose(heads.astype(jnp.bfloat16), (1, 2, 0, 3, 4))
    query = query.reshape(reqs, kv_heads, steps * group, head)
    fresh = jnp.mean(heads, axis=3).astype(jnp.bfloat16)
    fresh = jnp.transpose(fresh, (1, 2, 0, 3))
    factor = 1.0 / math.sqrt(head)
    wide_query = jnp.broadcast_to(query[:, None], (reqs, pages) + query.shape[1:])
    cache_scores = (
        jnp.einsum("rjgxd,rjgpd->rjgxp", wide_query, keys, preferred_element_type=jnp.float32)
        * factor
    )
    positions = jnp.arange(pages)[:, None] * page_len + jnp.arange(page_len)[None, :]
    live = positions[None] < lens[:, None, None]
    cache_scores = jnp.where(live[:, :, None, None, :], cache_scores, -1e30)
    new_scores = (
        jnp.einsum("rgxd,rgsd->rgxs", query, fresh, preferred_element_type=jnp.float32) * factor
    )
    step_of = jnp.arange(steps * group) // group
    done = jnp.arange(steps)[None, :] <= step_of[:, None]
    new_scores = jnp.where(done[None, None], new_scores, -1e30)
    top = jnp.maximum(
        jnp.max(cache_scores, axis=(1, 4)), jnp.max(new_scores, axis=-1)
    )[..., None]
    cache_exp = jnp.exp(cache_scores - top[:, None])
    new_exp = jnp.exp(new_scores - top)
    total = jnp.sum(cache_exp, axis=(1, 4))[..., None] + jnp.sum(new_exp, axis=-1, keepdims=True)
    cache_w = (cache_exp / total[:, None]).astype(jnp.bfloat16)
    new_w = (new_exp / total).astype(jnp.bfloat16)
    attended = jnp.einsum(
        "rjgxp,rjgpd->rjgxd", cache_w, values, preferred_element_type=jnp.float32
    ).sum(axis=1)
    attended = attended + jnp.einsum(
        "rgxs,rgsd->rgxd", new_w, fresh, preferred_element_type=jnp.float32
    )
    attended = attended.reshape(reqs, kv_heads, steps, group, head)
    attended = jnp.transpose(attended, (2, 0, 1, 3, 4)).reshape(steps, reqs, width)
    return (wide + scale * attended).astype(jnp.bfloat16)


def per_device(tokens, kv_pool, page_table, lengths, migrate_ids, norm_gain, out_scale):
    inputs = tokens[0]
    pool = kv_pool[0, 0]
    table = page_table[0]
    lens = lengths[0]
    moving = migrate_ids[0]
    gain = norm_gain[0]
    scale = out_scale[0]
    steps, reqs, width = inputs.shape
    page_len = pool.shape[3]
    chosen = table[moving]
    outgoing = pool[chosen]
    spots = jnp.arange(chosen.shape[1])[:, None] * page_len + jnp.arange(page_len)[None, :]
    keep = spots[None, :, :] < lens[moving][:, None, None]
    outgoing = jnp.where(keep[:, :, None, None, :, None], outgoing, jnp.zeros((), jnp.bfloat16))
    received = partner(outgoing, "inst", 0)
    flat_pool = pool.reshape((-1,) + pool.shape[2:])
    keys = flat_pool[table * 2]
    values = flat_pool[table * 2 + 1]
    lens_used = lens
    section = lax.axis_index("section")
    count = lax.axis_size("section")
    chunks = CHUNKS
    block = reqs // chunks

    incoming = jnp.zeros((steps, block, width), jnp.bfloat16)
    finished = jnp.zeros((steps, reqs, width), jnp.bfloat16)
    zero = jnp.zeros((), jnp.int32)
    for k in range(chunks + count - 1):
        item = k - section
        live = jnp.logical_and(item >= 0, item < chunks)
        start = jnp.clip(item, 0, chunks - 1) * block
        if k > 0:
            start, incoming = lax.optimization_barrier((start, incoming))
        first = lax.dynamic_slice_in_dim(inputs, start, block, 1)
        rows = jnp.where(section == 0, first, incoming)
        part_keys = lax.dynamic_slice_in_dim(keys, start, block, 0)
        part_values = lax.dynamic_slice_in_dim(values, start, block, 0)
        part_lens = lax.dynamic_slice_in_dim(lens_used, start, block, 0)
        result = layer(rows, part_keys, part_values, part_lens, gain, scale)
        previous = lax.dynamic_slice_in_dim(finished, start, block, 1)
        finished = lax.dynamic_update_slice(
            finished, jnp.where(live, result, previous), (zero, start, zero)
        )
        pairs = [(s, s + 1) for s in range(count - 1) if 0 <= k - s < chunks]
        if pairs:
            incoming = lax.ppermute(result, "section", pairs)
    handed = partner(finished[:, moving], "inst", 0)
    finished = finished.at[:, moving].set(handed)
    return (finished[None, None], received[None, None])


def solution(mesh):
    in_specs = (
        P(("groups", "inst"), None, None, None),
        P(("groups", "inst"), "section", None, None, None, None, None),
        P(("groups", "inst"), None, None),
        P(("groups", "inst"), None),
        P(("groups", "inst"), None),
        P("section", None),
        P("section", None),
    )
    out_specs = (
        P(("groups", "inst"), "section", None, None, None),
        P(("groups", "inst"), "section", None, None, None, None, None, None),
    )
    return jax.shard_map(
        per_device, mesh=mesh, in_specs=in_specs, out_specs=out_specs, check_vma=False
    )
```

profile of v0, /device:TPU:26, one launch (start us, length us, event | category | flops | bytes accessed | tf_op | source)
XLA Modules:
  0.0 157.5 jit_solution(5067955192966706006)
XLA Ops:
  5.2 6.4 %gather_fusion = bf16[16,8,128,128]{3,2,1,0:T(8,128)(2,1)} fusion(bf16[32,8,128,128]{3,2,1,0:T(8,128)(2,1)} %bitcast.337, s32[1024]{0:T(1024)S(1)} %pad_clamp_fusion.3), kind=kCustom, calls=%fused_computation | custom fusion | bytes 8388672 | tf_op jit(solution)/shard_map/gather | solution.py:92
  11.8 2.0 %fusion.237 = (f32[2,8,32]{2,1,0:T(8,128)S(1)}, f32[2,2,8,32,128]{4,3,2,1,0:T(8,128)S(1)}) fusion(bf16[8,2,8,128,128]{4,3,2,1,0:T(8,128)(2,1)} %bitcast.325, s32[]{:T(128)S(6)} %select_n.366, bf16[2,8,32,128]{3,2,1,0:T(8,128)(2,1)S(1)} %get-tuple-element.91, pred[2,2,128]{2,1,0:T(4,128)(4,1)S(1)} %broadcast_compare_fusion.11), kind=kOutput, calls=%fused_computation.471 | convolution fusion | flops 33947136 | bytes 1706500 | tf_op jit(solution)/shard_map/rjgxd,rjgpd->rjgxp/dot_general | solution.py:44
  14.3 6.4 %gather_fusion.1 = bf16[16,8,128,128]{3,2,1,0:T(8,128)(2,1)} fusion(bf16[32,8,128,128]{3,2,1,0:T(8,128)(2,1)} %bitcast.338, s32[1024]{0:T(1024)S(1)} %pad_clamp_fusion.2), kind=kCustom, calls=%fused_computation.1 | custom fusion | bytes 8388672 | tf_op jit(solution)/shard_map/gather | solution.py:93
  20.7 1.6 %convolution_bitcast_fusion.10 = f32[2,8,32,128]{3,2,1,0:T(8,128)S(1)} fusion(bf16[8,2,8,128,128]{4,3,2,1,0:T(8,128)(2,1)} %bitcast.341, s32[]{:T(128)S(6)} %select_n.366, f32[2,2,8,32,128]{4,3,2,1,0:T(8,128)S(1)} %get-tuple-element.97, f32[2,8,32]{2,1,0:T(8,128)S(1)} %add.601, f32[2,8,32]{2,1,0:T(8,128)S(1)} %max.156), kind=kOutput, calls=%fused_computation.62 | convolution fusion | flops 33947648 | bytes 1839108 | tf_op jit(solution)/shard_map/rjgxp,rjgpd->rjgxd/dot_general | solution.py:64
  25.6 2.0 %fusion.239 = (f32[2,8,32]{2,1,0:T(8,128)S(1)}, f32[2,2,8,32,128]{4,3,2,1,0:T(8,128)S(1)}) fusion(bf16[8,2,8,128,128]{4,3,2,1,0:T(8,128)(2,1)} %bitcast.326, s32[]{:T(128)S(6)} %select_n.376, bf16[2,8,32,128]{3,2,1,0:T(8,128)(2,1)S(1)} %bitcast.377, pred[2,2,128]{2,1,0:T(4,128)(4,1)S(1)} %get-tuple-element.93), kind=kOutput, calls=%fused_computation.473 | convolution fusion | flops 33947136 | bytes 1706500 | tf_op jit(solution)/shard_map/rjgxd,rjgpd->rjgxp/dot_general | solution.py:44
  32.0 2.0 %fusion.241 = (f32[2,8,32]{2,1,0:T(8,128)S(1)}, f32[2,2,8,32,128]{4,3,2,1,0:T(8,128)S(1)}) fusion(bf16[8,2,8,128,128]{4,3,2,1,0:T(8,128)(2,1)} %bitcast.327, s32[]{:T(128)S(6)} %select_n.382, bf16[2,8,32,128]{3,2,1,0:T(8,128)(2,1)S(1)} %bitcast.379, pred[2,2,128]{2,1,0:T(4,128)(4,1)S(1)} %broadcast_compare_fusion.9), kind=kOutput, calls=%fused_computation.475 | convolution fusion | flops 33947136 | bytes 1706500 | tf_op jit(solution)/shard_map/rjgxd,rjgpd->rjgxp/dot_general | solution.py:44
  38.4 2.0 %fusion.243 = (f32[2,8,32]{2,1,0:T(8,128)S(1)}, f32[2,2,8,32,128]{4,3,2,1,0:T(8,128)S(1)}) fusion(bf16[8,2,8,128,128]{4,3,2,1,0:T(8,128)(2,1)} %bitcast.328, s32[]{:T(128)S(6)} %select_n.388, bf16[2,8,32,128]{3,2,1,0:T(8,128)(2,1)S(1)} %bitcast.381, pred[2,2,128]{2,1,0:T(4,128)(4,1)S(1)} %broadcast_compare_fusion.8), kind=kOutput, calls=%fused_computation.477 | convolution fusion | flops 33947136 | bytes 1706500 | tf_op jit(solution)/shard_map/rjgxd,rjgpd->rjgxp/dot_general | solution.py:44
  44.9 2.0 %fusion.245 = (f32[2,8,32]{2,1,0:T(8,128)S(1)}, f32[2,2,8,32,128]{4,3,2,1,0:T(8,128)S(1)}) fusion(bf16[8,2,8,128,128]{4,3,2,1,0:T(8,128)(2,1)} %bitcast.329, s32[]{:T(128)S(6)} %select_n.394, bf16[2,8,32,128]{3,2,1,0:T(8,128)(2,1)S(1)} %bitcast.383, pred[2,2,128]{2,1,0:T(4,128)(4,1)S(1)} %broadcast_compare_fusion.7), kind=kOutput, calls=%fused_computation.479 | convolution fusion | flops 33947136 | bytes 1706500 | tf_op jit(solution)/shard_map/rjgxd,rjgpd->rjgxp/dot_general | solution.py:44
  51.3 2.0 %fusion.247 = (f32[2,8,32]{2,1,0:T(8,128)S(1)}, f32[2,2,8,32,128]{4,3,2,1,0:T(8,128)S(1)}) fusion(bf16[8,2,8,128,128]{4,3,2,1,0:T(8,128)(2,1)} %bitcast.330, s32[]{:T(128)S(6)} %select_n.400, bf16[2,8,32,128]{3,2,1,0:T(8,128)(2,1)S(1)} %bitcast.385, pred[2,2,128]{2,1,0:T(4,128)(4,1)S(1)} %broadcast_compare_fusion.6), kind=kOutput, calls=%fused_computation.481 | convolution fusion | flops 33947136 | bytes 1706500 | tf_op jit(solution)/shard_map/rjgxd,rjgpd->rjgxp/dot_general | solution.py:44
  57.0 30.9 %collective-permute-done.5 = bf16[4,2,8192]{2,0,1:T(4,128)(2,1)S(1)} collective-permute-done((bf16[4,2,8192]{2,0,1:T(4,128)(2,1)S(1)}, bf16[4,2,8192]{2,0,1:T(4,128)(2,1)S(1)}, u32[]{:S(2)}, u32[]{:S(2)}) %collective-permute-start.5) | collective-permute-done | bytes 131104 | tf_op jit(solution)/shard_map/ppermute | solution.py:121
  89.2 2.0 %fusion.249 = (f32[2,8,32]{2,1,0:T(8,128)S(1)}, f32[2,2,8,32,128]{4,3,2,1,0:T(8,128)S(1)}) fusion(bf16[8,2,8,128,128]{4,3,2,1,0:T(8,128)(2,1)} %bitcast.331, s32[]{:T(128)S(6)} %select_n.406, bf16[2,8,32,128]{3,2,1,0:T(8,128)(2,1)S(1)} %bitcast.387, pred[2,2,128]{2,1,0:T(4,128)(4,1)S(1)} %broadcast_compare_fusion.5), kind=kOutput, calls=%fused_computation.483 | convolution fusion | flops 33947136 | bytes 1706500 | tf_op jit(solution)/shard_map/rjgxd,rjgpd->rjgxp/dot_general | solution.py:44
  93.6 1.9 %collective-permute-start.6 = (bf16[4,2,8192]{2,0,1:T(4,128)(2,1)S(1)}, bf16[4,2,8192]{2,0,1:T(4,128)(2,1)S(1)}, u32[]{:S(2)}, u32[]{:S(2)}) collective-permute-start(bf16[4,2,8192]{2,0,1:T(4,128)(2,1)S(1)} %get-tuple-element.65), channel_id=1, source_target_pairs={{3,4},{4,5},{5,6},{6,7},{11,12},{12,13},{13,14},{14,15},{19,20},{2... | collective-permute-start | bytes 393224 | tf_op jit(solution)/shard_map/ppermute | solution.py:121
  95.5 5.8 %collective-permute-done.6 = bf16[4,2,8192]{2,0,1:T(4,128)(2,1)S(1)} collective-permute-done((bf16[4,2,8192]{2,0,1:T(4,128)(2,1)S(1)}, bf16[4,2,8192]{2,0,1:T(4,128)(2,1)S(1)}, u32[]{:S(2)}, u32[]{:S(2)}) %collective-permute-start.6) | collective-permute-done | bytes 131104 | tf_op jit(solution)/shard_map/ppermute | solution.py:121
  102.6 2.0 %fusion.251 = (f32[2,8,32]{2,1,0:T(8,128)S(1)}, f32[2,2,8,32,128]{4,3,2,1,0:T(8,128)S(1)}) fusion(bf16[8,2,8,128,128]{4,3,2,1,0:T(8,128)(2,1)} %bitcast.332, s32[]{:T(128)S(6)} %select_n.412, bf16[2,8,32,128]{3,2,1,0:T(8,128)(2,1)S(1)} %bitcast.389, pred[2,2,128]{2,1,0:T(4,128)(4,1)S(1)} %broadcast_compare_fusion.4), kind=kOutput, calls=%fused_computation.485 | convolution fusion | flops 33947136 | bytes 1706500 | tf_op jit(solution)/shard_map/rjgxd,rjgpd->rjgxp/dot_general | solution.py:44
  107.0 1.9 %collective-permute-start.7 = (bf16[4,2,8192]{2,0,1:T(4,128)(2,1)S(1)}, bf16[4,2,8192]{2,0,1:T(4,128)(2,1)S(1)}, u32[]{:S(2)}, u32[]{:S(2)}) collective-permute-start(bf16[4,2,8192]{2,0,1:T(4,128)(2,1)S(1)} %get-tuple-element.61), channel_id=1, source_target_pairs={{4,5},{5,6},{6,7},{12,13},{13,14},{14,15},{20,21},{21,22},{22,23},... | collective-permute-start | bytes 393224 | tf_op jit(solution)/shard_map/ppermute | solution.py:121
  109.6 5.2 %collective-permute-done.7 = bf16[4,2,8192]{2,0,1:T(4,128)(2,1)S(1)} collective-permute-done((bf16[4,2,8192]{2,0,1:T(4,128)(2,1)S(1)}, bf16[4,2,8192]{2,0,1:T(4,128)(2,1)S(1)}, u32[]{:S(2)}, u32[]{:S(2)}) %collective-permute-start.7) | collective-permute-done | bytes 131104 | tf_op jit(solution)/shard_map/ppermute | solution.py:121
  116.0 2.0 %fusion.253 = (f32[2,8,32]{2,1,0:T(8,128)S(1)}, f32[2,2,8,32,128]{4,3,2,1,0:T(8,128)S(1)}) fusion(bf16[8,2,8,128,128]{4,3,2,1,0:T(8,128)(2,1)} %bitcast.333, s32[]{:T(128)S(6)} %select_n.418, bf16[2,8,32,128]{3,2,1,0:T(8,128)(2,1)S(1)} %bitcast.391, pred[2,2,128]{2,1,0:T(4,128)(4,1)S(1)} %broadcast_compare_fusion.3), kind=kOutput, calls=%fused_computation.487 | convolution fusion | flops 33947136 | bytes 1706500 | tf_op jit(solution)/shard_map/rjgxd,rjgpd->rjgxp/dot_general | solution.py:44
  120.5 2.1 %collective-permute-start.8 = (bf16[4,2,8192]{2,0,1:T(4,128)(2,1)S(1)}, bf16[4,2,8192]{2,0,1:T(4,128)(2,1)S(1)}, u32[]{:S(2)}, u32[]{:S(2)}) collective-permute-start(bf16[4,2,8192]{2,0,1:T(4,128)(2,1)S(1)} %get-tuple-element.57), channel_id=1, source_target_pairs={{5,6},{6,7},{13,14},{14,15},{21,22},{22,23},{29,30},{30,31}} | collective-permute-start | bytes 393224 | tf_op jit(solution)/shard_map/ppermute | solution.py:121
  122.7 4.3 %gather_fusion.5 = bf16[4,2,8,128,128]{4,3,2,1,0:T(8,128)(2,1)S(1)} fusion(bf16[16,2,8,128,128]{4,3,2,1,0:T(8,128)(2,1)} %bitcast.339, s32[1024]{0:T(1024)S(1)} %pad_clamp_fusion), kind=kCustom, calls=%fused_computation.5 | custom fusion | bytes 4194320 | tf_op jit(solution)/shard_map/gather | solution.py:86
  133.3 2.0 %fusion.255 = (f32[2,8,32]{2,1,0:T(8,128)S(1)}, f32[2,2,8,32,128]{4,3,2,1,0:T(8,128)S(1)}) fusion(bf16[8,2,8,128,128]{4,3,2,1,0:T(8,128)(2,1)} %bitcast.334, s32[]{:T(128)S(6)} %select_n.424, bf16[2,8,32,128]{3,2,1,0:T(8,128)(2,1)} %bitcast.393, pred[2,2,128]{2,1,0:T(4,128)(4,1)S(1)} %broadcast_compare_fusion.2), kind=kOutput, calls=%fused_computation.489 | convolution fusion | flops 33947136 | bytes 1706500 | tf_op jit(solution)/shard_map/rjgxd,rjgpd->rjgxp/dot_general | solution.py:44
  138.2 1.8 %reshape.680 = f32[4,2,8192]{2,0,1:T(4,128)} reshape(f32[4,2,8,8,128]{4,3,2,0,1:T(8,128)} %copy.258) | data formatting | bytes 524288 | tf_op jit(solution)/shard_map/reshape | solution.py:71
  142.4 1.6 %broadcast_select_fusion = bf16[2,2,2,8,128,128]{5,4,3,2,1,0:T(8,128)(2,1)} fusion(bf16[2,2,2,8,128,128]{5,4,3,2,1,0:T(8,128)(2,1)S(1)} %bitcast.340, pred[2,2,128]{2,1,0:T(4,128)(4,1)S(1)} %get-tuple-element.92), kind=kLoop, calls=%fused_computation.7 | loop fusion | flops 1048576 | bytes 4194816 | tf_op jit(solution)/shard_map/jit(_where)/select_n | solution.py:89
  146.1 2.0 %fusion.257 = (f32[2,8,32]{2,1,0:T(8,128)S(1)}, f32[2,2,8,32,128]{4,3,2,1,0:T(8,128)S(1)}) fusion(bf16[8,2,8,128,128]{4,3,2,1,0:T(8,128)(2,1)} %bitcast.335, s32[]{:T(128)S(6)} %select_n.430, bf16[2,8,32,128]{3,2,1,0:T(8,128)(2,1)S(1)} %bitcast.375, pred[2,2,128]{2,1,0:T(4,128)(4,1)S(1)} %broadcast_compare_fusion.1), kind=kOutput, calls=%fused_computation.491 | convolution fusion | flops 33947136 | bytes 1706500 | tf_op jit(solution)/shard_map/rjgxd,rjgpd->rjgxp/dot_general | solution.py:44
  154.3 3.2 %copy.497 = bf16[1,1,2,2,2,8,128,128]{7,6,5,4,3,2,1,0:T(8,128)(2,1)} copy(bf16[1,1,2,2,2,8,128,128]{7,6,5,4,3,2,1,0:T(8,128)(2,1)} %bitcast.127) | data formatting | bytes 4194304
  (274 shorter events, 60.5 us)
Async XLA Ops:
  0.6 1.0 copy-start
  20.7 2.2 %copy-start.2 = (f32[1,8192]{1,0:T(1,128)S(1)}, f32[1,8192]{1,0:T(1,128)}, u32[]{:S(2)}) copy-start(f32[1,8192]{1,0:T(1,128)} %param.13) | copy-start | bytes 98308
  20.7 3.1 %copy-start.7 = (s32[1,2]{1,0:T(1,128)S(1)}, s32[1,2]{1,0:T(1,128)}, u32[]{:S(2)}) copy-start(s32[1,2]{1,0:T(1,128)} %param.11) | copy-start | bytes 28
  20.7 3.1 %copy-start.1 = (s32[1,8]{1,0:T(1,128)S(1)}, s32[1,8]{1,0:T(1,128)}, u32[]{:S(2)}) copy-start(s32[1,8]{1,0:T(1,128)} %param.10) | copy-start | bytes 100
  20.7 4.3 %copy-start.3 = (f32[1,8192]{1,0:T(1,128)S(1)}, f32[1,8192]{1,0:T(1,128)}, u32[]{:S(2)}) copy-start(f32[1,8192]{1,0:T(1,128)} %param.12) | copy-start | bytes 98308
  23.0 1.4 collective-permute-start
  30.1 0.7 collective-permute-start.1
  36.4 0.7 collective-permute-start.2
  42.8 0.9 collective-permute-start.3
  49.4 0.7 collective-permute-start.4
  55.7 32.2 %collective-permute-start.5 = (bf16[4,2,8192]{2,0,1:T(4,128)(2,1)S(1)}, bf16[4,2,8192]{2,0,1:T(4,128)(2,1)S(1)}, u32[]{:S(2)}, u32[]{:S(2)}) collective-permute-start(bf16[4,2,8192]{2,0,1:T(4,128)(2,1)S(1)} %get-tuple-element.69), channel_id=1, source_target_pairs={{2,3},{3,4},{4,5},{5,6},{10,11},{11,12},{12,13},{13,14},{18,19},{1... | collective-permute-start | bytes 393224 | tf_op jit(solution)/shard_map/ppermute | solution.py:121
  93.6 7.8 %collective-permute-start.6 = (bf16[4,2,8192]{2,0,1:T(4,128)(2,1)S(1)}, bf16[4,2,8192]{2,0,1:T(4,128)(2,1)S(1)}, u32[]{:S(2)}, u32[]{:S(2)}) collective-permute-start(bf16[4,2,8192]{2,0,1:T(4,128)(2,1)S(1)} %get-tuple-element.65), channel_id=1, source_target_pairs={{3,4},{4,5},{5,6},{6,7},{11,12},{12,13},{13,14},{14,15},{19,20},{2... | collective-permute-start | bytes 393224 | tf_op jit(solution)/shard_map/ppermute | solution.py:121
  102.4 6.6 %copy-start.6 = (s32[1,8,2]{1,2,0:T(2,128)S(1)}, s32[1,8,2]{1,2,0:T(2,128)}, u32[]{:S(2)}) copy-start(s32[1,8,2]{1,2,0:T(2,128)} %param.9) | copy-start | bytes 196
  107.0 7.8 %collective-permute-start.7 = (bf16[4,2,8192]{2,0,1:T(4,128)(2,1)S(1)}, bf16[4,2,8192]{2,0,1:T(4,128)(2,1)S(1)}, u32[]{:S(2)}, u32[]{:S(2)}) collective-permute-start(bf16[4,2,8192]{2,0,1:T(4,128)(2,1)S(1)} %get-tuple-element.61), channel_id=1, source_target_pairs={{4,5},{5,6},{6,7},{12,13},{13,14},{14,15},{20,21},{21,22},{22,23},... | collective-permute-start | bytes 393224 | tf_op jit(solution)/shard_map/ppermute | solution.py:121
  120.5 7.8 %collective-permute-start.8 = (bf16[4,2,8192]{2,0,1:T(4,128)(2,1)S(1)}, bf16[4,2,8192]{2,0,1:T(4,128)(2,1)S(1)}, u32[]{:S(2)}, u32[]{:S(2)}) collective-permute-start(bf16[4,2,8192]{2,0,1:T(4,128)(2,1)S(1)} %get-tuple-element.57), channel_id=1, source_target_pairs={{5,6},{6,7},{13,14},{14,15},{21,22},{22,23},{29,30},{30,31}} | collective-permute-start | bytes 393224 | tf_op jit(solution)/shard_map/ppermute | solution.py:121
  128.6 0.7 copy-start.4
  132.0 8.0 %copy-start.5 = (bf16[4,2,8192]{2,0,1:T(4,128)(2,1)S(1)}, bf16[4,2,8192]{2,0,1:T(4,128)(2,1)}, u32[]{:S(2)}) copy-start(bf16[4,2,8192]{2,0,1:T(4,128)(2,1)} %copy-done.4) | copy-start | bytes 393220
  141.1 3.8 %collective-permute-start.9 = (bf16[4,2,8192]{2,0,1:T(4,128)(2,1)S(1)}, bf16[4,2,8192]{2,0,1:T(4,128)(2,1)S(1)}, u32[]{:S(2)}, u32[]{:S(2)}) collective-permute-start(bf16[4,2,8192]{2,0,1:T(4,128)(2,1)S(1)} %get-tuple-element.53), channel_id=1, source_target_pairs={{6,7},{14,15},{22,23},{30,31}} | collective-permute-start | bytes 393224 | tf_op jit(solution)/shard_map/ppermute | solution.py:121
  144.0 10.4 %collective-permute-start.11 = (bf16[2,2,2,8,128,128]{5,4,3,2,1,0:T(8,128)(2,1)}, bf16[2,2,2,8,128,128]{5,4,3,2,1,0:T(8,128)(2,1)}, u32[]{:S(2)}, u32[]{:S(2)}) collective-permute-start(bf16[2,2,2,8,128,128]{5,4,3,2,1,0:T(8,128)(2,1)} %broadcast_select_fusion), channel_id=1, source_target_pairs={{0,8},{8,0},{1,9},{9,1},{2,10},{10,2},{3,11},{11,3},{4,12},{12,4},... | collective-permute-start | bytes 6291464 | tf_op jit(solution)/shard_map/ppermute | solution.py:18
  151.2 1.4 collective-permute-start.10
where the time goes:
time: 160 us; the launch traced here: 157 us
  waiting for transfers between devices  45.3 us (28%)
  matrix products  44.7 us (28%)
  local copies, waits for them, and re-layouts  36.7 us (23%)
  other arithmetic  16.5 us (10%)
  starting transfers between devices  12.2 us (8%)
  between operations  2.09 us (1%)
    ppermute x10, waiting for transfers between devices, per_device(): incoming = lax.ppermute(result, 'section', pairs)  44 us
    dot_general x11, matrix products, layer(): jnp.einsum('rjgxd,rjgpd->rjgxp', wide_query, keys, preferred_element_type...  21.7 us
    dot_general x11, matrix products, layer(): jnp.einsum('rjgxp,rjgpd->rjgxd', cache_w, values, preferred_element_type=...  17.3 us
    ppermute x10, starting transfers between devices, per_device(): incoming = lax.ppermute(result, 'section', pairs)  12.1 us
    gather x1, local copies, waits for them, and re-layouts, per_device(): keys = flat_pool[table * 2]  6.44 us
    gather x1, local copies, waits for them, and re-layouts, per_device(): values = flat_pool[table * 2 + 1]  6.39 us
    unnamed x18, local copies, waits for them, and re-layouts  5.94 us
    gather x1, local copies, waits for them, and re-layouts, per_device(): outgoing = pool[chosen]  4.33 us
  transfers between devices with their start and end apart: 12, of which 6 were waited for; matrix products, arithmetic and copies ran while one was open for 10% of the time, Pallas kernels for 0%

commit v1 on v0

--- a/solution.py
+++ b/solution.py
@@ -4,6 +4,8 @@
 import jax.numpy as jnp
 from jax import lax
 from jax.sharding import PartitionSpec as P
+from jax.experimental import pallas as pl
+from jax.experimental.pallas import tpu as pltpu
 
 CHUNKS = 4
 
@@ -72,6 +74,49 @@
     return (wide + scale * attended).astype(jnp.bfloat16)
 
 
+def gather_kernel(table_ref, moving_ref, pool_ref, keys_ref, values_ref, out_ref, sems):
+    reqs, pages = keys_ref.shape[0], keys_ref.shape[1]
+    copies = []
+    for r in range(reqs):
+        for j in range(pages):
+            page = table_ref[r * pages + j]
+            copies.append(
+                pltpu.make_async_copy(pool_ref.at[page, 0], keys_ref.at[r, j], sems.at[len(copies)])
+            )
+            copies.append(
+                pltpu.make_async_copy(pool_ref.at[page, 1], values_ref.at[r, j], sems.at[len(copies)])
+            )
+    for m in range(out_ref.shape[0]):
+        for j in range(pages):
+            page = table_ref[moving_ref[m] * pages + j]
+            copies.append(
+                pltpu.make_async_copy(pool_ref.at[page], out_ref.at[m, j], sems.at[len(copies)])
+            )
+    for copy in copies:
+        copy.start()
+    for copy in copies:
+        copy.wait()
+
+
+def gather_pages(pool, table, moving):
+    reqs, pages = table.shape
+    kv_heads, page_len, head = pool.shape[2:]
+    count = 2 * reqs * pages + moving.shape[0] * pages
+    any_spec = pl.BlockSpec(memory_space=pl.ANY)
+    grid_spec = pltpu.PrefetchScalarGridSpec(
+        num_scalar_prefetch=2,
+        grid=(1,),
+        in_specs=[any_spec],
+        out_specs=[any_spec, any_spec, any_spec],
+        scratch_shapes=[pltpu.SemaphoreType.DMA((count,))],
+    )
+    half = jax.ShapeDtypeStruct((reqs, pages, kv_heads, page_len, head), pool.dtype)
+    whole = jax.ShapeDtypeStruct((moving.shape[0], pages) + pool.shape[1:], pool.dtype)
+    return pl.pallas_call(
+        gather_kernel, grid_spec=grid_spec, out_shape=[half, half, whole]
+    )(table.reshape(-1), moving, pool)
+
+
 def per_device(tokens, kv_pool, page_table, lengths, migrate_ids, norm_gain, out_scale):
     inputs = tokens[0]
     pool = kv_pool[0, 0]
@@ -82,15 +127,12 @@
     scale = out_scale[0]
     steps, reqs, width = inputs.shape
     page_len = pool.shape[3]
-    chosen = table[moving]
-    outgoing = pool[chosen]
-    spots = jnp.arange(chosen.shape[1])[:, None] * page_len + jnp.arange(page_len)[None, :]
-    keep = spots[None, :, :] < lens[moving][:, None, None]
-    outgoing = jnp.where(keep[:, :, None, None, :, None], outgoing, jnp.zeros((), jnp.bfloat16))
+    keys, values, outgoing = gather_pages(pool, table, moving)
     received = partner(outgoing, "inst", 0)
-    flat_pool = pool.reshape((-1,) + pool.shape[2:])
-    keys = flat_pool[table * 2]
-    values = flat_pool[table * 2 + 1]
+    arrived_lens = partner(lens[moving], "inst", 0)
+    spots = jnp.arange(table.shape[1])[:, None] * page_len + jnp.arange(page_len)[None, :]
+    keep = spots[None, :, :] < arrived_lens[:, None, None]
+    arrived = jnp.where(keep[:, :, None, None, :, None], received, jnp.zeros((), jnp.bfloat16))
     lens_used = lens
     section = lax.axis_index("section")
     count = lax.axis_size("section")
@@ -121,7 +163,7 @@
             incoming = lax.ppermute(result, "section", pairs)
     handed = partner(finished[:, moving], "inst", 0)
     finished = finished.at[:, moving].set(handed)
-    return (finished[None, None], received[None, None])
+    return (finished[None, None], arrived[None, None])
 
 
 def solution(mesh):

time: 160 us -> 466 us (2.91)
  Pallas kernels: 0 us -> 320 us
  local copies, waits for them, and re-layouts: 36.7 us -> 16.7 us
  waiting for transfers between devices: 45.3 us -> 51.9 us
    pallas_call x0 -> x1, Pallas kernels: none -> 320 us  [gather_pages(): pl.pallas_call(gather_kernel, grid_spec=grid_spec, out_shape=[half, half,...]
    gather x5 -> x1, local copies, waits for them, and re-layouts: 18.4 us -> 0.64 us  [per_device(): arrived_lens = partner(lens[moving], 'inst', 0)]
    ppermute x10, waiting for transfers between devices: 44 us -> 50.6 us  [per_device(): incoming = lax.ppermute(result, 'section', pairs)]
  transfers between devices with their start and end apart: 12 -> 13, of which waited for: 6 -> 6; matrix products, arithmetic and copies ran while one was open for 10% -> 4% of each run, Pallas kernels for 0% -> 0%
where the time goes in v1:
time: 466 us; the launch traced here: 463 us
  Pallas kernels  320 us (69%)
  waiting for transfers between devices  51.9 us (11%)
  matrix products  44.7 us (10%)
  local copies, waits for them, and re-layouts  16.7 us (4%)
  other arithmetic  15.8 us (3%)
  starting transfers between devices  12.2 us (3%)
    pallas_call x1, Pallas kernels, gather_pages(): pl.pallas_call(gather_kernel, grid_spec=grid_spec, out_shape=[half, half,...  320 us
    ppermute x10, waiting for transfers between devices, per_device(): incoming = lax.ppermute(result, 'section', pairs)  50.6 us
    dot_general x11, matrix products, layer(): jnp.einsum('rjgxd,rjgpd->rjgxp', wide_query, keys, preferred_element_type...  21.7 us
    dot_general x11, matrix products, layer(): jnp.einsum('rjgxp,rjgpd->rjgxd', cache_w, values, preferred_element_type=...  17.3 us
    ppermute x10, starting transfers between devices, per_device(): incoming = lax.ppermute(result, 'section', pairs)  12.1 us
  transfers between devices with their start and end apart: 13, of which 6 were waited for; matrix products, arithmetic and copies ran while one was open for 4% of the time, Pallas kernels for 0%

profile of v1, /device:TPU:26, one launch (start us, length us, event | category | flops | bytes accessed | tf_op | source)
XLA Modules:
  0.0 463.2 jit_solution(3506475147677906501)
XLA Ops:
  5.8 319.8 %shard_map.86 = (bf16[8,2,8,128,128]{4,3,2,1,0:T(8,128)(2,1)}, bf16[8,2,8,128,128]{4,3,2,1,0:T(8,128)(2,1)}, bf16[2,2,2,8,128,128]{5,4,3,2,1,0:T(8,128)(2,1)}) custom-call(s32[16]{0:T(128)} %reshape_squeeze.3.table_ref, s32[2]{0:T(128)} %bitcast.352, bf16[16,2,8,128,128]{4,3,2,1,0:T(8,128)(2,1)} %bitcast.307), custom_call_target="tpu_custom_call" | custom-call | tf_op jit(solution)/shard_map/pallas_call | solution.py:115
  325.6 2.0 fusion.237
  332.9 2.0 fusion.239
  339.3 2.0 fusion.241
  345.6 2.0 fusion.243
  352.2 2.0 fusion.245
  358.5 2.0 fusion.247
  360.9 1.6 convolution_bitcast_fusion.5
  364.3 30.9 %collective-permute-done.5 = bf16[4,2,8192]{2,0,1:T(4,128)(2,1)S(1)} collective-permute-done((bf16[4,2,8192]{2,0,1:T(4,128)(2,1)S(1)}, bf16[4,2,8192]{2,0,1:T(4,128)(2,1)S(1)}, u32[]{:S(2)}, u32[]{:S(2)}) %collective-permute-start.5) | collective-permute-done | bytes 131104 | tf_op jit(solution)/shard_map/ppermute | solution.py:163
  396.4 2.0 fusion.249
  400.9 1.9 collective-permute-start.6
  402.8 5.8 %collective-permute-done.6 = bf16[4,2,8192]{2,0,1:T(4,128)(2,1)S(1)} collective-permute-done((bf16[4,2,8192]{2,0,1:T(4,128)(2,1)S(1)}, bf16[4,2,8192]{2,0,1:T(4,128)(2,1)S(1)}, u32[]{:S(2)}, u32[]{:S(2)}) %collective-permute-start.6) | collective-permute-done | bytes 131104 | tf_op jit(solution)/shard_map/ppermute | solution.py:163
  409.8 2.0 fusion.251
  414.3 1.9 collective-permute-start.7
  416.2 5.8 %collective-permute-done.7 = bf16[4,2,8192]{2,0,1:T(4,128)(2,1)S(1)} collective-permute-done((bf16[4,2,8192]{2,0,1:T(4,128)(2,1)S(1)}, bf16[4,2,8192]{2,0,1:T(4,128)(2,1)S(1)}, u32[]{:S(2)}, u32[]{:S(2)}) %collective-permute-start.7) | collective-permute-done | bytes 131104 | tf_op jit(solution)/shard_map/ppermute | solution.py:163
  423.3 2.0 fusion.253
  427.7 2.1 collective-permute-start.8
  429.9 5.6 %collective-permute-done.8 = bf16[4,2,8192]{2,0,1:T(4,128)(2,1)S(1)} collective-permute-done((bf16[4,2,8192]{2,0,1:T(4,128)(2,1)S(1)}, bf16[4,2,8192]{2,0,1:T(4,128)(2,1)S(1)}, u32[]{:S(2)}, u32[]{:S(2)}) %collective-permute-start.8) | collective-permute-done | bytes 131104 | tf_op jit(solution)/shard_map/ppermute | solution.py:163
  436.7 2.0 fusion.255
  442.5 2.4 collective-permute-done.9
  450.0 2.0 fusion.257
  452.4 1.6 convolution_bitcast_fusion
  454.9 1.7 reshape.633
  461.6 1.6 select_bitcast_fusion
  (261 shorter events, 56.6 us)
Async XLA Ops:
  0.6 1.0 copy-start
  325.6 4.5 copy-start.2
  325.6 5.3 %copy-start.6 = (s32[1,2]{1,0:T(1,128)S(1)}, s32[1,2]{1,0:T(1,128)}, u32[]{:S(2)}) copy-start(s32[1,2]{1,0:T(1,128)} %param.11) | copy-start | bytes 28
  325.6 5.4 %copy-start.1 = (s32[1,8]{1,0:T(1,128)S(1)}, s32[1,8]{1,0:T(1,128)}, u32[]{:S(2)}) copy-start(s32[1,8]{1,0:T(1,128)} %param.10) | copy-start | bytes 100
  327.6 4.6 copy-start.3
  330.3 1.4 collective-permute-start
  331.6 1.2 collective-permute-start.11
  337.4 0.7 collective-permute-start.1
  343.7 0.7 collective-permute-start.2
  350.1 0.9 collective-permute-start.3
  356.6 0.7 collective-permute-start.4
  363.0 32.2 %collective-permute-start.5 = (bf16[4,2,8192]{2,0,1:T(4,128)(2,1)S(1)}, bf16[4,2,8192]{2,0,1:T(4,128)(2,1)S(1)}, u32[]{:S(2)}, u32[]{:S(2)}) collective-permute-start(bf16[4,2,8192]{2,0,1:T(4,128)(2,1)S(1)} %get-tuple-element.75), channel_id=1, source_target_pairs={{2,3},{3,4},{4,5},{5,6},{10,11},{11,12},{12,13},{13,14},{18,19},{1... | collective-permute-start | bytes 393224 | tf_op jit(solution)/shard_map/ppermute | solution.py:163
  400.9 7.8 %collective-permute-start.6 = (bf16[4,2,8192]{2,0,1:T(4,128)(2,1)S(1)}, bf16[4,2,8192]{2,0,1:T(4,128)(2,1)S(1)}, u32[]{:S(2)}, u32[]{:S(2)}) collective-permute-start(bf16[4,2,8192]{2,0,1:T(4,128)(2,1)S(1)} %get-tuple-element.71), channel_id=1, source_target_pairs={{3,4},{4,5},{5,6},{6,7},{11,12},{12,13},{13,14},{14,15},{19,20},{2... | collective-permute-start | bytes 393224 | tf_op jit(solution)/shard_map/ppermute | solution.py:163
  414.3 7.8 %collective-permute-start.7 = (bf16[4,2,8192]{2,0,1:T(4,128)(2,1)S(1)}, bf16[4,2,8192]{2,0,1:T(4,128)(2,1)S(1)}, u32[]{:S(2)}, u32[]{:S(2)}) collective-permute-start(bf16[4,2,8192]{2,0,1:T(4,128)(2,1)S(1)} %get-tuple-element.67), channel_id=1, source_target_pairs={{4,5},{5,6},{6,7},{12,13},{13,14},{14,15},{20,21},{21,22},{22,23},... | collective-permute-start | bytes 393224 | tf_op jit(solution)/shard_map/ppermute | solution.py:163
  427.7 7.8 %collective-permute-start.8 = (bf16[4,2,8192]{2,0,1:T(4,128)(2,1)S(1)}, bf16[4,2,8192]{2,0,1:T(4,128)(2,1)S(1)}, u32[]{:S(2)}, u32[]{:S(2)}) collective-permute-start(bf16[4,2,8192]{2,0,1:T(4,128)(2,1)S(1)} %get-tuple-element.63), channel_id=1, source_target_pairs={{5,6},{6,7},{13,14},{14,15},{21,22},{22,23},{29,30},{30,31}} | collective-permute-start | bytes 393224 | tf_op jit(solution)/shard_map/ppermute | solution.py:163
  441.1 3.8 collective-permute-start.9
  442.4 19.1 %collective-permute-start.12 = (bf16[2,2,2,8,128,128]{5,4,3,2,1,0:T(8,128)(2,1)}, bf16[2,2,2,8,128,128]{5,4,3,2,1,0:T(8,128)(2,1)S(1)}, u32[]{:S(2)}, u32[]{:S(2)}) collective-permute-start(bf16[2,2,2,8,128,128]{5,4,3,2,1,0:T(8,128)(2,1)} %get-tuple-element.47), channel_id=1, source_target_pairs={{0,8},{8,0},{1,9},{9,1},{2,10},{10,2},{3,11},{11,3},{4,12},{12,4},... | collective-permute-start | bytes 6291464 | tf_op jit(solution)/shard_map/ppermute | solution.py:20
  445.4 0.7 copy-start.4
  448.7 8.0 %copy-start.5 = (bf16[4,2,8192]{2,0,1:T(4,128)(2,1)S(1)}, bf16[4,2,8192]{2,0,1:T(4,128)(2,1)}, u32[]{:S(2)}) copy-start(bf16[4,2,8192]{2,0,1:T(4,128)(2,1)} %copy-done.4) | copy-start | bytes 393220
  458.4 1.4 collective-permute-start.10

commit v2 on v0

--- a/solution.py
+++ b/solution.py
@@ -83,11 +83,17 @@
     steps, reqs, width = inputs.shape
     page_len = pool.shape[3]
     chosen = table[moving]
-    outgoing = pool[chosen]
+    outgoing = jnp.stack(
+        [
+            jnp.stack([lax.dynamic_index_in_dim(pool, chosen[m, j], 0, False) for j in range(chosen.shape[1])])
+            for m in range(chosen.shape[0])
+        ]
+    )
+    received = partner(outgoing, "inst", 0)
+    arrived_lens = partner(lens[moving], "inst", 0)
     spots = jnp.arange(chosen.shape[1])[:, None] * page_len + jnp.arange(page_len)[None, :]
-    keep = spots[None, :, :] < lens[moving][:, None, None]
-    outgoing = jnp.where(keep[:, :, None, None, :, None], outgoing, jnp.zeros((), jnp.bfloat16))
-    received = partner(outgoing, "inst", 0)
+    keep = spots[None, :, :] < arrived_lens[:, None, None]
+    arrived = jnp.where(keep[:, :, None, None, :, None], received, jnp.zeros((), jnp.bfloat16))
     flat_pool = pool.reshape((-1,) + pool.shape[2:])
     keys = flat_pool[table * 2]
     values = flat_pool[table * 2 + 1]
@@ -121,7 +127,7 @@
             incoming = lax.ppermute(result, "section", pairs)
     handed = partner(finished[:, moving], "inst", 0)
     finished = finished.at[:, moving].set(handed)
-    return (finished[None, None], received[None, None])
+    return (finished[None, None], arrived[None, None])
 
 
 def solution(mesh):

time: 160 us -> 163 us (1.019)
  between operations: 2.09 us -> 9.58 us
  waiting for transfers between devices: 45.3 us -> 40 us
  other arithmetic: 16.5 us -> 21.3 us
  local copies, waits for them, and re-layouts: 36.7 us -> 32.7 us
    ppermute x10, waiting for transfers between devices: 44 us -> 38.7 us  [per_device(): incoming = lax.ppermute(result, 'section', pairs)]
    gather x2 -> x1, local copies, waits for them, and re-layouts: 4.97 us -> 0.64 us  [per_device(): arrived_lens = partner(lens[moving], 'inst', 0)]
    another operation x0 -> x2, other arithmetic: none -> 3.2 us  [per_device(): jnp.stack([jnp.stack([lax.dynamic_index_in_dim(pool, chosen[m, j], 0, Fal...]
    broadcast_in_dim x0 -> x1, other arithmetic: none -> 3.19 us  [per_device(): return (finished[None, None], arrived[None, None])]
    unnamed x18 -> x17, local copies, waits for them, and re-layouts: 5.94 us -> 2.78 us
    dynamic_slice x0 -> x1, local copies, waits for them, and re-layouts: none -> 2.97 us  [per_device(): lax.dynamic_index_in_dim(pool, chosen[m, j], 0, False)]
  transfers between devices with their start and end apart: 12 -> 13, of which waited for: 6 -> 5; matrix products, arithmetic and copies ran while one was open for 10% -> 11% of each run, Pallas kernels for 0% -> 0%
where the time goes in v2:
time: 163 us; the launch traced here: 161 us
  matrix products  44.7 us (27%)
  waiting for transfers between devices  40 us (25%)
  local copies, waits for them, and re-layouts  32.7 us (20%)
  other arithmetic  21.3 us (13%)
  starting transfers between devices  12.2 us (7%)
  between operations  9.58 us (6%)
    ppermute x10, waiting for transfers between devices, per_device(): incoming = lax.ppermute(result, 'section', pairs)  38.7 us
    dot_general x11, matrix products, layer(): jnp.einsum('rjgxd,rjgpd->rjgxp', wide_query, keys, preferred_element_type...  21.7 us
    dot_general x11, matrix products, layer(): jnp.einsum('rjgxp,rjgpd->rjgxd', cache_w, values, preferred_element_type=...  17.3 us
    ppermute x10, starting transfers between devices, per_device(): incoming = lax.ppermute(result, 'section', pairs)  12.1 us
    gather x1, local copies, waits for them, and re-layouts, per_device(): keys = flat_pool[table * 2]  6.44 us
    gather x1, local copies, waits for them, and re-layouts, per_device(): values = flat_pool[table * 2 + 1]  6.39 us
    reshape x20, local copies, waits for them, and re-layouts, layer(): heads = normed.reshape(steps, reqs, kv_heads, group, head)  3.62 us
  transfers between devices with their start and end apart: 13, of which 5 were waited for; matrix products, arithmetic and copies ran while one was open for 11% of the time, Pallas kernels for 0%

profile of v2, /device:TPU:26, one launch (start us, length us, event | category | flops | bytes accessed | tf_op | source)
XLA Modules:
  0.0 160.5 jit_solution(7752414215474364361)
XLA Ops:
  5.2 6.4 %gather_fusion = bf16[16,8,128,128]{3,2,1,0:T(8,128)(2,1)} fusion(bf16[32,8,128,128]{3,2,1,0:T(8,128)(2,1)} %bitcast.348, s32[1024]{0:T(1024)S(1)} %pad_clamp_fusion.2), kind=kCustom, calls=%fused_computation | custom fusion | bytes 8388672 | tf_op jit(solution)/shard_map/gather | solution.py:98
  11.8 2.0 %fusion.238 = (f32[2,8,32]{2,1,0:T(8,128)S(1)}, f32[2,2,8,32,128]{4,3,2,1,0:T(8,128)S(1)}) fusion(bf16[8,2,8,128,128]{4,3,2,1,0:T(8,128)(2,1)} %bitcast.336, s32[]{:T(128)S(6)} %select_n.369, bf16[2,8,32,128]{3,2,1,0:T(8,128)(2,1)S(1)} %get-tuple-element.95, pred[2,2,128]{2,1,0:T(4,128)(4,1)S(1)} %broadcast_compare_fusion.11), kind=kOutput, calls=%fused_computation.476 | convolution fusion | flops 33947136 | bytes 1706500 | tf_op jit(solution)/shard_map/rjgxd,rjgpd->rjgxp/dot_general | solution.py:44
  14.3 6.4 %gather_fusion.1 = bf16[16,8,128,128]{3,2,1,0:T(8,128)(2,1)} fusion(bf16[32,8,128,128]{3,2,1,0:T(8,128)(2,1)} %bitcast.349, s32[1024]{0:T(1024)S(1)} %pad_clamp_fusion.1), kind=kCustom, calls=%fused_computation.1 | custom fusion | bytes 8388672 | tf_op jit(solution)/shard_map/gather | solution.py:99
  20.7 1.6 convolution_bitcast_fusion.10
  25.7 2.0 %fusion.240 = (f32[2,8,32]{2,1,0:T(8,128)S(1)}, f32[2,2,8,32,128]{4,3,2,1,0:T(8,128)S(1)}) fusion(bf16[8,2,8,128,128]{4,3,2,1,0:T(8,128)(2,1)} %bitcast.337, s32[]{:T(128)S(6)} %select_n.379, bf16[2,8,32,128]{3,2,1,0:T(8,128)(2,1)S(1)} %bitcast.384, pred[2,2,128]{2,1,0:T(4,128)(4,1)S(1)} %get-tuple-element.97), kind=kOutput, calls=%fused_computation.478 | convolution fusion | flops 33947136 | bytes 1706500 | tf_op jit(solution)/shard_map/rjgxd,rjgpd->rjgxp/dot_general | solution.py:44
  32.0 2.0 %fusion.242 = (f32[2,8,32]{2,1,0:T(8,128)S(1)}, f32[2,2,8,32,128]{4,3,2,1,0:T(8,128)S(1)}) fusion(bf16[8,2,8,128,128]{4,3,2,1,0:T(8,128)(2,1)} %bitcast.338, s32[]{:T(128)S(6)} %select_n.385, bf16[2,8,32,128]{3,2,1,0:T(8,128)(2,1)S(1)} %bitcast.388, pred[2,2,128]{2,1,0:T(4,128)(4,1)S(1)} %broadcast_compare_fusion.9), kind=kOutput, calls=%fused_computation.480 | convolution fusion | flops 33947136 | bytes 1706500 | tf_op jit(solution)/shard_map/rjgxd,rjgpd->rjgxp/dot_general | solution.py:44
  38.4 2.0 %fusion.244 = (f32[2,8,32]{2,1,0:T(8,128)S(1)}, f32[2,2,8,32,128]{4,3,2,1,0:T(8,128)S(1)}) fusion(bf16[8,2,8,128,128]{4,3,2,1,0:T(8,128)(2,1)} %bitcast.339, s32[]{:T(128)S(6)} %select_n.391, bf16[2,8,32,128]{3,2,1,0:T(8,128)(2,1)S(1)} %bitcast.390, pred[2,2,128]{2,1,0:T(4,128)(4,1)S(1)} %broadcast_compare_fusion.8), kind=kOutput, calls=%fused_computation.482 | convolution fusion | flops 33947136 | bytes 1706500 | tf_op jit(solution)/shard_map/rjgxd,rjgpd->rjgxp/dot_general | solution.py:44
  44.9 2.0 %fusion.246 = (f32[2,8,32]{2,1,0:T(8,128)S(1)}, f32[2,2,8,32,128]{4,3,2,1,0:T(8,128)S(1)}) fusion(bf16[8,2,8,128,128]{4,3,2,1,0:T(8,128)(2,1)} %bitcast.340, s32[]{:T(128)S(6)} %select_n.397, bf16[2,8,32,128]{3,2,1,0:T(8,128)(2,1)S(1)} %bitcast.392, pred[2,2,128]{2,1,0:T(4,128)(4,1)S(1)} %broadcast_compare_fusion.7), kind=kOutput, calls=%fused_computation.484 | convolution fusion | flops 33947136 | bytes 1706500 | tf_op jit(solution)/shard_map/rjgxd,rjgpd->rjgxp/dot_general | solution.py:44
  51.3 2.0 %fusion.248 = (f32[2,8,32]{2,1,0:T(8,128)S(1)}, f32[2,2,8,32,128]{4,3,2,1,0:T(8,128)S(1)}) fusion(bf16[8,2,8,128,128]{4,3,2,1,0:T(8,128)(2,1)} %bitcast.341, s32[]{:T(128)S(6)} %select_n.403, bf16[2,8,32,128]{3,2,1,0:T(8,128)(2,1)S(1)} %bitcast.394, pred[2,2,128]{2,1,0:T(4,128)(4,1)S(1)} %broadcast_compare_fusion.6), kind=kOutput, calls=%fused_computation.486 | convolution fusion | flops 33947136 | bytes 1706500 | tf_op jit(solution)/shard_map/rjgxd,rjgpd->rjgxp/dot_general | solution.py:44
  57.1 30.9 %collective-permute-done.5 = bf16[4,2,8192]{2,0,1:T(4,128)(2,1)S(1)} collective-permute-done((bf16[4,2,8192]{2,0,1:T(4,128)(2,1)S(1)}, bf16[4,2,8192]{2,0,1:T(4,128)(2,1)S(1)}, u32[]{:S(2)}, u32[]{:S(2)}) %collective-permute-start.5) | collective-permute-done | bytes 131104 | tf_op jit(solution)/shard_map/ppermute | solution.py:127
  89.2 2.0 %fusion.250 = (f32[2,8,32]{2,1,0:T(8,128)S(1)}, f32[2,2,8,32,128]{4,3,2,1,0:T(8,128)S(1)}) fusion(bf16[8,2,8,128,128]{4,3,2,1,0:T(8,128)(2,1)} %bitcast.342, s32[]{:T(128)S(6)} %select_n.409, bf16[2,8,32,128]{3,2,1,0:T(8,128)(2,1)S(1)} %bitcast.396, pred[2,2,128]{2,1,0:T(4,128)(4,1)S(1)} %broadcast_compare_fusion.5), kind=kOutput, calls=%fused_computation.488 | convolution fusion | flops 33947136 | bytes 1706500 | tf_op jit(solution)/shard_map/rjgxd,rjgpd->rjgxp/dot_general | solution.py:44
  93.6 1.9 %collective-permute-start.6 = (bf16[4,2,8192]{2,0,1:T(4,128)(2,1)S(1)}, bf16[4,2,8192]{2,0,1:T(4,128)(2,1)S(1)}, u32[]{:S(2)}, u32[]{:S(2)}) collective-permute-start(bf16[4,2,8192]{2,0,1:T(4,128)(2,1)S(1)} %get-tuple-element.65), channel_id=1, source_target_pairs={{3,4},{4,5},{5,6},{6,7},{11,12},{12,13},{13,14},{14,15},{19,20},{2... | collective-permute-start | bytes 393224 | tf_op jit(solution)/shard_map/ppermute | solution.py:127
  105.6 2.0 %fusion.252 = (f32[2,8,32]{2,1,0:T(8,128)S(1)}, f32[2,2,8,32,128]{4,3,2,1,0:T(8,128)S(1)}) fusion(bf16[8,2,8,128,128]{4,3,2,1,0:T(8,128)(2,1)} %bitcast.343, s32[]{:T(128)S(6)} %select_n.415, bf16[2,8,32,128]{3,2,1,0:T(8,128)(2,1)S(1)} %bitcast.398, pred[2,2,128]{2,1,0:T(4,128)(4,1)S(1)} %broadcast_compare_fusion.4), kind=kOutput, calls=%fused_computation.490 | convolution fusion | flops 33947136 | bytes 1706500 | tf_op jit(solution)/shard_map/rjgxd,rjgpd->rjgxp/dot_general | solution.py:44
  110.0 1.9 %collective-permute-start.7 = (bf16[4,2,8192]{2,0,1:T(4,128)(2,1)S(1)}, bf16[4,2,8192]{2,0,1:T(4,128)(2,1)S(1)}, u32[]{:S(2)}, u32[]{:S(2)}) collective-permute-start(bf16[4,2,8192]{2,0,1:T(4,128)(2,1)S(1)} %get-tuple-element.61), channel_id=1, source_target_pairs={{4,5},{5,6},{6,7},{12,13},{13,14},{14,15},{20,21},{21,22},{22,23},... | collective-permute-start | bytes 393224 | tf_op jit(solution)/shard_map/ppermute | solution.py:127
  111.9 3.0 %dynamic-slice_bitcast_fusion.3 = (bf16[1,2,8,128,128]{4,3,2,1,0:T(8,128)(2,1)}, bf16[1,2,8,128,128]{4,3,2,1,0:T(8,128)(2,1)}, bf16[1,2,8,128,128]{4,3,2,1,0:T(8,128)(2,1)}, bf16[1,2,8,128,128]{4,3,2,1,0:T(8,128)(2,1)}) fusion(bf16[1,1,16,2,8,128,128]{6,5,4,3,2,1,0:T(8,128)(2,1)} %param.8, s32[]{:T(128)S(6)} %select_n.439, s32[]{:T(128)S(6)} %select_n.440, ...), kind=kLoop, calls=%fused_computation.112 | loop fusion | bytes 4194320 | tf_op jit(solution)/shard_map/jit(dynamic_index_in_dim)/dynamic_slice | solution.py:88
  114.9 2.9 %collective-permute-done.7 = bf16[4,2,8192]{2,0,1:T(4,128)(2,1)S(1)} collective-permute-done((bf16[4,2,8192]{2,0,1:T(4,128)(2,1)S(1)}, bf16[4,2,8192]{2,0,1:T(4,128)(2,1)S(1)}, u32[]{:S(2)}, u32[]{:S(2)}) %collective-permute-start.7) | collective-permute-done | bytes 131104 | tf_op jit(solution)/shard_map/ppermute | solution.py:127
  119.0 2.0 %fusion.254 = (f32[2,8,32]{2,1,0:T(8,128)S(1)}, f32[2,2,8,32,128]{4,3,2,1,0:T(8,128)S(1)}) fusion(bf16[8,2,8,128,128]{4,3,2,1,0:T(8,128)(2,1)} %bitcast.344, s32[]{:T(128)S(6)} %select_n.421, bf16[2,8,32,128]{3,2,1,0:T(8,128)(2,1)S(1)} %bitcast.400, pred[2,2,128]{2,1,0:T(4,128)(4,1)S(1)} %broadcast_compare_fusion.3), kind=kOutput, calls=%fused_computation.492 | convolution fusion | flops 33947136 | bytes 1706500 | tf_op jit(solution)/shard_map/rjgxd,rjgpd->rjgxp/dot_general | solution.py:44
  123.4 2.1 %collective-permute-start.8 = (bf16[4,2,8192]{2,0,1:T(4,128)(2,1)S(1)}, bf16[4,2,8192]{2,0,1:T(4,128)(2,1)S(1)}, u32[]{:S(2)}, u32[]{:S(2)}) collective-permute-start(bf16[4,2,8192]{2,0,1:T(4,128)(2,1)S(1)} %get-tuple-element.57), channel_id=1, source_target_pairs={{5,6},{6,7},{13,14},{14,15},{21,22},{22,23},{29,30},{30,31}} | collective-permute-start | bytes 393224 | tf_op jit(solution)/shard_map/ppermute | solution.py:127
  125.6 1.7 %maximum_bitcast_fusion = (bf16[1,2,2,8,128,128]{5,4,3,2,1,0:T(8,128)(2,1)S(1)}, bf16[1,2,2,8,128,128]{5,4,3,2,1,0:T(8,128)(2,1)S(1)}) fusion(bf16[1,2,8,128,128]{4,3,2,1,0:T(8,128)(2,1)} %get-tuple-element.91, bf16[1,2,8,128,128]{4,3,2,1,0:T(8,128)(2,1)} %get-tuple-element.90, bf16[1,2,8,128,128]{4,3,2,1,0:T(8,128)(2,1)} %get-tuple-element.92, ...), kind=kLoop, calls=%fused_computation.85 | loop fusion | flops 1048576 | bytes 4194304 | tf_op jit(solution)/shard_map/stack | solution.py:86
  127.3 3.9 %collective-permute-done.8 = bf16[4,2,8192]{2,0,1:T(4,128)(2,1)S(1)} collective-permute-done((bf16[4,2,8192]{2,0,1:T(4,128)(2,1)S(1)}, bf16[4,2,8192]{2,0,1:T(4,128)(2,1)S(1)}, u32[]{:S(2)}, u32[]{:S(2)}) %collective-permute-start.8) | collective-permute-done | bytes 131104 | tf_op jit(solution)/shard_map/ppermute | solution.py:127
  136.2 2.0 %fusion.256 = (f32[2,8,32]{2,1,0:T(8,128)S(1)}, f32[2,2,8,32,128]{4,3,2,1,0:T(8,128)S(1)}) fusion(bf16[8,2,8,128,128]{4,3,2,1,0:T(8,128)(2,1)} %bitcast.345, s32[]{:T(128)S(6)} %select_n.427, bf16[2,8,32,128]{3,2,1,0:T(8,128)(2,1)} %bitcast.402, pred[2,2,128]{2,1,0:T(4,128)(4,1)S(1)} %broadcast_compare_fusion.2), kind=kOutput, calls=%fused_computation.494 | convolution fusion | flops 33947136 | bytes 1706500 | tf_op jit(solution)/shard_map/rjgxd,rjgpd->rjgxp/dot_general | solution.py:44
  141.2 1.8 %reshape.671 = f32[4,2,8192]{2,0,1:T(4,128)} reshape(f32[4,2,8,8,128]{4,3,2,0,1:T(8,128)} %copy.258) | data formatting | bytes 524288 | tf_op jit(solution)/shard_map/reshape | solution.py:71
  149.1 2.0 %fusion.258 = (f32[2,8,32]{2,1,0:T(8,128)S(1)}, f32[2,2,8,32,128]{4,3,2,1,0:T(8,128)S(1)}) fusion(bf16[8,2,8,128,128]{4,3,2,1,0:T(8,128)(2,1)} %bitcast.346, s32[]{:T(128)S(6)} %select_n.433, bf16[2,8,32,128]{3,2,1,0:T(8,128)(2,1)S(1)} %bitcast.386, pred[2,2,128]{2,1,0:T(4,128)(4,1)S(1)} %broadcast_compare_fusion.1), kind=kOutput, calls=%fused_computation.496 | convolution fusion | flops 33947136 | bytes 1706500 | tf_op jit(solution)/shard_map/rjgxd,rjgpd->rjgxp/dot_general | solution.py:44
  157.3 3.2 %select_bitcast_fusion = bf16[1,1,2,2,2,8,128,128]{7,6,5,4,3,2,1,0:T(8,128)(2,1)} fusion(bf16[2,2,2,8,128,128]{5,4,3,2,1,0:T(8,128)(2,1)} %collective-permute-done.12, pred[2,2,128]{2,1,0:T(4,128)(4,1)S(1)} %get-tuple-element.96), kind=kLoop, calls=%fused_computation.7 | loop fusion | flops 1048576 | bytes 4194816 | tf_op jit(solution)/shard_map/broadcast_in_dim | solution.py:130
  (275 shorter events, 61.5 us)
Async XLA Ops:
  0.6 1.0 copy-start
  20.7 2.2 %copy-start.2 = (f32[1,8192]{1,0:T(1,128)S(1)}, f32[1,8192]{1,0:T(1,128)}, u32[]{:S(2)}) copy-start(f32[1,8192]{1,0:T(1,128)} %param.13) | copy-start | bytes 98308
  20.7 3.1 %copy-start.7 = (s32[1,2]{1,0:T(1,128)S(1)}, s32[1,2]{1,0:T(1,128)}, u32[]{:S(2)}) copy-start(s32[1,2]{1,0:T(1,128)} %param.11) | copy-start | bytes 28
  20.7 3.1 %copy-start.1 = (s32[1,8]{1,0:T(1,128)S(1)}, s32[1,8]{1,0:T(1,128)}, u32[]{:S(2)}) copy-start(s32[1,8]{1,0:T(1,128)} %param.10) | copy-start | bytes 100
  20.7 4.3 %copy-start.3 = (f32[1,8192]{1,0:T(1,128)S(1)}, f32[1,8192]{1,0:T(1,128)}, u32[]{:S(2)}) copy-start(f32[1,8192]{1,0:T(1,128)} %param.12) | copy-start | bytes 98308
  23.0 1.4 collective-permute-start
  24.4 1.2 collective-permute-start.11
  30.1 0.7 collective-permute-start.1
  36.5 0.7 collective-permute-start.2
  42.8 0.9 collective-permute-start.3
  49.4 0.7 collective-permute-start.4
  55.8 32.2 %collective-permute-start.5 = (bf16[4,2,8192]{2,0,1:T(4,128)(2,1)S(1)}, bf16[4,2,8192]{2,0,1:T(4,128)(2,1)S(1)}, u32[]{:S(2)}, u32[]{:S(2)}) collective-permute-start(bf16[4,2,8192]{2,0,1:T(4,128)(2,1)S(1)} %get-tuple-element.69), channel_id=1, source_target_pairs={{2,3},{3,4},{4,5},{5,6},{10,11},{11,12},{12,13},{13,14},{18,19},{1... | collective-permute-start | bytes 393224 | tf_op jit(solution)/shard_map/ppermute | solution.py:127
  89.0 6.6 %copy-start.6 = (s32[1,8,2]{1,2,0:T(2,128)S(1)}, s32[1,8,2]{1,2,0:T(2,128)}, u32[]{:S(2)}) copy-start(s32[1,8,2]{1,2,0:T(2,128)} %param.9) | copy-start | bytes 196
  93.6 10.7 %collective-permute-start.6 = (bf16[4,2,8192]{2,0,1:T(4,128)(2,1)S(1)}, bf16[4,2,8192]{2,0,1:T(4,128)(2,1)S(1)}, u32[]{:S(2)}, u32[]{:S(2)}) collective-permute-start(bf16[4,2,8192]{2,0,1:T(4,128)(2,1)S(1)} %get-tuple-element.65), channel_id=1, source_target_pairs={{3,4},{4,5},{5,6},{6,7},{11,12},{12,13},{13,14},{14,15},{19,20},{2... | collective-permute-start | bytes 393224 | tf_op jit(solution)/shard_map/ppermute | solution.py:127
  110.0 7.8 %collective-permute-start.7 = (bf16[4,2,8192]{2,0,1:T(4,128)(2,1)S(1)}, bf16[4,2,8192]{2,0,1:T(4,128)(2,1)S(1)}, u32[]{:S(2)}, u32[]{:S(2)}) collective-permute-start(bf16[4,2,8192]{2,0,1:T(4,128)(2,1)S(1)} %get-tuple-element.61), channel_id=1, source_target_pairs={{4,5},{5,6},{6,7},{12,13},{13,14},{14,15},{20,21},{21,22},{22,23},... | collective-permute-start | bytes 393224 | tf_op jit(solution)/shard_map/ppermute | solution.py:127
  123.4 7.8 %collective-permute-start.8 = (bf16[4,2,8192]{2,0,1:T(4,128)(2,1)S(1)}, bf16[4,2,8192]{2,0,1:T(4,128)(2,1)S(1)}, u32[]{:S(2)}, u32[]{:S(2)}) collective-permute-start(bf16[4,2,8192]{2,0,1:T(4,128)(2,1)S(1)} %get-tuple-element.57), channel_id=1, source_target_pairs={{5,6},{6,7},{13,14},{14,15},{21,22},{22,23},{29,30},{30,31}} | collective-permute-start | bytes 393224 | tf_op jit(solution)/shard_map/ppermute | solution.py:127
  131.6 0.7 copy-start.4
  135.0 8.0 %copy-start.5 = (bf16[4,2,8192]{2,0,1:T(4,128)(2,1)S(1)}, bf16[4,2,8192]{2,0,1:T(4,128)(2,1)}, u32[]{:S(2)}) copy-start(bf16[4,2,8192]{2,0,1:T(4,128)(2,1)} %copy-done.4) | copy-start | bytes 393220
  144.0 3.8 %collective-permute-start.9 = (bf16[4,2,8192]{2,0,1:T(4,128)(2,1)S(1)}, bf16[4,2,8192]{2,0,1:T(4,128)(2,1)S(1)}, u32[]{:S(2)}, u32[]{:S(2)}) collective-permute-start(bf16[4,2,8192]{2,0,1:T(4,128)(2,1)S(1)} %get-tuple-element.53), channel_id=1, source_target_pairs={{6,7},{14,15},{22,23},{30,31}} | collective-permute-start | bytes 393224 | tf_op jit(solution)/shard_map/ppermute | solution.py:127
  146.9 10.5 %collective-permute-start.12 = (bf16[2,2,2,8,128,128]{5,4,3,2,1,0:T(8,128)(2,1)}, bf16[2,2,2,8,128,128]{5,4,3,2,1,0:T(8,128)(2,1)}, u32[]{:S(2)}, u32[]{:S(2)}) collective-permute-start(bf16[2,2,2,8,128,128]{5,4,3,2,1,0:T(8,128)(2,1)} %pad_maximum_fusion), channel_id=1, source_target_pairs={{0,8},{8,0},{1,9},{9,1},{2,10},{10,2},{3,11},{11,3},{4,12},{12,4},... | collective-permute-start | bytes 6291464 | tf_op jit(solution)/shard_map/ppermute | solution.py:18
  154.2 1.4 collective-permute-start.10

commit v3 on v0

--- a/solution.py
+++ b/solution.py
@@ -41,12 +41,12 @@
     factor = 1.0 / math.sqrt(head)
     wide_query = jnp.broadcast_to(query[:, None], (reqs, pages) + query.shape[1:])
     cache_scores = (
-        jnp.einsum("rjgxd,rjgpd->rjgxp", wide_query, keys, preferred_element_type=jnp.float32)
+        jnp.einsum("rjgpd,rjgxd->rjgpx", keys, wide_query, preferred_element_type=jnp.float32)
         * factor
     )
     positions = jnp.arange(pages)[:, None] * page_len + jnp.arange(page_len)[None, :]
     live = positions[None] < lens[:, None, None]
-    cache_scores = jnp.where(live[:, :, None, None, :], cache_scores, -1e30)
+    cache_scores = jnp.where(live[:, :, None, :, None], cache_scores, -1e30)
     new_scores = (
         jnp.einsum("rgxd,rgsd->rgxs", query, fresh, preferred_element_type=jnp.float32) * factor
     )
@@ -54,15 +54,15 @@
     done = jnp.arange(steps)[None, :] <= step_of[:, None]
     new_scores = jnp.where(done[None, None], new_scores, -1e30)
     top = jnp.maximum(
-        jnp.max(cache_scores, axis=(1, 4)), jnp.max(new_scores, axis=-1)
-    )[..., None]
-    cache_exp = jnp.exp(cache_scores - top[:, None])
-    new_exp = jnp.exp(new_scores - top)
-    total = jnp.sum(cache_exp, axis=(1, 4))[..., None] + jnp.sum(new_exp, axis=-1, keepdims=True)
-    cache_w = (cache_exp / total[:, None]).astype(jnp.bfloat16)
-    new_w = (new_exp / total).astype(jnp.bfloat16)
+        jnp.max(cache_scores, axis=(1, 3)), jnp.max(new_scores, axis=-1)
+    )
+    cache_exp = jnp.exp(cache_scores - top[:, None, :, None, :])
+    new_exp = jnp.exp(new_scores - top[..., None])
+    total = jnp.sum(cache_exp, axis=(1, 3)) + jnp.sum(new_exp, axis=-1)
+    cache_w = (cache_exp / total[:, None, :, None, :]).astype(jnp.bfloat16)
+    new_w = (new_exp / total[..., None]).astype(jnp.bfloat16)
     attended = jnp.einsum(
-        "rjgxp,rjgpd->rjgxd", cache_w, values, preferred_element_type=jnp.float32
+        "rjgpx,rjgpd->rjgxd", cache_w, values, preferred_element_type=jnp.float32
     ).sum(axis=1)
     attended = attended + jnp.einsum(
         "rgxs,rgsd->rgxd", new_w, fresh, preferred_element_type=jnp.float32

time: 160 us -> 160 us (level)
  no operation moved by 1% of the time
where the time goes in v3:
time: 160 us; the launch traced here: 157 us
  waiting for transfers between devices  45.3 us (28%)
  matrix products  44.6 us (28%)
  local copies, waits for them, and re-layouts  36.7 us (23%)
  other arithmetic  16.5 us (10%)
  starting transfers between devices  12.2 us (8%)
  between operations  2.09 us (1%)
    ppermute x10, waiting for transfers between devices, per_device(): incoming = lax.ppermute(result, 'section', pairs)  44 us
    dot_general x11, matrix products, layer(): jnp.einsum('rjgpd,rjgxd->rjgpx', keys, wide_query, preferred_element_type...  21.6 us
    dot_general x11, matrix products, layer(): jnp.einsum('rjgpx,rjgpd->rjgxd', cache_w, values, preferred_element_type=...  17.3 us
    ppermute x10, starting transfers between devices, per_device(): incoming = lax.ppermute(result, 'section', pairs)  12.1 us
    gather x1, local copies, waits for them, and re-layouts, per_device(): keys = flat_pool[table * 2]  6.44 us
    gather x1, local copies, waits for them, and re-layouts, per_device(): values = flat_pool[table * 2 + 1]  6.39 us
    unnamed x18, local copies, waits for them, and re-layouts  5.94 us
    gather x1, local copies, waits for them, and re-layouts, per_device(): outgoing = pool[chosen]  4.33 us
  transfers between devices with their start and end apart: 12, of which 6 were waited for; matrix products, arithmetic and copies ran while one was open for 10% of the time, Pallas kernels for 0%

profile of v3, /device:TPU:26, one launch (start us, length us, event | category | flops | bytes accessed | tf_op | source)
XLA Modules:
  0.0 157.4 jit_solution(3250623407680983223)
XLA Ops:
  5.2 6.4 %gather_fusion = bf16[16,8,128,128]{3,2,1,0:T(8,128)(2,1)} fusion(bf16[32,8,128,128]{3,2,1,0:T(8,128)(2,1)} %bitcast.337, s32[1024]{0:T(1024)S(1)} %pad_clamp_fusion.3), kind=kCustom, calls=%fused_computation | custom fusion | bytes 8388672 | tf_op jit(solution)/shard_map/gather | solution.py:92
  11.8 2.0 %fusion.237 = (f32[2,8,32]{2,1,0:T(8,128)S(1)}, f32[2,2,8,128,32]{3,4,2,1,0:T(8,128)S(1)}) fusion(bf16[2,8,32,128]{3,2,1,0:T(8,128)(2,1)S(1)} %get-tuple-element.91, bf16[8,2,8,128,128]{4,3,2,1,0:T(8,128)(2,1)} %bitcast.325, s32[]{:T(128)S(6)} %select_n.366, pred[2,2,128]{2,1,0:T(4,128)(4,1)S(1)} %broadcast_compare_fusion.11), kind=kOutput, calls=%fused_computation.471 | convolution fusion | flops 33947136 | bytes 1706500 | tf_op jit(solution)/shard_map/rjgpd,rjgxd->rjgpx/dot_general | solution.py:44
  14.3 6.4 %gather_fusion.1 = bf16[16,8,128,128]{3,2,1,0:T(8,128)(2,1)} fusion(bf16[32,8,128,128]{3,2,1,0:T(8,128)(2,1)} %bitcast.338, s32[1024]{0:T(1024)S(1)} %pad_clamp_fusion.2), kind=kCustom, calls=%fused_computation.1 | custom fusion | bytes 8388672 | tf_op jit(solution)/shard_map/gather | solution.py:93
  20.7 1.6 %convolution_bitcast_fusion.10 = f32[2,8,32,128]{3,2,1,0:T(8,128)S(1)} fusion(bf16[8,2,8,128,128]{4,3,2,1,0:T(8,128)(2,1)} %bitcast.341, s32[]{:T(128)S(6)} %select_n.366, f32[2,2,8,128,32]{3,4,2,1,0:T(8,128)S(1)} %get-tuple-element.97, f32[2,8,32]{2,1,0:T(8,128)S(1)} %add.590, f32[2,8,32]{2,1,0:T(8,128)S(1)} %max.156), kind=kOutput, calls=%fused_computation.62 | convolution fusion | flops 33947648 | bytes 1839108 | tf_op jit(solution)/shard_map/rjgpx,rjgpd->rjgxd/dot_general | solution.py:64
  25.6 2.0 %fusion.239 = (f32[2,8,32]{2,1,0:T(8,128)S(1)}, f32[2,2,8,128,32]{3,4,2,1,0:T(8,128)S(1)}) fusion(bf16[2,8,32,128]{3,2,1,0:T(8,128)(2,1)S(1)} %bitcast.377, bf16[8,2,8,128,128]{4,3,2,1,0:T(8,128)(2,1)} %bitcast.326, s32[]{:T(128)S(6)} %select_n.376, pred[2,2,128]{2,1,0:T(4,128)(4,1)S(1)} %get-tuple-element.93), kind=kOutput, calls=%fused_computation.473 | convolution fusion | flops 33947136 | bytes 1706500 | tf_op jit(solution)/shard_map/rjgpd,rjgxd->rjgpx/dot_general | solution.py:44
  32.0 2.0 %fusion.241 = (f32[2,8,32]{2,1,0:T(8,128)S(1)}, f32[2,2,8,128,32]{3,4,2,1,0:T(8,128)S(1)}) fusion(bf16[2,8,32,128]{3,2,1,0:T(8,128)(2,1)S(1)} %bitcast.379, bf16[8,2,8,128,128]{4,3,2,1,0:T(8,128)(2,1)} %bitcast.327, s32[]{:T(128)S(6)} %select_n.382, pred[2,2,128]{2,1,0:T(4,128)(4,1)S(1)} %broadcast_compare_fusion.9), kind=kOutput, calls=%fused_computation.475 | convolution fusion | flops 33947136 | bytes 1706500 | tf_op jit(solution)/shard_map/rjgpd,rjgxd->rjgpx/dot_general | solution.py:44
  38.4 2.0 %fusion.243 = (f32[2,8,32]{2,1,0:T(8,128)S(1)}, f32[2,2,8,128,32]{3,4,2,1,0:T(8,128)S(1)}) fusion(bf16[2,8,32,128]{3,2,1,0:T(8,128)(2,1)S(1)} %bitcast.381, bf16[8,2,8,128,128]{4,3,2,1,0:T(8,128)(2,1)} %bitcast.328, s32[]{:T(128)S(6)} %select_n.388, pred[2,2,128]{2,1,0:T(4,128)(4,1)S(1)} %broadcast_compare_fusion.8), kind=kOutput, calls=%fused_computation.477 | convolution fusion | flops 33947136 | bytes 1706500 | tf_op jit(solution)/shard_map/rjgpd,rjgxd->rjgpx/dot_general | solution.py:44
  44.9 2.0 %fusion.245 = (f32[2,8,32]{2,1,0:T(8,128)S(1)}, f32[2,2,8,128,32]{3,4,2,1,0:T(8,128)S(1)}) fusion(bf16[2,8,32,128]{3,2,1,0:T(8,128)(2,1)S(1)} %bitcast.383, bf16[8,2,8,128,128]{4,3,2,1,0:T(8,128)(2,1)} %bitcast.329, s32[]{:T(128)S(6)} %select_n.394, pred[2,2,128]{2,1,0:T(4,128)(4,1)S(1)} %broadcast_compare_fusion.7), kind=kOutput, calls=%fused_computation.479 | convolution fusion | flops 33947136 | bytes 1706500 | tf_op jit(solution)/shard_map/rjgpd,rjgxd->rjgpx/dot_general | solution.py:44
  51.3 2.0 %fusion.247 = (f32[2,8,32]{2,1,0:T(8,128)S(1)}, f32[2,2,8,128,32]{3,4,2,1,0:T(8,128)S(1)}) fusion(bf16[2,8,32,128]{3,2,1,0:T(8,128)(2,1)S(1)} %bitcast.385, bf16[8,2,8,128,128]{4,3,2,1,0:T(8,128)(2,1)} %bitcast.330, s32[]{:T(128)S(6)} %select_n.400, pred[2,2,128]{2,1,0:T(4,128)(4,1)S(1)} %broadcast_compare_fusion.6), kind=kOutput, calls=%fused_computation.481 | convolution fusion | flops 33947136 | bytes 1706500 | tf_op jit(solution)/shard_map/rjgpd,rjgxd->rjgpx/dot_general | solution.py:44
  57.0 30.9 %collective-permute-done.5 = bf16[4,2,8192]{2,0,1:T(4,128)(2,1)S(1)} collective-permute-done((bf16[4,2,8192]{2,0,1:T(4,128)(2,1)S(1)}, bf16[4,2,8192]{2,0,1:T(4,128)(2,1)S(1)}, u32[]{:S(2)}, u32[]{:S(2)}) %collective-permute-start.5) | collective-permute-done | bytes 131104 | tf_op jit(solution)/shard_map/ppermute | solution.py:121
  89.2 2.0 %fusion.249 = (f32[2,8,32]{2,1,0:T(8,128)S(1)}, f32[2,2,8,128,32]{3,4,2,1,0:T(8,128)S(1)}) fusion(bf16[2,8,32,128]{3,2,1,0:T(8,128)(2,1)S(1)} %bitcast.387, bf16[8,2,8,128,128]{4,3,2,1,0:T(8,128)(2,1)} %bitcast.331, s32[]{:T(128)S(6)} %select_n.406, pred[2,2,128]{2,1,0:T(4,128)(4,1)S(1)} %broadcast_compare_fusion.5), kind=kOutput, calls=%fused_computation.483 | convolution fusion | flops 33947136 | bytes 1706500 | tf_op jit(solution)/shard_map/rjgpd,rjgxd->rjgpx/dot_general | solution.py:44
  93.6 1.9 %collective-permute-start.6 = (bf16[4,2,8192]{2,0,1:T(4,128)(2,1)S(1)}, bf16[4,2,8192]{2,0,1:T(4,128)(2,1)S(1)}, u32[]{:S(2)}, u32[]{:S(2)}) collective-permute-start(bf16[4,2,8192]{2,0,1:T(4,128)(2,1)S(1)} %get-tuple-element.65), channel_id=1, source_target_pairs={{3,4},{4,5},{5,6},{6,7},{11,12},{12,13},{13,14},{14,15},{19,20},{2... | collective-permute-start | bytes 393224 | tf_op jit(solution)/shard_map/ppermute | solution.py:121
  95.6 5.8 %collective-permute-done.6 = bf16[4,2,8192]{2,0,1:T(4,128)(2,1)S(1)} collective-permute-done((bf16[4,2,8192]{2,0,1:T(4,128)(2,1)S(1)}, bf16[4,2,8192]{2,0,1:T(4,128)(2,1)S(1)}, u32[]{:S(2)}, u32[]{:S(2)}) %collective-permute-start.6) | collective-permute-done | bytes 131104 | tf_op jit(solution)/shard_map/ppermute | solution.py:121
  102.6 2.0 %fusion.251 = (f32[2,8,32]{2,1,0:T(8,128)S(1)}, f32[2,2,8,128,32]{3,4,2,1,0:T(8,128)S(1)}) fusion(bf16[2,8,32,128]{3,2,1,0:T(8,128)(2,1)S(1)} %bitcast.389, bf16[8,2,8,128,128]{4,3,2,1,0:T(8,128)(2,1)} %bitcast.332, s32[]{:T(128)S(6)} %select_n.412, pred[2,2,128]{2,1,0:T(4,128)(4,1)S(1)} %broadcast_compare_fusion.4), kind=kOutput, calls=%fused_computation.485 | convolution fusion | flops 33947136 | bytes 1706500 | tf_op jit(solution)/shard_map/rjgpd,rjgxd->rjgpx/dot_general | solution.py:44
  107.0 1.9 %collective-permute-start.7 = (bf16[4,2,8192]{2,0,1:T(4,128)(2,1)S(1)}, bf16[4,2,8192]{2,0,1:T(4,128)(2,1)S(1)}, u32[]{:S(2)}, u32[]{:S(2)}) collective-permute-start(bf16[4,2,8192]{2,0,1:T(4,128)(2,1)S(1)} %get-tuple-element.61), channel_id=1, source_target_pairs={{4,5},{5,6},{6,7},{12,13},{13,14},{14,15},{20,21},{21,22},{22,23},... | collective-permute-start | bytes 393224 | tf_op jit(solution)/shard_map/ppermute | solution.py:121
  109.6 5.2 %collective-permute-done.7 = bf16[4,2,8192]{2,0,1:T(4,128)(2,1)S(1)} collective-permute-done((bf16[4,2,8192]{2,0,1:T(4,128)(2,1)S(1)}, bf16[4,2,8192]{2,0,1:T(4,128)(2,1)S(1)}, u32[]{:S(2)}, u32[]{:S(2)}) %collective-permute-start.7) | collective-permute-done | bytes 131104 | tf_op jit(solution)/shard_map/ppermute | solution.py:121
  116.0 2.0 %fusion.253 = (f32[2,8,32]{2,1,0:T(8,128)S(1)}, f32[2,2,8,128,32]{3,4,2,1,0:T(8,128)S(1)}) fusion(bf16[2,8,32,128]{3,2,1,0:T(8,128)(2,1)S(1)} %bitcast.391, bf16[8,2,8,128,128]{4,3,2,1,0:T(8,128)(2,1)} %bitcast.333, s32[]{:T(128)S(6)} %select_n.418, pred[2,2,128]{2,1,0:T(4,128)(4,1)S(1)} %broadcast_compare_fusion.3), kind=kOutput, calls=%fused_computation.487 | convolution fusion | flops 33947136 | bytes 1706500 | tf_op jit(solution)/shard_map/rjgpd,rjgxd->rjgpx/dot_general | solution.py:44
  120.5 2.1 %collective-permute-start.8 = (bf16[4,2,8192]{2,0,1:T(4,128)(2,1)S(1)}, bf16[4,2,8192]{2,0,1:T(4,128)(2,1)S(1)}, u32[]{:S(2)}, u32[]{:S(2)}) collective-permute-start(bf16[4,2,8192]{2,0,1:T(4,128)(2,1)S(1)} %get-tuple-element.57), channel_id=1, source_target_pairs={{5,6},{6,7},{13,14},{14,15},{21,22},{22,23},{29,30},{30,31}} | collective-permute-start | bytes 393224 | tf_op jit(solution)/shard_map/ppermute | solution.py:121
  122.7 4.3 %gather_fusion.5 = bf16[4,2,8,128,128]{4,3,2,1,0:T(8,128)(2,1)S(1)} fusion(bf16[16,2,8,128,128]{4,3,2,1,0:T(8,128)(2,1)} %bitcast.339, s32[1024]{0:T(1024)S(1)} %pad_clamp_fusion), kind=kCustom, calls=%fused_computation.5 | custom fusion | bytes 4194320 | tf_op jit(solution)/shard_map/gather | solution.py:86
  133.3 2.0 %fusion.255 = (f32[2,8,32]{2,1,0:T(8,128)S(1)}, f32[2,2,8,128,32]{3,4,2,1,0:T(8,128)S(1)}) fusion(bf16[2,8,32,128]{3,2,1,0:T(8,128)(2,1)} %bitcast.393, bf16[8,2,8,128,128]{4,3,2,1,0:T(8,128)(2,1)} %bitcast.334, s32[]{:T(128)S(6)} %select_n.424, pred[2,2,128]{2,1,0:T(4,128)(4,1)S(1)} %broadcast_compare_fusion.2), kind=kOutput, calls=%fused_computation.489 | convolution fusion | flops 33947136 | bytes 1706500 | tf_op jit(solution)/shard_map/rjgpd,rjgxd->rjgpx/dot_general | solution.py:44
  138.1 1.8 %reshape.669 = f32[4,2,8192]{2,0,1:T(4,128)} reshape(f32[4,2,8,8,128]{4,3,2,0,1:T(8,128)} %copy.258) | data formatting | bytes 524288 | tf_op jit(solution)/shard_map/reshape | solution.py:71
  142.3 1.6 %broadcast_select_fusion = bf16[2,2,2,8,128,128]{5,4,3,2,1,0:T(8,128)(2,1)} fusion(bf16[2,2,2,8,128,128]{5,4,3,2,1,0:T(8,128)(2,1)S(1)} %bitcast.340, pred[2,2,128]{2,1,0:T(4,128)(4,1)S(1)} %get-tuple-element.92), kind=kLoop, calls=%fused_computation.7 | loop fusion | flops 1048576 | bytes 4194816 | tf_op jit(solution)/shard_map/jit(_where)/select_n | solution.py:89
  146.0 2.0 %fusion.257 = (f32[2,8,32]{2,1,0:T(8,128)S(1)}, f32[2,2,8,128,32]{3,4,2,1,0:T(8,128)S(1)}) fusion(bf16[2,8,32,128]{3,2,1,0:T(8,128)(2,1)S(1)} %bitcast.375, bf16[8,2,8,128,128]{4,3,2,1,0:T(8,128)(2,1)} %bitcast.335, s32[]{:T(128)S(6)} %select_n.430, pred[2,2,128]{2,1,0:T(4,128)(4,1)S(1)} %broadcast_compare_fusion.1), kind=kOutput, calls=%fused_computation.491 | convolution fusion | flops 33947136 | bytes 1706500 | tf_op jit(solution)/shard_map/rjgpd,rjgxd->rjgpx/dot_general | solution.py:44
  154.3 3.2 %copy.497 = bf16[1,1,2,2,2,8,128,128]{7,6,5,4,3,2,1,0:T(8,128)(2,1)} copy(bf16[1,1,2,2,2,8,128,128]{7,6,5,4,3,2,1,0:T(8,128)(2,1)} %bitcast.127) | data formatting | bytes 4194304
  (274 shorter events, 60.6 us)
Async XLA Ops:
  0.6 1.0 copy-start
  20.7 2.2 %copy-start.2 = (f32[1,8192]{1,0:T(1,128)S(1)}, f32[1,8192]{1,0:T(1,128)}, u32[]{:S(2)}) copy-start(f32[1,8192]{1,0:T(1,128)} %param.13) | copy-start | bytes 98308
  20.7 3.1 %copy-start.7 = (s32[1,2]{1,0:T(1,128)S(1)}, s32[1,2]{1,0:T(1,128)}, u32[]{:S(2)}) copy-start(s32[1,2]{1,0:T(1,128)} %param.11) | copy-start | bytes 28
  20.7 3.1 %copy-start.1 = (s32[1,8]{1,0:T(1,128)S(1)}, s32[1,8]{1,0:T(1,128)}, u32[]{:S(2)}) copy-start(s32[1,8]{1,0:T(1,128)} %param.10) | copy-start | bytes 100
  20.7 4.3 %copy-start.3 = (f32[1,8192]{1,0:T(1,128)S(1)}, f32[1,8192]{1,0:T(1,128)}, u32[]{:S(2)}) copy-start(f32[1,8192]{1,0:T(1,128)} %param.12) | copy-start | bytes 98308
  23.0 1.4 collective-permute-start
  30.1 0.7 collective-permute-start.1
  36.5 0.7 collective-permute-start.2
  42.8 0.9 collective-permute-start.3
  49.4 0.7 collective-permute-start.4
  55.7 32.2 %collective-permute-start.5 = (bf16[4,2,8192]{2,0,1:T(4,128)(2,1)S(1)}, bf16[4,2,8192]{2,0,1:T(4,128)(2,1)S(1)}, u32[]{:S(2)}, u32[]{:S(2)}) collective-permute-start(bf16[4,2,8192]{2,0,1:T(4,128)(2,1)S(1)} %get-tuple-element.69), channel_id=1, source_target_pairs={{2,3},{3,4},{4,5},{5,6},{10,11},{11,12},{12,13},{13,14},{18,19},{1... | collective-permute-start | bytes 393224 | tf_op jit(solution)/shard_map/ppermute | solution.py:121
  93.6 7.8 %collective-permute-start.6 = (bf16[4,2,8192]{2,0,1:T(4,128)(2,1)S(1)}, bf16[4,2,8192]{2,0,1:T(4,128)(2,1)S(1)}, u32[]{:S(2)}, u32[]{:S(2)}) collective-permute-start(bf16[4,2,8192]{2,0,1:T(4,128)(2,1)S(1)} %get-tuple-element.65), channel_id=1, source_target_pairs={{3,4},{4,5},{5,6},{6,7},{11,12},{12,13},{13,14},{14,15},{19,20},{2... | collective-permute-start | bytes 393224 | tf_op jit(solution)/shard_map/ppermute | solution.py:121
  102.4 6.6 %copy-start.6 = (s32[1,8,2]{1,2,0:T(2,128)S(1)}, s32[1,8,2]{1,2,0:T(2,128)}, u32[]{:S(2)}) copy-start(s32[1,8,2]{1,2,0:T(2,128)} %param.9) | copy-start | bytes 196
  107.0 7.8 %collective-permute-start.7 = (bf16[4,2,8192]{2,0,1:T(4,128)(2,1)S(1)}, bf16[4,2,8192]{2,0,1:T(4,128)(2,1)S(1)}, u32[]{:S(2)}, u32[]{:S(2)}) collective-permute-start(bf16[4,2,8192]{2,0,1:T(4,128)(2,1)S(1)} %get-tuple-element.61), channel_id=1, source_target_pairs={{4,5},{5,6},{6,7},{12,13},{13,14},{14,15},{20,21},{21,22},{22,23},... | collective-permute-start | bytes 393224 | tf_op jit(solution)/shard_map/ppermute | solution.py:121
  120.5 7.8 %collective-permute-start.8 = (bf16[4,2,8192]{2,0,1:T(4,128)(2,1)S(1)}, bf16[4,2,8192]{2,0,1:T(4,128)(2,1)S(1)}, u32[]{:S(2)}, u32[]{:S(2)}) collective-permute-start(bf16[4,2,8192]{2,0,1:T(4,128)(2,1)S(1)} %get-tuple-element.57), channel_id=1, source_target_pairs={{5,6},{6,7},{13,14},{14,15},{21,22},{22,23},{29,30},{30,31}} | collective-permute-start | bytes 393224 | tf_op jit(solution)/shard_map/ppermute | solution.py:121
  128.7 0.7 copy-start.4
  132.0 7.9 %copy-start.5 = (bf16[4,2,8192]{2,0,1:T(4,128)(2,1)S(1)}, bf16[4,2,8192]{2,0,1:T(4,128)(2,1)}, u32[]{:S(2)}) copy-start(bf16[4,2,8192]{2,0,1:T(4,128)(2,1)} %copy-done.4) | copy-start | bytes 393220
  141.0 3.8 %collective-permute-start.9 = (bf16[4,2,8192]{2,0,1:T(4,128)(2,1)S(1)}, bf16[4,2,8192]{2,0,1:T(4,128)(2,1)S(1)}, u32[]{:S(2)}, u32[]{:S(2)}) collective-permute-start(bf16[4,2,8192]{2,0,1:T(4,128)(2,1)S(1)} %get-tuple-element.53), channel_id=1, source_target_pairs={{6,7},{14,15},{22,23},{30,31}} | collective-permute-start | bytes 393224 | tf_op jit(solution)/shard_map/ppermute | solution.py:121
  143.9 10.4 %collective-permute-start.11 = (bf16[2,2,2,8,128,128]{5,4,3,2,1,0:T(8,128)(2,1)}, bf16[2,2,2,8,128,128]{5,4,3,2,1,0:T(8,128)(2,1)}, u32[]{:S(2)}, u32[]{:S(2)}) collective-permute-start(bf16[2,2,2,8,128,128]{5,4,3,2,1,0:T(8,128)(2,1)} %broadcast_select_fusion), channel_id=1, source_target_pairs={{0,8},{8,0},{1,9},{9,1},{2,10},{10,2},{3,11},{11,3},{4,12},{12,4},... | collective-permute-start | bytes 6291464 | tf_op jit(solution)/shard_map/ppermute | solution.py:18
  151.1 1.4 collective-permute-start.10

commit v4 on v3

--- a/solution.py
+++ b/solution.py
@@ -117,7 +117,13 @@
             finished, jnp.where(live, result, previous), (zero, start, zero)
         )
         pairs = [(s, s + 1) for s in range(count - 1) if 0 <= k - s < chunks]
-        if pairs:
+        even = [pair for pair in pairs if pair[0] % 2 == 0]
+        odd = [pair for pair in pairs if pair[0] % 2 == 1]
+        if even and odd:
+            from_even = lax.ppermute(result, "section", even)
+            from_odd = lax.ppermute(result, "section", odd)
+            incoming = jnp.where(section % 2 == 1, from_even, from_odd)
+        elif pairs:
             incoming = lax.ppermute(result, "section", pairs)
     handed = partner(finished[:, moving], "inst", 0)
     finished = finished.at[:, moving].set(handed)

time: 160 us -> 166 us (1.038)
  starting transfers between devices: 12.2 us -> 17.5 us
    ppermute x10 -> x2, waiting for transfers between devices: 44 us -> 0.9 us  [per_device(): incoming = lax.ppermute(result, 'section', pairs)]
    ppermute x0 -> x16, waiting for transfers between devices: none -> 42.4 us  [the longest x8 40.7 us: per_device(): from_odd = lax.ppermute(result, 'section', odd)]
    ppermute x0 -> x16, starting transfers between devices: none -> 15.5 us  [the longest x8 8.25 us: per_device(): from_odd = lax.ppermute(result, 'section', odd)]
    ppermute x10 -> x2, starting transfers between devices: 12.1 us -> 1.96 us  [per_device(): incoming = lax.ppermute(result, 'section', pairs)]
  transfers between devices with their start and end apart: 12 -> 20, of which waited for: 6 -> 8; matrix products, arithmetic and copies ran while one was open for 10% -> 9% of each run, Pallas kernels for 0% -> 0%
where the time goes in v4:
time: 166 us; the launch traced here: 163 us
  matrix products  44.6 us (27%)
  waiting for transfers between devices  44.6 us (27%)
  local copies, waits for them, and re-layouts  36.8 us (22%)
  other arithmetic  17.5 us (11%)
  starting transfers between devices  17.5 us (11%)
  between operations  2.27 us (1%)
    ppermute x8, waiting for transfers between devices, per_device(): from_odd = lax.ppermute(result, 'section', odd)  40.7 us
    dot_general x11, matrix products, layer(): jnp.einsum('rjgpd,rjgxd->rjgpx', keys, wide_query, preferred_element_type...  21.6 us
    dot_general x11, matrix products, layer(): jnp.einsum('rjgpx,rjgpd->rjgxd', cache_w, values, preferred_element_type=...  17.3 us
    ppermute x8, starting transfers between devices, per_device(): from_odd = lax.ppermute(result, 'section', odd)  8.25 us
    ppermute x8, starting transfers between devices, per_device(): from_even = lax.ppermute(result, 'section', even)  7.23 us
    gather x1, local copies, waits for them, and re-layouts, per_device(): keys = flat_pool[table * 2]  6.44 us
    gather x1, local copies, waits for them, and re-layouts, per_device(): values = flat_pool[table * 2 + 1]  6.39 us
    unnamed x18, local copies, waits for them, and re-layouts  5.94 us
  transfers between devices with their start and end apart: 20, of which 8 were waited for; matrix products, arithmetic and copies ran while one was open for 9% of the time, Pallas kernels for 0%

profile of v4, /device:TPU:26, one launch (start us, length us, event | category | flops | bytes accessed | tf_op | source)
XLA Modules:
  0.0 163.3 jit_solution(6676496273587089950)
XLA Ops:
  5.2 6.4 %gather_fusion = bf16[16,8,128,128]{3,2,1,0:T(8,128)(2,1)} fusion(bf16[32,8,128,128]{3,2,1,0:T(8,128)(2,1)} %bitcast.361, s32[1024]{0:T(1024)S(1)} %pad_clamp_fusion.3), kind=kCustom, calls=%fused_computation | custom fusion | bytes 8388672 | tf_op jit(solution)/shard_map/gather | solution.py:92
  11.8 2.0 %fusion.237 = (f32[2,8,32]{2,1,0:T(8,128)S(1)}, f32[2,2,8,128,32]{3,4,2,1,0:T(8,128)S(1)}) fusion(bf16[2,8,32,128]{3,2,1,0:T(8,128)(2,1)S(1)} %get-tuple-element.91, bf16[8,2,8,128,128]{4,3,2,1,0:T(8,128)(2,1)} %bitcast.349, s32[]{:T(128)S(6)} %select_n.421, pred[2,2,128]{2,1,0:T(4,128)(4,1)S(1)} %broadcast_compare_fusion.11), kind=kOutput, calls=%fused_computation.479 | convolution fusion | flops 33947136 | bytes 1706500 | tf_op jit(solution)/shard_map/rjgpd,rjgxd->rjgpx/dot_general | solution.py:44
  14.3 6.4 %gather_fusion.1 = bf16[16,8,128,128]{3,2,1,0:T(8,128)(2,1)} fusion(bf16[32,8,128,128]{3,2,1,0:T(8,128)(2,1)} %bitcast.362, s32[1024]{0:T(1024)S(1)} %pad_clamp_fusion.2), kind=kCustom, calls=%fused_computation.1 | custom fusion | bytes 8388672 | tf_op jit(solution)/shard_map/gather | solution.py:93
  20.7 1.6 convolution_bitcast_fusion.10
  25.6 2.0 %fusion.239 = (f32[2,8,32]{2,1,0:T(8,128)S(1)}, f32[2,2,8,128,32]{3,4,2,1,0:T(8,128)S(1)}) fusion(bf16[2,8,32,128]{3,2,1,0:T(8,128)(2,1)S(1)} %bitcast.409, bf16[8,2,8,128,128]{4,3,2,1,0:T(8,128)(2,1)} %bitcast.350, s32[]{:T(128)S(6)} %select_n.431, pred[2,2,128]{2,1,0:T(4,128)(4,1)S(1)} %get-tuple-element.93), kind=kOutput, calls=%fused_computation.481 | convolution fusion | flops 33947136 | bytes 1706500 | tf_op jit(solution)/shard_map/rjgpd,rjgxd->rjgpx/dot_general | solution.py:44
  32.7 2.0 %fusion.241 = (f32[2,8,32]{2,1,0:T(8,128)S(1)}, f32[2,2,8,128,32]{3,4,2,1,0:T(8,128)S(1)}) fusion(bf16[2,8,32,128]{3,2,1,0:T(8,128)(2,1)S(1)} %bitcast.411, bf16[8,2,8,128,128]{4,3,2,1,0:T(8,128)(2,1)} %bitcast.351, s32[]{:T(128)S(6)} %select_n.440, pred[2,2,128]{2,1,0:T(4,128)(4,1)S(1)} %broadcast_compare_fusion.9), kind=kOutput, calls=%fused_computation.483 | convolution fusion | flops 33947136 | bytes 1706500 | tf_op jit(solution)/shard_map/rjgpd,rjgxd->rjgpx/dot_general | solution.py:44
  39.8 2.0 %fusion.243 = (f32[2,8,32]{2,1,0:T(8,128)S(1)}, f32[2,2,8,128,32]{3,4,2,1,0:T(8,128)S(1)}) fusion(bf16[2,8,32,128]{3,2,1,0:T(8,128)(2,1)S(1)} %bitcast.413, bf16[8,2,8,128,128]{4,3,2,1,0:T(8,128)(2,1)} %bitcast.352, s32[]{:T(128)S(6)} %select_n.447, pred[2,2,128]{2,1,0:T(4,128)(4,1)S(1)} %broadcast_compare_fusion.8), kind=kOutput, calls=%fused_computation.485 | convolution fusion | flops 33947136 | bytes 1706500 | tf_op jit(solution)/shard_map/rjgpd,rjgxd->rjgpx/dot_general | solution.py:44
  47.1 2.0 %fusion.245 = (f32[2,8,32]{2,1,0:T(8,128)S(1)}, f32[2,2,8,128,32]{3,4,2,1,0:T(8,128)S(1)}) fusion(bf16[2,8,32,128]{3,2,1,0:T(8,128)(2,1)S(1)} %bitcast.415, bf16[8,2,8,128,128]{4,3,2,1,0:T(8,128)(2,1)} %bitcast.353, s32[]{:T(128)S(6)} %select_n.454, pred[2,2,128]{2,1,0:T(4,128)(4,1)S(1)} %broadcast_compare_fusion.7), kind=kOutput, calls=%fused_computation.487 | convolution fusion | flops 33947136 | bytes 1706500 | tf_op jit(solution)/shard_map/rjgpd,rjgxd->rjgpx/dot_general | solution.py:44
  54.1 2.0 %fusion.247 = (f32[2,8,32]{2,1,0:T(8,128)S(1)}, f32[2,2,8,128,32]{3,4,2,1,0:T(8,128)S(1)}) fusion(bf16[2,8,32,128]{3,2,1,0:T(8,128)(2,1)S(1)} %bitcast.417, bf16[8,2,8,128,128]{4,3,2,1,0:T(8,128)(2,1)} %bitcast.354, s32[]{:T(128)S(6)} %select_n.461, pred[2,2,128]{2,1,0:T(4,128)(4,1)S(1)} %broadcast_compare_fusion.6), kind=kOutput, calls=%fused_computation.489 | convolution fusion | flops 33947136 | bytes 1706500 | tf_op jit(solution)/shard_map/rjgpd,rjgxd->rjgpx/dot_general | solution.py:44
  60.6 28.2 %collective-permute-done.10 = bf16[4,2,8192]{2,0,1:T(4,128)(2,1)S(1)} collective-permute-done((bf16[4,2,8192]{2,0,1:T(4,128)(2,1)S(1)}, bf16[4,2,8192]{2,0,1:T(4,128)(2,1)S(1)}, u32[]{:S(2)}, u32[]{:S(2)}) %collective-permute-start.10) | collective-permute-done | bytes 131104 | tf_op jit(solution)/shard_map/ppermute | solution.py:124
  90.1 2.0 %fusion.249 = (f32[2,8,32]{2,1,0:T(8,128)S(1)}, f32[2,2,8,128,32]{3,4,2,1,0:T(8,128)S(1)}) fusion(bf16[2,8,32,128]{3,2,1,0:T(8,128)(2,1)S(1)} %bitcast.419, bf16[8,2,8,128,128]{4,3,2,1,0:T(8,128)(2,1)} %bitcast.355, s32[]{:T(128)S(6)} %select_n.468, pred[2,2,128]{2,1,0:T(4,128)(4,1)S(1)} %broadcast_compare_fusion.5), kind=kOutput, calls=%fused_computation.491 | convolution fusion | flops 33947136 | bytes 1706500 | tf_op jit(solution)/shard_map/rjgpd,rjgxd->rjgpx/dot_general | solution.py:44
  98.3 5.3 %collective-permute-done.12 = bf16[4,2,8192]{2,0,1:T(4,128)(2,1)S(1)} collective-permute-done((bf16[4,2,8192]{2,0,1:T(4,128)(2,1)S(1)}, bf16[4,2,8192]{2,0,1:T(4,128)(2,1)S(1)}, u32[]{:S(2)}, u32[]{:S(2)}) %collective-permute-start.12) | collective-permute-done | bytes 131104 | tf_op jit(solution)/shard_map/ppermute | solution.py:124
  104.8 2.0 %fusion.251 = (f32[2,8,32]{2,1,0:T(8,128)S(1)}, f32[2,2,8,128,32]{3,4,2,1,0:T(8,128)S(1)}) fusion(bf16[2,8,32,128]{3,2,1,0:T(8,128)(2,1)S(1)} %bitcast.421, bf16[8,2,8,128,128]{4,3,2,1,0:T(8,128)(2,1)} %bitcast.356, s32[]{:T(128)S(6)} %select_n.475, pred[2,2,128]{2,1,0:T(4,128)(4,1)S(1)} %broadcast_compare_fusion.4), kind=kOutput, calls=%fused_computation.493 | convolution fusion | flops 33947136 | bytes 1706500 | tf_op jit(solution)/shard_map/rjgpd,rjgxd->rjgpx/dot_general | solution.py:44
  113.1 5.3 %collective-permute-done.14 = bf16[4,2,8192]{2,0,1:T(4,128)(2,1)S(1)} collective-permute-done((bf16[4,2,8192]{2,0,1:T(4,128)(2,1)S(1)}, bf16[4,2,8192]{2,0,1:T(4,128)(2,1)S(1)}, u32[]{:S(2)}, u32[]{:S(2)}) %collective-permute-start.14) | collective-permute-done | bytes 131104 | tf_op jit(solution)/shard_map/ppermute | solution.py:124
  119.6 2.0 %fusion.253 = (f32[2,8,32]{2,1,0:T(8,128)S(1)}, f32[2,2,8,128,32]{3,4,2,1,0:T(8,128)S(1)}) fusion(bf16[2,8,32,128]{3,2,1,0:T(8,128)(2,1)S(1)} %bitcast.423, bf16[8,2,8,128,128]{4,3,2,1,0:T(8,128)(2,1)} %bitcast.357, s32[]{:T(128)S(6)} %select_n.482, pred[2,2,128]{2,1,0:T(4,128)(4,1)S(1)} %broadcast_compare_fusion.3), kind=kOutput, calls=%fused_computation.495 | convolution fusion | flops 33947136 | bytes 1706500 | tf_op jit(solution)/shard_map/rjgpd,rjgxd->rjgpx/dot_general | solution.py:44
  121.9 1.6 convolution_bitcast_fusion.2
  127.0 4.3 %gather_fusion.5 = bf16[4,2,8,128,128]{4,3,2,1,0:T(8,128)(2,1)S(1)} fusion(bf16[16,2,8,128,128]{4,3,2,1,0:T(8,128)(2,1)} %bitcast.363, s32[1024]{0:T(1024)S(1)} %pad_clamp_fusion), kind=kCustom, calls=%fused_computation.5 | custom fusion | bytes 4194320 | tf_op jit(solution)/shard_map/gather | solution.py:86
  131.3 1.9 %collective-permute-done.16 = bf16[4,2,8192]{2,0,1:T(4,128)(2,1)} collective-permute-done((bf16[4,2,8192]{2,0,1:T(4,128)(2,1)S(1)}, bf16[4,2,8192]{2,0,1:T(4,128)(2,1)}, u32[]{:S(2)}, u32[]{:S(2)}) %collective-permute-start.16) | collective-permute-done | bytes 131104 | tf_op jit(solution)/shard_map/ppermute | solution.py:124
  139.2 2.0 %fusion.255 = (f32[2,8,32]{2,1,0:T(8,128)S(1)}, f32[2,2,8,128,32]{3,4,2,1,0:T(8,128)S(1)}) fusion(bf16[2,8,32,128]{3,2,1,0:T(8,128)(2,1)} %bitcast.425, bf16[8,2,8,128,128]{4,3,2,1,0:T(8,128)(2,1)} %bitcast.358, s32[]{:T(128)S(6)} %select_n.489, pred[2,2,128]{2,1,0:T(4,128)(4,1)S(1)} %broadcast_compare_fusion.2), kind=kOutput, calls=%fused_computation.497 | convolution fusion | flops 33947136 | bytes 1706500 | tf_op jit(solution)/shard_map/rjgpd,rjgxd->rjgpx/dot_general | solution.py:44
  144.1 1.8 %reshape.669 = f32[4,2,8192]{2,0,1:T(4,128)} reshape(f32[4,2,8,8,128]{4,3,2,0,1:T(8,128)} %copy.258) | data formatting | bytes 524288 | tf_op jit(solution)/shard_map/reshape | solution.py:71
  148.2 1.6 broadcast_select_fusion
  151.9 2.0 %fusion.257 = (f32[2,8,32]{2,1,0:T(8,128)S(1)}, f32[2,2,8,128,32]{3,4,2,1,0:T(8,128)S(1)}) fusion(bf16[2,8,32,128]{3,2,1,0:T(8,128)(2,1)S(1)} %bitcast.407, bf16[8,2,8,128,128]{4,3,2,1,0:T(8,128)(2,1)} %bitcast.359, s32[]{:T(128)S(6)} %select_n.495, pred[2,2,128]{2,1,0:T(4,128)(4,1)S(1)} %broadcast_compare_fusion.1), kind=kOutput, calls=%fused_computation.499 | convolution fusion | flops 33947136 | bytes 1706500 | tf_op jit(solution)/shard_map/rjgpd,rjgxd->rjgpx/dot_general | solution.py:44
  154.2 1.6 convolution_bitcast_fusion
  160.2 3.2 %copy.497 = bf16[1,1,2,2,2,8,128,128]{7,6,5,4,3,2,1,0:T(8,128)(2,1)} copy(bf16[1,1,2,2,2,8,128,128]{7,6,5,4,3,2,1,0:T(8,128)(2,1)} %bitcast.127) | data formatting | bytes 4194304
  (298 shorter events, 70.4 us)
Async XLA Ops:
  20.7 3.1 %copy-start.1 = (s32[1,8]{1,0:T(1,128)S(1)}, s32[1,8]{1,0:T(1,128)}, u32[]{:S(2)}) copy-start(s32[1,8]{1,0:T(1,128)} %param.10) | copy-start | bytes 100
  20.7 4.3 %copy-start.3 = (f32[1,8192]{1,0:T(1,128)S(1)}, f32[1,8192]{1,0:T(1,128)}, u32[]{:S(2)}) copy-start(f32[1,8192]{1,0:T(1,128)} %param.12) | copy-start | bytes 98308
  23.0 1.4 collective-permute-start
  30.1 1.4 collective-permute-start.1
  30.8 0.7 collective-permute-start.2
  37.2 1.4 collective-permute-start.3
  37.8 0.7 collective-permute-start.4
  44.2 1.5 collective-permute-start.5
  44.9 0.9 collective-permute-start.6
  51.5 1.4 collective-permute-start.7
  52.2 0.7 collective-permute-start.8
  58.6 2.0 %collective-permute-start.9 = (bf16[4,2,8192]{2,0,1:T(4,128)(2,1)S(1)}, bf16[4,2,8192]{2,0,1:T(4,128)(2,1)S(1)}, u32[]{:S(2)}, u32[]{:S(2)}) collective-permute-start(bf16[4,2,8192]{2,0,1:T(4,128)(2,1)S(1)} %get-tuple-element.69), channel_id=1, source_target_pairs={{2,3},{4,5},{10,11},{12,13},{18,19},{20,21},{26,27},{28,29}} | collective-permute-start | bytes 393224 | tf_op jit(solution)/shard_map/ppermute | solution.py:123
  59.3 29.6 %collective-permute-start.10 = (bf16[4,2,8192]{2,0,1:T(4,128)(2,1)S(1)}, bf16[4,2,8192]{2,0,1:T(4,128)(2,1)S(1)}, u32[]{:S(2)}, u32[]{:S(2)}) collective-permute-start(bf16[4,2,8192]{2,0,1:T(4,128)(2,1)S(1)} %get-tuple-element.69), channel_id=1, source_target_pairs={{3,4},{5,6},{11,12},{13,14},{19,20},{21,22},{27,28},{29,30}} | collective-permute-start | bytes 393224 | tf_op jit(solution)/shard_map/ppermute | solution.py:124
  94.5 3.8 %collective-permute-start.11 = (bf16[4,2,8192]{2,0,1:T(4,128)(2,1)S(1)}, bf16[4,2,8192]{2,0,1:T(4,128)(2,1)S(1)}, u32[]{:S(2)}, u32[]{:S(2)}) collective-permute-start(bf16[4,2,8192]{2,0,1:T(4,128)(2,1)S(1)} %get-tuple-element.65), channel_id=1, source_target_pairs={{4,5},{6,7},{12,13},{14,15},{20,21},{22,23},{28,29},{30,31}} | collective-permute-start | bytes 393224 | tf_op jit(solution)/shard_map/ppermute | solution.py:123
  95.8 7.8 %collective-permute-start.12 = (bf16[4,2,8192]{2,0,1:T(4,128)(2,1)S(1)}, bf16[4,2,8192]{2,0,1:T(4,128)(2,1)S(1)}, u32[]{:S(2)}, u32[]{:S(2)}) collective-permute-start(bf16[4,2,8192]{2,0,1:T(4,128)(2,1)S(1)} %get-tuple-element.65), channel_id=1, source_target_pairs={{3,4},{5,6},{11,12},{13,14},{19,20},{21,22},{27,28},{29,30}} | collective-permute-start | bytes 393224 | tf_op jit(solution)/shard_map/ppermute | solution.py:124
  104.6 7.3 %copy-start.6 = (s32[1,8,2]{1,2,0:T(2,128)S(1)}, s32[1,8,2]{1,2,0:T(2,128)}, u32[]{:S(2)}) copy-start(s32[1,8,2]{1,2,0:T(2,128)} %param.9) | copy-start | bytes 196
  109.3 3.8 %collective-permute-start.13 = (bf16[4,2,8192]{2,0,1:T(4,128)(2,1)S(1)}, bf16[4,2,8192]{2,0,1:T(4,128)(2,1)S(1)}, u32[]{:S(2)}, u32[]{:S(2)}) collective-permute-start(bf16[4,2,8192]{2,0,1:T(4,128)(2,1)S(1)} %get-tuple-element.61), channel_id=1, source_target_pairs={{4,5},{6,7},{12,13},{14,15},{20,21},{22,23},{28,29},{30,31}} | collective-permute-start | bytes 393224 | tf_op jit(solution)/shard_map/ppermute | solution.py:123
  110.6 7.8 %collective-permute-start.14 = (bf16[4,2,8192]{2,0,1:T(4,128)(2,1)S(1)}, bf16[4,2,8192]{2,0,1:T(4,128)(2,1)S(1)}, u32[]{:S(2)}, u32[]{:S(2)}) collective-permute-start(bf16[4,2,8192]{2,0,1:T(4,128)(2,1)S(1)} %get-tuple-element.61), channel_id=1, source_target_pairs={{5,6},{13,14},{21,22},{29,30}} | collective-permute-start | bytes 393224 | tf_op jit(solution)/shard_map/ppermute | solution.py:124
  124.0 7.3 %collective-permute-start.15 = (bf16[4,2,8192]{2,0,1:T(4,128)(2,1)S(1)}, bf16[4,2,8192]{2,0,1:T(4,128)(2,1)S(1)}, u32[]{:S(2)}, u32[]{:S(2)}) collective-permute-start(bf16[4,2,8192]{2,0,1:T(4,128)(2,1)S(1)} %get-tuple-element.57), channel_id=1, source_target_pairs={{6,7},{14,15},{22,23},{30,31}} | collective-permute-start | bytes 393224 | tf_op jit(solution)/shard_map/ppermute | solution.py:123
  125.3 7.9 %collective-permute-start.16 = (bf16[4,2,8192]{2,0,1:T(4,128)(2,1)S(1)}, bf16[4,2,8192]{2,0,1:T(4,128)(2,1)}, u32[]{:S(2)}, u32[]{:S(2)}) collective-permute-start(bf16[4,2,8192]{2,0,1:T(4,128)(2,1)S(1)} %get-tuple-element.57), channel_id=1, source_target_pairs={{5,6},{13,14},{21,22},{29,30}} | collective-permute-start | bytes 393224 | tf_op jit(solution)/shard_map/ppermute | solution.py:124
  137.9 7.9 %copy-start.5 = (bf16[4,2,8192]{2,0,1:T(4,128)(2,1)S(1)}, bf16[4,2,8192]{2,0,1:T(4,128)(2,1)}, u32[]{:S(2)}) copy-start(bf16[4,2,8192]{2,0,1:T(4,128)(2,1)} %copy-done.4) | copy-start | bytes 393220
  146.9 3.8 %collective-permute-start.17 = (bf16[4,2,8192]{2,0,1:T(4,128)(2,1)S(1)}, bf16[4,2,8192]{2,0,1:T(4,128)(2,1)S(1)}, u32[]{:S(2)}, u32[]{:S(2)}) collective-permute-start(bf16[4,2,8192]{2,0,1:T(4,128)(2,1)S(1)} %get-tuple-element.53), channel_id=1, source_target_pairs={{6,7},{14,15},{22,23},{30,31}} | collective-permute-start | bytes 393224 | tf_op jit(solution)/shard_map/ppermute | solution.py:127
  149.8 10.4 %collective-permute-start.19 = (bf16[2,2,2,8,128,128]{5,4,3,2,1,0:T(8,128)(2,1)}, bf16[2,2,2,8,128,128]{5,4,3,2,1,0:T(8,128)(2,1)}, u32[]{:S(2)}, u32[]{:S(2)}) collective-permute-start(bf16[2,2,2,8,128,128]{5,4,3,2,1,0:T(8,128)(2,1)} %broadcast_select_fusion), channel_id=1, source_target_pairs={{0,8},{8,0},{1,9},{9,1},{2,10},{10,2},{3,11},{11,3},{4,12},{12,4},... | collective-permute-start | bytes 6291464 | tf_op jit(solution)/shard_map/ppermute | solution.py:18
  157.0 1.4 collective-permute-start.18
  (4 other events, 6.9 us)

commit v5 on v0

--- a/solution.py
+++ b/solution.py
@@ -4,6 +4,8 @@
 import jax.numpy as jnp
 from jax import lax
 from jax.sharding import PartitionSpec as P
+from jax.experimental import pallas as pl
+from jax.experimental.pallas import tpu as pltpu
 
 CHUNKS = 4
 
@@ -72,6 +74,34 @@
     return (wide + scale * attended).astype(jnp.bfloat16)
 
 
+def copy_kernel(table_ref, page_ref, keys_ref, values_ref):
+    keys_ref[0, 0] = page_ref[0, 0]
+    values_ref[0, 0] = page_ref[0, 1]
+
+
+def gather_pages(pool, table):
+    reqs, pages = table.shape
+    kv_heads, page_len, head = pool.shape[2:]
+
+    def page_index(r, j, table_ref):
+        return (table_ref[r * pages + j], 0, 0, 0, 0)
+
+    def slot_index(r, j, table_ref):
+        return (r, j, 0, 0, 0)
+
+    slot = pl.BlockSpec((1, 1, kv_heads, page_len, head), slot_index)
+    grid_spec = pltpu.PrefetchScalarGridSpec(
+        num_scalar_prefetch=1,
+        grid=(reqs, pages),
+        in_specs=[pl.BlockSpec((1, 2, kv_heads, page_len, head), page_index)],
+        out_specs=[slot, slot],
+    )
+    half = jax.ShapeDtypeStruct((reqs, pages, kv_heads, page_len, head), pool.dtype)
+    return pl.pallas_call(copy_kernel, grid_spec=grid_spec, out_shape=[half, half])(
+        table.reshape(-1), pool
+    )
+
+
 def per_device(tokens, kv_pool, page_table, lengths, migrate_ids, norm_gain, out_scale):
     inputs = tokens[0]
     pool = kv_pool[0, 0]
@@ -88,9 +118,7 @@
     keep = spots[None, :, :] < lens[moving][:, None, None]
     outgoing = jnp.where(keep[:, :, None, None, :, None], outgoing, jnp.zeros((), jnp.bfloat16))
     received = partner(outgoing, "inst", 0)
-    flat_pool = pool.reshape((-1,) + pool.shape[2:])
-    keys = flat_pool[table * 2]
-    values = flat_pool[table * 2 + 1]
+    keys, values = gather_pages(pool, table)
     lens_used = lens
     section = lax.axis_index("section")
     count = lax.axis_size("section")

time: 160 us -> 161 us (level)
  Pallas kernels: 0 us -> 12.6 us
  local copies, waits for them, and re-layouts: 36.7 us -> 24.9 us
    gather x2 -> x0, local copies, waits for them, and re-layouts: 12.8 us -> none  [the longest x1 6.44 us: per_device(): keys = flat_pool[table * 2]]
    pallas_call x0 -> x1, Pallas kernels: none -> 12.6 us  [gather_pages(): pl.pallas_call(copy_kernel, grid_spec=grid_spec, out_shape=[half, half])]
    unnamed x18 -> x19, local copies, waits for them, and re-layouts: 5.94 us -> 6.7 us
where the time goes in v5:
time: 161 us; the launch traced here: 158 us
  waiting for transfers between devices  45.5 us (28%)
  matrix products  44.7 us (28%)
  local copies, waits for them, and re-layouts  24.9 us (15%)
  other arithmetic  15.8 us (10%)
  Pallas kernels  12.6 us (8%)
  starting transfers between devices  12.2 us (8%)
  between operations  2.11 us (1%)
    ppermute x10, waiting for transfers between devices, per_device(): incoming = lax.ppermute(result, 'section', pairs)  44.2 us
    dot_general x11, matrix products, layer(): jnp.einsum('rjgxd,rjgpd->rjgxp', wide_query, keys, preferred_element_type...  21.7 us
    dot_general x11, matrix products, layer(): jnp.einsum('rjgxp,rjgpd->rjgxd', cache_w, values, preferred_element_type=...  17.3 us
    pallas_call x1, Pallas kernels, gather_pages(): pl.pallas_call(copy_kernel, grid_spec=grid_spec, out_shape=[half, half])  12.6 us
    ppermute x10, starting transfers between devices, per_device(): incoming = lax.ppermute(result, 'section', pairs)  12.1 us
    unnamed x19, local copies, waits for them, and re-layouts  6.7 us
    gather x1, local copies, waits for them, and re-layouts, per_device(): outgoing = pool[chosen]  4.33 us
    reshape x20, local copies, waits for them, and re-layouts, layer(): heads = normed.reshape(steps, reqs, kv_heads, group, head)  3.62 us
  transfers between devices with their start and end apart: 12, of which 6 were waited for; matrix products, arithmetic and copies ran while one was open for 10% of the time, Pallas kernels for 0%

profile of v5, /device:TPU:26, one launch (start us, length us, event | category | flops | bytes accessed | tf_op | source)
XLA Modules:
  0.0 157.7 jit_solution(2000234873606600401)
XLA Ops:
  5.7 12.6 %shard_map.86 = (bf16[8,2,8,128,128]{4,3,2,1,0:T(8,128)(2,1)}, bf16[8,2,8,128,128]{4,3,2,1,0:T(8,128)(2,1)}) custom-call(s32[16]{0:T(128)} %reshape_squeeze.3.table_ref, bf16[16,2,8,128,128]{4,3,2,1,0:T(8,128)(2,1)} %bitcast.310), custom_call_target="tpu_custom_call" | custom-call | tf_op jit(solution)/shard_map/pallas_call | solution.py:100
  18.4 2.0 %fusion.237 = (f32[2,8,32]{2,1,0:T(8,128)S(1)}, f32[2,2,8,32,128]{4,3,2,1,0:T(8,128)S(1)}) fusion(bf16[8,2,8,128,128]{4,3,2,1,0:T(8,128)(2,1)} %get-tuple-element.24, s32[]{:T(128)S(6)} %select_n.346, bf16[2,8,32,128]{3,2,1,0:T(8,128)(2,1)S(1)} %get-tuple-element.95, pred[2,2,128]{2,1,0:T(4,128)(4,1)S(1)} %broadcast_compare_fusion.11), kind=kOutput, calls=%fused_computation.463 | convolution fusion | flops 33947136 | bytes 1706500 | tf_op jit(solution)/shard_map/rjgxd,rjgpd->rjgxp/dot_general | solution.py:46
  25.7 2.0 %fusion.239 = (f32[2,8,32]{2,1,0:T(8,128)S(1)}, f32[2,2,8,32,128]{4,3,2,1,0:T(8,128)S(1)}) fusion(bf16[8,2,8,128,128]{4,3,2,1,0:T(8,128)(2,1)} %get-tuple-element.24, s32[]{:T(128)S(6)} %select_n.354, bf16[2,8,32,128]{3,2,1,0:T(8,128)(2,1)S(1)} %bitcast.339, pred[2,2,128]{2,1,0:T(4,128)(4,1)S(1)} %get-tuple-element.97), kind=kOutput, calls=%fused_computation.465 | convolution fusion | flops 33947136 | bytes 1706500 | tf_op jit(solution)/shard_map/rjgxd,rjgpd->rjgxp/dot_general | solution.py:46
  28.0 1.6 convolution_bitcast_fusion.9
  32.0 2.0 %fusion.241 = (f32[2,8,32]{2,1,0:T(8,128)S(1)}, f32[2,2,8,32,128]{4,3,2,1,0:T(8,128)S(1)}) fusion(bf16[8,2,8,128,128]{4,3,2,1,0:T(8,128)(2,1)} %get-tuple-element.24, s32[]{:T(128)S(6)} %select_n.360, bf16[2,8,32,128]{3,2,1,0:T(8,128)(2,1)S(1)} %bitcast.341, pred[2,2,128]{2,1,0:T(4,128)(4,1)S(1)} %broadcast_compare_fusion.9), kind=kOutput, calls=%fused_computation.467 | convolution fusion | flops 33947136 | bytes 1706500 | tf_op jit(solution)/shard_map/rjgxd,rjgpd->rjgxp/dot_general | solution.py:46
  38.4 2.0 %fusion.243 = (f32[2,8,32]{2,1,0:T(8,128)S(1)}, f32[2,2,8,32,128]{4,3,2,1,0:T(8,128)S(1)}) fusion(bf16[8,2,8,128,128]{4,3,2,1,0:T(8,128)(2,1)} %get-tuple-element.24, s32[]{:T(128)S(6)} %select_n.366, bf16[2,8,32,128]{3,2,1,0:T(8,128)(2,1)S(1)} %bitcast.343, pred[2,2,128]{2,1,0:T(4,128)(4,1)S(1)} %broadcast_compare_fusion.8), kind=kOutput, calls=%fused_computation.469 | convolution fusion | flops 33947136 | bytes 1706500 | tf_op jit(solution)/shard_map/rjgxd,rjgpd->rjgxp/dot_general | solution.py:46
  44.8 2.0 %fusion.245 = (f32[2,8,32]{2,1,0:T(8,128)S(1)}, f32[2,2,8,32,128]{4,3,2,1,0:T(8,128)S(1)}) fusion(bf16[8,2,8,128,128]{4,3,2,1,0:T(8,128)(2,1)} %get-tuple-element.24, s32[]{:T(128)S(6)} %select_n.372, bf16[2,8,32,128]{3,2,1,0:T(8,128)(2,1)S(1)} %bitcast.345, pred[2,2,128]{2,1,0:T(4,128)(4,1)S(1)} %broadcast_compare_fusion.7), kind=kOutput, calls=%fused_computation.471 | convolution fusion | flops 33947136 | bytes 1706500 | tf_op jit(solution)/shard_map/rjgxd,rjgpd->rjgxp/dot_general | solution.py:46
  51.3 2.0 %fusion.247 = (f32[2,8,32]{2,1,0:T(8,128)S(1)}, f32[2,2,8,32,128]{4,3,2,1,0:T(8,128)S(1)}) fusion(bf16[8,2,8,128,128]{4,3,2,1,0:T(8,128)(2,1)} %get-tuple-element.24, s32[]{:T(128)S(6)} %select_n.378, bf16[2,8,32,128]{3,2,1,0:T(8,128)(2,1)S(1)} %bitcast.347, pred[2,2,128]{2,1,0:T(4,128)(4,1)S(1)} %broadcast_compare_fusion.6), kind=kOutput, calls=%fused_computation.473 | convolution fusion | flops 33947136 | bytes 1706500 | tf_op jit(solution)/shard_map/rjgxd,rjgpd->rjgxp/dot_general | solution.py:46
  57.1 31.1 %collective-permute-done.5 = bf16[4,2,8192]{2,0,1:T(4,128)(2,1)S(1)} collective-permute-done((bf16[4,2,8192]{2,0,1:T(4,128)(2,1)S(1)}, bf16[4,2,8192]{2,0,1:T(4,128)(2,1)S(1)}, u32[]{:S(2)}, u32[]{:S(2)}) %collective-permute-start.5) | collective-permute-done | bytes 131104 | tf_op jit(solution)/shard_map/ppermute | solution.py:149
  89.4 2.0 %fusion.249 = (f32[2,8,32]{2,1,0:T(8,128)S(1)}, f32[2,2,8,32,128]{4,3,2,1,0:T(8,128)S(1)}) fusion(bf16[8,2,8,128,128]{4,3,2,1,0:T(8,128)(2,1)} %get-tuple-element.24, s32[]{:T(128)S(6)} %select_n.384, bf16[2,8,32,128]{3,2,1,0:T(8,128)(2,1)S(1)} %bitcast.349, pred[2,2,128]{2,1,0:T(4,128)(4,1)S(1)} %broadcast_compare_fusion.5), kind=kOutput, calls=%fused_computation.475 | convolution fusion | flops 33947136 | bytes 1706500 | tf_op jit(solution)/shard_map/rjgxd,rjgpd->rjgxp/dot_general | solution.py:46
  93.8 1.9 %collective-permute-start.6 = (bf16[4,2,8192]{2,0,1:T(4,128)(2,1)S(1)}, bf16[4,2,8192]{2,0,1:T(4,128)(2,1)S(1)}, u32[]{:S(2)}, u32[]{:S(2)}) collective-permute-start(bf16[4,2,8192]{2,0,1:T(4,128)(2,1)S(1)} %get-tuple-element.69), channel_id=1, source_target_pairs={{3,4},{4,5},{5,6},{6,7},{11,12},{12,13},{13,14},{14,15},{19,20},{2... | collective-permute-start | bytes 393224 | tf_op jit(solution)/shard_map/ppermute | solution.py:149
  95.8 5.8 %collective-permute-done.6 = bf16[4,2,8192]{2,0,1:T(4,128)(2,1)S(1)} collective-permute-done((bf16[4,2,8192]{2,0,1:T(4,128)(2,1)S(1)}, bf16[4,2,8192]{2,0,1:T(4,128)(2,1)S(1)}, u32[]{:S(2)}, u32[]{:S(2)}) %collective-permute-start.6) | collective-permute-done | bytes 131104 | tf_op jit(solution)/shard_map/ppermute | solution.py:149
  102.8 2.0 %fusion.251 = (f32[2,8,32]{2,1,0:T(8,128)S(1)}, f32[2,2,8,32,128]{4,3,2,1,0:T(8,128)S(1)}) fusion(bf16[8,2,8,128,128]{4,3,2,1,0:T(8,128)(2,1)} %get-tuple-element.24, s32[]{:T(128)S(6)} %select_n.390, bf16[2,8,32,128]{3,2,1,0:T(8,128)(2,1)S(1)} %bitcast.351, pred[2,2,128]{2,1,0:T(4,128)(4,1)S(1)} %broadcast_compare_fusion.4), kind=kOutput, calls=%fused_computation.477 | convolution fusion | flops 33947136 | bytes 1706500 | tf_op jit(solution)/shard_map/rjgxd,rjgpd->rjgxp/dot_general | solution.py:46
  107.2 1.9 %collective-permute-start.7 = (bf16[4,2,8192]{2,0,1:T(4,128)(2,1)S(1)}, bf16[4,2,8192]{2,0,1:T(4,128)(2,1)S(1)}, u32[]{:S(2)}, u32[]{:S(2)}) collective-permute-start(bf16[4,2,8192]{2,0,1:T(4,128)(2,1)S(1)} %get-tuple-element.65), channel_id=1, source_target_pairs={{4,5},{5,6},{6,7},{12,13},{13,14},{14,15},{20,21},{21,22},{22,23},... | collective-permute-start | bytes 393224 | tf_op jit(solution)/shard_map/ppermute | solution.py:149
  109.8 5.2 %collective-permute-done.7 = bf16[4,2,8192]{2,0,1:T(4,128)(2,1)S(1)} collective-permute-done((bf16[4,2,8192]{2,0,1:T(4,128)(2,1)S(1)}, bf16[4,2,8192]{2,0,1:T(4,128)(2,1)S(1)}, u32[]{:S(2)}, u32[]{:S(2)}) %collective-permute-start.7) | collective-permute-done | bytes 131104 | tf_op jit(solution)/shard_map/ppermute | solution.py:149
  116.2 2.0 %fusion.253 = (f32[2,8,32]{2,1,0:T(8,128)S(1)}, f32[2,2,8,32,128]{4,3,2,1,0:T(8,128)S(1)}) fusion(bf16[8,2,8,128,128]{4,3,2,1,0:T(8,128)(2,1)} %get-tuple-element.24, s32[]{:T(128)S(6)} %select_n.396, bf16[2,8,32,128]{3,2,1,0:T(8,128)(2,1)S(1)} %bitcast.353, pred[2,2,128]{2,1,0:T(4,128)(4,1)S(1)} %broadcast_compare_fusion.3), kind=kOutput, calls=%fused_computation.479 | convolution fusion | flops 33947136 | bytes 1706500 | tf_op jit(solution)/shard_map/rjgxd,rjgpd->rjgxp/dot_general | solution.py:46
  120.7 1.9 %collective-permute-start.8 = (bf16[4,2,8192]{2,0,1:T(4,128)(2,1)S(1)}, bf16[4,2,8192]{2,0,1:T(4,128)(2,1)S(1)}, u32[]{:S(2)}, u32[]{:S(2)}) collective-permute-start(bf16[4,2,8192]{2,0,1:T(4,128)(2,1)S(1)} %get-tuple-element.61), channel_id=1, source_target_pairs={{5,6},{6,7},{13,14},{14,15},{21,22},{22,23},{29,30},{30,31}} | collective-permute-start | bytes 393224 | tf_op jit(solution)/shard_map/ppermute | solution.py:149
  122.7 4.3 %gather_fusion.3 = bf16[4,2,8,128,128]{4,3,2,1,0:T(8,128)(2,1)S(1)} fusion(bf16[16,2,8,128,128]{4,3,2,1,0:T(8,128)(2,1)} %bitcast.311, s32[1024]{0:T(1024)S(1)} %pad_clamp_fusion), kind=kCustom, calls=%fused_computation.3 | custom fusion | bytes 4194320 | tf_op jit(solution)/shard_map/gather | solution.py:116
  133.5 2.0 %fusion.255 = (f32[2,8,32]{2,1,0:T(8,128)S(1)}, f32[2,2,8,32,128]{4,3,2,1,0:T(8,128)S(1)}) fusion(bf16[8,2,8,128,128]{4,3,2,1,0:T(8,128)(2,1)} %get-tuple-element.24, s32[]{:T(128)S(6)} %select_n.402, bf16[2,8,32,128]{3,2,1,0:T(8,128)(2,1)} %bitcast.355, pred[2,2,128]{2,1,0:T(4,128)(4,1)S(1)} %broadcast_compare_fusion.2), kind=kOutput, calls=%fused_computation.481 | convolution fusion | flops 33947136 | bytes 1706500 | tf_op jit(solution)/shard_map/rjgxd,rjgpd->rjgxp/dot_general | solution.py:46
  138.4 1.8 %reshape.643 = f32[4,2,8192]{2,0,1:T(4,128)} reshape(f32[4,2,8,8,128]{4,3,2,0,1:T(8,128)} %copy.265) | data formatting | bytes 524288 | tf_op jit(solution)/shard_map/reshape | solution.py:73
  142.8 1.6 %broadcast_select_fusion = bf16[2,2,2,8,128,128]{5,4,3,2,1,0:T(8,128)(2,1)} fusion(bf16[2,2,2,8,128,128]{5,4,3,2,1,0:T(8,128)(2,1)S(1)} %bitcast.313, pred[2,2,128]{2,1,0:T(4,128)(4,1)S(1)} %get-tuple-element.96), kind=kLoop, calls=%fused_computation.5 | loop fusion | flops 1048576 | bytes 4194816 | tf_op jit(solution)/shard_map/jit(_where)/select_n | solution.py:119
  146.3 2.0 %fusion.257 = (f32[2,8,32]{2,1,0:T(8,128)S(1)}, f32[2,2,8,32,128]{4,3,2,1,0:T(8,128)S(1)}) fusion(bf16[8,2,8,128,128]{4,3,2,1,0:T(8,128)(2,1)} %get-tuple-element.24, s32[]{:T(128)S(6)} %select_n.408, bf16[2,8,32,128]{3,2,1,0:T(8,128)(2,1)S(1)} %bitcast.337, pred[2,2,128]{2,1,0:T(4,128)(4,1)S(1)} %broadcast_compare_fusion.1), kind=kOutput, calls=%fused_computation.483 | convolution fusion | flops 33947136 | bytes 1706500 | tf_op jit(solution)/shard_map/rjgxd,rjgpd->rjgxp/dot_general | solution.py:46
  148.6 1.6 convolution_bitcast_fusion
  154.5 3.2 %copy.493 = bf16[1,1,2,2,2,8,128,128]{7,6,5,4,3,2,1,0:T(8,128)(2,1)} copy(bf16[1,1,2,2,2,8,128,128]{7,6,5,4,3,2,1,0:T(8,128)(2,1)} %bitcast.123) | data formatting | bytes 4194304
  (268 shorter events, 59.5 us)
Async XLA Ops:
  0.6 1.0 copy-start
  18.2 4.6 %copy-start.2 = (f32[1,8192]{1,0:T(1,128)S(1)}, f32[1,8192]{1,0:T(1,128)}, u32[]{:S(2)}) copy-start(f32[1,8192]{1,0:T(1,128)} %param.13) | copy-start | bytes 98308
  18.4 5.3 %copy-start.7 = (s32[1,2]{1,0:T(1,128)S(1)}, s32[1,2]{1,0:T(1,128)}, u32[]{:S(2)}) copy-start(s32[1,2]{1,0:T(1,128)} %param.11) | copy-start | bytes 28
  18.4 5.4 %copy-start.1 = (s32[1,8]{1,0:T(1,128)S(1)}, s32[1,8]{1,0:T(1,128)}, u32[]{:S(2)}) copy-start(s32[1,8]{1,0:T(1,128)} %param.10) | copy-start | bytes 100
  20.4 4.6 %copy-start.3 = (f32[1,8192]{1,0:T(1,128)S(1)}, f32[1,8192]{1,0:T(1,128)}, u32[]{:S(2)}) copy-start(f32[1,8192]{1,0:T(1,128)} %param.12) | copy-start | bytes 98308
  23.1 1.4 collective-permute-start
  30.1 0.7 collective-permute-start.1
  36.5 0.7 collective-permute-start.2
  42.8 0.7 collective-permute-start.3
  49.2 0.9 collective-permute-start.4
  55.7 32.4 %collective-permute-start.5 = (bf16[4,2,8192]{2,0,1:T(4,128)(2,1)S(1)}, bf16[4,2,8192]{2,0,1:T(4,128)(2,1)S(1)}, u32[]{:S(2)}, u32[]{:S(2)}) collective-permute-start(bf16[4,2,8192]{2,0,1:T(4,128)(2,1)S(1)} %get-tuple-element.73), channel_id=1, source_target_pairs={{2,3},{3,4},{4,5},{5,6},{10,11},{11,12},{12,13},{13,14},{18,19},{1... | collective-permute-start | bytes 393224 | tf_op jit(solution)/shard_map/ppermute | solution.py:149
  93.8 7.8 %collective-permute-start.6 = (bf16[4,2,8192]{2,0,1:T(4,128)(2,1)S(1)}, bf16[4,2,8192]{2,0,1:T(4,128)(2,1)S(1)}, u32[]{:S(2)}, u32[]{:S(2)}) collective-permute-start(bf16[4,2,8192]{2,0,1:T(4,128)(2,1)S(1)} %get-tuple-element.69), channel_id=1, source_target_pairs={{3,4},{4,5},{5,6},{6,7},{11,12},{12,13},{13,14},{14,15},{19,20},{2... | collective-permute-start | bytes 393224 | tf_op jit(solution)/shard_map/ppermute | solution.py:149
  102.6 6.6 %copy-start.6 = (s32[1,8,2]{1,2,0:T(2,128)S(1)}, s32[1,8,2]{1,2,0:T(2,128)}, u32[]{:S(2)}) copy-start(s32[1,8,2]{1,2,0:T(2,128)} %param.9) | copy-start | bytes 196
  107.2 7.8 %collective-permute-start.7 = (bf16[4,2,8192]{2,0,1:T(4,128)(2,1)S(1)}, bf16[4,2,8192]{2,0,1:T(4,128)(2,1)S(1)}, u32[]{:S(2)}, u32[]{:S(2)}) collective-permute-start(bf16[4,2,8192]{2,0,1:T(4,128)(2,1)S(1)} %get-tuple-element.65), channel_id=1, source_target_pairs={{4,5},{5,6},{6,7},{12,13},{13,14},{14,15},{20,21},{21,22},{22,23},... | collective-permute-start | bytes 393224 | tf_op jit(solution)/shard_map/ppermute | solution.py:149
  120.7 7.8 %collective-permute-start.8 = (bf16[4,2,8192]{2,0,1:T(4,128)(2,1)S(1)}, bf16[4,2,8192]{2,0,1:T(4,128)(2,1)S(1)}, u32[]{:S(2)}, u32[]{:S(2)}) collective-permute-start(bf16[4,2,8192]{2,0,1:T(4,128)(2,1)S(1)} %get-tuple-element.61), channel_id=1, source_target_pairs={{5,6},{6,7},{13,14},{14,15},{21,22},{22,23},{29,30},{30,31}} | collective-permute-start | bytes 393224 | tf_op jit(solution)/shard_map/ppermute | solution.py:149
  128.9 0.7 copy-start.4
  132.2 8.0 %copy-start.5 = (bf16[4,2,8192]{2,0,1:T(4,128)(2,1)S(1)}, bf16[4,2,8192]{2,0,1:T(4,128)(2,1)}, u32[]{:S(2)}) copy-start(bf16[4,2,8192]{2,0,1:T(4,128)(2,1)} %copy-done.4) | copy-start | bytes 393220
  141.3 3.8 %collective-permute-start.9 = (bf16[4,2,8192]{2,0,1:T(4,128)(2,1)S(1)}, bf16[4,2,8192]{2,0,1:T(4,128)(2,1)S(1)}, u32[]{:S(2)}, u32[]{:S(2)}) collective-permute-start(bf16[4,2,8192]{2,0,1:T(4,128)(2,1)S(1)} %get-tuple-element.57), channel_id=1, source_target_pairs={{6,7},{14,15},{22,23},{30,31}} | collective-permute-start | bytes 393224 | tf_op jit(solution)/shard_map/ppermute | solution.py:149
  144.4 10.1 %collective-permute-start.11 = (bf16[2,2,2,8,128,128]{5,4,3,2,1,0:T(8,128)(2,1)}, bf16[2,2,2,8,128,128]{5,4,3,2,1,0:T(8,128)(2,1)}, u32[]{:S(2)}, u32[]{:S(2)}) collective-permute-start(bf16[2,2,2,8,128,128]{5,4,3,2,1,0:T(8,128)(2,1)} %broadcast_select_fusion), channel_id=1, source_target_pairs={{0,8},{8,0},{1,9},{9,1},{2,10},{10,2},{3,11},{11,3},{4,12},{12,4},... | collective-permute-start | bytes 6291464 | tf_op jit(solution)/shard_map/ppermute | solution.py:20
  151.4 1.4 collective-permute-start.10

commit v6 on v5

--- a/solution.py
+++ b/solution.py
@@ -74,33 +74,40 @@
     return (wide + scale * attended).astype(jnp.bfloat16)
 
 
-def copy_kernel(table_ref, page_ref, keys_ref, values_ref):
+def copy_kernel(table_ref, page_ref, *refs):
+    keys_ref, values_ref = refs[-2], refs[-1]
     keys_ref[0, 0] = page_ref[0, 0]
     values_ref[0, 0] = page_ref[0, 1]
 
 
-def gather_pages(pool, table):
+def gather_chunk(pool, table, chunk, block, previous):
     reqs, pages = table.shape
     kv_heads, page_len, head = pool.shape[2:]
 
     def page_index(r, j, table_ref):
-        return (table_ref[r * pages + j], 0, 0, 0, 0)
+        return (table_ref[(chunk * block + r) * pages + j], 0, 0, 0, 0)
 
     def slot_index(r, j, table_ref):
-        return (r, j, 0, 0, 0)
+        return (chunk * block + r, j, 0, 0, 0)
 
     slot = pl.BlockSpec((1, 1, kv_heads, page_len, head), slot_index)
+    in_specs = [pl.BlockSpec((1, 2, kv_heads, page_len, head), page_index)]
+    operands = [table.reshape(-1), pool]
+    aliases = {}
+    if previous is not None:
+        in_specs += [pl.BlockSpec(memory_space=pl.ANY)] * 2
+        operands += list(previous)
+        aliases = {2: 0, 3: 1}
     grid_spec = pltpu.PrefetchScalarGridSpec(
         num_scalar_prefetch=1,
-        grid=(reqs, pages),
-        in_specs=[pl.BlockSpec((1, 2, kv_heads, page_len, head), page_index)],
+        grid=(block, pages),
+        in_specs=in_specs,
         out_specs=[slot, slot],
     )
     half = jax.ShapeDtypeStruct((reqs, pages, kv_heads, page_len, head), pool.dtype)
-    return pl.pallas_call(copy_kernel, grid_spec=grid_spec, out_shape=[half, half])(
-        table.reshape(-1), pool
-    )
-
+    return pl.pallas_call(
+        copy_kernel, grid_spec=grid_spec, out_shape=[half, half], input_output_aliases=aliases
+    )(*operands)
 
 def per_device(tokens, kv_pool, page_table, lengths, migrate_ids, norm_gain, out_scale):
     inputs = tokens[0]
@@ -118,7 +125,6 @@
     keep = spots[None, :, :] < lens[moving][:, None, None]
     outgoing = jnp.where(keep[:, :, None, None, :, None], outgoing, jnp.zeros((), jnp.bfloat16))
     received = partner(outgoing, "inst", 0)
-    keys, values = gather_pages(pool, table)
     lens_used = lens
     section = lax.axis_index("section")
     count = lax.axis_size("section")
@@ -128,7 +134,11 @@
     incoming = jnp.zeros((steps, block, width), jnp.bfloat16)
     finished = jnp.zeros((steps, reqs, width), jnp.bfloat16)
     zero = jnp.zeros((), jnp.int32)
+    keys, values = None, None
     for k in range(chunks + count - 1):
+        if k < chunks:
+            previous = None if keys is None else (keys, values)
+            keys, values = gather_chunk(pool, table, k, block, previous)
         item = k - section
         live = jnp.logical_and(item >= 0, item < chunks)
         start = jnp.clip(item, 0, chunks - 1) * block

time: 161 us -> 153 us (0.950)
  waiting for transfers between devices: 45.5 us -> 32.4 us
  Pallas kernels: 12.6 us -> 18 us
    ppermute x10, waiting for transfers between devices: 44.2 us -> 31.1 us  [per_device(): incoming = lax.ppermute(result, 'section', pairs)]
    pallas_call x1 -> x4, Pallas kernels: 12.6 us -> 18 us  [gather_chunk(): pl.pallas_call(copy_kernel, grid_spec=grid_spec, out_shape=[half, half],...]
  transfers between devices with their start and end apart: 12 -> 12, of which waited for: 6 -> 6; matrix products, arithmetic and copies ran while one was open for 10% -> 10% of each run, Pallas kernels for 0% -> 9%
where the time goes in v6:
time: 153 us; the launch traced here: 150 us
  matrix products  44.8 us (29%)
  waiting for transfers between devices  32.4 us (21%)
  local copies, waits for them, and re-layouts  24.9 us (16%)
  Pallas kernels  18 us (12%)
  other arithmetic  15.7 us (10%)
  starting transfers between devices  12.2 us (8%)
  between operations  2.12 us (1%)
    ppermute x10, waiting for transfers between devices, per_device(): incoming = lax.ppermute(result, 'section', pairs)  31.1 us
    dot_general x11, matrix products, layer(): jnp.einsum('rjgxd,rjgpd->rjgxp', wide_query, keys, preferred_element_type...  21.7 us
    pallas_call x4, Pallas kernels, gather_chunk(): pl.pallas_call(copy_kernel, grid_spec=grid_spec, out_shape=[half, half],...  18 us
    dot_general x11, matrix products, layer(): jnp.einsum('rjgxp,rjgpd->rjgxd', cache_w, values, preferred_element_type=...  17.3 us
    ppermute x10, starting transfers between devices, per_device(): incoming = lax.ppermute(result, 'section', pairs)  12.1 us
    unnamed x19, local copies, waits for them, and re-layouts  6.7 us
    gather x1, local copies, waits for them, and re-layouts, per_device(): outgoing = pool[chosen]  4.33 us
    reshape x20, local copies, waits for them, and re-layouts, layer(): heads = normed.reshape(steps, reqs, kv_heads, group, head)  3.62 us
  transfers between devices with their start and end apart: 12, of which 6 were waited for; matrix products, arithmetic and copies ran while one was open for 10% of the time, Pallas kernels for 9%

profile of v6, /device:TPU:26, one launch (start us, length us, event | category | flops | bytes accessed | tf_op | source)
XLA Modules:
  0.0 150.1 jit_solution(2758878799195697918)
XLA Ops:
  5.6 4.5 %shard_map.86 = (bf16[8,2,8,128,128]{4,3,2,1,0:T(8,128)(2,1)}, bf16[8,2,8,128,128]{4,3,2,1,0:T(8,128)(2,1)}) custom-call(s32[16]{0:T(128)} %reshape_squeeze.2.table_ref, bf16[16,2,8,128,128]{4,3,2,1,0:T(8,128)(2,1)} %bitcast.310), custom_call_target="tpu_custom_call" | custom-call | tf_op jit(solution)/shard_map/pallas_call | solution.py:108
  10.1 2.0 %fusion.237 = (f32[2,8,32]{2,1,0:T(8,128)S(1)}, f32[2,2,8,32,128]{4,3,2,1,0:T(8,128)S(1)}) fusion(bf16[8,2,8,128,128]{4,3,2,1,0:T(8,128)(2,1)} %get-tuple-element.30.refs_0_, s32[]{:T(128)S(6)} %select_n.346, bf16[2,8,32,128]{3,2,1,0:T(8,128)(2,1)S(1)} %get-tuple-element.107, pred[2,2,128]{2,1,0:T(4,128)(4,1)S(1)} %broadcast_compare_fusion.11), kind=kOutput, calls=%fused_computation.463 | convolution fusion | flops 33947136 | bytes 1706500 | tf_op jit(solution)/shard_map/rjgxd,rjgpd->rjgxp/dot_general | solution.py:46
  15.7 4.6 %shard_map.87 = (bf16[8,2,8,128,128]{4,3,2,1,0:T(8,128)(2,1)}, bf16[8,2,8,128,128]{4,3,2,1,0:T(8,128)(2,1)}) custom-call(s32[16]{0:T(128)} %reshape_squeeze.2.table_ref, bf16[16,2,8,128,128]{4,3,2,1,0:T(8,128)(2,1)} %bitcast.311, bf16[8,2,8,128,128]{4,3,2,1,0:T(8,128)(2,1)} %get-tuple-element.30.refs_0_, ...), custom_call_target="tpu_custom_call", output_to_operand_aliasing={{0}: (2, {}), {1}: (3, {})} | custom-call | tf_op jit(solution)/shard_map/pallas_call | solution.py:108
  22.1 2.0 %fusion.239 = (f32[2,8,32]{2,1,0:T(8,128)S(1)}, f32[2,2,8,32,128]{4,3,2,1,0:T(8,128)S(1)}) fusion(bf16[8,2,8,128,128]{4,3,2,1,0:T(8,128)(2,1)} %get-tuple-element.34.refs_0_, s32[]{:T(128)S(6)} %select_n.354, bf16[2,8,32,128]{3,2,1,0:T(8,128)(2,1)S(1)} %bitcast.342, pred[2,2,128]{2,1,0:T(4,128)(4,1)S(1)} %get-tuple-element.109), kind=kOutput, calls=%fused_computation.465 | convolution fusion | flops 33947136 | bytes 1706500 | tf_op jit(solution)/shard_map/rjgxd,rjgpd->rjgxp/dot_general | solution.py:46
  27.3 4.5 %shard_map.88 = (bf16[8,2,8,128,128]{4,3,2,1,0:T(8,128)(2,1)}, bf16[8,2,8,128,128]{4,3,2,1,0:T(8,128)(2,1)}) custom-call(s32[16]{0:T(128)} %reshape_squeeze.2.table_ref, bf16[16,2,8,128,128]{4,3,2,1,0:T(8,128)(2,1)} %bitcast.312, bf16[8,2,8,128,128]{4,3,2,1,0:T(8,128)(2,1)} %get-tuple-element.34.refs_0_, ...), custom_call_target="tpu_custom_call", output_to_operand_aliasing={{0}: (2, {}), {1}: (3, {})} | custom-call | tf_op jit(solution)/shard_map/pallas_call | solution.py:108
  33.0 2.0 %fusion.241 = (f32[2,8,32]{2,1,0:T(8,128)S(1)}, f32[2,2,8,32,128]{4,3,2,1,0:T(8,128)S(1)}) fusion(bf16[8,2,8,128,128]{4,3,2,1,0:T(8,128)(2,1)} %get-tuple-element.38.refs_0_, s32[]{:T(128)S(6)} %select_n.360, bf16[2,8,32,128]{3,2,1,0:T(8,128)(2,1)S(1)} %bitcast.356, pred[2,2,128]{2,1,0:T(4,128)(4,1)S(1)} %broadcast_compare_fusion.9), kind=kOutput, calls=%fused_computation.467 | convolution fusion | flops 33947136 | bytes 1706500 | tf_op jit(solution)/shard_map/rjgxd,rjgpd->rjgxp/dot_general | solution.py:46
  38.1 4.5 %shard_map.89 = (bf16[8,2,8,128,128]{4,3,2,1,0:T(8,128)(2,1)}, bf16[8,2,8,128,128]{4,3,2,1,0:T(8,128)(2,1)}) custom-call(s32[16]{0:T(128)} %reshape_squeeze.2.table_ref, bf16[16,2,8,128,128]{4,3,2,1,0:T(8,128)(2,1)} %bitcast.313, bf16[8,2,8,128,128]{4,3,2,1,0:T(8,128)(2,1)} %get-tuple-element.38.refs_0_, ...), custom_call_target="tpu_custom_call", output_to_operand_aliasing={{0}: (2, {}), {1}: (3, {})} | custom-call | tf_op jit(solution)/shard_map/pallas_call | solution.py:108
  43.8 2.0 %fusion.243 = (f32[2,8,32]{2,1,0:T(8,128)S(1)}, f32[2,2,8,32,128]{4,3,2,1,0:T(8,128)S(1)}) fusion(bf16[8,2,8,128,128]{4,3,2,1,0:T(8,128)(2,1)} %get-tuple-element.42, s32[]{:T(128)S(6)} %select_n.366, bf16[2,8,32,128]{3,2,1,0:T(8,128)(2,1)S(1)} %bitcast.358, pred[2,2,128]{2,1,0:T(4,128)(4,1)S(1)} %broadcast_compare_fusion.8), kind=kOutput, calls=%fused_computation.469 | convolution fusion | flops 33947136 | bytes 1706500 | tf_op jit(solution)/shard_map/rjgxd,rjgpd->rjgxp/dot_general | solution.py:46
  50.1 2.0 %fusion.245 = (f32[2,8,32]{2,1,0:T(8,128)S(1)}, f32[2,2,8,32,128]{4,3,2,1,0:T(8,128)S(1)}) fusion(bf16[8,2,8,128,128]{4,3,2,1,0:T(8,128)(2,1)} %get-tuple-element.42, s32[]{:T(128)S(6)} %select_n.372, bf16[2,8,32,128]{3,2,1,0:T(8,128)(2,1)S(1)} %bitcast.343, pred[2,2,128]{2,1,0:T(4,128)(4,1)S(1)} %broadcast_compare_fusion.7), kind=kOutput, calls=%fused_computation.471 | convolution fusion | flops 33947136 | bytes 1706500 | tf_op jit(solution)/shard_map/rjgxd,rjgpd->rjgxp/dot_general | solution.py:46
  56.5 2.0 %fusion.247 = (f32[2,8,32]{2,1,0:T(8,128)S(1)}, f32[2,2,8,32,128]{4,3,2,1,0:T(8,128)S(1)}) fusion(bf16[8,2,8,128,128]{4,3,2,1,0:T(8,128)(2,1)} %get-tuple-element.42, s32[]{:T(128)S(6)} %select_n.378, bf16[2,8,32,128]{3,2,1,0:T(8,128)(2,1)S(1)} %bitcast.345, pred[2,2,128]{2,1,0:T(4,128)(4,1)S(1)} %broadcast_compare_fusion.6), kind=kOutput, calls=%fused_computation.473 | convolution fusion | flops 33947136 | bytes 1706500 | tf_op jit(solution)/shard_map/rjgxd,rjgpd->rjgxp/dot_general | solution.py:46
  62.5 18.0 %collective-permute-done.5 = bf16[4,2,8192]{2,0,1:T(4,128)(2,1)S(1)} collective-permute-done((bf16[4,2,8192]{2,0,1:T(4,128)(2,1)S(1)}, bf16[4,2,8192]{2,0,1:T(4,128)(2,1)S(1)}, u32[]{:S(2)}, u32[]{:S(2)}) %collective-permute-start.5) | collective-permute-done | bytes 131104 | tf_op jit(solution)/shard_map/ppermute | solution.py:159
  81.5 2.0 %fusion.249 = (f32[2,8,32]{2,1,0:T(8,128)S(1)}, f32[2,2,8,32,128]{4,3,2,1,0:T(8,128)S(1)}) fusion(bf16[8,2,8,128,128]{4,3,2,1,0:T(8,128)(2,1)} %get-tuple-element.42, s32[]{:T(128)S(6)} %select_n.384, bf16[2,8,32,128]{3,2,1,0:T(8,128)(2,1)S(1)} %bitcast.347, pred[2,2,128]{2,1,0:T(4,128)(4,1)S(1)} %broadcast_compare_fusion.5), kind=kOutput, calls=%fused_computation.475 | convolution fusion | flops 33947136 | bytes 1706500 | tf_op jit(solution)/shard_map/rjgxd,rjgpd->rjgxp/dot_general | solution.py:46
  86.2 1.9 %collective-permute-start.6 = (bf16[4,2,8192]{2,0,1:T(4,128)(2,1)S(1)}, bf16[4,2,8192]{2,0,1:T(4,128)(2,1)S(1)}, u32[]{:S(2)}, u32[]{:S(2)}) collective-permute-start(bf16[4,2,8192]{2,0,1:T(4,128)(2,1)S(1)} %get-tuple-element.81), channel_id=1, source_target_pairs={{3,4},{4,5},{5,6},{6,7},{11,12},{12,13},{13,14},{14,15},{19,20},{2... | collective-permute-start | bytes 393224 | tf_op jit(solution)/shard_map/ppermute | solution.py:159
  88.1 5.8 %collective-permute-done.6 = bf16[4,2,8192]{2,0,1:T(4,128)(2,1)S(1)} collective-permute-done((bf16[4,2,8192]{2,0,1:T(4,128)(2,1)S(1)}, bf16[4,2,8192]{2,0,1:T(4,128)(2,1)S(1)}, u32[]{:S(2)}, u32[]{:S(2)}) %collective-permute-start.6) | collective-permute-done | bytes 131104 | tf_op jit(solution)/shard_map/ppermute | solution.py:159
  95.0 2.0 %fusion.251 = (f32[2,8,32]{2,1,0:T(8,128)S(1)}, f32[2,2,8,32,128]{4,3,2,1,0:T(8,128)S(1)}) fusion(bf16[8,2,8,128,128]{4,3,2,1,0:T(8,128)(2,1)} %get-tuple-element.42, s32[]{:T(128)S(6)} %select_n.390, bf16[2,8,32,128]{3,2,1,0:T(8,128)(2,1)S(1)} %bitcast.349, pred[2,2,128]{2,1,0:T(4,128)(4,1)S(1)} %broadcast_compare_fusion.4), kind=kOutput, calls=%fused_computation.477 | convolution fusion | flops 33947136 | bytes 1706500 | tf_op jit(solution)/shard_map/rjgxd,rjgpd->rjgxp/dot_general | solution.py:46
  99.6 1.9 %collective-permute-start.7 = (bf16[4,2,8192]{2,0,1:T(4,128)(2,1)S(1)}, bf16[4,2,8192]{2,0,1:T(4,128)(2,1)S(1)}, u32[]{:S(2)}, u32[]{:S(2)}) collective-permute-start(bf16[4,2,8192]{2,0,1:T(4,128)(2,1)S(1)} %get-tuple-element.77), channel_id=1, source_target_pairs={{4,5},{5,6},{6,7},{12,13},{13,14},{14,15},{20,21},{21,22},{22,23},... | collective-permute-start | bytes 393224 | tf_op jit(solution)/shard_map/ppermute | solution.py:159
  102.2 5.2 %collective-permute-done.7 = bf16[4,2,8192]{2,0,1:T(4,128)(2,1)S(1)} collective-permute-done((bf16[4,2,8192]{2,0,1:T(4,128)(2,1)S(1)}, bf16[4,2,8192]{2,0,1:T(4,128)(2,1)S(1)}, u32[]{:S(2)}, u32[]{:S(2)}) %collective-permute-start.7) | collective-permute-done | bytes 131104 | tf_op jit(solution)/shard_map/ppermute | solution.py:159
  108.4 2.0 %fusion.253 = (f32[2,8,32]{2,1,0:T(8,128)S(1)}, f32[2,2,8,32,128]{4,3,2,1,0:T(8,128)S(1)}) fusion(bf16[8,2,8,128,128]{4,3,2,1,0:T(8,128)(2,1)} %get-tuple-element.42, s32[]{:T(128)S(6)} %select_n.396, bf16[2,8,32,128]{3,2,1,0:T(8,128)(2,1)S(1)} %bitcast.351, pred[2,2,128]{2,1,0:T(4,128)(4,1)S(1)} %broadcast_compare_fusion.3), kind=kOutput, calls=%fused_computation.479 | convolution fusion | flops 33947136 | bytes 1706500 | tf_op jit(solution)/shard_map/rjgxd,rjgpd->rjgxp/dot_general | solution.py:46
  113.0 2.1 %collective-permute-start.8 = (bf16[4,2,8192]{2,0,1:T(4,128)(2,1)S(1)}, bf16[4,2,8192]{2,0,1:T(4,128)(2,1)S(1)}, u32[]{:S(2)}, u32[]{:S(2)}) collective-permute-start(bf16[4,2,8192]{2,0,1:T(4,128)(2,1)S(1)} %get-tuple-element.73), channel_id=1, source_target_pairs={{5,6},{6,7},{13,14},{14,15},{21,22},{22,23},{29,30},{30,31}} | collective-permute-start | bytes 393224 | tf_op jit(solution)/shard_map/ppermute | solution.py:159
  115.3 4.3 %gather_fusion.3 = bf16[4,2,8,128,128]{4,3,2,1,0:T(8,128)(2,1)S(1)} fusion(bf16[16,2,8,128,128]{4,3,2,1,0:T(8,128)(2,1)} %bitcast.314, s32[1024]{0:T(1024)S(1)} %pad_clamp_fusion), kind=kCustom, calls=%fused_computation.3 | custom fusion | bytes 4194320 | tf_op jit(solution)/shard_map/gather | solution.py:123
  124.7 2.0 %fusion.255 = (f32[2,8,32]{2,1,0:T(8,128)S(1)}, f32[2,2,8,32,128]{4,3,2,1,0:T(8,128)S(1)}) fusion(bf16[8,2,8,128,128]{4,3,2,1,0:T(8,128)(2,1)} %get-tuple-element.42, s32[]{:T(128)S(6)} %select_n.402, bf16[2,8,32,128]{3,2,1,0:T(8,128)(2,1)} %bitcast.353, pred[2,2,128]{2,1,0:T(4,128)(4,1)S(1)} %broadcast_compare_fusion.2), kind=kOutput, calls=%fused_computation.481 | convolution fusion | flops 33947136 | bytes 1706500 | tf_op jit(solution)/shard_map/rjgxd,rjgpd->rjgxp/dot_general | solution.py:46
  130.8 1.8 %reshape.643 = f32[4,2,8192]{2,0,1:T(4,128)} reshape(f32[4,2,8,8,128]{4,3,2,0,1:T(8,128)} %copy.271) | data formatting | bytes 524288 | tf_op jit(solution)/shard_map/reshape | solution.py:73
  138.5 2.0 %fusion.257 = (f32[2,8,32]{2,1,0:T(8,128)S(1)}, f32[2,2,8,32,128]{4,3,2,1,0:T(8,128)S(1)}) fusion(bf16[8,2,8,128,128]{4,3,2,1,0:T(8,128)(2,1)} %get-tuple-element.42, s32[]{:T(128)S(6)} %select_n.408, bf16[2,8,32,128]{3,2,1,0:T(8,128)(2,1)S(1)} %bitcast.339, pred[2,2,128]{2,1,0:T(4,128)(4,1)S(1)} %broadcast_compare_fusion.1), kind=kOutput, calls=%fused_computation.483 | convolution fusion | flops 33947136 | bytes 1706500 | tf_op jit(solution)/shard_map/rjgxd,rjgpd->rjgxp/dot_general | solution.py:46
  146.9 3.2 %copy.505 = bf16[1,1,2,2,2,8,128,128]{7,6,5,4,3,2,1,0:T(8,128)(2,1)} copy(bf16[1,1,2,2,2,8,128,128]{7,6,5,4,3,2,1,0:T(8,128)(2,1)} %bitcast.123) | data formatting | bytes 4194304
  (271 shorter events, 64.0 us)
Async XLA Ops:
  0.6 1.0 copy-start
  10.0 4.7 %copy-start.2 = (f32[1,8192]{1,0:T(1,128)S(1)}, f32[1,8192]{1,0:T(1,128)}, u32[]{:S(2)}) copy-start(f32[1,8192]{1,0:T(1,128)} %param.13) | copy-start | bytes 98308
  10.1 5.5 %copy-start.7 = (s32[1,2]{1,0:T(1,128)S(1)}, s32[1,2]{1,0:T(1,128)}, u32[]{:S(2)}) copy-start(s32[1,2]{1,0:T(1,128)} %param.11) | copy-start | bytes 28
  14.9 6.0 %collective-permute-start = (bf16[4,2,8192]{2,0,1:T(4,128)(2,1)S(1)}, bf16[4,2,8192]{2,0,1:T(4,128)(2,1)S(1)}, u32[]{:S(2)}, u32[]{:S(2)}) collective-permute-start(bf16[4,2,8192]{2,0,1:T(4,128)(2,1)S(1)} %get-tuple-element.105), channel_id=1, source_target_pairs={{0,1},{8,9},{16,17},{24,25}} | collective-permute-start | bytes 393224 | tf_op jit(solution)/shard_map/ppermute | solution.py:159
  15.7 4.6 %copy-start.1 = (s32[1,8]{1,0:T(1,128)S(1)}, s32[1,8]{1,0:T(1,128)}, u32[]{:S(2)}) copy-start(s32[1,8]{1,0:T(1,128)} %param.10) | copy-start | bytes 100
  15.7 5.8 %copy-start.3 = (f32[1,8192]{1,0:T(1,128)S(1)}, f32[1,8192]{1,0:T(1,128)}, u32[]{:S(2)}) copy-start(f32[1,8192]{1,0:T(1,128)} %param.12) | copy-start | bytes 98308
  26.6 5.1 %collective-permute-start.1 = (bf16[4,2,8192]{2,0,1:T(4,128)(2,1)S(1)}, bf16[4,2,8192]{2,0,1:T(4,128)(2,1)S(1)}, u32[]{:S(2)}, u32[]{:S(2)}) collective-permute-start(bf16[4,2,8192]{2,0,1:T(4,128)(2,1)S(1)} %get-tuple-element.101), channel_id=1, source_target_pairs={{0,1},{1,2},{8,9},{9,10},{16,17},{17,18},{24,25},{25,26}} | collective-permute-start | bytes 393224 | tf_op jit(solution)/shard_map/ppermute | solution.py:159
  37.4 5.1 %collective-permute-start.2 = (bf16[4,2,8192]{2,0,1:T(4,128)(2,1)S(1)}, bf16[4,2,8192]{2,0,1:T(4,128)(2,1)S(1)}, u32[]{:S(2)}, u32[]{:S(2)}) collective-permute-start(bf16[4,2,8192]{2,0,1:T(4,128)(2,1)S(1)} %get-tuple-element.97), channel_id=1, source_target_pairs={{0,1},{1,2},{2,3},{8,9},{9,10},{10,11},{16,17},{17,18},{18,19},{24... | collective-permute-start | bytes 393224 | tf_op jit(solution)/shard_map/ppermute | solution.py:159
  48.2 0.9 collective-permute-start.3
  54.8 0.7 collective-permute-start.4
  61.1 19.4 %collective-permute-start.5 = (bf16[4,2,8192]{2,0,1:T(4,128)(2,1)S(1)}, bf16[4,2,8192]{2,0,1:T(4,128)(2,1)S(1)}, u32[]{:S(2)}, u32[]{:S(2)}) collective-permute-start(bf16[4,2,8192]{2,0,1:T(4,128)(2,1)S(1)} %get-tuple-element.85), channel_id=1, source_target_pairs={{2,3},{3,4},{4,5},{5,6},{10,11},{11,12},{12,13},{13,14},{18,19},{1... | collective-permute-start | bytes 393224 | tf_op jit(solution)/shard_map/ppermute | solution.py:159
  86.2 7.8 %collective-permute-start.6 = (bf16[4,2,8192]{2,0,1:T(4,128)(2,1)S(1)}, bf16[4,2,8192]{2,0,1:T(4,128)(2,1)S(1)}, u32[]{:S(2)}, u32[]{:S(2)}) collective-permute-start(bf16[4,2,8192]{2,0,1:T(4,128)(2,1)S(1)} %get-tuple-element.81), channel_id=1, source_target_pairs={{3,4},{4,5},{5,6},{6,7},{11,12},{12,13},{13,14},{14,15},{19,20},{2... | collective-permute-start | bytes 393224 | tf_op jit(solution)/shard_map/ppermute | solution.py:159
  95.0 6.6 %copy-start.6 = (s32[1,8,2]{1,2,0:T(2,128)S(1)}, s32[1,8,2]{1,2,0:T(2,128)}, u32[]{:S(2)}) copy-start(s32[1,8,2]{1,2,0:T(2,128)} %param.9) | copy-start | bytes 196
  99.6 7.8 %collective-permute-start.7 = (bf16[4,2,8192]{2,0,1:T(4,128)(2,1)S(1)}, bf16[4,2,8192]{2,0,1:T(4,128)(2,1)S(1)}, u32[]{:S(2)}, u32[]{:S(2)}) collective-permute-start(bf16[4,2,8192]{2,0,1:T(4,128)(2,1)S(1)} %get-tuple-element.77), channel_id=1, source_target_pairs={{4,5},{5,6},{6,7},{12,13},{13,14},{14,15},{20,21},{21,22},{22,23},... | collective-permute-start | bytes 393224 | tf_op jit(solution)/shard_map/ppermute | solution.py:159
  113.0 7.8 %collective-permute-start.8 = (bf16[4,2,8192]{2,0,1:T(4,128)(2,1)S(1)}, bf16[4,2,8192]{2,0,1:T(4,128)(2,1)S(1)}, u32[]{:S(2)}, u32[]{:S(2)}) collective-permute-start(bf16[4,2,8192]{2,0,1:T(4,128)(2,1)S(1)} %get-tuple-element.73), channel_id=1, source_target_pairs={{5,6},{6,7},{13,14},{14,15},{21,22},{22,23},{29,30},{30,31}} | collective-permute-start | bytes 393224 | tf_op jit(solution)/shard_map/ppermute | solution.py:159
  121.3 0.7 copy-start.4
  124.6 7.9 %copy-start.5 = (bf16[4,2,8192]{2,0,1:T(4,128)(2,1)S(1)}, bf16[4,2,8192]{2,0,1:T(4,128)(2,1)}, u32[]{:S(2)}) copy-start(bf16[4,2,8192]{2,0,1:T(4,128)(2,1)} %copy-done.4) | copy-start | bytes 393220
  133.7 3.8 %collective-permute-start.9 = (bf16[4,2,8192]{2,0,1:T(4,128)(2,1)S(1)}, bf16[4,2,8192]{2,0,1:T(4,128)(2,1)S(1)}, u32[]{:S(2)}, u32[]{:S(2)}) collective-permute-start(bf16[4,2,8192]{2,0,1:T(4,128)(2,1)S(1)} %get-tuple-element.69), channel_id=1, source_target_pairs={{6,7},{14,15},{22,23},{30,31}} | collective-permute-start | bytes 393224 | tf_op jit(solution)/shard_map/ppermute | solution.py:159
  136.6 10.4 %collective-permute-start.11 = (bf16[2,2,2,8,128,128]{5,4,3,2,1,0:T(8,128)(2,1)}, bf16[2,2,2,8,128,128]{5,4,3,2,1,0:T(8,128)(2,1)}, u32[]{:S(2)}, u32[]{:S(2)}) collective-permute-start(bf16[2,2,2,8,128,128]{5,4,3,2,1,0:T(8,128)(2,1)} %broadcast_select_fusion), channel_id=1, source_target_pairs={{0,8},{8,0},{1,9},{9,1},{2,10},{10,2},{3,11},{11,3},{4,12},{12,4},... | collective-permute-start | bytes 6291464 | tf_op jit(solution)/shard_map/ppermute | solution.py:20
  143.8 1.4 collective-permute-start.10

commit v7 on v6

--- a/solution.py
+++ b/solution.py
@@ -120,11 +120,8 @@
     steps, reqs, width = inputs.shape
     page_len = pool.shape[3]
     chosen = table[moving]
-    outgoing = pool[chosen]
     spots = jnp.arange(chosen.shape[1])[:, None] * page_len + jnp.arange(page_len)[None, :]
-    keep = spots[None, :, :] < lens[moving][:, None, None]
-    outgoing = jnp.where(keep[:, :, None, None, :, None], outgoing, jnp.zeros((), jnp.bfloat16))
-    received = partner(outgoing, "inst", 0)
+    arrived_lens = partner(lens[moving], "inst", 0)
     lens_used = lens
     section = lax.axis_index("section")
     count = lax.axis_size("section")
@@ -142,7 +139,16 @@
         item = k - section
         live = jnp.logical_and(item >= 0, item < chunks)
         start = jnp.clip(item, 0, chunks - 1) * block
-        if k > 0:
+        if k == 3:
+            start, incoming, chosen = lax.optimization_barrier((start, incoming, chosen))
+            received = partner(pool[chosen], "inst", 0)
+            keep = spots[None, :, :] < arrived_lens[:, None, None]
+            arrived = jnp.where(
+                keep[:, :, None, None, :, None], received, jnp.zeros((), jnp.bfloat16)
+            )
+        elif k == 6:
+            start, incoming, arrived = lax.optimization_barrier((start, incoming, arrived))
+        elif k > 0:
             start, incoming = lax.optimization_barrier((start, incoming))
         first = lax.dynamic_slice_in_dim(inputs, start, block, 1)
         rows = jnp.where(section == 0, first, incoming)
@@ -159,7 +165,7 @@
             incoming = lax.ppermute(result, "section", pairs)
     handed = partner(finished[:, moving], "inst", 0)
     finished = finished.at[:, moving].set(handed)
-    return (finished[None, None], received[None, None])
+    return (finished[None, None], arrived[None, None])
 
 
 def solution(mesh):

time: 153 us -> 153 us (level)
  local copies, waits for them, and re-layouts: 24.9 us -> 22.9 us
    unnamed x19 -> x18, local copies, waits for them, and re-layouts: 6.7 us -> 3.54 us
  transfers between devices with their start and end apart: 12 -> 13, of which waited for: 6 -> 6; matrix products, arithmetic and copies ran while one was open for 10% -> 15% of each run, Pallas kernels for 9% -> 9%
where the time goes in v7:
time: 153 us; the launch traced here: 150 us
  matrix products  44.9 us (29%)
  waiting for transfers between devices  33.4 us (22%)
  local copies, waits for them, and re-layouts  22.9 us (15%)
  Pallas kernels  18 us (12%)
  other arithmetic  15.7 us (10%)
  starting transfers between devices  12.6 us (8%)
  between operations  2.08 us (1%)
    ppermute x10, waiting for transfers between devices, per_device(): incoming = lax.ppermute(result, 'section', pairs)  32.1 us
    dot_general x11, matrix products, layer(): jnp.einsum('rjgxd,rjgpd->rjgxp', wide_query, keys, preferred_element_type...  21.7 us
    pallas_call x4, Pallas kernels, gather_chunk(): pl.pallas_call(copy_kernel, grid_spec=grid_spec, out_shape=[half, half],...  18 us
    dot_general x11, matrix products, layer(): jnp.einsum('rjgxp,rjgpd->rjgxd', cache_w, values, preferred_element_type=...  17.3 us
    ppermute x10, starting transfers between devices, per_device(): incoming = lax.ppermute(result, 'section', pairs)  12.1 us
    gather x1, local copies, waits for them, and re-layouts, per_device(): received = partner(pool[chosen], 'inst', 0)  5.51 us
    reshape x20, local copies, waits for them, and re-layouts, layer(): heads = normed.reshape(steps, reqs, kv_heads, group, head)  3.62 us
    unnamed x18, local copies, waits for them, and re-layouts  3.54 us
  transfers between devices with their start and end apart: 13, of which 6 were waited for; matrix products, arithmetic and copies ran while one was open for 15% of the time, Pallas kernels for 9%

profile of v7, /device:TPU:26, one launch (start us, length us, event | category | flops | bytes accessed | tf_op | source)
XLA Modules:
  0.0 149.6 jit_solution(8596926320076811576)
XLA Ops:
  5.6 4.5 %shard_map.86 = (bf16[8,2,8,128,128]{4,3,2,1,0:T(8,128)(2,1)}, bf16[8,2,8,128,128]{4,3,2,1,0:T(8,128)(2,1)}) custom-call(s32[16]{0:T(128)} %reshape_squeeze.2.table_ref, bf16[16,2,8,128,128]{4,3,2,1,0:T(8,128)(2,1)} %bitcast.306), custom_call_target="tpu_custom_call" | custom-call | tf_op jit(solution)/shard_map/pallas_call | solution.py:108
  10.1 2.0 %fusion.237 = (f32[2,8,32]{2,1,0:T(8,128)S(1)}, f32[2,2,8,32,128]{4,3,2,1,0:T(8,128)S(1)}) fusion(bf16[8,2,8,128,128]{4,3,2,1,0:T(8,128)(2,1)} %get-tuple-element.32.refs_0_, s32[]{:T(128)S(6)} %select_n.339, bf16[2,8,32,128]{3,2,1,0:T(8,128)(2,1)S(1)} %get-tuple-element.111, pred[2,2,128]{2,1,0:T(4,128)(4,1)S(1)} %broadcast_compare_fusion.11), kind=kOutput, calls=%fused_computation.463 | convolution fusion | flops 33947136 | bytes 1706500 | tf_op jit(solution)/shard_map/rjgxd,rjgpd->rjgxp/dot_general | solution.py:46
  16.3 4.6 %shard_map.87 = (bf16[8,2,8,128,128]{4,3,2,1,0:T(8,128)(2,1)}, bf16[8,2,8,128,128]{4,3,2,1,0:T(8,128)(2,1)}) custom-call(s32[16]{0:T(128)} %reshape_squeeze.2.table_ref, bf16[16,2,8,128,128]{4,3,2,1,0:T(8,128)(2,1)} %bitcast.307, bf16[8,2,8,128,128]{4,3,2,1,0:T(8,128)(2,1)} %get-tuple-element.32.refs_0_, ...), custom_call_target="tpu_custom_call", output_to_operand_aliasing={{0}: (2, {}), {1}: (3, {})} | custom-call | tf_op jit(solution)/shard_map/pallas_call | solution.py:108
  22.2 2.0 %fusion.239 = (f32[2,8,32]{2,1,0:T(8,128)S(1)}, f32[2,2,8,32,128]{4,3,2,1,0:T(8,128)S(1)}) fusion(bf16[8,2,8,128,128]{4,3,2,1,0:T(8,128)(2,1)} %get-tuple-element.36.refs_0_, s32[]{:T(128)S(6)} %select_n.347, bf16[2,8,32,128]{3,2,1,0:T(8,128)(2,1)S(1)} %bitcast.337, pred[2,2,128]{2,1,0:T(4,128)(4,1)S(1)} %get-tuple-element.113), kind=kOutput, calls=%fused_computation.465 | convolution fusion | flops 33947136 | bytes 1706500 | tf_op jit(solution)/shard_map/rjgxd,rjgpd->rjgxp/dot_general | solution.py:46
  27.3 4.5 %shard_map.88 = (bf16[8,2,8,128,128]{4,3,2,1,0:T(8,128)(2,1)}, bf16[8,2,8,128,128]{4,3,2,1,0:T(8,128)(2,1)}) custom-call(s32[16]{0:T(128)} %reshape_squeeze.2.table_ref, bf16[16,2,8,128,128]{4,3,2,1,0:T(8,128)(2,1)} %bitcast.308, bf16[8,2,8,128,128]{4,3,2,1,0:T(8,128)(2,1)} %get-tuple-element.36.refs_0_, ...), custom_call_target="tpu_custom_call", output_to_operand_aliasing={{0}: (2, {}), {1}: (3, {})} | custom-call | tf_op jit(solution)/shard_map/pallas_call | solution.py:108
  33.0 2.0 %fusion.241 = (f32[2,8,32]{2,1,0:T(8,128)S(1)}, f32[2,2,8,32,128]{4,3,2,1,0:T(8,128)S(1)}) fusion(bf16[8,2,8,128,128]{4,3,2,1,0:T(8,128)(2,1)} %get-tuple-element.40.refs_0_, s32[]{:T(128)S(6)} %select_n.353, bf16[2,8,32,128]{3,2,1,0:T(8,128)(2,1)S(1)} %bitcast.353, pred[2,2,128]{2,1,0:T(4,128)(4,1)S(1)} %broadcast_compare_fusion.9), kind=kOutput, calls=%fused_computation.467 | convolution fusion | flops 33947136 | bytes 1706500 | tf_op jit(solution)/shard_map/rjgxd,rjgpd->rjgxp/dot_general | solution.py:46
  38.8 4.5 %shard_map.89 = (bf16[8,2,8,128,128]{4,3,2,1,0:T(8,128)(2,1)}, bf16[8,2,8,128,128]{4,3,2,1,0:T(8,128)(2,1)}) custom-call(s32[16]{0:T(128)} %reshape_squeeze.2.table_ref, bf16[16,2,8,128,128]{4,3,2,1,0:T(8,128)(2,1)} %bitcast.309, bf16[8,2,8,128,128]{4,3,2,1,0:T(8,128)(2,1)} %get-tuple-element.40.refs_0_, ...), custom_call_target="tpu_custom_call", output_to_operand_aliasing={{0}: (2, {}), {1}: (3, {})} | custom-call | tf_op jit(solution)/shard_map/pallas_call | solution.py:108
  44.5 2.0 %fusion.243 = (f32[2,8,32]{2,1,0:T(8,128)S(1)}, f32[2,2,8,32,128]{4,3,2,1,0:T(8,128)S(1)}) fusion(bf16[8,2,8,128,128]{4,3,2,1,0:T(8,128)(2,1)} %get-tuple-element.44, s32[]{:T(128)S(6)} %select_n.360, bf16[2,8,32,128]{3,2,1,0:T(8,128)(2,1)S(1)} %bitcast.355, pred[2,2,128]{2,1,0:T(4,128)(4,1)S(1)} %broadcast_compare_fusion.8), kind=kOutput, calls=%fused_computation.469 | convolution fusion | flops 33947136 | bytes 1706500 | tf_op jit(solution)/shard_map/rjgxd,rjgpd->rjgxp/dot_general | solution.py:46
  50.8 2.0 %fusion.245 = (f32[2,8,32]{2,1,0:T(8,128)S(1)}, f32[2,2,8,32,128]{4,3,2,1,0:T(8,128)S(1)}) fusion(bf16[8,2,8,128,128]{4,3,2,1,0:T(8,128)(2,1)} %get-tuple-element.44, s32[]{:T(128)S(6)} %select_n.366, bf16[2,8,32,128]{3,2,1,0:T(8,128)(2,1)S(1)} %bitcast.340, pred[2,2,128]{2,1,0:T(4,128)(4,1)S(1)} %broadcast_compare_fusion.7), kind=kOutput, calls=%fused_computation.471 | convolution fusion | flops 33947136 | bytes 1706500 | tf_op jit(solution)/shard_map/rjgxd,rjgpd->rjgxp/dot_general | solution.py:46
  56.3 5.5 %gather_fusion.2 = bf16[4,2,8,128,128]{4,3,2,1,0:T(8,128)(2,1)} fusion(bf16[16,2,8,128,128]{4,3,2,1,0:T(8,128)(2,1)} %bitcast.310, s32[1024]{0:T(1024)S(1)} %pad_clamp_fusion), kind=kCustom, calls=%fused_computation.2 | custom fusion | bytes 4194320 | tf_op jit(solution)/shard_map/gather | solution.py:144
  66.2 2.0 %fusion.247 = (f32[2,8,32]{2,1,0:T(8,128)S(1)}, f32[2,2,8,32,128]{4,3,2,1,0:T(8,128)S(1)}) fusion(bf16[8,2,8,128,128]{4,3,2,1,0:T(8,128)(2,1)} %get-tuple-element.44, s32[]{:T(128)S(6)} %select_n.372, bf16[2,8,32,128]{3,2,1,0:T(8,128)(2,1)} %bitcast.342, pred[2,2,128]{2,1,0:T(4,128)(4,1)S(1)} %broadcast_compare_fusion.6), kind=kOutput, calls=%fused_computation.473 | convolution fusion | flops 33947136 | bytes 1706500 | tf_op jit(solution)/shard_map/rjgxd,rjgpd->rjgxp/dot_general | solution.py:46
  78.0 10.8 %collective-permute-done.5 = bf16[4,2,8192]{2,0,1:T(4,128)(2,1)S(1)} collective-permute-done((bf16[4,2,8192]{2,0,1:T(4,128)(2,1)S(1)}, bf16[4,2,8192]{2,0,1:T(4,128)(2,1)S(1)}, u32[]{:S(2)}, u32[]{:S(2)}) %collective-permute-start.5) | collective-permute-done | bytes 131104 | tf_op jit(solution)/shard_map/ppermute | solution.py:165
  89.8 2.0 %fusion.249 = (f32[2,8,32]{2,1,0:T(8,128)S(1)}, f32[2,2,8,32,128]{4,3,2,1,0:T(8,128)S(1)}) fusion(bf16[8,2,8,128,128]{4,3,2,1,0:T(8,128)(2,1)} %get-tuple-element.44, s32[]{:T(128)S(6)} %select_n.380, bf16[2,8,32,128]{3,2,1,0:T(8,128)(2,1)S(1)} %bitcast.344, pred[2,2,128]{2,1,0:T(4,128)(4,1)S(1)} %broadcast_compare_fusion.4), kind=kOutput, calls=%fused_computation.475 | convolution fusion | flops 33947136 | bytes 1706500 | tf_op jit(solution)/shard_map/rjgxd,rjgpd->rjgxp/dot_general | solution.py:46
  94.5 1.9 %collective-permute-start.8 = (bf16[4,2,8192]{2,0,1:T(4,128)(2,1)S(1)}, bf16[4,2,8192]{2,0,1:T(4,128)(2,1)S(1)}, u32[]{:S(2)}, u32[]{:S(2)}) collective-permute-start(bf16[4,2,8192]{2,0,1:T(4,128)(2,1)S(1)} %get-tuple-element.85), channel_id=1, source_target_pairs={{3,4},{4,5},{5,6},{6,7},{11,12},{12,13},{13,14},{14,15},{19,20},{2... | collective-permute-start | bytes 393224 | tf_op jit(solution)/shard_map/ppermute | solution.py:165
  96.4 7.4 %collective-permute-done.8 = bf16[4,2,8192]{2,0,1:T(4,128)(2,1)S(1)} collective-permute-done((bf16[4,2,8192]{2,0,1:T(4,128)(2,1)S(1)}, bf16[4,2,8192]{2,0,1:T(4,128)(2,1)S(1)}, u32[]{:S(2)}, u32[]{:S(2)}) %collective-permute-start.8) | collective-permute-done | bytes 131104 | tf_op jit(solution)/shard_map/ppermute | solution.py:165
  104.8 2.0 %fusion.251 = (f32[2,8,32]{2,1,0:T(8,128)S(1)}, f32[2,2,8,32,128]{4,3,2,1,0:T(8,128)S(1)}) fusion(bf16[8,2,8,128,128]{4,3,2,1,0:T(8,128)(2,1)} %get-tuple-element.44, s32[]{:T(128)S(6)} %select_n.386, bf16[2,8,32,128]{3,2,1,0:T(8,128)(2,1)S(1)} %bitcast.346, pred[2,2,128]{2,1,0:T(4,128)(4,1)S(1)} %broadcast_compare_fusion.3), kind=kOutput, calls=%fused_computation.477 | convolution fusion | flops 33947136 | bytes 1706500 | tf_op jit(solution)/shard_map/rjgxd,rjgpd->rjgxp/dot_general | solution.py:46
  109.5 1.9 %collective-permute-start.9 = (bf16[4,2,8192]{2,0,1:T(4,128)(2,1)S(1)}, bf16[4,2,8192]{2,0,1:T(4,128)(2,1)S(1)}, u32[]{:S(2)}, u32[]{:S(2)}) collective-permute-start(bf16[4,2,8192]{2,0,1:T(4,128)(2,1)S(1)} %get-tuple-element.81), channel_id=1, source_target_pairs={{4,5},{5,6},{6,7},{12,13},{13,14},{14,15},{20,21},{21,22},{22,23},... | collective-permute-start | bytes 393224 | tf_op jit(solution)/shard_map/ppermute | solution.py:165
  111.4 5.8 %collective-permute-done.9 = bf16[4,2,8192]{2,0,1:T(4,128)(2,1)S(1)} collective-permute-done((bf16[4,2,8192]{2,0,1:T(4,128)(2,1)S(1)}, bf16[4,2,8192]{2,0,1:T(4,128)(2,1)S(1)}, u32[]{:S(2)}, u32[]{:S(2)}) %collective-permute-start.9) | collective-permute-done | bytes 131104 | tf_op jit(solution)/shard_map/ppermute | solution.py:165
  118.2 2.0 %fusion.253 = (f32[2,8,32]{2,1,0:T(8,128)S(1)}, f32[2,2,8,32,128]{4,3,2,1,0:T(8,128)S(1)}) fusion(bf16[8,2,8,128,128]{4,3,2,1,0:T(8,128)(2,1)} %get-tuple-element.44, s32[]{:T(128)S(6)} %select_n.392, bf16[2,8,32,128]{3,2,1,0:T(8,128)(2,1)S(1)} %bitcast.348, pred[2,2,128]{2,1,0:T(4,128)(4,1)S(1)} %broadcast_compare_fusion.2), kind=kOutput, calls=%fused_computation.479 | convolution fusion | flops 33947136 | bytes 1706500 | tf_op jit(solution)/shard_map/rjgxd,rjgpd->rjgxp/dot_general | solution.py:46
  122.9 2.1 %collective-permute-start.10 = (bf16[4,2,8192]{2,0,1:T(4,128)(2,1)S(1)}, bf16[4,2,8192]{2,0,1:T(4,128)(2,1)S(1)}, u32[]{:S(2)}, u32[]{:S(2)}) collective-permute-start(bf16[4,2,8192]{2,0,1:T(4,128)(2,1)S(1)} %get-tuple-element.77), channel_id=1, source_target_pairs={{5,6},{6,7},{13,14},{14,15},{21,22},{22,23},{29,30},{30,31}} | collective-permute-start | bytes 393224 | tf_op jit(solution)/shard_map/ppermute | solution.py:165
  125.0 5.6 %collective-permute-done.10 = bf16[4,2,8192]{2,0,1:T(4,128)(2,1)S(1)} collective-permute-done((bf16[4,2,8192]{2,0,1:T(4,128)(2,1)S(1)}, bf16[4,2,8192]{2,0,1:T(4,128)(2,1)S(1)}, u32[]{:S(2)}, u32[]{:S(2)}) %collective-permute-start.10) | collective-permute-done | bytes 131104 | tf_op jit(solution)/shard_map/ppermute | solution.py:165
  131.7 2.0 %fusion.255 = (f32[2,8,32]{2,1,0:T(8,128)S(1)}, f32[2,2,8,32,128]{4,3,2,1,0:T(8,128)S(1)}) fusion(bf16[8,2,8,128,128]{4,3,2,1,0:T(8,128)(2,1)} %get-tuple-element.44, s32[]{:T(128)S(6)} %select_n.398, bf16[2,8,32,128]{3,2,1,0:T(8,128)(2,1)S(1)} %bitcast.350, pred[2,2,128]{2,1,0:T(4,128)(4,1)S(1)} %broadcast_compare_fusion.1), kind=kOutput, calls=%fused_computation.481 | convolution fusion | flops 33947136 | bytes 1706500 | tf_op jit(solution)/shard_map/rjgxd,rjgpd->rjgxp/dot_general | solution.py:46
  137.6 2.5 %collective-permute-done.11 = bf16[4,2,8192]{2,0,1:T(4,128)(2,1)S(1)} collective-permute-done((bf16[4,2,8192]{2,0,1:T(4,128)(2,1)S(1)}, bf16[4,2,8192]{2,0,1:T(4,128)(2,1)S(1)}, u32[]{:S(2)}, u32[]{:S(2)}) %collective-permute-start.11) | collective-permute-done | bytes 131104 | tf_op jit(solution)/shard_map/ppermute | solution.py:165
  141.1 2.0 %fusion.257 = (f32[2,8,32]{2,1,0:T(8,128)S(1)}, f32[2,2,8,32,128]{4,3,2,1,0:T(8,128)S(1)}) fusion(bf16[8,2,8,128,128]{4,3,2,1,0:T(8,128)(2,1)} %get-tuple-element.44, s32[]{:T(128)S(6)} %select_n.404, bf16[2,8,32,128]{3,2,1,0:T(8,128)(2,1)S(1)} %bitcast.338, pred[2,2,128]{2,1,0:T(4,128)(4,1)S(1)} %broadcast_compare_fusion), kind=kOutput, calls=%fused_computation.483 | convolution fusion | flops 33947136 | bytes 1706500 | tf_op jit(solution)/shard_map/rjgxd,rjgpd->rjgxp/dot_general | solution.py:46
  (272 shorter events, 64.3 us)
Async XLA Ops:
  0.6 1.0 copy-start
  10.0 4.7 %copy-start.2 = (f32[1,8192]{1,0:T(1,128)S(1)}, f32[1,8192]{1,0:T(1,128)}, u32[]{:S(2)}) copy-start(f32[1,8192]{1,0:T(1,128)} %param.13) | copy-start | bytes 98308
  10.1 5.5 %copy-start.7 = (s32[1,2]{1,0:T(1,128)S(1)}, s32[1,2]{1,0:T(1,128)}, u32[]{:S(2)}) copy-start(s32[1,2]{1,0:T(1,128)} %param.11) | copy-start | bytes 28
  10.1 5.6 %copy-start.1 = (s32[1,8]{1,0:T(1,128)S(1)}, s32[1,8]{1,0:T(1,128)}, u32[]{:S(2)}) copy-start(s32[1,8]{1,0:T(1,128)} %param.10) | copy-start | bytes 100
  15.0 6.0 %collective-permute-start = (bf16[4,2,8192]{2,0,1:T(4,128)(2,1)S(1)}, bf16[4,2,8192]{2,0,1:T(4,128)(2,1)S(1)}, u32[]{:S(2)}, u32[]{:S(2)}) collective-permute-start(bf16[4,2,8192]{2,0,1:T(4,128)(2,1)S(1)} %get-tuple-element.109), channel_id=1, source_target_pairs={{0,1},{8,9},{16,17},{24,25}} | collective-permute-start | bytes 393224 | tf_op jit(solution)/shard_map/ppermute | solution.py:165
  16.3 5.8 %collective-permute-start.6 = (s32[2]{0:T(128)S(1)}, s32[2]{0:T(128)S(1)}, u32[]{:S(2)}, u32[]{:S(2)}) collective-permute-start(s32[2]{0:T(128)S(1)} %gather_fusion.1), channel_id=1, source_target_pairs={{0,8},{8,0},{1,9},{9,1},{2,10},{10,2},{3,11},{11,3},{4,12},{12,4},... | collective-permute-start | bytes 32 | tf_op jit(solution)/shard_map/ppermute | solution.py:20
  16.3 5.1 %copy-start.3 = (f32[1,8192]{1,0:T(1,128)S(1)}, f32[1,8192]{1,0:T(1,128)}, u32[]{:S(2)}) copy-start(f32[1,8192]{1,0:T(1,128)} %param.12) | copy-start | bytes 98308
  26.6 5.1 %collective-permute-start.1 = (bf16[4,2,8192]{2,0,1:T(4,128)(2,1)S(1)}, bf16[4,2,8192]{2,0,1:T(4,128)(2,1)S(1)}, u32[]{:S(2)}, u32[]{:S(2)}) collective-permute-start(bf16[4,2,8192]{2,0,1:T(4,128)(2,1)S(1)} %get-tuple-element.105), channel_id=1, source_target_pairs={{0,1},{1,2},{8,9},{9,10},{16,17},{17,18},{24,25},{25,26}} | collective-permute-start | bytes 393224 | tf_op jit(solution)/shard_map/ppermute | solution.py:165
  32.8 5.3 %copy-start.6 = (s32[1,8,2]{1,2,0:T(2,128)S(1)}, s32[1,8,2]{1,2,0:T(2,128)}, u32[]{:S(2)}) copy-start(s32[1,8,2]{1,2,0:T(2,128)} %param.9) | copy-start | bytes 196
  37.5 5.8 %collective-permute-start.2 = (bf16[4,2,8192]{2,0,1:T(4,128)(2,1)S(1)}, bf16[4,2,8192]{2,0,1:T(4,128)(2,1)S(1)}, u32[]{:S(2)}, u32[]{:S(2)}) collective-permute-start(bf16[4,2,8192]{2,0,1:T(4,128)(2,1)S(1)} %get-tuple-element.101), channel_id=1, source_target_pairs={{0,1},{1,2},{2,3},{8,9},{9,10},{10,11},{16,17},{17,18},{18,19},{24... | collective-permute-start | bytes 393224 | tf_op jit(solution)/shard_map/ppermute | solution.py:165
  48.9 0.9 collective-permute-start.3
  55.5 6.8 %collective-permute-start.4 = (bf16[4,2,8192]{2,0,1:T(4,128)(2,1)S(1)}, bf16[4,2,8192]{2,0,1:T(4,128)(2,1)S(1)}, u32[]{:S(2)}, u32[]{:S(2)}) collective-permute-start(bf16[4,2,8192]{2,0,1:T(4,128)(2,1)S(1)} %get-tuple-element.93), channel_id=1, source_target_pairs={{1,2},{2,3},{3,4},{4,5},{9,10},{10,11},{11,12},{12,13},{17,18},{18... | collective-permute-start | bytes 393224 | tf_op jit(solution)/shard_map/ppermute | solution.py:165
  61.8 14.7 %collective-permute-start.7 = (bf16[2,2,2,8,128,128]{5,4,3,2,1,0:T(8,128)(2,1)}, bf16[2,2,2,8,128,128]{5,4,3,2,1,0:T(8,128)(2,1)S(1)}, u32[]{:S(2)}, u32[]{:S(2)}) collective-permute-start(bf16[2,2,2,8,128,128]{5,4,3,2,1,0:T(8,128)(2,1)} %bitcast.335), channel_id=1, source_target_pairs={{0,8},{8,0},{1,9},{9,1},{2,10},{10,2},{3,11},{11,3},{4,12},{12,4},... | collective-permute-start | bytes 6291464 | tf_op jit(solution)/shard_map/ppermute | solution.py:20
  62.8 0.6 copy-start.4
  66.1 7.9 %copy-start.5 = (bf16[4,2,8192]{2,0,1:T(4,128)(2,1)S(1)}, bf16[4,2,8192]{2,0,1:T(4,128)(2,1)}, u32[]{:S(2)}) copy-start(bf16[4,2,8192]{2,0,1:T(4,128)(2,1)} %copy-done.4) | copy-start | bytes 393220
  75.1 13.7 %collective-permute-start.5 = (bf16[4,2,8192]{2,0,1:T(4,128)(2,1)S(1)}, bf16[4,2,8192]{2,0,1:T(4,128)(2,1)S(1)}, u32[]{:S(2)}, u32[]{:S(2)}) collective-permute-start(bf16[4,2,8192]{2,0,1:T(4,128)(2,1)S(1)} %get-tuple-element.89), channel_id=1, source_target_pairs={{2,3},{3,4},{4,5},{5,6},{10,11},{11,12},{12,13},{13,14},{18,19},{1... | collective-permute-start | bytes 393224 | tf_op jit(solution)/shard_map/ppermute | solution.py:165
  94.5 9.3 %collective-permute-start.8 = (bf16[4,2,8192]{2,0,1:T(4,128)(2,1)S(1)}, bf16[4,2,8192]{2,0,1:T(4,128)(2,1)S(1)}, u32[]{:S(2)}, u32[]{:S(2)}) collective-permute-start(bf16[4,2,8192]{2,0,1:T(4,128)(2,1)S(1)} %get-tuple-element.85), channel_id=1, source_target_pairs={{3,4},{4,5},{5,6},{6,7},{11,12},{12,13},{13,14},{14,15},{19,20},{2... | collective-permute-start | bytes 393224 | tf_op jit(solution)/shard_map/ppermute | solution.py:165
  109.5 7.8 %collective-permute-start.9 = (bf16[4,2,8192]{2,0,1:T(4,128)(2,1)S(1)}, bf16[4,2,8192]{2,0,1:T(4,128)(2,1)S(1)}, u32[]{:S(2)}, u32[]{:S(2)}) collective-permute-start(bf16[4,2,8192]{2,0,1:T(4,128)(2,1)S(1)} %get-tuple-element.81), channel_id=1, source_target_pairs={{4,5},{5,6},{6,7},{12,13},{13,14},{14,15},{20,21},{21,22},{22,23},... | collective-permute-start | bytes 393224 | tf_op jit(solution)/shard_map/ppermute | solution.py:165
  122.9 7.8 %collective-permute-start.10 = (bf16[4,2,8192]{2,0,1:T(4,128)(2,1)S(1)}, bf16[4,2,8192]{2,0,1:T(4,128)(2,1)S(1)}, u32[]{:S(2)}, u32[]{:S(2)}) collective-permute-start(bf16[4,2,8192]{2,0,1:T(4,128)(2,1)S(1)} %get-tuple-element.77), channel_id=1, source_target_pairs={{5,6},{6,7},{13,14},{14,15},{21,22},{22,23},{29,30},{30,31}} | collective-permute-start | bytes 393224 | tf_op jit(solution)/shard_map/ppermute | solution.py:165
  136.3 3.8 %collective-permute-start.11 = (bf16[4,2,8192]{2,0,1:T(4,128)(2,1)S(1)}, bf16[4,2,8192]{2,0,1:T(4,128)(2,1)S(1)}, u32[]{:S(2)}, u32[]{:S(2)}) collective-permute-start(bf16[4,2,8192]{2,0,1:T(4,128)(2,1)S(1)} %get-tuple-element.73), channel_id=1, source_target_pairs={{6,7},{14,15},{22,23},{30,31}} | collective-permute-start | bytes 393224 | tf_op jit(solution)/shard_map/ppermute | solution.py:165
  146.4 1.4 collective-permute-start.12

commit v8 on v7

--- a/solution.py
+++ b/solution.py
@@ -7,7 +7,7 @@
 from jax.experimental import pallas as pl
 from jax.experimental.pallas import tpu as pltpu
 
-CHUNKS = 4
+CHUNKS = 8
 
 
 def partner(block, axis, stride):

time: 153 us -> 189 us (1.24)
  waiting for transfers between devices: 33.4 us -> 44.3 us
  other arithmetic: 15.7 us -> 24 us
  starting transfers between devices: 12.6 us -> 20 us
  Pallas kernels: 18 us -> 22 us
  matrix products: 44.9 us -> 47.8 us
    ppermute x10 -> x14, waiting for transfers between devices: 32.1 us -> 42.9 us  [per_device(): incoming = lax.ppermute(result, 'section', pairs)]
    lt x10 -> x15, other arithmetic: 0.74 us -> 10.7 us  [layer(): live = positions[None] < lens[:, None, None]]
    dynamic_slice x0 -> x15, local copies, waits for them, and re-layouts: none -> 9.47 us  [per_device(): part_lens = lax.dynamic_slice_in_dim(lens_used, start, block, 0)]
    ppermute x10 -> x14, starting transfers between devices: 12.1 us -> 19.5 us  [per_device(): incoming = lax.ppermute(result, 'section', pairs)]
    pallas_call x4 -> x8, Pallas kernels: 18 us -> 22 us  [gather_chunk(): pl.pallas_call(copy_kernel, grid_spec=grid_spec, out_shape=[half, half],...]
    reshape x20 -> x0, local copies, waits for them, and re-layouts: 3.62 us -> none  [layer(): heads = normed.reshape(steps, reqs, kv_heads, group, head)]
    dot_general x11 -> x15, matrix products: 17.3 us -> 19.8 us  [layer(): jnp.einsum('rjgxp,rjgpd->rjgxd', cache_w, values, preferred_element_type=...]
    reshape x11 -> x15, local copies, waits for them, and re-layouts: 2.75 us -> 0.74 us  [layer(): jnp.transpose(attended, (2, 0, 1, 3, 4)).reshape(steps, reqs, width)]
  transfers between devices with their start and end apart: 13 -> 17, of which waited for: 6 -> 10; matrix products, arithmetic and copies ran while one was open for 15% -> 13% of each run, Pallas kernels for 9% -> 10%
where the time goes in v8:
time: 189 us; the launch traced here: 185 us
  matrix products  47.8 us (25%)
  waiting for transfers between devices  44.3 us (23%)
  local copies, waits for them, and re-layouts  24.4 us (13%)
  other arithmetic  24 us (13%)
  Pallas kernels  22 us (12%)
  starting transfers between devices  20 us (11%)
  between operations  2.52 us (1%)
    ppermute x14, waiting for transfers between devices, per_device(): incoming = lax.ppermute(result, 'section', pairs)  42.9 us
    dot_general x15, matrix products, layer(): jnp.einsum('rjgxd,rjgpd->rjgxp', wide_query, keys, preferred_element_type...  22.5 us
    pallas_call x8, Pallas kernels, gather_chunk(): pl.pallas_call(copy_kernel, grid_spec=grid_spec, out_shape=[half, half],...  22 us
    dot_general x15, matrix products, layer(): jnp.einsum('rjgxp,rjgpd->rjgxd', cache_w, values, preferred_element_type=...  19.8 us
    ppermute x14, starting transfers between devices, per_device(): incoming = lax.ppermute(result, 'section', pairs)  19.5 us
    lt x15, other arithmetic, layer(): live = positions[None] < lens[:, None, None]  10.7 us
    dynamic_slice x15, local copies, waits for them, and re-layouts, per_device(): part_lens = lax.dynamic_slice_in_dim(lens_used, start, block, 0)  9.47 us
    gather x1, local copies, waits for them, and re-layouts, per_device(): received = partner(pool[chosen], 'inst', 0)  5.52 us
  transfers between devices with their start and end apart: 17, of which 10 were waited for; matrix products, arithmetic and copies ran while one was open for 13% of the time, Pallas kernels for 10%

profile of v8, /device:TPU:26, one launch (start us, length us, event | category | flops | bytes accessed | tf_op | source)
XLA Modules:
  0.0 185.0 jit_solution(2548189184939044681)
XLA Ops:
  5.6 2.8 %shard_map.89 = (bf16[8,2,8,128,128]{4,3,2,1,0:T(8,128)(2,1)}, bf16[8,2,8,128,128]{4,3,2,1,0:T(8,128)(2,1)}) custom-call(s32[16]{0:T(128)} %reshape_squeeze.2.table_ref, bf16[16,2,8,128,128]{4,3,2,1,0:T(8,128)(2,1)} %bitcast.909), custom_call_target="tpu_custom_call" | custom-call | tf_op jit(solution)/shard_map/pallas_call | solution.py:108
  14.3 2.9 %shard_map.90 = (bf16[8,2,8,128,128]{4,3,2,1,0:T(8,128)(2,1)}, bf16[8,2,8,128,128]{4,3,2,1,0:T(8,128)(2,1)}) custom-call(s32[16]{0:T(128)} %reshape_squeeze.2.table_ref, bf16[16,2,8,128,128]{4,3,2,1,0:T(8,128)(2,1)} %bitcast.910, bf16[8,2,8,128,128]{4,3,2,1,0:T(8,128)(2,1)} %get-tuple-element.48.refs_0_, ...), custom_call_target="tpu_custom_call", output_to_operand_aliasing={{0}: (2, {}), {1}: (3, {})} | custom-call | tf_op jit(solution)/shard_map/pallas_call | solution.py:108
  24.1 2.7 %shard_map.91 = (bf16[8,2,8,128,128]{4,3,2,1,0:T(8,128)(2,1)}, bf16[8,2,8,128,128]{4,3,2,1,0:T(8,128)(2,1)}) custom-call(s32[16]{0:T(128)} %reshape_squeeze.2.table_ref, bf16[16,2,8,128,128]{4,3,2,1,0:T(8,128)(2,1)} %bitcast.911, bf16[8,2,8,128,128]{4,3,2,1,0:T(8,128)(2,1)} %get-tuple-element.52.refs_0_, ...), custom_call_target="tpu_custom_call", output_to_operand_aliasing={{0}: (2, {}), {1}: (3, {})} | custom-call | tf_op jit(solution)/shard_map/pallas_call | solution.py:108
  33.1 2.7 %shard_map.92 = (bf16[8,2,8,128,128]{4,3,2,1,0:T(8,128)(2,1)}, bf16[8,2,8,128,128]{4,3,2,1,0:T(8,128)(2,1)}) custom-call(s32[16]{0:T(128)} %reshape_squeeze.2.table_ref, bf16[16,2,8,128,128]{4,3,2,1,0:T(8,128)(2,1)} %bitcast.912, bf16[8,2,8,128,128]{4,3,2,1,0:T(8,128)(2,1)} %get-tuple-element.56.refs_0_, ...), custom_call_target="tpu_custom_call", output_to_operand_aliasing={{0}: (2, {}), {1}: (3, {})} | custom-call | tf_op jit(solution)/shard_map/pallas_call | solution.py:108
  42.1 2.7 %shard_map.93 = (bf16[8,2,8,128,128]{4,3,2,1,0:T(8,128)(2,1)}, bf16[8,2,8,128,128]{4,3,2,1,0:T(8,128)(2,1)}) custom-call(s32[16]{0:T(128)} %reshape_squeeze.2.table_ref, bf16[16,2,8,128,128]{4,3,2,1,0:T(8,128)(2,1)} %bitcast.913, bf16[8,2,8,128,128]{4,3,2,1,0:T(8,128)(2,1)} %get-tuple-element.60.refs_0_, ...), custom_call_target="tpu_custom_call", output_to_operand_aliasing={{0}: (2, {}), {1}: (3, {})} | custom-call | tf_op jit(solution)/shard_map/pallas_call | solution.py:108
  51.1 5.5 %gather_fusion.2 = bf16[4,2,8,128,128]{4,3,2,1,0:T(8,128)(2,1)} fusion(bf16[16,2,8,128,128]{4,3,2,1,0:T(8,128)(2,1)} %bitcast.914, s32[1024]{0:T(1024)S(1)} %pad_clamp_fusion), kind=kCustom, calls=%fused_computation.2 | custom fusion | bytes 4194320 | tf_op jit(solution)/shard_map/gather | solution.py:144
  57.1 2.7 %shard_map.94 = (bf16[8,2,8,128,128]{4,3,2,1,0:T(8,128)(2,1)}, bf16[8,2,8,128,128]{4,3,2,1,0:T(8,128)(2,1)}) custom-call(s32[16]{0:T(128)} %reshape_squeeze.2.table_ref, bf16[16,2,8,128,128]{4,3,2,1,0:T(8,128)(2,1)} %bitcast.915, bf16[8,2,8,128,128]{4,3,2,1,0:T(8,128)(2,1)} %get-tuple-element.64.refs_0_, ...), custom_call_target="tpu_custom_call", output_to_operand_aliasing={{0}: (2, {}), {1}: (3, {})} | custom-call | tf_op jit(solution)/shard_map/pallas_call | solution.py:108
  65.1 2.7 %shard_map.95 = (bf16[8,2,8,128,128]{4,3,2,1,0:T(8,128)(2,1)}, bf16[8,2,8,128,128]{4,3,2,1,0:T(8,128)(2,1)}) custom-call(s32[16]{0:T(128)} %reshape_squeeze.2.table_ref, bf16[16,2,8,128,128]{4,3,2,1,0:T(8,128)(2,1)} %bitcast.916, bf16[8,2,8,128,128]{4,3,2,1,0:T(8,128)(2,1)} %get-tuple-element.68.refs_0_, ...), custom_call_target="tpu_custom_call", output_to_operand_aliasing={{0}: (2, {}), {1}: (3, {})} | custom-call | tf_op jit(solution)/shard_map/pallas_call | solution.py:108
  70.9 4.5 %collective-permute-done.5 = bf16[4,1,8192]{2,0,1:T(4,128)(2,1)S(1)} collective-permute-done((bf16[4,1,8192]{2,0,1:T(4,128)(2,1)S(1)}, bf16[4,1,8192]{2,0,1:T(4,128)(2,1)S(1)}, u32[]{:S(2)}, u32[]{:S(2)}) %collective-permute-start.5) | collective-permute-done | bytes 65568 | tf_op jit(solution)/shard_map/ppermute | solution.py:165
  80.8 2.1 %collective-permute-start.8 = (bf16[4,1,8192]{2,0,1:T(4,128)(2,1)S(1)}, bf16[4,1,8192]{2,0,1:T(4,128)(2,1)S(1)}, u32[]{:S(2)}, u32[]{:S(2)}) collective-permute-start(bf16[4,1,8192]{2,0,1:T(4,128)(2,1)S(1)} %get-tuple-element.133), channel_id=1, source_target_pairs={{0,1},{1,2},{2,3},{3,4},{4,5},{5,6},{6,7},{8,9},{9,10},{10,11},{11... | collective-permute-start | bytes 196616 | tf_op jit(solution)/shard_map/ppermute | solution.py:165
  82.9 2.7 %shard_map.96 = (bf16[8,2,8,128,128]{4,3,2,1,0:T(8,128)(2,1)}, bf16[8,2,8,128,128]{4,3,2,1,0:T(8,128)(2,1)}) custom-call(s32[16]{0:T(128)} %reshape_squeeze.2.table_ref, bf16[16,2,8,128,128]{4,3,2,1,0:T(8,128)(2,1)} %bitcast.917, bf16[8,2,8,128,128]{4,3,2,1,0:T(8,128)(2,1)} %get-tuple-element.73.refs_0_, ...), custom_call_target="tpu_custom_call", output_to_operand_aliasing={{0}: (2, {}), {1}: (3, {})} | custom-call | tf_op jit(solution)/shard_map/pallas_call | solution.py:108
  85.6 5.9 %collective-permute-done.8 = bf16[4,1,8192]{2,0,1:T(4,128)(2,1)S(1)} collective-permute-done((bf16[4,1,8192]{2,0,1:T(4,128)(2,1)S(1)}, bf16[4,1,8192]{2,0,1:T(4,128)(2,1)S(1)}, u32[]{:S(2)}, u32[]{:S(2)}) %collective-permute-start.8) | collective-permute-done | bytes 65568 | tf_op jit(solution)/shard_map/ppermute | solution.py:165
  97.0 1.9 %collective-permute-start.9 = (bf16[4,1,8192]{2,0,1:T(4,128)(2,1)S(1)}, bf16[4,1,8192]{2,0,1:T(4,128)(2,1)S(1)}, u32[]{:S(2)}, u32[]{:S(2)}) collective-permute-start(bf16[4,1,8192]{2,0,1:T(4,128)(2,1)S(1)} %get-tuple-element.129), channel_id=1, source_target_pairs={{0,1},{1,2},{2,3},{3,4},{4,5},{5,6},{6,7},{8,9},{9,10},{10,11},{11... | collective-permute-start | bytes 196616 | tf_op jit(solution)/shard_map/ppermute | solution.py:165
  99.0 5.1 %collective-permute-done.9 = bf16[4,1,8192]{2,0,1:T(4,128)(2,1)S(1)} collective-permute-done((bf16[4,1,8192]{2,0,1:T(4,128)(2,1)S(1)}, bf16[4,1,8192]{2,0,1:T(4,128)(2,1)S(1)}, u32[]{:S(2)}, u32[]{:S(2)}) %collective-permute-start.9) | collective-permute-done | bytes 65568 | tf_op jit(solution)/shard_map/ppermute | solution.py:165
  109.6 1.9 %collective-permute-start.10 = (bf16[4,1,8192]{2,0,1:T(4,128)(2,1)S(1)}, bf16[4,1,8192]{2,0,1:T(4,128)(2,1)S(1)}, u32[]{:S(2)}, u32[]{:S(2)}) collective-permute-start(bf16[4,1,8192]{2,0,1:T(4,128)(2,1)S(1)} %get-tuple-element.125), channel_id=1, source_target_pairs={{1,2},{2,3},{3,4},{4,5},{5,6},{6,7},{9,10},{10,11},{11,12},{12,13}... | collective-permute-start | bytes 196616 | tf_op jit(solution)/shard_map/ppermute | solution.py:165
  111.5 5.1 %collective-permute-done.10 = bf16[4,1,8192]{2,0,1:T(4,128)(2,1)S(1)} collective-permute-done((bf16[4,1,8192]{2,0,1:T(4,128)(2,1)S(1)}, bf16[4,1,8192]{2,0,1:T(4,128)(2,1)S(1)}, u32[]{:S(2)}, u32[]{:S(2)}) %collective-permute-start.10) | collective-permute-done | bytes 65568 | tf_op jit(solution)/shard_map/ppermute | solution.py:165
  122.2 1.9 %collective-permute-start.11 = (bf16[4,1,8192]{2,0,1:T(4,128)(2,1)S(1)}, bf16[4,1,8192]{2,0,1:T(4,128)(2,1)S(1)}, u32[]{:S(2)}, u32[]{:S(2)}) collective-permute-start(bf16[4,1,8192]{2,0,1:T(4,128)(2,1)S(1)} %get-tuple-element.121), channel_id=1, source_target_pairs={{2,3},{3,4},{4,5},{5,6},{6,7},{10,11},{11,12},{12,13},{13,14},{14,... | collective-permute-start | bytes 196616 | tf_op jit(solution)/shard_map/ppermute | solution.py:165
  124.1 5.1 %collective-permute-done.11 = bf16[4,1,8192]{2,0,1:T(4,128)(2,1)S(1)} collective-permute-done((bf16[4,1,8192]{2,0,1:T(4,128)(2,1)S(1)}, bf16[4,1,8192]{2,0,1:T(4,128)(2,1)S(1)}, u32[]{:S(2)}, u32[]{:S(2)}) %collective-permute-start.11) | collective-permute-done | bytes 65568 | tf_op jit(solution)/shard_map/ppermute | solution.py:165
  134.8 1.9 %collective-permute-start.12 = (bf16[4,1,8192]{2,0,1:T(4,128)(2,1)S(1)}, bf16[4,1,8192]{2,0,1:T(4,128)(2,1)S(1)}, u32[]{:S(2)}, u32[]{:S(2)}) collective-permute-start(bf16[4,1,8192]{2,0,1:T(4,128)(2,1)S(1)} %get-tuple-element.117), channel_id=1, source_target_pairs={{3,4},{4,5},{5,6},{6,7},{11,12},{12,13},{13,14},{14,15},{19,20},{2... | collective-permute-start | bytes 196616 | tf_op jit(solution)/shard_map/ppermute | solution.py:165
  136.7 5.1 %collective-permute-done.12 = bf16[4,1,8192]{2,0,1:T(4,128)(2,1)S(1)} collective-permute-done((bf16[4,1,8192]{2,0,1:T(4,128)(2,1)S(1)}, bf16[4,1,8192]{2,0,1:T(4,128)(2,1)S(1)}, u32[]{:S(2)}, u32[]{:S(2)}) %collective-permute-start.12) | collective-permute-done | bytes 65568 | tf_op jit(solution)/shard_map/ppermute | solution.py:165
  147.3 1.9 %collective-permute-start.13 = (bf16[4,1,8192]{2,0,1:T(4,128)(2,1)S(1)}, bf16[4,1,8192]{2,0,1:T(4,128)(2,1)S(1)}, u32[]{:S(2)}, u32[]{:S(2)}) collective-permute-start(bf16[4,1,8192]{2,0,1:T(4,128)(2,1)S(1)} %get-tuple-element.113), channel_id=1, source_target_pairs={{4,5},{5,6},{6,7},{12,13},{13,14},{14,15},{20,21},{21,22},{22,23},... | collective-permute-start | bytes 196616 | tf_op jit(solution)/shard_map/ppermute | solution.py:165
  149.3 5.1 %collective-permute-done.13 = bf16[4,1,8192]{2,0,1:T(4,128)(2,1)S(1)} collective-permute-done((bf16[4,1,8192]{2,0,1:T(4,128)(2,1)S(1)}, bf16[4,1,8192]{2,0,1:T(4,128)(2,1)S(1)}, u32[]{:S(2)}, u32[]{:S(2)}) %collective-permute-start.13) | collective-permute-done | bytes 65568 | tf_op jit(solution)/shard_map/ppermute | solution.py:165
  159.9 1.9 %collective-permute-start.14 = (bf16[4,1,8192]{2,0,1:T(4,128)(2,1)S(1)}, bf16[4,1,8192]{2,0,1:T(4,128)(2,1)S(1)}, u32[]{:S(2)}, u32[]{:S(2)}) collective-permute-start(bf16[4,1,8192]{2,0,1:T(4,128)(2,1)S(1)} %get-tuple-element.109), channel_id=1, source_target_pairs={{5,6},{6,7},{13,14},{14,15},{21,22},{22,23},{29,30},{30,31}} | collective-permute-start | bytes 196616 | tf_op jit(solution)/shard_map/ppermute | solution.py:165
  161.8 5.1 %collective-permute-done.14 = bf16[4,1,8192]{2,0,1:T(4,128)(2,1)S(1)} collective-permute-done((bf16[4,1,8192]{2,0,1:T(4,128)(2,1)S(1)}, bf16[4,1,8192]{2,0,1:T(4,128)(2,1)S(1)}, u32[]{:S(2)}, u32[]{:S(2)}) %collective-permute-start.14) | collective-permute-done | bytes 65568 | tf_op jit(solution)/shard_map/ppermute | solution.py:165
  (358 shorter events, 100.3 us)
Async XLA Ops:
  0.7 60.4 %copy-start.6 = (s32[2]{0:T(128)}, s32[2]{0:T(128)S(1)}, u32[]{:S(2)}) copy-start(s32[2]{0:T(128)S(1)} %iota_multiply_fusion) | copy-start | bytes 28
  3.0 58.0 %copy-start.8 = (pred[32,4]{0,1:T(4,128)(4,1)}, pred[32,4]{0,1:T(4,128)(4,1)S(1)}, u32[]{:S(2)}) copy-start(pred[32,4]{0,1:T(4,128)(4,1)S(1)} %iota_compare_fusion) | copy-start | bytes 388
  5.6 7.3 %copy-start.3 = (f32[1,8192]{1,0:T(1,128)S(1)}, f32[1,8192]{1,0:T(1,128)}, u32[]{:S(2)}) copy-start(f32[1,8192]{1,0:T(1,128)} %param.13) | copy-start | bytes 98308
  8.4 5.2 %copy-start.1 = (s32[1,8]{1,0:T(1,128)S(1)}, s32[1,8]{1,0:T(1,128)}, u32[]{:S(2)}) copy-start(s32[1,8]{1,0:T(1,128)} %param.10) | copy-start | bytes 100
  13.0 4.2 %collective-permute-start = (bf16[4,1,8192]{2,0,1:T(4,128)(2,1)S(1)}, bf16[4,1,8192]{2,0,1:T(4,128)(2,1)S(1)}, u32[]{:S(2)}, u32[]{:S(2)}) collective-permute-start(bf16[4,1,8192]{2,0,1:T(4,128)(2,1)S(1)} %get-tuple-element.157), channel_id=1, source_target_pairs={{0,1},{8,9},{16,17},{24,25}} | collective-permute-start | bytes 196616 | tf_op jit(solution)/shard_map/ppermute | solution.py:165
  14.3 18.7 %collective-permute-start.6 = (s32[2]{0:T(128)S(1)}, s32[2]{0:T(128)S(1)}, u32[]{:S(2)}, u32[]{:S(2)}) collective-permute-start(s32[2]{0:T(128)S(1)} %gather_fusion.1), channel_id=1, source_target_pairs={{0,8},{8,0},{1,9},{9,1},{2,10},{10,2},{3,11},{11,3},{4,12},{12,4},... | collective-permute-start | bytes 32 | tf_op jit(solution)/shard_map/ppermute | solution.py:20
  17.2 6.3 %copy-start.4 = (s32[1,8,2]{1,2,0:T(2,128)S(1)}, s32[1,8,2]{1,2,0:T(2,128)}, u32[]{:S(2)}) copy-start(s32[1,8,2]{1,2,0:T(2,128)} %param.9) | copy-start | bytes 196
  22.7 4.1 %collective-permute-start.1 = (bf16[4,1,8192]{2,0,1:T(4,128)(2,1)S(1)}, bf16[4,1,8192]{2,0,1:T(4,128)(2,1)S(1)}, u32[]{:S(2)}, u32[]{:S(2)}) collective-permute-start(bf16[4,1,8192]{2,0,1:T(4,128)(2,1)S(1)} %get-tuple-element.153), channel_id=1, source_target_pairs={{0,1},{1,2},{8,9},{9,10},{16,17},{17,18},{24,25},{25,26}} | collective-permute-start | bytes 196616 | tf_op jit(solution)/shard_map/ppermute | solution.py:165
  32.4 3.5 %collective-permute-start.2 = (bf16[4,1,8192]{2,0,1:T(4,128)(2,1)S(1)}, bf16[4,1,8192]{2,0,1:T(4,128)(2,1)S(1)}, u32[]{:S(2)}, u32[]{:S(2)}) collective-permute-start(bf16[4,1,8192]{2,0,1:T(4,128)(2,1)S(1)} %get-tuple-element.149), channel_id=1, source_target_pairs={{0,1},{1,2},{2,3},{8,9},{9,10},{10,11},{16,17},{17,18},{18,19},{24... | collective-permute-start | bytes 196616 | tf_op jit(solution)/shard_map/ppermute | solution.py:165
  41.4 3.5 %collective-permute-start.3 = (bf16[4,1,8192]{2,0,1:T(4,128)(2,1)S(1)}, bf16[4,1,8192]{2,0,1:T(4,128)(2,1)S(1)}, u32[]{:S(2)}, u32[]{:S(2)}) collective-permute-start(bf16[4,1,8192]{2,0,1:T(4,128)(2,1)S(1)} %get-tuple-element.145), channel_id=1, source_target_pairs={{0,1},{1,2},{2,3},{3,4},{8,9},{9,10},{10,11},{11,12},{16,17},{17,1... | collective-permute-start | bytes 196616 | tf_op jit(solution)/shard_map/ppermute | solution.py:165
  50.4 9.4 %collective-permute-start.4 = (bf16[4,1,8192]{2,0,1:T(4,128)(2,1)S(1)}, bf16[4,1,8192]{2,0,1:T(4,128)(2,1)S(1)}, u32[]{:S(2)}, u32[]{:S(2)}) collective-permute-start(bf16[4,1,8192]{2,0,1:T(4,128)(2,1)S(1)} %get-tuple-element.141), channel_id=1, source_target_pairs={{0,1},{1,2},{2,3},{3,4},{4,5},{8,9},{9,10},{10,11},{11,12},{12,13}... | collective-permute-start | bytes 196616 | tf_op jit(solution)/shard_map/ppermute | solution.py:165
  56.6 12.7 %collective-permute-start.7 = (bf16[2,2,2,8,128,128]{5,4,3,2,1,0:T(8,128)(2,1)}, bf16[2,2,2,8,128,128]{5,4,3,2,1,0:T(8,128)(2,1)S(1)}, u32[]{:S(2)}, u32[]{:S(2)}) collective-permute-start(bf16[2,2,2,8,128,128]{5,4,3,2,1,0:T(8,128)(2,1)} %bitcast.951), channel_id=1, source_target_pairs={{0,8},{8,0},{1,9},{9,1},{2,10},{10,2},{3,11},{11,3},{4,12},{12,4},... | collective-permute-start | bytes 6291464 | tf_op jit(solution)/shard_map/ppermute | solution.py:20
  67.9 8.6 %copy-start.9 = (pred[32,4]{0,1:T(4,128)(4,1)S(1)}, pred[32,4]{0,1:T(4,128)(4,1)}, u32[]{:S(2)}) copy-start(pred[32,4]{0,1:T(4,128)(4,1)} %copy-done.8) | copy-start | bytes 388
  67.9 8.8 %copy-start.7 = (s32[2]{0:T(128)S(1)}, s32[2]{0:T(128)}, u32[]{:S(2)}) copy-start(s32[2]{0:T(128)} %copy-done.6) | copy-start | bytes 28
  68.0 7.4 %collective-permute-start.5 = (bf16[4,1,8192]{2,0,1:T(4,128)(2,1)S(1)}, bf16[4,1,8192]{2,0,1:T(4,128)(2,1)S(1)}, u32[]{:S(2)}, u32[]{:S(2)}) collective-permute-start(bf16[4,1,8192]{2,0,1:T(4,128)(2,1)S(1)} %get-tuple-element.137), channel_id=1, source_target_pairs={{0,1},{1,2},{2,3},{3,4},{4,5},{5,6},{8,9},{9,10},{10,11},{11,12},{... | collective-permute-start | bytes 196616 | tf_op jit(solution)/shard_map/ppermute | solution.py:165
  80.8 10.7 %collective-permute-start.8 = (bf16[4,1,8192]{2,0,1:T(4,128)(2,1)S(1)}, bf16[4,1,8192]{2,0,1:T(4,128)(2,1)S(1)}, u32[]{:S(2)}, u32[]{:S(2)}) collective-permute-start(bf16[4,1,8192]{2,0,1:T(4,128)(2,1)S(1)} %get-tuple-element.133), channel_id=1, source_target_pairs={{0,1},{1,2},{2,3},{3,4},{4,5},{5,6},{6,7},{8,9},{9,10},{10,11},{11... | collective-permute-start | bytes 196616 | tf_op jit(solution)/shard_map/ppermute | solution.py:165
  97.0 7.1 %collective-permute-start.9 = (bf16[4,1,8192]{2,0,1:T(4,128)(2,1)S(1)}, bf16[4,1,8192]{2,0,1:T(4,128)(2,1)S(1)}, u32[]{:S(2)}, u32[]{:S(2)}) collective-permute-start(bf16[4,1,8192]{2,0,1:T(4,128)(2,1)S(1)} %get-tuple-element.129), channel_id=1, source_target_pairs={{0,1},{1,2},{2,3},{3,4},{4,5},{5,6},{6,7},{8,9},{9,10},{10,11},{11... | collective-permute-start | bytes 196616 | tf_op jit(solution)/shard_map/ppermute | solution.py:165
  109.6 7.1 %collective-permute-start.10 = (bf16[4,1,8192]{2,0,1:T(4,128)(2,1)S(1)}, bf16[4,1,8192]{2,0,1:T(4,128)(2,1)S(1)}, u32[]{:S(2)}, u32[]{:S(2)}) collective-permute-start(bf16[4,1,8192]{2,0,1:T(4,128)(2,1)S(1)} %get-tuple-element.125), channel_id=1, source_target_pairs={{1,2},{2,3},{3,4},{4,5},{5,6},{6,7},{9,10},{10,11},{11,12},{12,13}... | collective-permute-start | bytes 196616 | tf_op jit(solution)/shard_map/ppermute | solution.py:165
  122.2 7.1 %collective-permute-start.11 = (bf16[4,1,8192]{2,0,1:T(4,128)(2,1)S(1)}, bf16[4,1,8192]{2,0,1:T(4,128)(2,1)S(1)}, u32[]{:S(2)}, u32[]{:S(2)}) collective-permute-start(bf16[4,1,8192]{2,0,1:T(4,128)(2,1)S(1)} %get-tuple-element.121), channel_id=1, source_target_pairs={{2,3},{3,4},{4,5},{5,6},{6,7},{10,11},{11,12},{12,13},{13,14},{14,... | collective-permute-start | bytes 196616 | tf_op jit(solution)/shard_map/ppermute | solution.py:165
  134.8 7.1 %collective-permute-start.12 = (bf16[4,1,8192]{2,0,1:T(4,128)(2,1)S(1)}, bf16[4,1,8192]{2,0,1:T(4,128)(2,1)S(1)}, u32[]{:S(2)}, u32[]{:S(2)}) collective-permute-start(bf16[4,1,8192]{2,0,1:T(4,128)(2,1)S(1)} %get-tuple-element.117), channel_id=1, source_target_pairs={{3,4},{4,5},{5,6},{6,7},{11,12},{12,13},{13,14},{14,15},{19,20},{2... | collective-permute-start | bytes 196616 | tf_op jit(solution)/shard_map/ppermute | solution.py:165
  147.3 7.1 %collective-permute-start.13 = (bf16[4,1,8192]{2,0,1:T(4,128)(2,1)S(1)}, bf16[4,1,8192]{2,0,1:T(4,128)(2,1)S(1)}, u32[]{:S(2)}, u32[]{:S(2)}) collective-permute-start(bf16[4,1,8192]{2,0,1:T(4,128)(2,1)S(1)} %get-tuple-element.113), channel_id=1, source_target_pairs={{4,5},{5,6},{6,7},{12,13},{13,14},{14,15},{20,21},{21,22},{22,23},... | collective-permute-start | bytes 196616 | tf_op jit(solution)/shard_map/ppermute | solution.py:165
  159.9 7.1 %collective-permute-start.14 = (bf16[4,1,8192]{2,0,1:T(4,128)(2,1)S(1)}, bf16[4,1,8192]{2,0,1:T(4,128)(2,1)S(1)}, u32[]{:S(2)}, u32[]{:S(2)}) collective-permute-start(bf16[4,1,8192]{2,0,1:T(4,128)(2,1)S(1)} %get-tuple-element.109), channel_id=1, source_target_pairs={{5,6},{6,7},{13,14},{14,15},{21,22},{22,23},{29,30},{30,31}} | collective-permute-start | bytes 196616 | tf_op jit(solution)/shard_map/ppermute | solution.py:165
  172.5 3.2 %collective-permute-start.15 = (bf16[4,1,8192]{2,0,1:T(4,128)(2,1)S(1)}, bf16[4,1,8192]{2,0,1:T(4,128)(2,1)S(1)}, u32[]{:S(2)}, u32[]{:S(2)}) collective-permute-start(bf16[4,1,8192]{2,0,1:T(4,128)(2,1)S(1)} %get-tuple-element.105), channel_id=1, source_target_pairs={{6,7},{14,15},{22,23},{30,31}} | collective-permute-start | bytes 196616 | tf_op jit(solution)/shard_map/ppermute | solution.py:165
  181.8 1.4 collective-permute-start.16
  (3 other events, 10.1 us)

commit v9 on v7

--- a/solution.py
+++ b/solution.py
@@ -129,15 +129,13 @@
     block = reqs // chunks
 
     incoming = jnp.zeros((steps, block, width), jnp.bfloat16)
-    finished = jnp.zeros((steps, reqs, width), jnp.bfloat16)
-    zero = jnp.zeros((), jnp.int32)
     keys, values = None, None
+    results = []
     for k in range(chunks + count - 1):
         if k < chunks:
             previous = None if keys is None else (keys, values)
             keys, values = gather_chunk(pool, table, k, block, previous)
         item = k - section
-        live = jnp.logical_and(item >= 0, item < chunks)
         start = jnp.clip(item, 0, chunks - 1) * block
         if k == 3:
             start, incoming, chosen = lax.optimization_barrier((start, incoming, chosen))
@@ -156,13 +154,14 @@
         part_values = lax.dynamic_slice_in_dim(values, start, block, 0)
         part_lens = lax.dynamic_slice_in_dim(lens_used, start, block, 0)
         result = layer(rows, part_keys, part_values, part_lens, gain, scale)
-        previous = lax.dynamic_slice_in_dim(finished, start, block, 1)
-        finished = lax.dynamic_update_slice(
-            finished, jnp.where(live, result, previous), (zero, start, zero)
-        )
+        results.append(result)
         pairs = [(s, s + 1) for s in range(count - 1) if 0 <= k - s < chunks]
         if pairs:
             incoming = lax.ppermute(result, "section", pairs)
+    stacked = jnp.stack(results)
+    finished = jnp.concatenate(
+        [lax.dynamic_index_in_dim(stacked, c + section, 0, False) for c in range(chunks)], axis=1
+    )
     handed = partner(finished[:, moving], "inst", 0)
     finished = finished.at[:, moving].set(handed)
     return (finished[None, None], arrived[None, None])

time: 153 us -> 149 us (0.974)
  local copies, waits for them, and re-layouts: 22.9 us -> 17 us
  other arithmetic: 15.7 us -> 19.5 us
    unnamed x0 -> x10, other arithmetic: none -> 2.78 us
    dynamic_update_slice x11 -> x0, other arithmetic: 2.75 us -> none  [per_device(): lax.dynamic_update_slice(finished, jnp.where(live, result, previous), (ze...]
    reduce_sum x11, other arithmetic: 3.14 us -> 4.96 us  [layer(): jnp.mean(wide * wide, axis=-1, keepdims=True) + 1e-05]
    unnamed x18, local copies, waits for them, and re-layouts: 3.54 us -> 1.88 us
    reshape x20 -> x10, local copies, waits for them, and re-layouts: 3.62 us -> 2.27 us  [layer(): heads = normed.reshape(steps, reqs, kv_heads, group, head)]
  transfers between devices with their start and end apart: 13 -> 13, of which waited for: 6 -> 6; matrix products, arithmetic and copies ran while one was open for 15% -> 11% of each run, Pallas kernels for 9% -> 9%
where the time goes in v9:
time: 149 us; the launch traced here: 146 us
  matrix products  43.7 us (29%)
  waiting for transfers between devices  33.5 us (22%)
  other arithmetic  19.5 us (13%)
  Pallas kernels  18 us (12%)
  local copies, waits for them, and re-layouts  17 us (11%)
  starting transfers between devices  12.7 us (9%)
  between operations  2.15 us (1%)
    ppermute x10, waiting for transfers between devices, per_device(): incoming = lax.ppermute(result, 'section', pairs)  32.1 us
    dot_general x11, matrix products, layer(): jnp.einsum('rjgxd,rjgpd->rjgxp', wide_query, keys, preferred_element_type...  21.7 us
    pallas_call x4, Pallas kernels, gather_chunk(): pl.pallas_call(copy_kernel, grid_spec=grid_spec, out_shape=[half, half],...  18 us
    dot_general x11, matrix products, layer(): jnp.einsum('rjgxp,rjgpd->rjgxd', cache_w, values, preferred_element_type=...  17.3 us
    ppermute x10, starting transfers between devices, per_device(): incoming = lax.ppermute(result, 'section', pairs)  12.1 us
    gather x1, local copies, waits for them, and re-layouts, per_device(): received = partner(pool[chosen], 'inst', 0)  5.51 us
    reduce_sum x11, other arithmetic, layer(): jnp.mean(wide * wide, axis=-1, keepdims=True) + 1e-05  4.96 us
    reduce_sum x11, other arithmetic, layer(): jnp.sum(cache_exp, axis=(1, 4))[..., None]  2.99 us
  transfers between devices with their start and end apart: 13, of which 6 were waited for; matrix products, arithmetic and copies ran while one was open for 11% of the time, Pallas kernels for 9%

profile of v9, /device:TPU:26, one launch (start us, length us, event | category | flops | bytes accessed | tf_op | source)
XLA Modules:
  0.0 146.4 jit_solution(4617834224828749824)
XLA Ops:
  5.9 4.5 %shard_map.86 = (bf16[8,2,8,128,128]{4,3,2,1,0:T(8,128)(2,1)}, bf16[8,2,8,128,128]{4,3,2,1,0:T(8,128)(2,1)}) custom-call(s32[16]{0:T(128)} %reshape_squeeze.2.table_ref, bf16[16,2,8,128,128]{4,3,2,1,0:T(8,128)(2,1)} %bitcast.316), custom_call_target="tpu_custom_call" | custom-call | tf_op jit(solution)/shard_map/pallas_call | solution.py:108
  10.7 2.0 %fusion.235 = (f32[2,8,32]{2,1,0:T(8,128)S(1)}, f32[2,2,8,32,128]{4,3,2,1,0:T(8,128)S(1)}) fusion(bf16[8,2,8,128,128]{4,3,2,1,0:T(8,128)(2,1)} %get-tuple-element.32.refs_0_, s32[]{:T(128)S(6)} %select_n.265, bf16[2,8,32,128]{3,2,1,0:T(8,128)(2,1)S(1)} %bitcast.347, pred[2,2,128]{2,1,0:T(4,128)(4,1)S(1)} %broadcast_compare_fusion.11), kind=kOutput, calls=%fused_computation.471 | convolution fusion | flops 33947136 | bytes 1706500 | tf_op jit(solution)/shard_map/rjgxd,rjgpd->rjgxp/dot_general | solution.py:46
  17.0 4.6 %shard_map.87 = (bf16[8,2,8,128,128]{4,3,2,1,0:T(8,128)(2,1)}, bf16[8,2,8,128,128]{4,3,2,1,0:T(8,128)(2,1)}) custom-call(s32[16]{0:T(128)} %reshape_squeeze.2.table_ref, bf16[16,2,8,128,128]{4,3,2,1,0:T(8,128)(2,1)} %bitcast.317, bf16[8,2,8,128,128]{4,3,2,1,0:T(8,128)(2,1)} %get-tuple-element.32.refs_0_, ...), custom_call_target="tpu_custom_call", output_to_operand_aliasing={{0}: (2, {}), {1}: (3, {})} | custom-call | tf_op jit(solution)/shard_map/pallas_call | solution.py:108
  22.9 2.0 %fusion.237 = (f32[2,8,32]{2,1,0:T(8,128)S(1)}, f32[2,2,8,32,128]{4,3,2,1,0:T(8,128)S(1)}) fusion(bf16[8,2,8,128,128]{4,3,2,1,0:T(8,128)(2,1)} %get-tuple-element.36.refs_0_, s32[]{:T(128)S(6)} %select_n.271, bf16[2,8,32,128]{3,2,1,0:T(8,128)(2,1)S(1)} %bitcast.348, pred[2,2,128]{2,1,0:T(4,128)(4,1)S(1)} %get-tuple-element.139), kind=kOutput, calls=%fused_computation.473 | convolution fusion | flops 33947136 | bytes 1706500 | tf_op jit(solution)/shard_map/rjgxd,rjgpd->rjgxp/dot_general | solution.py:46
  28.1 4.5 %shard_map.88 = (bf16[8,2,8,128,128]{4,3,2,1,0:T(8,128)(2,1)}, bf16[8,2,8,128,128]{4,3,2,1,0:T(8,128)(2,1)}) custom-call(s32[16]{0:T(128)} %reshape_squeeze.2.table_ref, bf16[16,2,8,128,128]{4,3,2,1,0:T(8,128)(2,1)} %bitcast.318, bf16[8,2,8,128,128]{4,3,2,1,0:T(8,128)(2,1)} %get-tuple-element.36.refs_0_, ...), custom_call_target="tpu_custom_call", output_to_operand_aliasing={{0}: (2, {}), {1}: (3, {})} | custom-call | tf_op jit(solution)/shard_map/pallas_call | solution.py:108
  33.9 2.0 %fusion.239 = (f32[2,8,32]{2,1,0:T(8,128)S(1)}, f32[2,2,8,32,128]{4,3,2,1,0:T(8,128)S(1)}) fusion(bf16[8,2,8,128,128]{4,3,2,1,0:T(8,128)(2,1)} %get-tuple-element.40.refs_0_, s32[]{:T(128)S(6)} %select_n.275, bf16[2,8,32,128]{3,2,1,0:T(8,128)(2,1)S(1)} %bitcast.350, pred[2,2,128]{2,1,0:T(4,128)(4,1)S(1)} %broadcast_compare_fusion.9), kind=kOutput, calls=%fused_computation.475 | convolution fusion | flops 33947136 | bytes 1706500 | tf_op jit(solution)/shard_map/rjgxd,rjgpd->rjgxp/dot_general | solution.py:46
  39.8 4.5 %shard_map.89 = (bf16[8,2,8,128,128]{4,3,2,1,0:T(8,128)(2,1)}, bf16[8,2,8,128,128]{4,3,2,1,0:T(8,128)(2,1)}) custom-call(s32[16]{0:T(128)} %reshape_squeeze.2.table_ref, bf16[16,2,8,128,128]{4,3,2,1,0:T(8,128)(2,1)} %bitcast.319, bf16[8,2,8,128,128]{4,3,2,1,0:T(8,128)(2,1)} %get-tuple-element.40.refs_0_, ...), custom_call_target="tpu_custom_call", output_to_operand_aliasing={{0}: (2, {}), {1}: (3, {})} | custom-call | tf_op jit(solution)/shard_map/pallas_call | solution.py:108
  45.5 2.0 %fusion.241 = (f32[2,8,32]{2,1,0:T(8,128)S(1)}, f32[2,2,8,32,128]{4,3,2,1,0:T(8,128)S(1)}) fusion(bf16[8,2,8,128,128]{4,3,2,1,0:T(8,128)(2,1)} %get-tuple-element.44, s32[]{:T(128)S(6)} %select_n.280, bf16[2,8,32,128]{3,2,1,0:T(8,128)(2,1)S(1)} %bitcast.351, pred[2,2,128]{2,1,0:T(4,128)(4,1)S(1)} %broadcast_compare_fusion.8), kind=kOutput, calls=%fused_computation.477 | convolution fusion | flops 33947136 | bytes 1706500 | tf_op jit(solution)/shard_map/rjgxd,rjgpd->rjgxp/dot_general | solution.py:46
  52.2 2.0 %fusion.243 = (f32[2,8,32]{2,1,0:T(8,128)S(1)}, f32[2,2,8,32,128]{4,3,2,1,0:T(8,128)S(1)}) fusion(bf16[8,2,8,128,128]{4,3,2,1,0:T(8,128)(2,1)} %get-tuple-element.44, s32[]{:T(128)S(6)} %select_n.284, bf16[2,8,32,128]{3,2,1,0:T(8,128)(2,1)S(1)} %bitcast.352, pred[2,2,128]{2,1,0:T(4,128)(4,1)S(1)} %broadcast_compare_fusion.7), kind=kOutput, calls=%fused_computation.479 | convolution fusion | flops 33947136 | bytes 1706500 | tf_op jit(solution)/shard_map/rjgxd,rjgpd->rjgxp/dot_general | solution.py:46
  57.5 5.5 %gather_fusion.2 = bf16[4,2,8,128,128]{4,3,2,1,0:T(8,128)(2,1)} fusion(bf16[16,2,8,128,128]{4,3,2,1,0:T(8,128)(2,1)} %bitcast.320, s32[1024]{0:T(1024)S(1)} %pad_clamp_fusion), kind=kCustom, calls=%fused_computation.2 | custom fusion | bytes 4194320 | tf_op jit(solution)/shard_map/gather | solution.py:142
  64.8 2.0 %fusion.245 = (f32[2,8,32]{2,1,0:T(8,128)S(1)}, f32[2,2,8,32,128]{4,3,2,1,0:T(8,128)S(1)}) fusion(bf16[8,2,8,128,128]{4,3,2,1,0:T(8,128)(2,1)} %get-tuple-element.44, s32[]{:T(128)S(6)} %select_n.288, bf16[2,8,32,128]{3,2,1,0:T(8,128)(2,1)S(1)} %bitcast.353, pred[2,2,128]{2,1,0:T(4,128)(4,1)S(1)} %broadcast_compare_fusion.6), kind=kOutput, calls=%fused_computation.481 | convolution fusion | flops 33947136 | bytes 1706500 | tf_op jit(solution)/shard_map/rjgxd,rjgpd->rjgxp/dot_general | solution.py:46
  72.9 10.8 %collective-permute-done.5 = bf16[4,2,8192]{2,1,0:T(2,128)(2,1)S(1)} collective-permute-done((bf16[4,2,8192]{2,1,0:T(2,128)(2,1)S(1)}, bf16[4,2,8192]{2,1,0:T(2,128)(2,1)S(1)}, u32[]{:S(2)}, u32[]{:S(2)}) %collective-permute-start.5) | collective-permute-done | bytes 131104 | tf_op jit(solution)/shard_map/ppermute | solution.py:160
  84.9 2.0 %fusion.247 = (f32[2,8,32]{2,1,0:T(8,128)S(1)}, f32[2,2,8,32,128]{4,3,2,1,0:T(8,128)S(1)}) fusion(bf16[8,2,8,128,128]{4,3,2,1,0:T(8,128)(2,1)} %get-tuple-element.44, s32[]{:T(128)S(6)} %select_n.294, bf16[2,8,32,128]{3,2,1,0:T(8,128)(2,1)S(1)} %bitcast.354, pred[2,2,128]{2,1,0:T(4,128)(4,1)S(1)} %broadcast_compare_fusion.4), kind=kOutput, calls=%fused_computation.483 | convolution fusion | flops 33947136 | bytes 1706500 | tf_op jit(solution)/shard_map/rjgxd,rjgpd->rjgxp/dot_general | solution.py:46
  89.5 1.9 %collective-permute-start.8 = (bf16[4,2,8192]{2,1,0:T(2,128)(2,1)S(1)}, bf16[4,2,8192]{2,1,0:T(2,128)(2,1)S(1)}, u32[]{:S(2)}, u32[]{:S(2)}) collective-permute-start(bf16[4,2,8192]{2,1,0:T(2,128)(2,1)S(1)} %get-tuple-element.89), channel_id=1, source_target_pairs={{3,4},{4,5},{5,6},{6,7},{11,12},{12,13},{13,14},{14,15},{19,20},{2... | collective-permute-start | bytes 393224 | tf_op jit(solution)/shard_map/ppermute | solution.py:160
  91.5 7.4 %collective-permute-done.8 = bf16[4,2,8192]{2,1,0:T(2,128)(2,1)S(1)} collective-permute-done((bf16[4,2,8192]{2,1,0:T(2,128)(2,1)S(1)}, bf16[4,2,8192]{2,1,0:T(2,128)(2,1)S(1)}, u32[]{:S(2)}, u32[]{:S(2)}) %collective-permute-start.8) | collective-permute-done | bytes 131104 | tf_op jit(solution)/shard_map/ppermute | solution.py:160
  100.1 2.0 %fusion.249 = (f32[2,8,32]{2,1,0:T(8,128)S(1)}, f32[2,2,8,32,128]{4,3,2,1,0:T(8,128)S(1)}) fusion(bf16[8,2,8,128,128]{4,3,2,1,0:T(8,128)(2,1)} %get-tuple-element.44, s32[]{:T(128)S(6)} %select_n.298, bf16[2,8,32,128]{3,2,1,0:T(8,128)(2,1)S(1)} %bitcast.355, pred[2,2,128]{2,1,0:T(4,128)(4,1)S(1)} %broadcast_compare_fusion.3), kind=kOutput, calls=%fused_computation.485 | convolution fusion | flops 33947136 | bytes 1706500 | tf_op jit(solution)/shard_map/rjgxd,rjgpd->rjgxp/dot_general | solution.py:46
  104.6 2.1 %collective-permute-start.9 = (bf16[4,2,8192]{2,1,0:T(2,128)(2,1)S(1)}, bf16[4,2,8192]{2,1,0:T(2,128)(2,1)S(1)}, u32[]{:S(2)}, u32[]{:S(2)}) collective-permute-start(bf16[4,2,8192]{2,1,0:T(2,128)(2,1)S(1)} %get-tuple-element.85), channel_id=1, source_target_pairs={{4,5},{5,6},{6,7},{12,13},{13,14},{14,15},{20,21},{21,22},{22,23},... | collective-permute-start | bytes 393224 | tf_op jit(solution)/shard_map/ppermute | solution.py:160
  106.8 5.6 %collective-permute-done.9 = bf16[4,2,8192]{2,1,0:T(2,128)(2,1)S(1)} collective-permute-done((bf16[4,2,8192]{2,1,0:T(2,128)(2,1)S(1)}, bf16[4,2,8192]{2,1,0:T(2,128)(2,1)S(1)}, u32[]{:S(2)}, u32[]{:S(2)}) %collective-permute-start.9) | collective-permute-done | bytes 131104 | tf_op jit(solution)/shard_map/ppermute | solution.py:160
  113.7 2.0 %fusion.251 = (f32[2,8,32]{2,1,0:T(8,128)S(1)}, f32[2,2,8,32,128]{4,3,2,1,0:T(8,128)S(1)}) fusion(bf16[8,2,8,128,128]{4,3,2,1,0:T(8,128)(2,1)} %get-tuple-element.44, s32[]{:T(128)S(6)} %select_n.302, bf16[2,8,32,128]{3,2,1,0:T(8,128)(2,1)S(1)} %bitcast.356, pred[2,2,128]{2,1,0:T(4,128)(4,1)S(1)} %broadcast_compare_fusion.2), kind=kOutput, calls=%fused_computation.487 | convolution fusion | flops 33947136 | bytes 1706500 | tf_op jit(solution)/shard_map/rjgxd,rjgpd->rjgxp/dot_general | solution.py:46
  118.2 1.9 %collective-permute-start.10 = (bf16[4,2,8192]{2,1,0:T(2,128)(2,1)S(1)}, bf16[4,2,8192]{2,1,0:T(2,128)(2,1)S(1)}, u32[]{:S(2)}, u32[]{:S(2)}) collective-permute-start(bf16[4,2,8192]{2,1,0:T(2,128)(2,1)S(1)} %get-tuple-element.81), channel_id=1, source_target_pairs={{5,6},{6,7},{13,14},{14,15},{21,22},{22,23},{29,30},{30,31}} | collective-permute-start | bytes 393224 | tf_op jit(solution)/shard_map/ppermute | solution.py:160
  120.1 5.8 %collective-permute-done.10 = bf16[4,2,8192]{2,1,0:T(2,128)(2,1)S(1)} collective-permute-done((bf16[4,2,8192]{2,1,0:T(2,128)(2,1)S(1)}, bf16[4,2,8192]{2,1,0:T(2,128)(2,1)S(1)}, u32[]{:S(2)}, u32[]{:S(2)}) %collective-permute-start.10) | collective-permute-done | bytes 131104 | tf_op jit(solution)/shard_map/ppermute | solution.py:160
  127.2 2.0 %fusion.253 = (f32[2,8,32]{2,1,0:T(8,128)S(1)}, f32[2,2,8,32,128]{4,3,2,1,0:T(8,128)S(1)}) fusion(bf16[8,2,8,128,128]{4,3,2,1,0:T(8,128)(2,1)} %get-tuple-element.44, s32[]{:T(128)S(6)} %select_n.306, bf16[2,8,32,128]{3,2,1,0:T(8,128)(2,1)S(1)} %bitcast.357, pred[2,2,128]{2,1,0:T(4,128)(4,1)S(1)} %broadcast_compare_fusion.1), kind=kOutput, calls=%fused_computation.489 | convolution fusion | flops 33947136 | bytes 1706500 | tf_op jit(solution)/shard_map/rjgxd,rjgpd->rjgxp/dot_general | solution.py:46
  133.1 2.5 %collective-permute-done.11 = bf16[4,2,8192]{2,1,0:T(2,128)(2,1)S(1)} collective-permute-done((bf16[4,2,8192]{2,1,0:T(2,128)(2,1)S(1)}, bf16[4,2,8192]{2,1,0:T(2,128)(2,1)S(1)}, u32[]{:S(2)}, u32[]{:S(2)}) %collective-permute-start.11) | collective-permute-done | bytes 131104 | tf_op jit(solution)/shard_map/ppermute | solution.py:160
  136.8 2.0 %fusion.255 = (f32[2,8,32]{2,1,0:T(8,128)S(1)}, f32[2,2,8,32,128]{4,3,2,1,0:T(8,128)S(1)}) fusion(bf16[8,2,8,128,128]{4,3,2,1,0:T(8,128)(2,1)} %get-tuple-element.44, s32[]{:T(128)S(6)} %select_n.310, bf16[2,8,32,128]{3,2,1,0:T(8,128)(2,1)S(1)} %bitcast.349, pred[2,2,128]{2,1,0:T(4,128)(4,1)S(1)} %broadcast_compare_fusion), kind=kOutput, calls=%fused_computation.491 | convolution fusion | flops 33947136 | bytes 1706500 | tf_op jit(solution)/shard_map/rjgxd,rjgpd->rjgxp/dot_general | solution.py:46
  (267 shorter events, 61.1 us)
Async XLA Ops:
  0.6 5.2 %copy-start = (s32[1,8]{1,0:T(1,128)S(1)}, s32[1,8]{1,0:T(1,128)}, u32[]{:S(2)}) copy-start(s32[1,8]{1,0:T(1,128)} %param.10) | copy-start | bytes 100
  10.4 4.6 %copy-start.1 = (bf16[1,4,8,8192]{3,2,1,0:T(8,128)(2,1)S(1)}, bf16[1,4,8,8192]{3,2,1,0:T(8,128)(2,1)}, u32[]{:S(2)}) copy-start(bf16[1,4,8,8192]{3,2,1,0:T(8,128)(2,1)} %param.7) | copy-start | bytes 1572868
  10.4 4.6 %copy-start.2 = (f32[1,8192]{1,0:T(1,128)S(1)}, f32[1,8192]{1,0:T(1,128)}, u32[]{:S(2)}) copy-start(f32[1,8192]{1,0:T(1,128)} %param.13) | copy-start | bytes 98308
  10.4 5.6 %copy-start.7 = (s32[1,2]{1,0:T(1,128)S(1)}, s32[1,2]{1,0:T(1,128)}, u32[]{:S(2)}) copy-start(s32[1,2]{1,0:T(1,128)} %param.11) | copy-start | bytes 28
  15.3 6.4 %collective-permute-start = (bf16[4,2,8192]{2,1,0:T(2,128)(2,1)S(1)}, bf16[4,2,8192]{2,1,0:T(2,128)(2,1)S(1)}, u32[]{:S(2)}, u32[]{:S(2)}) collective-permute-start(bf16[4,2,8192]{2,1,0:T(2,128)(2,1)S(1)} %fusion.97), channel_id=1, source_target_pairs={{0,1},{8,9},{16,17},{24,25}} | collective-permute-start | bytes 393224 | tf_op jit(solution)/shard_map/ppermute | solution.py:160
  16.6 6.2 %collective-permute-start.6 = (s32[2]{0:T(128)S(1)}, s32[2]{0:T(128)S(1)}, u32[]{:S(2)}, u32[]{:S(2)}) collective-permute-start(s32[2]{0:T(128)S(1)} %gather_fusion.1), channel_id=1, source_target_pairs={{0,8},{8,0},{1,9},{9,1},{2,10},{10,2},{3,11},{11,3},{4,12},{12,4},... | collective-permute-start | bytes 32 | tf_op jit(solution)/shard_map/ppermute | solution.py:20
  17.0 5.0 %copy-start.3 = (f32[1,8192]{1,0:T(1,128)S(1)}, f32[1,8192]{1,0:T(1,128)}, u32[]{:S(2)}) copy-start(f32[1,8192]{1,0:T(1,128)} %param.12) | copy-start | bytes 98308
  27.5 5.1 %collective-permute-start.1 = (bf16[4,2,8192]{2,1,0:T(2,128)(2,1)S(1)}, bf16[4,2,8192]{2,1,0:T(2,128)(2,1)S(1)}, u32[]{:S(2)}, u32[]{:S(2)}) collective-permute-start(bf16[4,2,8192]{2,1,0:T(2,128)(2,1)S(1)} %get-tuple-element.109), channel_id=1, source_target_pairs={{0,1},{1,2},{8,9},{9,10},{16,17},{17,18},{24,25},{25,26}} | collective-permute-start | bytes 393224 | tf_op jit(solution)/shard_map/ppermute | solution.py:160
  33.7 5.4 %copy-start.6 = (s32[1,8,2]{1,2,0:T(2,128)S(1)}, s32[1,8,2]{1,2,0:T(2,128)}, u32[]{:S(2)}) copy-start(s32[1,8,2]{1,2,0:T(2,128)} %param.9) | copy-start | bytes 196
  38.4 5.8 %collective-permute-start.2 = (bf16[4,2,8192]{2,1,0:T(2,128)(2,1)S(1)}, bf16[4,2,8192]{2,1,0:T(2,128)(2,1)S(1)}, u32[]{:S(2)}, u32[]{:S(2)}) collective-permute-start(bf16[4,2,8192]{2,1,0:T(2,128)(2,1)S(1)} %get-tuple-element.105), channel_id=1, source_target_pairs={{0,1},{1,2},{2,3},{8,9},{9,10},{10,11},{16,17},{17,18},{18,19},{24... | collective-permute-start | bytes 393224 | tf_op jit(solution)/shard_map/ppermute | solution.py:160
  50.0 0.9 collective-permute-start.3
  56.7 6.3 %copy-start.4 = (bf16[11,4,2,8192]{3,2,1,0:T(2,128)(2,1)}, bf16[11,4,2,8192]{3,2,1,0:T(2,128)(2,1)S(1)}, u32[]{:S(2)}) copy-start(bf16[11,4,2,8192]{3,2,1,0:T(2,128)(2,1)S(1)} %get-tuple-element.96) | copy-start | bytes 4325380
  56.7 6.8 %collective-permute-start.4 = (bf16[4,2,8192]{2,1,0:T(2,128)(2,1)S(1)}, bf16[4,2,8192]{2,1,0:T(2,128)(2,1)S(1)}, u32[]{:S(2)}, u32[]{:S(2)}) collective-permute-start(bf16[4,2,8192]{2,1,0:T(2,128)(2,1)S(1)} %get-tuple-element.97), channel_id=1, source_target_pairs={{1,2},{2,3},{3,4},{4,5},{9,10},{10,11},{11,12},{12,13},{17,18},{18... | collective-permute-start | bytes 393224 | tf_op jit(solution)/shard_map/ppermute | solution.py:160
  63.0 8.2 %collective-permute-start.7 = (bf16[2,2,2,8,128,128]{5,4,3,2,1,0:T(8,128)(2,1)}, bf16[2,2,2,8,128,128]{5,4,3,2,1,0:T(8,128)(2,1)S(1)}, u32[]{:S(2)}, u32[]{:S(2)}) collective-permute-start(bf16[2,2,2,8,128,128]{5,4,3,2,1,0:T(8,128)(2,1)} %bitcast.346), channel_id=1, source_target_pairs={{0,8},{8,0},{1,9},{9,1},{2,10},{10,2},{3,11},{11,3},{4,12},{12,4},... | collective-permute-start | bytes 6291464 | tf_op jit(solution)/shard_map/ppermute | solution.py:20
  70.0 13.7 %collective-permute-start.5 = (bf16[4,2,8192]{2,1,0:T(2,128)(2,1)S(1)}, bf16[4,2,8192]{2,1,0:T(2,128)(2,1)S(1)}, u32[]{:S(2)}, u32[]{:S(2)}) collective-permute-start(bf16[4,2,8192]{2,1,0:T(2,128)(2,1)S(1)} %get-tuple-element.93), channel_id=1, source_target_pairs={{2,3},{3,4},{4,5},{5,6},{10,11},{11,12},{12,13},{13,14},{18,19},{1... | collective-permute-start | bytes 393224 | tf_op jit(solution)/shard_map/ppermute | solution.py:160
  84.5 4.8 %copy-start.5 = (bf16[11,4,2,8192]{3,2,1,0:T(2,128)(2,1)S(1)}, bf16[11,4,2,8192]{3,2,1,0:T(2,128)(2,1)}, u32[]{:S(2)}) copy-start(bf16[11,4,2,8192]{3,2,1,0:T(2,128)(2,1)} %get-tuple-element.92) | copy-start | bytes 4325380
  89.5 9.3 %collective-permute-start.8 = (bf16[4,2,8192]{2,1,0:T(2,128)(2,1)S(1)}, bf16[4,2,8192]{2,1,0:T(2,128)(2,1)S(1)}, u32[]{:S(2)}, u32[]{:S(2)}) collective-permute-start(bf16[4,2,8192]{2,1,0:T(2,128)(2,1)S(1)} %get-tuple-element.89), channel_id=1, source_target_pairs={{3,4},{4,5},{5,6},{6,7},{11,12},{12,13},{13,14},{14,15},{19,20},{2... | collective-permute-start | bytes 393224 | tf_op jit(solution)/shard_map/ppermute | solution.py:160
  104.6 7.8 %collective-permute-start.9 = (bf16[4,2,8192]{2,1,0:T(2,128)(2,1)S(1)}, bf16[4,2,8192]{2,1,0:T(2,128)(2,1)S(1)}, u32[]{:S(2)}, u32[]{:S(2)}) collective-permute-start(bf16[4,2,8192]{2,1,0:T(2,128)(2,1)S(1)} %get-tuple-element.85), channel_id=1, source_target_pairs={{4,5},{5,6},{6,7},{12,13},{13,14},{14,15},{20,21},{21,22},{22,23},... | collective-permute-start | bytes 393224 | tf_op jit(solution)/shard_map/ppermute | solution.py:160
  118.2 7.8 %collective-permute-start.10 = (bf16[4,2,8192]{2,1,0:T(2,128)(2,1)S(1)}, bf16[4,2,8192]{2,1,0:T(2,128)(2,1)S(1)}, u32[]{:S(2)}, u32[]{:S(2)}) collective-permute-start(bf16[4,2,8192]{2,1,0:T(2,128)(2,1)S(1)} %get-tuple-element.81), channel_id=1, source_target_pairs={{5,6},{6,7},{13,14},{14,15},{21,22},{22,23},{29,30},{30,31}} | collective-permute-start | bytes 393224 | tf_op jit(solution)/shard_map/ppermute | solution.py:160
  131.8 3.8 %collective-permute-start.11 = (bf16[4,2,8192]{2,1,0:T(2,128)(2,1)S(1)}, bf16[4,2,8192]{2,1,0:T(2,128)(2,1)S(1)}, u32[]{:S(2)}, u32[]{:S(2)}) collective-permute-start(bf16[4,2,8192]{2,1,0:T(2,128)(2,1)S(1)} %get-tuple-element.77), channel_id=1, source_target_pairs={{6,7},{14,15},{22,23},{30,31}} | collective-permute-start | bytes 393224 | tf_op jit(solution)/shard_map/ppermute | solution.py:160
  143.3 1.4 collective-permute-start.12

commit v10 on v9

--- a/solution.py
+++ b/solution.py
@@ -163,7 +163,9 @@
         [lax.dynamic_index_in_dim(stacked, c + section, 0, False) for c in range(chunks)], axis=1
     )
     handed = partner(finished[:, moving], "inst", 0)
-    finished = finished.at[:, moving].set(handed)
+    hit = jnp.arange(reqs)[:, None] == moving[None, :]
+    handed_full = jnp.take(handed, jnp.argmax(hit, axis=1), axis=1)
+    finished = jnp.where(jnp.any(hit, axis=1)[None, :, None], handed_full, finished)
     return (finished[None, None], arrived[None, None])
 
 

time: 149 us -> 150 us (level)
  transfers between devices with their start and end apart: 13 -> 13, of which waited for: 6 -> 6; matrix products, arithmetic and copies ran while one was open for 11% -> 12% of each run, Pallas kernels for 9% -> 9%
where the time goes in v10:
time: 150 us; the launch traced here: 147 us
  matrix products  43.7 us (29%)
  waiting for transfers between devices  32.7 us (22%)
  other arithmetic  20.7 us (14%)
  Pallas kernels  18 us (12%)
  local copies, waits for them, and re-layouts  17.5 us (12%)
  starting transfers between devices  12.7 us (8%)
  between operations  2.17 us (1%)
    ppermute x10, waiting for transfers between devices, per_device(): incoming = lax.ppermute(result, 'section', pairs)  31.5 us
    dot_general x11, matrix products, layer(): jnp.einsum('rjgxd,rjgpd->rjgxp', wide_query, keys, preferred_element_type...  21.7 us
    pallas_call x4, Pallas kernels, gather_chunk(): pl.pallas_call(copy_kernel, grid_spec=grid_spec, out_shape=[half, half],...  18 us
    dot_general x11, matrix products, layer(): jnp.einsum('rjgxp,rjgpd->rjgxd', cache_w, values, preferred_element_type=...  17.3 us
    ppermute x10, starting transfers between devices, per_device(): incoming = lax.ppermute(result, 'section', pairs)  12.1 us
    gather x1, local copies, waits for them, and re-layouts, per_device(): received = partner(pool[chosen], 'inst', 0)  5.51 us
    reduce_sum x11, other arithmetic, layer(): jnp.mean(wide * wide, axis=-1, keepdims=True) + 1e-05  4.96 us
  transfers between devices with their start and end apart: 13, of which 6 were waited for; matrix products, arithmetic and copies ran while one was open for 12% of the time, Pallas kernels for 9%

profile of v10, /device:TPU:26, one launch (start us, length us, event | category | flops | bytes accessed | tf_op | source)
XLA Modules:
  0.0 147.5 jit_solution(3849305979673745806)
XLA Ops:
  5.9 4.5 %shard_map.86 = (bf16[8,2,8,128,128]{4,3,2,1,0:T(8,128)(2,1)}, bf16[8,2,8,128,128]{4,3,2,1,0:T(8,128)(2,1)}) custom-call(s32[16]{0:T(128)} %reshape_squeeze.2.table_ref, bf16[16,2,8,128,128]{4,3,2,1,0:T(8,128)(2,1)} %bitcast.329), custom_call_target="tpu_custom_call" | custom-call | tf_op jit(solution)/shard_map/pallas_call | solution.py:108
  10.7 2.0 %fusion.236 = (f32[2,8,32]{2,1,0:T(8,128)S(1)}, f32[2,2,8,32,128]{4,3,2,1,0:T(8,128)S(1)}) fusion(bf16[8,2,8,128,128]{4,3,2,1,0:T(8,128)(2,1)} %get-tuple-element.34.refs_0_, s32[]{:T(128)S(6)} %select_n.296, bf16[2,8,32,128]{3,2,1,0:T(8,128)(2,1)S(1)} %bitcast.359, pred[2,2,128]{2,1,0:T(4,128)(4,1)S(1)} %broadcast_compare_fusion.11), kind=kOutput, calls=%fused_computation.483 | convolution fusion | flops 33947136 | bytes 1706500 | tf_op jit(solution)/shard_map/rjgxd,rjgpd->rjgxp/dot_general | solution.py:46
  17.0 4.6 %shard_map.87 = (bf16[8,2,8,128,128]{4,3,2,1,0:T(8,128)(2,1)}, bf16[8,2,8,128,128]{4,3,2,1,0:T(8,128)(2,1)}) custom-call(s32[16]{0:T(128)} %reshape_squeeze.2.table_ref, bf16[16,2,8,128,128]{4,3,2,1,0:T(8,128)(2,1)} %bitcast.330, bf16[8,2,8,128,128]{4,3,2,1,0:T(8,128)(2,1)} %get-tuple-element.34.refs_0_, ...), custom_call_target="tpu_custom_call", output_to_operand_aliasing={{0}: (2, {}), {1}: (3, {})} | custom-call | tf_op jit(solution)/shard_map/pallas_call | solution.py:108
  22.9 2.0 %fusion.238 = (f32[2,8,32]{2,1,0:T(8,128)S(1)}, f32[2,2,8,32,128]{4,3,2,1,0:T(8,128)S(1)}) fusion(bf16[8,2,8,128,128]{4,3,2,1,0:T(8,128)(2,1)} %get-tuple-element.38.refs_0_, s32[]{:T(128)S(6)} %select_n.302, bf16[2,8,32,128]{3,2,1,0:T(8,128)(2,1)S(1)} %bitcast.360, pred[2,2,128]{2,1,0:T(4,128)(4,1)S(1)} %get-tuple-element.149), kind=kOutput, calls=%fused_computation.485 | convolution fusion | flops 33947136 | bytes 1706500 | tf_op jit(solution)/shard_map/rjgxd,rjgpd->rjgxp/dot_general | solution.py:46
  28.1 4.5 %shard_map.88 = (bf16[8,2,8,128,128]{4,3,2,1,0:T(8,128)(2,1)}, bf16[8,2,8,128,128]{4,3,2,1,0:T(8,128)(2,1)}) custom-call(s32[16]{0:T(128)} %reshape_squeeze.2.table_ref, bf16[16,2,8,128,128]{4,3,2,1,0:T(8,128)(2,1)} %bitcast.331, bf16[8,2,8,128,128]{4,3,2,1,0:T(8,128)(2,1)} %get-tuple-element.38.refs_0_, ...), custom_call_target="tpu_custom_call", output_to_operand_aliasing={{0}: (2, {}), {1}: (3, {})} | custom-call | tf_op jit(solution)/shard_map/pallas_call | solution.py:108
  33.9 2.0 %fusion.240 = (f32[2,8,32]{2,1,0:T(8,128)S(1)}, f32[2,2,8,32,128]{4,3,2,1,0:T(8,128)S(1)}) fusion(bf16[8,2,8,128,128]{4,3,2,1,0:T(8,128)(2,1)} %get-tuple-element.42.refs_0_, s32[]{:T(128)S(6)} %select_n.306, bf16[2,8,32,128]{3,2,1,0:T(8,128)(2,1)S(1)} %bitcast.362, pred[2,2,128]{2,1,0:T(4,128)(4,1)S(1)} %broadcast_compare_fusion.9), kind=kOutput, calls=%fused_computation.487 | convolution fusion | flops 33947136 | bytes 1706500 | tf_op jit(solution)/shard_map/rjgxd,rjgpd->rjgxp/dot_general | solution.py:46
  39.8 4.5 %shard_map.89 = (bf16[8,2,8,128,128]{4,3,2,1,0:T(8,128)(2,1)}, bf16[8,2,8,128,128]{4,3,2,1,0:T(8,128)(2,1)}) custom-call(s32[16]{0:T(128)} %reshape_squeeze.2.table_ref, bf16[16,2,8,128,128]{4,3,2,1,0:T(8,128)(2,1)} %bitcast.332, bf16[8,2,8,128,128]{4,3,2,1,0:T(8,128)(2,1)} %get-tuple-element.42.refs_0_, ...), custom_call_target="tpu_custom_call", output_to_operand_aliasing={{0}: (2, {}), {1}: (3, {})} | custom-call | tf_op jit(solution)/shard_map/pallas_call | solution.py:108
  45.5 2.0 %fusion.242 = (f32[2,8,32]{2,1,0:T(8,128)S(1)}, f32[2,2,8,32,128]{4,3,2,1,0:T(8,128)S(1)}) fusion(bf16[8,2,8,128,128]{4,3,2,1,0:T(8,128)(2,1)} %get-tuple-element.46, s32[]{:T(128)S(6)} %select_n.311, bf16[2,8,32,128]{3,2,1,0:T(8,128)(2,1)S(1)} %bitcast.363, pred[2,2,128]{2,1,0:T(4,128)(4,1)S(1)} %broadcast_compare_fusion.8), kind=kOutput, calls=%fused_computation.489 | convolution fusion | flops 33947136 | bytes 1706500 | tf_op jit(solution)/shard_map/rjgxd,rjgpd->rjgxp/dot_general | solution.py:46
  52.2 2.0 %fusion.244 = (f32[2,8,32]{2,1,0:T(8,128)S(1)}, f32[2,2,8,32,128]{4,3,2,1,0:T(8,128)S(1)}) fusion(bf16[8,2,8,128,128]{4,3,2,1,0:T(8,128)(2,1)} %get-tuple-element.46, s32[]{:T(128)S(6)} %select_n.315, bf16[2,8,32,128]{3,2,1,0:T(8,128)(2,1)S(1)} %bitcast.364, pred[2,2,128]{2,1,0:T(4,128)(4,1)S(1)} %broadcast_compare_fusion.7), kind=kOutput, calls=%fused_computation.491 | convolution fusion | flops 33947136 | bytes 1706500 | tf_op jit(solution)/shard_map/rjgxd,rjgpd->rjgxp/dot_general | solution.py:46
  57.5 5.5 %gather_fusion.2 = bf16[4,2,8,128,128]{4,3,2,1,0:T(8,128)(2,1)} fusion(bf16[16,2,8,128,128]{4,3,2,1,0:T(8,128)(2,1)} %bitcast.333, s32[1024]{0:T(1024)S(1)} %pad_clamp_fusion.1), kind=kCustom, calls=%fused_computation.2 | custom fusion | bytes 4194320 | tf_op jit(solution)/shard_map/gather | solution.py:142
  64.8 2.0 %fusion.246 = (f32[2,8,32]{2,1,0:T(8,128)S(1)}, f32[2,2,8,32,128]{4,3,2,1,0:T(8,128)S(1)}) fusion(bf16[8,2,8,128,128]{4,3,2,1,0:T(8,128)(2,1)} %get-tuple-element.46, s32[]{:T(128)S(6)} %select_n.319, bf16[2,8,32,128]{3,2,1,0:T(8,128)(2,1)S(1)} %bitcast.365, pred[2,2,128]{2,1,0:T(4,128)(4,1)S(1)} %broadcast_compare_fusion.6), kind=kOutput, calls=%fused_computation.493 | convolution fusion | flops 33947136 | bytes 1706500 | tf_op jit(solution)/shard_map/rjgxd,rjgpd->rjgxp/dot_general | solution.py:46
  72.9 10.8 %collective-permute-done.5 = bf16[4,2,8192]{2,1,0:T(2,128)(2,1)S(1)} collective-permute-done((bf16[4,2,8192]{2,1,0:T(2,128)(2,1)S(1)}, bf16[4,2,8192]{2,1,0:T(2,128)(2,1)S(1)}, u32[]{:S(2)}, u32[]{:S(2)}) %collective-permute-start.5) | collective-permute-done | bytes 131104 | tf_op jit(solution)/shard_map/ppermute | solution.py:160
  84.9 2.0 %fusion.248 = (f32[2,8,32]{2,1,0:T(8,128)S(1)}, f32[2,2,8,32,128]{4,3,2,1,0:T(8,128)S(1)}) fusion(bf16[8,2,8,128,128]{4,3,2,1,0:T(8,128)(2,1)} %get-tuple-element.46, s32[]{:T(128)S(6)} %select_n.325, bf16[2,8,32,128]{3,2,1,0:T(8,128)(2,1)S(1)} %bitcast.366, pred[2,2,128]{2,1,0:T(4,128)(4,1)S(1)} %broadcast_compare_fusion.4), kind=kOutput, calls=%fused_computation.495 | convolution fusion | flops 33947136 | bytes 1706500 | tf_op jit(solution)/shard_map/rjgxd,rjgpd->rjgxp/dot_general | solution.py:46
  89.5 1.9 %collective-permute-start.8 = (bf16[4,2,8192]{2,1,0:T(2,128)(2,1)S(1)}, bf16[4,2,8192]{2,1,0:T(2,128)(2,1)S(1)}, u32[]{:S(2)}, u32[]{:S(2)}) collective-permute-start(bf16[4,2,8192]{2,1,0:T(2,128)(2,1)S(1)} %get-tuple-element.91), channel_id=1, source_target_pairs={{3,4},{4,5},{5,6},{6,7},{11,12},{12,13},{13,14},{14,15},{19,20},{2... | collective-permute-start | bytes 393224 | tf_op jit(solution)/shard_map/ppermute | solution.py:160
  91.5 7.4 %collective-permute-done.8 = bf16[4,2,8192]{2,1,0:T(2,128)(2,1)S(1)} collective-permute-done((bf16[4,2,8192]{2,1,0:T(2,128)(2,1)S(1)}, bf16[4,2,8192]{2,1,0:T(2,128)(2,1)S(1)}, u32[]{:S(2)}, u32[]{:S(2)}) %collective-permute-start.8) | collective-permute-done | bytes 131104 | tf_op jit(solution)/shard_map/ppermute | solution.py:160
  100.1 2.0 %fusion.250 = (f32[2,8,32]{2,1,0:T(8,128)S(1)}, f32[2,2,8,32,128]{4,3,2,1,0:T(8,128)S(1)}) fusion(bf16[8,2,8,128,128]{4,3,2,1,0:T(8,128)(2,1)} %get-tuple-element.46, s32[]{:T(128)S(6)} %select_n.329, bf16[2,8,32,128]{3,2,1,0:T(8,128)(2,1)S(1)} %bitcast.367, pred[2,2,128]{2,1,0:T(4,128)(4,1)S(1)} %broadcast_compare_fusion.3), kind=kOutput, calls=%fused_computation.497 | convolution fusion | flops 33947136 | bytes 1706500 | tf_op jit(solution)/shard_map/rjgxd,rjgpd->rjgxp/dot_general | solution.py:46
  104.6 2.1 %collective-permute-start.9 = (bf16[4,2,8192]{2,1,0:T(2,128)(2,1)S(1)}, bf16[4,2,8192]{2,1,0:T(2,128)(2,1)S(1)}, u32[]{:S(2)}, u32[]{:S(2)}) collective-permute-start(bf16[4,2,8192]{2,1,0:T(2,128)(2,1)S(1)} %get-tuple-element.87), channel_id=1, source_target_pairs={{4,5},{5,6},{6,7},{12,13},{13,14},{14,15},{20,21},{21,22},{22,23},... | collective-permute-start | bytes 393224 | tf_op jit(solution)/shard_map/ppermute | solution.py:160
  107.4 5.0 %collective-permute-done.9 = bf16[4,2,8192]{2,1,0:T(2,128)(2,1)S(1)} collective-permute-done((bf16[4,2,8192]{2,1,0:T(2,128)(2,1)S(1)}, bf16[4,2,8192]{2,1,0:T(2,128)(2,1)S(1)}, u32[]{:S(2)}, u32[]{:S(2)}) %collective-permute-start.9) | collective-permute-done | bytes 131104 | tf_op jit(solution)/shard_map/ppermute | solution.py:160
  113.7 2.0 %fusion.252 = (f32[2,8,32]{2,1,0:T(8,128)S(1)}, f32[2,2,8,32,128]{4,3,2,1,0:T(8,128)S(1)}) fusion(bf16[8,2,8,128,128]{4,3,2,1,0:T(8,128)(2,1)} %get-tuple-element.46, s32[]{:T(128)S(6)} %select_n.333, bf16[2,8,32,128]{3,2,1,0:T(8,128)(2,1)S(1)} %bitcast.368, pred[2,2,128]{2,1,0:T(4,128)(4,1)S(1)} %broadcast_compare_fusion.2), kind=kOutput, calls=%fused_computation.499 | convolution fusion | flops 33947136 | bytes 1706500 | tf_op jit(solution)/shard_map/rjgxd,rjgpd->rjgxp/dot_general | solution.py:46
  118.2 1.9 %collective-permute-start.10 = (bf16[4,2,8192]{2,1,0:T(2,128)(2,1)S(1)}, bf16[4,2,8192]{2,1,0:T(2,128)(2,1)S(1)}, u32[]{:S(2)}, u32[]{:S(2)}) collective-permute-start(bf16[4,2,8192]{2,1,0:T(2,128)(2,1)S(1)} %get-tuple-element.83), channel_id=1, source_target_pairs={{5,6},{6,7},{13,14},{14,15},{21,22},{22,23},{29,30},{30,31}} | collective-permute-start | bytes 393224 | tf_op jit(solution)/shard_map/ppermute | solution.py:160
  120.2 5.8 %collective-permute-done.10 = bf16[4,2,8192]{2,1,0:T(2,128)(2,1)S(1)} collective-permute-done((bf16[4,2,8192]{2,1,0:T(2,128)(2,1)S(1)}, bf16[4,2,8192]{2,1,0:T(2,128)(2,1)S(1)}, u32[]{:S(2)}, u32[]{:S(2)}) %collective-permute-start.10) | collective-permute-done | bytes 131104 | tf_op jit(solution)/shard_map/ppermute | solution.py:160
  127.2 2.0 %fusion.254 = (f32[2,8,32]{2,1,0:T(8,128)S(1)}, f32[2,2,8,32,128]{4,3,2,1,0:T(8,128)S(1)}) fusion(bf16[8,2,8,128,128]{4,3,2,1,0:T(8,128)(2,1)} %get-tuple-element.46, s32[]{:T(128)S(6)} %select_n.337, bf16[2,8,32,128]{3,2,1,0:T(8,128)(2,1)S(1)} %bitcast.369, pred[2,2,128]{2,1,0:T(4,128)(4,1)S(1)} %broadcast_compare_fusion.1), kind=kOutput, calls=%fused_computation.501 | convolution fusion | flops 33947136 | bytes 1706500 | tf_op jit(solution)/shard_map/rjgxd,rjgpd->rjgxp/dot_general | solution.py:46
  133.1 2.5 %collective-permute-done.11 = bf16[4,2,8192]{2,1,0:T(2,128)(2,1)S(1)} collective-permute-done((bf16[4,2,8192]{2,1,0:T(2,128)(2,1)S(1)}, bf16[4,2,8192]{2,1,0:T(2,128)(2,1)S(1)}, u32[]{:S(2)}, u32[]{:S(2)}) %collective-permute-start.11) | collective-permute-done | bytes 131104 | tf_op jit(solution)/shard_map/ppermute | solution.py:160
  136.8 2.0 %fusion.256 = (f32[2,8,32]{2,1,0:T(8,128)S(1)}, f32[2,2,8,32,128]{4,3,2,1,0:T(8,128)S(1)}) fusion(bf16[8,2,8,128,128]{4,3,2,1,0:T(8,128)(2,1)} %get-tuple-element.46, s32[]{:T(128)S(6)} %select_n.341, bf16[2,8,32,128]{3,2,1,0:T(8,128)(2,1)S(1)} %bitcast.361, pred[2,2,128]{2,1,0:T(4,128)(4,1)S(1)} %broadcast_compare_fusion), kind=kOutput, calls=%fused_computation.503 | convolution fusion | flops 33947136 | bytes 1706500 | tf_op jit(solution)/shard_map/rjgxd,rjgpd->rjgxp/dot_general | solution.py:46
  (273 shorter events, 62.7 us)
Async XLA Ops:
  0.6 5.2 %copy-start = (s32[1,8]{1,0:T(1,128)S(1)}, s32[1,8]{1,0:T(1,128)}, u32[]{:S(2)}) copy-start(s32[1,8]{1,0:T(1,128)} %param.10) | copy-start | bytes 100
  10.4 4.6 %copy-start.1 = (bf16[1,4,8,8192]{3,2,1,0:T(8,128)(2,1)S(1)}, bf16[1,4,8,8192]{3,2,1,0:T(8,128)(2,1)}, u32[]{:S(2)}) copy-start(bf16[1,4,8,8192]{3,2,1,0:T(8,128)(2,1)} %param.7) | copy-start | bytes 1572868
  10.4 4.6 %copy-start.2 = (f32[1,8192]{1,0:T(1,128)S(1)}, f32[1,8192]{1,0:T(1,128)}, u32[]{:S(2)}) copy-start(f32[1,8192]{1,0:T(1,128)} %param.13) | copy-start | bytes 98308
  10.4 5.6 %copy-start.7 = (s32[1,2]{1,0:T(1,128)S(1)}, s32[1,2]{1,0:T(1,128)}, u32[]{:S(2)}) copy-start(s32[1,2]{1,0:T(1,128)} %param.11) | copy-start | bytes 28
  15.3 6.4 %collective-permute-start = (bf16[4,2,8192]{2,1,0:T(2,128)(2,1)S(1)}, bf16[4,2,8192]{2,1,0:T(2,128)(2,1)S(1)}, u32[]{:S(2)}, u32[]{:S(2)}) collective-permute-start(bf16[4,2,8192]{2,1,0:T(2,128)(2,1)S(1)} %fusion.97), channel_id=1, source_target_pairs={{0,1},{8,9},{16,17},{24,25}} | collective-permute-start | bytes 393224 | tf_op jit(solution)/shard_map/ppermute | solution.py:160
  16.6 6.2 %collective-permute-start.6 = (s32[2]{0:T(128)S(1)}, s32[2]{0:T(128)S(1)}, u32[]{:S(2)}, u32[]{:S(2)}) collective-permute-start(s32[2]{0:T(128)S(1)} %gather_fusion.1), channel_id=1, source_target_pairs={{0,8},{8,0},{1,9},{9,1},{2,10},{10,2},{3,11},{11,3},{4,12},{12,4},... | collective-permute-start | bytes 32 | tf_op jit(solution)/shard_map/ppermute | solution.py:20
  17.0 5.0 %copy-start.3 = (f32[1,8192]{1,0:T(1,128)S(1)}, f32[1,8192]{1,0:T(1,128)}, u32[]{:S(2)}) copy-start(f32[1,8192]{1,0:T(1,128)} %param.12) | copy-start | bytes 98308
  27.5 5.1 %collective-permute-start.1 = (bf16[4,2,8192]{2,1,0:T(2,128)(2,1)S(1)}, bf16[4,2,8192]{2,1,0:T(2,128)(2,1)S(1)}, u32[]{:S(2)}, u32[]{:S(2)}) collective-permute-start(bf16[4,2,8192]{2,1,0:T(2,128)(2,1)S(1)} %get-tuple-element.111), channel_id=1, source_target_pairs={{0,1},{1,2},{8,9},{9,10},{16,17},{17,18},{24,25},{25,26}} | collective-permute-start | bytes 393224 | tf_op jit(solution)/shard_map/ppermute | solution.py:160
  33.7 5.4 %copy-start.6 = (s32[1,8,2]{1,2,0:T(2,128)S(1)}, s32[1,8,2]{1,2,0:T(2,128)}, u32[]{:S(2)}) copy-start(s32[1,8,2]{1,2,0:T(2,128)} %param.9) | copy-start | bytes 196
  38.4 5.8 %collective-permute-start.2 = (bf16[4,2,8192]{2,1,0:T(2,128)(2,1)S(1)}, bf16[4,2,8192]{2,1,0:T(2,128)(2,1)S(1)}, u32[]{:S(2)}, u32[]{:S(2)}) collective-permute-start(bf16[4,2,8192]{2,1,0:T(2,128)(2,1)S(1)} %get-tuple-element.107), channel_id=1, source_target_pairs={{0,1},{1,2},{2,3},{8,9},{9,10},{10,11},{16,17},{17,18},{18,19},{24... | collective-permute-start | bytes 393224 | tf_op jit(solution)/shard_map/ppermute | solution.py:160
  50.0 0.9 collective-permute-start.3
  56.7 6.3 %copy-start.4 = (bf16[11,4,2,8192]{3,2,1,0:T(2,128)(2,1)}, bf16[11,4,2,8192]{3,2,1,0:T(2,128)(2,1)S(1)}, u32[]{:S(2)}) copy-start(bf16[11,4,2,8192]{3,2,1,0:T(2,128)(2,1)S(1)} %get-tuple-element.98) | copy-start | bytes 4325380
  56.7 6.8 %collective-permute-start.4 = (bf16[4,2,8192]{2,1,0:T(2,128)(2,1)S(1)}, bf16[4,2,8192]{2,1,0:T(2,128)(2,1)S(1)}, u32[]{:S(2)}, u32[]{:S(2)}) collective-permute-start(bf16[4,2,8192]{2,1,0:T(2,128)(2,1)S(1)} %get-tuple-element.99), channel_id=1, source_target_pairs={{1,2},{2,3},{3,4},{4,5},{9,10},{10,11},{11,12},{12,13},{17,18},{18... | collective-permute-start | bytes 393224 | tf_op jit(solution)/shard_map/ppermute | solution.py:160
  63.0 8.2 %collective-permute-start.7 = (bf16[2,2,2,8,128,128]{5,4,3,2,1,0:T(8,128)(2,1)}, bf16[2,2,2,8,128,128]{5,4,3,2,1,0:T(8,128)(2,1)S(1)}, u32[]{:S(2)}, u32[]{:S(2)}) collective-permute-start(bf16[2,2,2,8,128,128]{5,4,3,2,1,0:T(8,128)(2,1)} %bitcast.358), channel_id=1, source_target_pairs={{0,8},{8,0},{1,9},{9,1},{2,10},{10,2},{3,11},{11,3},{4,12},{12,4},... | collective-permute-start | bytes 6291464 | tf_op jit(solution)/shard_map/ppermute | solution.py:20
  70.0 13.7 %collective-permute-start.5 = (bf16[4,2,8192]{2,1,0:T(2,128)(2,1)S(1)}, bf16[4,2,8192]{2,1,0:T(2,128)(2,1)S(1)}, u32[]{:S(2)}, u32[]{:S(2)}) collective-permute-start(bf16[4,2,8192]{2,1,0:T(2,128)(2,1)S(1)} %get-tuple-element.95), channel_id=1, source_target_pairs={{2,3},{3,4},{4,5},{5,6},{10,11},{11,12},{12,13},{13,14},{18,19},{1... | collective-permute-start | bytes 393224 | tf_op jit(solution)/shard_map/ppermute | solution.py:160
  84.5 4.8 %copy-start.5 = (bf16[11,4,2,8192]{3,2,1,0:T(2,128)(2,1)S(1)}, bf16[11,4,2,8192]{3,2,1,0:T(2,128)(2,1)}, u32[]{:S(2)}) copy-start(bf16[11,4,2,8192]{3,2,1,0:T(2,128)(2,1)} %get-tuple-element.94) | copy-start | bytes 4325380
  89.5 9.3 %collective-permute-start.8 = (bf16[4,2,8192]{2,1,0:T(2,128)(2,1)S(1)}, bf16[4,2,8192]{2,1,0:T(2,128)(2,1)S(1)}, u32[]{:S(2)}, u32[]{:S(2)}) collective-permute-start(bf16[4,2,8192]{2,1,0:T(2,128)(2,1)S(1)} %get-tuple-element.91), channel_id=1, source_target_pairs={{3,4},{4,5},{5,6},{6,7},{11,12},{12,13},{13,14},{14,15},{19,20},{2... | collective-permute-start | bytes 393224 | tf_op jit(solution)/shard_map/ppermute | solution.py:160
  104.6 7.8 %collective-permute-start.9 = (bf16[4,2,8192]{2,1,0:T(2,128)(2,1)S(1)}, bf16[4,2,8192]{2,1,0:T(2,128)(2,1)S(1)}, u32[]{:S(2)}, u32[]{:S(2)}) collective-permute-start(bf16[4,2,8192]{2,1,0:T(2,128)(2,1)S(1)} %get-tuple-element.87), channel_id=1, source_target_pairs={{4,5},{5,6},{6,7},{12,13},{13,14},{14,15},{20,21},{21,22},{22,23},... | collective-permute-start | bytes 393224 | tf_op jit(solution)/shard_map/ppermute | solution.py:160
  118.2 7.8 %collective-permute-start.10 = (bf16[4,2,8192]{2,1,0:T(2,128)(2,1)S(1)}, bf16[4,2,8192]{2,1,0:T(2,128)(2,1)S(1)}, u32[]{:S(2)}, u32[]{:S(2)}) collective-permute-start(bf16[4,2,8192]{2,1,0:T(2,128)(2,1)S(1)} %get-tuple-element.83), channel_id=1, source_target_pairs={{5,6},{6,7},{13,14},{14,15},{21,22},{22,23},{29,30},{30,31}} | collective-permute-start | bytes 393224 | tf_op jit(solution)/shard_map/ppermute | solution.py:160
  131.8 3.8 %collective-permute-start.11 = (bf16[4,2,8192]{2,1,0:T(2,128)(2,1)S(1)}, bf16[4,2,8192]{2,1,0:T(2,128)(2,1)S(1)}, u32[]{:S(2)}, u32[]{:S(2)}) collective-permute-start(bf16[4,2,8192]{2,1,0:T(2,128)(2,1)S(1)} %get-tuple-element.79), channel_id=1, source_target_pairs={{6,7},{14,15},{22,23},{30,31}} | collective-permute-start | bytes 393224 | tf_op jit(solution)/shard_map/ppermute | solution.py:160
  143.4 1.4 collective-permute-start.12

commit v11 on v9

--- a/solution.py
+++ b/solution.py
@@ -85,14 +85,14 @@
     kv_heads, page_len, head = pool.shape[2:]
 
     def page_index(r, j, table_ref):
-        return (table_ref[(chunk * block + r) * pages + j], 0, 0, 0, 0)
+        return (table_ref[chunk * block + r, j], 0, 0, 0, 0)
 
     def slot_index(r, j, table_ref):
         return (chunk * block + r, j, 0, 0, 0)
 
     slot = pl.BlockSpec((1, 1, kv_heads, page_len, head), slot_index)
     in_specs = [pl.BlockSpec((1, 2, kv_heads, page_len, head), page_index)]
-    operands = [table.reshape(-1), pool]
+    operands = [table, pool]
     aliases = {}
     if previous is not None:
         in_specs += [pl.BlockSpec(memory_space=pl.ANY)] * 2

time: 149 us -> 150 us (level)
  no operation moved by 1% of the time
where the time goes in v11:
time: 150 us; the launch traced here: 147 us
  matrix products  43.7 us (29%)
  waiting for transfers between devices  33.4 us (22%)
  other arithmetic  19.5 us (13%)
  Pallas kernels  18.2 us (12%)
  local copies, waits for them, and re-layouts  16.9 us (11%)
  starting transfers between devices  12.7 us (8%)
  between operations  2.15 us (1%)
    ppermute x10, waiting for transfers between devices, per_device(): incoming = lax.ppermute(result, 'section', pairs)  32.1 us
    dot_general x11, matrix products, layer(): jnp.einsum('rjgxd,rjgpd->rjgxp', wide_query, keys, preferred_element_type...  21.7 us
    pallas_call x4, Pallas kernels, gather_chunk(): pl.pallas_call(copy_kernel, grid_spec=grid_spec, out_shape=[half, half],...  18.2 us
    dot_general x11, matrix products, layer(): jnp.einsum('rjgxp,rjgpd->rjgxd', cache_w, values, preferred_element_type=...  17.3 us
    ppermute x10, starting transfers between devices, per_device(): incoming = lax.ppermute(result, 'section', pairs)  12.1 us
    gather x1, local copies, waits for them, and re-layouts, per_device(): received = partner(pool[chosen], 'inst', 0)  5.51 us
    reduce_sum x11, other arithmetic, layer(): jnp.mean(wide * wide, axis=-1, keepdims=True) + 1e-05  4.96 us
  transfers between devices with their start and end apart: 13, of which 6 were waited for; matrix products, arithmetic and copies ran while one was open for 11% of the time, Pallas kernels for 9%

profile of v11, /device:TPU:26, one launch (start us, length us, event | category | flops | bytes accessed | tf_op | source)
XLA Modules:
  0.0 146.6 jit_solution(11617401877733806360)
XLA Ops:
  5.9 4.5 %shard_map.86 = (bf16[8,2,8,128,128]{4,3,2,1,0:T(8,128)(2,1)}, bf16[8,2,8,128,128]{4,3,2,1,0:T(8,128)(2,1)}) custom-call(s32[8,2]{1,0:T(8,128)} %copy.324.table_ref, bf16[16,2,8,128,128]{4,3,2,1,0:T(8,128)(2,1)} %bitcast.316), custom_call_target="tpu_custom_call" | custom-call | tf_op jit(solution)/shard_map/pallas_call | solution.py:108
  10.7 2.0 %fusion.235 = (f32[2,8,32]{2,1,0:T(8,128)S(1)}, f32[2,2,8,32,128]{4,3,2,1,0:T(8,128)S(1)}) fusion(bf16[8,2,8,128,128]{4,3,2,1,0:T(8,128)(2,1)} %get-tuple-element.32.refs_0_, s32[]{:T(128)S(6)} %select_n.265, bf16[2,8,32,128]{3,2,1,0:T(8,128)(2,1)S(1)} %bitcast.347, pred[2,2,128]{2,1,0:T(4,128)(4,1)S(1)} %broadcast_compare_fusion.11), kind=kOutput, calls=%fused_computation.471 | convolution fusion | flops 33947136 | bytes 1706500 | tf_op jit(solution)/shard_map/rjgxd,rjgpd->rjgxp/dot_general | solution.py:46
  17.1 4.7 %shard_map.87 = (bf16[8,2,8,128,128]{4,3,2,1,0:T(8,128)(2,1)}, bf16[8,2,8,128,128]{4,3,2,1,0:T(8,128)(2,1)}) custom-call(s32[8,2]{1,0:T(8,128)} %copy.324.table_ref, bf16[16,2,8,128,128]{4,3,2,1,0:T(8,128)(2,1)} %bitcast.317, bf16[8,2,8,128,128]{4,3,2,1,0:T(8,128)(2,1)} %get-tuple-element.32.refs_0_, ...), custom_call_target="tpu_custom_call", output_to_operand_aliasing={{0}: (2, {}), {1}: (3, {})} | custom-call | tf_op jit(solution)/shard_map/pallas_call | solution.py:108
  23.0 2.0 %fusion.237 = (f32[2,8,32]{2,1,0:T(8,128)S(1)}, f32[2,2,8,32,128]{4,3,2,1,0:T(8,128)S(1)}) fusion(bf16[8,2,8,128,128]{4,3,2,1,0:T(8,128)(2,1)} %get-tuple-element.36.refs_0_, s32[]{:T(128)S(6)} %select_n.271, bf16[2,8,32,128]{3,2,1,0:T(8,128)(2,1)S(1)} %bitcast.348, pred[2,2,128]{2,1,0:T(4,128)(4,1)S(1)} %get-tuple-element.139), kind=kOutput, calls=%fused_computation.473 | convolution fusion | flops 33947136 | bytes 1706500 | tf_op jit(solution)/shard_map/rjgxd,rjgpd->rjgxp/dot_general | solution.py:46
  28.3 4.5 %shard_map.88 = (bf16[8,2,8,128,128]{4,3,2,1,0:T(8,128)(2,1)}, bf16[8,2,8,128,128]{4,3,2,1,0:T(8,128)(2,1)}) custom-call(s32[8,2]{1,0:T(8,128)} %copy.324.table_ref, bf16[16,2,8,128,128]{4,3,2,1,0:T(8,128)(2,1)} %bitcast.318, bf16[8,2,8,128,128]{4,3,2,1,0:T(8,128)(2,1)} %get-tuple-element.36.refs_0_, ...), custom_call_target="tpu_custom_call", output_to_operand_aliasing={{0}: (2, {}), {1}: (3, {})} | custom-call | tf_op jit(solution)/shard_map/pallas_call | solution.py:108
  34.0 2.0 %fusion.239 = (f32[2,8,32]{2,1,0:T(8,128)S(1)}, f32[2,2,8,32,128]{4,3,2,1,0:T(8,128)S(1)}) fusion(bf16[8,2,8,128,128]{4,3,2,1,0:T(8,128)(2,1)} %get-tuple-element.40.refs_0_, s32[]{:T(128)S(6)} %select_n.275, bf16[2,8,32,128]{3,2,1,0:T(8,128)(2,1)S(1)} %bitcast.350, pred[2,2,128]{2,1,0:T(4,128)(4,1)S(1)} %broadcast_compare_fusion.9), kind=kOutput, calls=%fused_computation.475 | convolution fusion | flops 33947136 | bytes 1706500 | tf_op jit(solution)/shard_map/rjgxd,rjgpd->rjgxp/dot_general | solution.py:46
  39.8 4.5 %shard_map.89 = (bf16[8,2,8,128,128]{4,3,2,1,0:T(8,128)(2,1)}, bf16[8,2,8,128,128]{4,3,2,1,0:T(8,128)(2,1)}) custom-call(s32[8,2]{1,0:T(8,128)} %copy.324.table_ref, bf16[16,2,8,128,128]{4,3,2,1,0:T(8,128)(2,1)} %bitcast.319, bf16[8,2,8,128,128]{4,3,2,1,0:T(8,128)(2,1)} %get-tuple-element.40.refs_0_, ...), custom_call_target="tpu_custom_call", output_to_operand_aliasing={{0}: (2, {}), {1}: (3, {})} | custom-call | tf_op jit(solution)/shard_map/pallas_call | solution.py:108
  45.6 2.0 %fusion.241 = (f32[2,8,32]{2,1,0:T(8,128)S(1)}, f32[2,2,8,32,128]{4,3,2,1,0:T(8,128)S(1)}) fusion(bf16[8,2,8,128,128]{4,3,2,1,0:T(8,128)(2,1)} %get-tuple-element.44, s32[]{:T(128)S(6)} %select_n.280, bf16[2,8,32,128]{3,2,1,0:T(8,128)(2,1)S(1)} %bitcast.351, pred[2,2,128]{2,1,0:T(4,128)(4,1)S(1)} %broadcast_compare_fusion.8), kind=kOutput, calls=%fused_computation.477 | convolution fusion | flops 33947136 | bytes 1706500 | tf_op jit(solution)/shard_map/rjgxd,rjgpd->rjgxp/dot_general | solution.py:46
  52.3 2.0 %fusion.243 = (f32[2,8,32]{2,1,0:T(8,128)S(1)}, f32[2,2,8,32,128]{4,3,2,1,0:T(8,128)S(1)}) fusion(bf16[8,2,8,128,128]{4,3,2,1,0:T(8,128)(2,1)} %get-tuple-element.44, s32[]{:T(128)S(6)} %select_n.284, bf16[2,8,32,128]{3,2,1,0:T(8,128)(2,1)S(1)} %bitcast.352, pred[2,2,128]{2,1,0:T(4,128)(4,1)S(1)} %broadcast_compare_fusion.7), kind=kOutput, calls=%fused_computation.479 | convolution fusion | flops 33947136 | bytes 1706500 | tf_op jit(solution)/shard_map/rjgxd,rjgpd->rjgxp/dot_general | solution.py:46
  57.7 5.5 %gather_fusion.2 = bf16[4,2,8,128,128]{4,3,2,1,0:T(8,128)(2,1)} fusion(bf16[16,2,8,128,128]{4,3,2,1,0:T(8,128)(2,1)} %bitcast.320, s32[1024]{0:T(1024)S(1)} %pad_clamp_fusion), kind=kCustom, calls=%fused_computation.2 | custom fusion | bytes 4194320 | tf_op jit(solution)/shard_map/gather | solution.py:142
  64.9 2.0 %fusion.245 = (f32[2,8,32]{2,1,0:T(8,128)S(1)}, f32[2,2,8,32,128]{4,3,2,1,0:T(8,128)S(1)}) fusion(bf16[8,2,8,128,128]{4,3,2,1,0:T(8,128)(2,1)} %get-tuple-element.44, s32[]{:T(128)S(6)} %select_n.288, bf16[2,8,32,128]{3,2,1,0:T(8,128)(2,1)S(1)} %bitcast.353, pred[2,2,128]{2,1,0:T(4,128)(4,1)S(1)} %broadcast_compare_fusion.6), kind=kOutput, calls=%fused_computation.481 | convolution fusion | flops 33947136 | bytes 1706500 | tf_op jit(solution)/shard_map/rjgxd,rjgpd->rjgxp/dot_general | solution.py:46
  73.0 10.8 %collective-permute-done.5 = bf16[4,2,8192]{2,1,0:T(2,128)(2,1)S(1)} collective-permute-done((bf16[4,2,8192]{2,1,0:T(2,128)(2,1)S(1)}, bf16[4,2,8192]{2,1,0:T(2,128)(2,1)S(1)}, u32[]{:S(2)}, u32[]{:S(2)}) %collective-permute-start.5) | collective-permute-done | bytes 131104 | tf_op jit(solution)/shard_map/ppermute | solution.py:160
  85.1 2.0 %fusion.247 = (f32[2,8,32]{2,1,0:T(8,128)S(1)}, f32[2,2,8,32,128]{4,3,2,1,0:T(8,128)S(1)}) fusion(bf16[8,2,8,128,128]{4,3,2,1,0:T(8,128)(2,1)} %get-tuple-element.44, s32[]{:T(128)S(6)} %select_n.294, bf16[2,8,32,128]{3,2,1,0:T(8,128)(2,1)S(1)} %bitcast.354, pred[2,2,128]{2,1,0:T(4,128)(4,1)S(1)} %broadcast_compare_fusion.4), kind=kOutput, calls=%fused_computation.483 | convolution fusion | flops 33947136 | bytes 1706500 | tf_op jit(solution)/shard_map/rjgxd,rjgpd->rjgxp/dot_general | solution.py:46
  89.7 1.9 %collective-permute-start.8 = (bf16[4,2,8192]{2,1,0:T(2,128)(2,1)S(1)}, bf16[4,2,8192]{2,1,0:T(2,128)(2,1)S(1)}, u32[]{:S(2)}, u32[]{:S(2)}) collective-permute-start(bf16[4,2,8192]{2,1,0:T(2,128)(2,1)S(1)} %get-tuple-element.89), channel_id=1, source_target_pairs={{3,4},{4,5},{5,6},{6,7},{11,12},{12,13},{13,14},{14,15},{19,20},{2... | collective-permute-start | bytes 393224 | tf_op jit(solution)/shard_map/ppermute | solution.py:160
  91.6 7.4 %collective-permute-done.8 = bf16[4,2,8192]{2,1,0:T(2,128)(2,1)S(1)} collective-permute-done((bf16[4,2,8192]{2,1,0:T(2,128)(2,1)S(1)}, bf16[4,2,8192]{2,1,0:T(2,128)(2,1)S(1)}, u32[]{:S(2)}, u32[]{:S(2)}) %collective-permute-start.8) | collective-permute-done | bytes 131104 | tf_op jit(solution)/shard_map/ppermute | solution.py:160
  100.2 2.0 %fusion.249 = (f32[2,8,32]{2,1,0:T(8,128)S(1)}, f32[2,2,8,32,128]{4,3,2,1,0:T(8,128)S(1)}) fusion(bf16[8,2,8,128,128]{4,3,2,1,0:T(8,128)(2,1)} %get-tuple-element.44, s32[]{:T(128)S(6)} %select_n.298, bf16[2,8,32,128]{3,2,1,0:T(8,128)(2,1)S(1)} %bitcast.355, pred[2,2,128]{2,1,0:T(4,128)(4,1)S(1)} %broadcast_compare_fusion.3), kind=kOutput, calls=%fused_computation.485 | convolution fusion | flops 33947136 | bytes 1706500 | tf_op jit(solution)/shard_map/rjgxd,rjgpd->rjgxp/dot_general | solution.py:46
  104.8 2.1 %collective-permute-start.9 = (bf16[4,2,8192]{2,1,0:T(2,128)(2,1)S(1)}, bf16[4,2,8192]{2,1,0:T(2,128)(2,1)S(1)}, u32[]{:S(2)}, u32[]{:S(2)}) collective-permute-start(bf16[4,2,8192]{2,1,0:T(2,128)(2,1)S(1)} %get-tuple-element.85), channel_id=1, source_target_pairs={{4,5},{5,6},{6,7},{12,13},{13,14},{14,15},{20,21},{21,22},{22,23},... | collective-permute-start | bytes 393224 | tf_op jit(solution)/shard_map/ppermute | solution.py:160
  106.9 5.6 %collective-permute-done.9 = bf16[4,2,8192]{2,1,0:T(2,128)(2,1)S(1)} collective-permute-done((bf16[4,2,8192]{2,1,0:T(2,128)(2,1)S(1)}, bf16[4,2,8192]{2,1,0:T(2,128)(2,1)S(1)}, u32[]{:S(2)}, u32[]{:S(2)}) %collective-permute-start.9) | collective-permute-done | bytes 131104 | tf_op jit(solution)/shard_map/ppermute | solution.py:160
  113.8 2.0 %fusion.251 = (f32[2,8,32]{2,1,0:T(8,128)S(1)}, f32[2,2,8,32,128]{4,3,2,1,0:T(8,128)S(1)}) fusion(bf16[8,2,8,128,128]{4,3,2,1,0:T(8,128)(2,1)} %get-tuple-element.44, s32[]{:T(128)S(6)} %select_n.302, bf16[2,8,32,128]{3,2,1,0:T(8,128)(2,1)S(1)} %bitcast.356, pred[2,2,128]{2,1,0:T(4,128)(4,1)S(1)} %broadcast_compare_fusion.2), kind=kOutput, calls=%fused_computation.487 | convolution fusion | flops 33947136 | bytes 1706500 | tf_op jit(solution)/shard_map/rjgxd,rjgpd->rjgxp/dot_general | solution.py:46
  118.3 1.9 %collective-permute-start.10 = (bf16[4,2,8192]{2,1,0:T(2,128)(2,1)S(1)}, bf16[4,2,8192]{2,1,0:T(2,128)(2,1)S(1)}, u32[]{:S(2)}, u32[]{:S(2)}) collective-permute-start(bf16[4,2,8192]{2,1,0:T(2,128)(2,1)S(1)} %get-tuple-element.81), channel_id=1, source_target_pairs={{5,6},{6,7},{13,14},{14,15},{21,22},{22,23},{29,30},{30,31}} | collective-permute-start | bytes 393224 | tf_op jit(solution)/shard_map/ppermute | solution.py:160
  120.3 5.8 %collective-permute-done.10 = bf16[4,2,8192]{2,1,0:T(2,128)(2,1)S(1)} collective-permute-done((bf16[4,2,8192]{2,1,0:T(2,128)(2,1)S(1)}, bf16[4,2,8192]{2,1,0:T(2,128)(2,1)S(1)}, u32[]{:S(2)}, u32[]{:S(2)}) %collective-permute-start.10) | collective-permute-done | bytes 131104 | tf_op jit(solution)/shard_map/ppermute | solution.py:160
  127.3 2.0 %fusion.253 = (f32[2,8,32]{2,1,0:T(8,128)S(1)}, f32[2,2,8,32,128]{4,3,2,1,0:T(8,128)S(1)}) fusion(bf16[8,2,8,128,128]{4,3,2,1,0:T(8,128)(2,1)} %get-tuple-element.44, s32[]{:T(128)S(6)} %select_n.306, bf16[2,8,32,128]{3,2,1,0:T(8,128)(2,1)S(1)} %bitcast.357, pred[2,2,128]{2,1,0:T(4,128)(4,1)S(1)} %broadcast_compare_fusion.1), kind=kOutput, calls=%fused_computation.489 | convolution fusion | flops 33947136 | bytes 1706500 | tf_op jit(solution)/shard_map/rjgxd,rjgpd->rjgxp/dot_general | solution.py:46
  133.2 2.5 %collective-permute-done.11 = bf16[4,2,8192]{2,1,0:T(2,128)(2,1)S(1)} collective-permute-done((bf16[4,2,8192]{2,1,0:T(2,128)(2,1)S(1)}, bf16[4,2,8192]{2,1,0:T(2,128)(2,1)S(1)}, u32[]{:S(2)}, u32[]{:S(2)}) %collective-permute-start.11) | collective-permute-done | bytes 131104 | tf_op jit(solution)/shard_map/ppermute | solution.py:160
  137.0 2.0 %fusion.255 = (f32[2,8,32]{2,1,0:T(8,128)S(1)}, f32[2,2,8,32,128]{4,3,2,1,0:T(8,128)S(1)}) fusion(bf16[8,2,8,128,128]{4,3,2,1,0:T(8,128)(2,1)} %get-tuple-element.44, s32[]{:T(128)S(6)} %select_n.310, bf16[2,8,32,128]{3,2,1,0:T(8,128)(2,1)S(1)} %bitcast.349, pred[2,2,128]{2,1,0:T(4,128)(4,1)S(1)} %broadcast_compare_fusion), kind=kOutput, calls=%fused_computation.491 | convolution fusion | flops 33947136 | bytes 1706500 | tf_op jit(solution)/shard_map/rjgxd,rjgpd->rjgxp/dot_general | solution.py:46
  (265 shorter events, 61.0 us)
Async XLA Ops:
  0.6 5.2 %copy-start = (s32[1,8]{1,0:T(1,128)S(1)}, s32[1,8]{1,0:T(1,128)}, u32[]{:S(2)}) copy-start(s32[1,8]{1,0:T(1,128)} %param.10) | copy-start | bytes 100
  10.4 4.6 %copy-start.1 = (bf16[1,4,8,8192]{3,2,1,0:T(8,128)(2,1)S(1)}, bf16[1,4,8,8192]{3,2,1,0:T(8,128)(2,1)}, u32[]{:S(2)}) copy-start(bf16[1,4,8,8192]{3,2,1,0:T(8,128)(2,1)} %param.7) | copy-start | bytes 1572868
  10.4 4.6 %copy-start.2 = (f32[1,8192]{1,0:T(1,128)S(1)}, f32[1,8192]{1,0:T(1,128)}, u32[]{:S(2)}) copy-start(f32[1,8192]{1,0:T(1,128)} %param.13) | copy-start | bytes 98308
  10.4 5.6 %copy-start.7 = (s32[1,2]{1,0:T(1,128)S(1)}, s32[1,2]{1,0:T(1,128)}, u32[]{:S(2)}) copy-start(s32[1,2]{1,0:T(1,128)} %param.11) | copy-start | bytes 28
  15.3 6.4 %collective-permute-start = (bf16[4,2,8192]{2,1,0:T(2,128)(2,1)S(1)}, bf16[4,2,8192]{2,1,0:T(2,128)(2,1)S(1)}, u32[]{:S(2)}, u32[]{:S(2)}) collective-permute-start(bf16[4,2,8192]{2,1,0:T(2,128)(2,1)S(1)} %fusion.97), channel_id=1, source_target_pairs={{0,1},{8,9},{16,17},{24,25}} | collective-permute-start | bytes 393224 | tf_op jit(solution)/shard_map/ppermute | solution.py:160
  16.7 6.3 %collective-permute-start.6 = (s32[2]{0:T(128)S(1)}, s32[2]{0:T(128)S(1)}, u32[]{:S(2)}, u32[]{:S(2)}) collective-permute-start(s32[2]{0:T(128)S(1)} %gather_fusion.1), channel_id=1, source_target_pairs={{0,8},{8,0},{1,9},{9,1},{2,10},{10,2},{3,11},{11,3},{4,12},{12,4},... | collective-permute-start | bytes 32 | tf_op jit(solution)/shard_map/ppermute | solution.py:20
  17.1 5.1 %copy-start.3 = (f32[1,8192]{1,0:T(1,128)S(1)}, f32[1,8192]{1,0:T(1,128)}, u32[]{:S(2)}) copy-start(f32[1,8192]{1,0:T(1,128)} %param.12) | copy-start | bytes 98308
  27.6 5.2 %collective-permute-start.1 = (bf16[4,2,8192]{2,1,0:T(2,128)(2,1)S(1)}, bf16[4,2,8192]{2,1,0:T(2,128)(2,1)S(1)}, u32[]{:S(2)}, u32[]{:S(2)}) collective-permute-start(bf16[4,2,8192]{2,1,0:T(2,128)(2,1)S(1)} %get-tuple-element.109), channel_id=1, source_target_pairs={{0,1},{1,2},{8,9},{9,10},{16,17},{17,18},{24,25},{25,26}} | collective-permute-start | bytes 393224 | tf_op jit(solution)/shard_map/ppermute | solution.py:160
  33.8 5.4 %copy-start.6 = (s32[8,2]{1,0:T(8,128)S(1)}, s32[8,2]{1,0:T(8,128)}, u32[]{:S(2)}) copy-start(s32[8,2]{1,0:T(8,128)} %copy.324.table_ref) | copy-start | bytes 196
  38.6 5.8 %collective-permute-start.2 = (bf16[4,2,8192]{2,1,0:T(2,128)(2,1)S(1)}, bf16[4,2,8192]{2,1,0:T(2,128)(2,1)S(1)}, u32[]{:S(2)}, u32[]{:S(2)}) collective-permute-start(bf16[4,2,8192]{2,1,0:T(2,128)(2,1)S(1)} %get-tuple-element.105), channel_id=1, source_target_pairs={{0,1},{1,2},{2,3},{8,9},{9,10},{10,11},{16,17},{17,18},{18,19},{24... | collective-permute-start | bytes 393224 | tf_op jit(solution)/shard_map/ppermute | solution.py:160
  50.2 0.9 collective-permute-start.3
  56.9 6.3 %copy-start.4 = (bf16[11,4,2,8192]{3,2,1,0:T(2,128)(2,1)}, bf16[11,4,2,8192]{3,2,1,0:T(2,128)(2,1)S(1)}, u32[]{:S(2)}) copy-start(bf16[11,4,2,8192]{3,2,1,0:T(2,128)(2,1)S(1)} %get-tuple-element.96) | copy-start | bytes 4325380
  56.9 6.8 %collective-permute-start.4 = (bf16[4,2,8192]{2,1,0:T(2,128)(2,1)S(1)}, bf16[4,2,8192]{2,1,0:T(2,128)(2,1)S(1)}, u32[]{:S(2)}, u32[]{:S(2)}) collective-permute-start(bf16[4,2,8192]{2,1,0:T(2,128)(2,1)S(1)} %get-tuple-element.97), channel_id=1, source_target_pairs={{1,2},{2,3},{3,4},{4,5},{9,10},{10,11},{11,12},{12,13},{17,18},{18... | collective-permute-start | bytes 393224 | tf_op jit(solution)/shard_map/ppermute | solution.py:160
  63.2 8.2 %collective-permute-start.7 = (bf16[2,2,2,8,128,128]{5,4,3,2,1,0:T(8,128)(2,1)}, bf16[2,2,2,8,128,128]{5,4,3,2,1,0:T(8,128)(2,1)S(1)}, u32[]{:S(2)}, u32[]{:S(2)}) collective-permute-start(bf16[2,2,2,8,128,128]{5,4,3,2,1,0:T(8,128)(2,1)} %bitcast.346), channel_id=1, source_target_pairs={{0,8},{8,0},{1,9},{9,1},{2,10},{10,2},{3,11},{11,3},{4,12},{12,4},... | collective-permute-start | bytes 6291464 | tf_op jit(solution)/shard_map/ppermute | solution.py:20
  70.1 13.7 %collective-permute-start.5 = (bf16[4,2,8192]{2,1,0:T(2,128)(2,1)S(1)}, bf16[4,2,8192]{2,1,0:T(2,128)(2,1)S(1)}, u32[]{:S(2)}, u32[]{:S(2)}) collective-permute-start(bf16[4,2,8192]{2,1,0:T(2,128)(2,1)S(1)} %get-tuple-element.93), channel_id=1, source_target_pairs={{2,3},{3,4},{4,5},{5,6},{10,11},{11,12},{12,13},{13,14},{18,19},{1... | collective-permute-start | bytes 393224 | tf_op jit(solution)/shard_map/ppermute | solution.py:160
  84.7 4.8 %copy-start.5 = (bf16[11,4,2,8192]{3,2,1,0:T(2,128)(2,1)S(1)}, bf16[11,4,2,8192]{3,2,1,0:T(2,128)(2,1)}, u32[]{:S(2)}) copy-start(bf16[11,4,2,8192]{3,2,1,0:T(2,128)(2,1)} %get-tuple-element.92) | copy-start | bytes 4325380
  89.7 9.3 %collective-permute-start.8 = (bf16[4,2,8192]{2,1,0:T(2,128)(2,1)S(1)}, bf16[4,2,8192]{2,1,0:T(2,128)(2,1)S(1)}, u32[]{:S(2)}, u32[]{:S(2)}) collective-permute-start(bf16[4,2,8192]{2,1,0:T(2,128)(2,1)S(1)} %get-tuple-element.89), channel_id=1, source_target_pairs={{3,4},{4,5},{5,6},{6,7},{11,12},{12,13},{13,14},{14,15},{19,20},{2... | collective-permute-start | bytes 393224 | tf_op jit(solution)/shard_map/ppermute | solution.py:160
  104.8 7.8 %collective-permute-start.9 = (bf16[4,2,8192]{2,1,0:T(2,128)(2,1)S(1)}, bf16[4,2,8192]{2,1,0:T(2,128)(2,1)S(1)}, u32[]{:S(2)}, u32[]{:S(2)}) collective-permute-start(bf16[4,2,8192]{2,1,0:T(2,128)(2,1)S(1)} %get-tuple-element.85), channel_id=1, source_target_pairs={{4,5},{5,6},{6,7},{12,13},{13,14},{14,15},{20,21},{21,22},{22,23},... | collective-permute-start | bytes 393224 | tf_op jit(solution)/shard_map/ppermute | solution.py:160
  118.3 7.8 %collective-permute-start.10 = (bf16[4,2,8192]{2,1,0:T(2,128)(2,1)S(1)}, bf16[4,2,8192]{2,1,0:T(2,128)(2,1)S(1)}, u32[]{:S(2)}, u32[]{:S(2)}) collective-permute-start(bf16[4,2,8192]{2,1,0:T(2,128)(2,1)S(1)} %get-tuple-element.81), channel_id=1, source_target_pairs={{5,6},{6,7},{13,14},{14,15},{21,22},{22,23},{29,30},{30,31}} | collective-permute-start | bytes 393224 | tf_op jit(solution)/shard_map/ppermute | solution.py:160
  131.9 3.8 %collective-permute-start.11 = (bf16[4,2,8192]{2,1,0:T(2,128)(2,1)S(1)}, bf16[4,2,8192]{2,1,0:T(2,128)(2,1)S(1)}, u32[]{:S(2)}, u32[]{:S(2)}) collective-permute-start(bf16[4,2,8192]{2,1,0:T(2,128)(2,1)S(1)} %get-tuple-element.77), channel_id=1, source_target_pairs={{6,7},{14,15},{22,23},{30,31}} | collective-permute-start | bytes 393224 | tf_op jit(solution)/shard_map/ppermute | solution.py:160
  143.4 1.4 collective-permute-start.12

commit v12 on v9

--- a/solution.py
+++ b/solution.py
@@ -148,8 +148,13 @@
             start, incoming, arrived = lax.optimization_barrier((start, incoming, arrived))
         elif k > 0:
             start, incoming = lax.optimization_barrier((start, incoming))
-        first = lax.dynamic_slice_in_dim(inputs, start, block, 1)
-        rows = jnp.where(section == 0, first, incoming)
+        if k == 0:
+            rows = inputs[:, :block]
+        elif k < chunks:
+            first = lax.dynamic_slice_in_dim(inputs, start, block, 1)
+            rows = jnp.where(section == 0, first, incoming)
+        else:
+            rows = incoming
         part_keys = lax.dynamic_slice_in_dim(keys, start, block, 0)
         part_values = lax.dynamic_slice_in_dim(values, start, block, 0)
         part_lens = lax.dynamic_slice_in_dim(lens_used, start, block, 0)

time: 149 us -> 148 us (level)
  other arithmetic: 19.5 us -> 17.5 us
    mul x10 -> x11, other arithmetic: 1.75 us -> 2.98 us  [layer(): wide * lax.rsqrt(jnp.mean(wide * wide, axis=-1, keepdims=True) + 1e-05)]
where the time goes in v12:
time: 148 us; the launch traced here: 145 us
  matrix products  43.7 us (30%)
  waiting for transfers between devices  33.5 us (23%)
  local copies, waits for them, and re-layouts  18.1 us (12%)
  Pallas kernels  17.8 us (12%)
  other arithmetic  17.5 us (12%)
  starting transfers between devices  12.6 us (9%)
  between operations  2.15 us (1%)
    ppermute x10, waiting for transfers between devices, per_device(): incoming = lax.ppermute(result, 'section', pairs)  32.1 us
    dot_general x11, matrix products, layer(): jnp.einsum('rjgxd,rjgpd->rjgxp', wide_query, keys, preferred_element_type...  21.6 us
    pallas_call x4, Pallas kernels, gather_chunk(): pl.pallas_call(copy_kernel, grid_spec=grid_spec, out_shape=[half, half],...  17.8 us
    dot_general x11, matrix products, layer(): jnp.einsum('rjgxp,rjgpd->rjgxd', cache_w, values, preferred_element_type=...  17.3 us
    ppermute x10, starting transfers between devices, per_device(): incoming = lax.ppermute(result, 'section', pairs)  12.1 us
    gather x1, local copies, waits for them, and re-layouts, per_device(): received = partner(pool[chosen], 'inst', 0)  5.51 us
    reduce_sum x11, other arithmetic, layer(): jnp.mean(wide * wide, axis=-1, keepdims=True) + 1e-05  4.06 us
    unnamed x18, local copies, waits for them, and re-layouts  3.07 us
  transfers between devices with their start and end apart: 13, of which 6 were waited for; matrix products, arithmetic and copies ran while one was open for 11% of the time, Pallas kernels for 9%

profile of v12, /device:TPU:26, one launch (start us, length us, event | category | flops | bytes accessed | tf_op | source)
XLA Modules:
  0.0 145.3 jit_solution(10743902035636858297)
XLA Ops:
  5.0 4.5 %shard_map.86 = (bf16[8,2,8,128,128]{4,3,2,1,0:T(8,128)(2,1)}, bf16[8,2,8,128,128]{4,3,2,1,0:T(8,128)(2,1)}) custom-call(s32[16]{0:T(128)} %reshape_squeeze.2.table_ref, bf16[16,2,8,128,128]{4,3,2,1,0:T(8,128)(2,1)} %bitcast.288), custom_call_target="tpu_custom_call" | custom-call | tf_op jit(solution)/shard_map/pallas_call | solution.py:108
  9.8 2.0 %fusion.233 = (f32[2,8,32]{2,1,0:T(8,128)S(1)}, f32[2,2,8,32,128]{4,3,2,1,0:T(8,128)S(1)}) fusion(bf16[8,2,8,128,128]{4,3,2,1,0:T(8,128)(2,1)} %get-tuple-element.32.refs_0_, s32[]{:T(128)S(6)} %select_n.214, bf16[2,8,32,128]{3,2,1,0:T(8,128)(2,1)S(1)} %bitcast.321, pred[2,2,128]{2,1,0:T(4,128)(4,1)S(1)} %broadcast_compare_fusion.11), kind=kOutput, calls=%fused_computation.461 | convolution fusion | flops 33947136 | bytes 1706500 | tf_op jit(solution)/shard_map/rjgxd,rjgpd->rjgxp/dot_general | solution.py:46
  15.7 4.5 %shard_map.87 = (bf16[8,2,8,128,128]{4,3,2,1,0:T(8,128)(2,1)}, bf16[8,2,8,128,128]{4,3,2,1,0:T(8,128)(2,1)}) custom-call(s32[16]{0:T(128)} %reshape_squeeze.2.table_ref, bf16[16,2,8,128,128]{4,3,2,1,0:T(8,128)(2,1)} %bitcast.289, bf16[8,2,8,128,128]{4,3,2,1,0:T(8,128)(2,1)} %get-tuple-element.32.refs_0_, ...), custom_call_target="tpu_custom_call", output_to_operand_aliasing={{0}: (2, {}), {1}: (3, {})} | custom-call | tf_op jit(solution)/shard_map/pallas_call | solution.py:108
  21.4 2.0 %fusion.235 = (f32[2,8,32]{2,1,0:T(8,128)S(1)}, f32[2,2,8,32,128]{4,3,2,1,0:T(8,128)S(1)}) fusion(bf16[8,2,8,128,128]{4,3,2,1,0:T(8,128)(2,1)} %get-tuple-element.36.refs_0_, s32[]{:T(128)S(6)} %select_n.219, bf16[2,8,32,128]{3,2,1,0:T(8,128)(2,1)S(1)} %bitcast.323, pred[2,2,128]{2,1,0:T(4,128)(4,1)S(1)} %get-tuple-element.125), kind=kOutput, calls=%fused_computation.463 | convolution fusion | flops 33947136 | bytes 1706500 | tf_op jit(solution)/shard_map/rjgxd,rjgpd->rjgxp/dot_general | solution.py:46
  26.7 4.5 %shard_map.88 = (bf16[8,2,8,128,128]{4,3,2,1,0:T(8,128)(2,1)}, bf16[8,2,8,128,128]{4,3,2,1,0:T(8,128)(2,1)}) custom-call(s32[16]{0:T(128)} %reshape_squeeze.2.table_ref, bf16[16,2,8,128,128]{4,3,2,1,0:T(8,128)(2,1)} %bitcast.290, bf16[8,2,8,128,128]{4,3,2,1,0:T(8,128)(2,1)} %get-tuple-element.36.refs_0_, ...), custom_call_target="tpu_custom_call", output_to_operand_aliasing={{0}: (2, {}), {1}: (3, {})} | custom-call | tf_op jit(solution)/shard_map/pallas_call | solution.py:108
  32.4 2.0 %fusion.237 = (f32[2,8,32]{2,1,0:T(8,128)S(1)}, f32[2,2,8,32,128]{4,3,2,1,0:T(8,128)S(1)}) fusion(bf16[8,2,8,128,128]{4,3,2,1,0:T(8,128)(2,1)} %get-tuple-element.40.refs_0_, s32[]{:T(128)S(6)} %select_n.223, bf16[2,8,32,128]{3,2,1,0:T(8,128)(2,1)S(1)} %bitcast.330, pred[2,2,128]{2,1,0:T(4,128)(4,1)S(1)} %broadcast_compare_fusion.9), kind=kOutput, calls=%fused_computation.465 | convolution fusion | flops 33947136 | bytes 1706500 | tf_op jit(solution)/shard_map/rjgxd,rjgpd->rjgxp/dot_general | solution.py:46
  38.3 4.5 %shard_map.89 = (bf16[8,2,8,128,128]{4,3,2,1,0:T(8,128)(2,1)}, bf16[8,2,8,128,128]{4,3,2,1,0:T(8,128)(2,1)}) custom-call(s32[16]{0:T(128)} %reshape_squeeze.2.table_ref, bf16[16,2,8,128,128]{4,3,2,1,0:T(8,128)(2,1)} %bitcast.291, bf16[8,2,8,128,128]{4,3,2,1,0:T(8,128)(2,1)} %get-tuple-element.40.refs_0_, ...), custom_call_target="tpu_custom_call", output_to_operand_aliasing={{0}: (2, {}), {1}: (3, {})} | custom-call | tf_op jit(solution)/shard_map/pallas_call | solution.py:108
  44.0 2.0 %fusion.239 = (f32[2,8,32]{2,1,0:T(8,128)S(1)}, f32[2,2,8,32,128]{4,3,2,1,0:T(8,128)S(1)}) fusion(bf16[8,2,8,128,128]{4,3,2,1,0:T(8,128)(2,1)} %get-tuple-element.44, s32[]{:T(128)S(6)} %select_n.228, bf16[2,8,32,128]{3,2,1,0:T(8,128)(2,1)S(1)} %bitcast.331, pred[2,2,128]{2,1,0:T(4,128)(4,1)S(1)} %broadcast_compare_fusion.8), kind=kOutput, calls=%fused_computation.467 | convolution fusion | flops 33947136 | bytes 1706500 | tf_op jit(solution)/shard_map/rjgxd,rjgpd->rjgxp/dot_general | solution.py:46
  50.6 2.0 %fusion.241 = (f32[2,8,32]{2,1,0:T(8,128)S(1)}, f32[2,2,8,32,128]{4,3,2,1,0:T(8,128)S(1)}) fusion(bf16[8,2,8,128,128]{4,3,2,1,0:T(8,128)(2,1)} %get-tuple-element.44, s32[]{:T(128)S(6)} %select_n.232, bf16[2,8,32,128]{3,2,1,0:T(8,128)(2,1)S(1)} %bitcast.324, pred[2,2,128]{2,1,0:T(4,128)(4,1)S(1)} %broadcast_compare_fusion.7), kind=kOutput, calls=%fused_computation.469 | convolution fusion | flops 33947136 | bytes 1706500 | tf_op jit(solution)/shard_map/rjgxd,rjgpd->rjgxp/dot_general | solution.py:46
  57.1 5.5 %gather_fusion.2 = bf16[4,2,8,128,128]{4,3,2,1,0:T(8,128)(2,1)} fusion(bf16[16,2,8,128,128]{4,3,2,1,0:T(8,128)(2,1)} %bitcast.292, s32[1024]{0:T(1024)S(1)} %pad_clamp_fusion), kind=kCustom, calls=%fused_computation.2 | custom fusion | bytes 4194320 | tf_op jit(solution)/shard_map/gather | solution.py:142
  64.3 2.0 %fusion.243 = (f32[2,8,32]{2,1,0:T(8,128)S(1)}, f32[2,2,8,32,128]{4,3,2,1,0:T(8,128)S(1)}) fusion(bf16[8,2,8,128,128]{4,3,2,1,0:T(8,128)(2,1)} %get-tuple-element.44, s32[]{:T(128)S(6)} %select_n.235, bf16[2,8,32,128]{3,2,1,0:T(8,128)(2,1)S(1)} %bitcast.325, pred[2,2,128]{2,1,0:T(4,128)(4,1)S(1)} %broadcast_compare_fusion.6), kind=kOutput, calls=%fused_computation.471 | convolution fusion | flops 33947136 | bytes 1706500 | tf_op jit(solution)/shard_map/rjgxd,rjgpd->rjgxp/dot_general | solution.py:46
  72.3 10.8 %collective-permute-done.5 = bf16[4,2,8192]{2,1,0:T(2,128)(2,1)S(1)} collective-permute-done((bf16[4,2,8192]{2,1,0:T(2,128)(2,1)S(1)}, bf16[4,2,8192]{2,1,0:T(2,128)(2,1)S(1)}, u32[]{:S(2)}, u32[]{:S(2)}) %collective-permute-start.5) | collective-permute-done | bytes 131104 | tf_op jit(solution)/shard_map/ppermute | solution.py:165
  84.3 2.0 %fusion.245 = (f32[2,8,32]{2,1,0:T(8,128)S(1)}, f32[2,2,8,32,128]{4,3,2,1,0:T(8,128)S(1)}) fusion(bf16[8,2,8,128,128]{4,3,2,1,0:T(8,128)(2,1)} %get-tuple-element.44, s32[]{:T(128)S(6)} %select_n.240, bf16[2,8,32,128]{3,2,1,0:T(8,128)(2,1)S(1)} %bitcast.326, pred[2,2,128]{2,1,0:T(4,128)(4,1)S(1)} %broadcast_compare_fusion.4), kind=kOutput, calls=%fused_computation.473 | convolution fusion | flops 33947136 | bytes 1706500 | tf_op jit(solution)/shard_map/rjgxd,rjgpd->rjgxp/dot_general | solution.py:46
  88.9 1.9 %collective-permute-start.8 = (bf16[4,2,8192]{2,1,0:T(2,128)(2,1)S(1)}, bf16[4,2,8192]{2,1,0:T(2,128)(2,1)S(1)}, u32[]{:S(2)}, u32[]{:S(2)}) collective-permute-start(bf16[4,2,8192]{2,1,0:T(2,128)(2,1)S(1)} %get-tuple-element.79), channel_id=1, source_target_pairs={{3,4},{4,5},{5,6},{6,7},{11,12},{12,13},{13,14},{14,15},{19,20},{2... | collective-permute-start | bytes 393224 | tf_op jit(solution)/shard_map/ppermute | solution.py:165
  90.8 7.4 %collective-permute-done.8 = bf16[4,2,8192]{2,1,0:T(2,128)(2,1)S(1)} collective-permute-done((bf16[4,2,8192]{2,1,0:T(2,128)(2,1)S(1)}, bf16[4,2,8192]{2,1,0:T(2,128)(2,1)S(1)}, u32[]{:S(2)}, u32[]{:S(2)}) %collective-permute-start.8) | collective-permute-done | bytes 131104 | tf_op jit(solution)/shard_map/ppermute | solution.py:165
  99.3 2.0 %fusion.247 = (f32[2,8,32]{2,1,0:T(8,128)S(1)}, f32[2,2,8,32,128]{4,3,2,1,0:T(8,128)S(1)}) fusion(bf16[8,2,8,128,128]{4,3,2,1,0:T(8,128)(2,1)} %get-tuple-element.44, s32[]{:T(128)S(6)} %select_n.243, bf16[2,8,32,128]{3,2,1,0:T(8,128)(2,1)S(1)} %bitcast.327, pred[2,2,128]{2,1,0:T(4,128)(4,1)S(1)} %broadcast_compare_fusion.3), kind=kOutput, calls=%fused_computation.475 | convolution fusion | flops 33947136 | bytes 1706500 | tf_op jit(solution)/shard_map/rjgxd,rjgpd->rjgxp/dot_general | solution.py:46
  103.9 2.1 %collective-permute-start.9 = (bf16[4,2,8192]{2,1,0:T(2,128)(2,1)S(1)}, bf16[4,2,8192]{2,1,0:T(2,128)(2,1)S(1)}, u32[]{:S(2)}, u32[]{:S(2)}) collective-permute-start(bf16[4,2,8192]{2,1,0:T(2,128)(2,1)S(1)} %get-tuple-element.77), channel_id=1, source_target_pairs={{4,5},{5,6},{6,7},{12,13},{13,14},{14,15},{20,21},{21,22},{22,23},... | collective-permute-start | bytes 393224 | tf_op jit(solution)/shard_map/ppermute | solution.py:165
  106.0 5.6 %collective-permute-done.9 = bf16[4,2,8192]{2,1,0:T(2,128)(2,1)S(1)} collective-permute-done((bf16[4,2,8192]{2,1,0:T(2,128)(2,1)S(1)}, bf16[4,2,8192]{2,1,0:T(2,128)(2,1)S(1)}, u32[]{:S(2)}, u32[]{:S(2)}) %collective-permute-start.9) | collective-permute-done | bytes 131104 | tf_op jit(solution)/shard_map/ppermute | solution.py:165
  112.8 2.0 %fusion.249 = (f32[2,8,32]{2,1,0:T(8,128)S(1)}, f32[2,2,8,32,128]{4,3,2,1,0:T(8,128)S(1)}) fusion(bf16[8,2,8,128,128]{4,3,2,1,0:T(8,128)(2,1)} %get-tuple-element.44, s32[]{:T(128)S(6)} %select_n.246, bf16[2,8,32,128]{3,2,1,0:T(8,128)(2,1)S(1)} %bitcast.328, pred[2,2,128]{2,1,0:T(4,128)(4,1)S(1)} %broadcast_compare_fusion.2), kind=kOutput, calls=%fused_computation.477 | convolution fusion | flops 33947136 | bytes 1706500 | tf_op jit(solution)/shard_map/rjgxd,rjgpd->rjgxp/dot_general | solution.py:46
  117.3 1.9 %collective-permute-start.10 = (bf16[4,2,8192]{2,1,0:T(2,128)(2,1)S(1)}, bf16[4,2,8192]{2,1,0:T(2,128)(2,1)S(1)}, u32[]{:S(2)}, u32[]{:S(2)}) collective-permute-start(bf16[4,2,8192]{2,1,0:T(2,128)(2,1)S(1)} %get-tuple-element.75), channel_id=1, source_target_pairs={{5,6},{6,7},{13,14},{14,15},{21,22},{22,23},{29,30},{30,31}} | collective-permute-start | bytes 393224 | tf_op jit(solution)/shard_map/ppermute | solution.py:165
  119.3 5.8 %collective-permute-done.10 = bf16[4,2,8192]{2,1,0:T(2,128)(2,1)S(1)} collective-permute-done((bf16[4,2,8192]{2,1,0:T(2,128)(2,1)S(1)}, bf16[4,2,8192]{2,1,0:T(2,128)(2,1)S(1)}, u32[]{:S(2)}, u32[]{:S(2)}) %collective-permute-start.10) | collective-permute-done | bytes 131104 | tf_op jit(solution)/shard_map/ppermute | solution.py:165
  126.2 2.0 %fusion.251 = (f32[2,8,32]{2,1,0:T(8,128)S(1)}, f32[2,2,8,32,128]{4,3,2,1,0:T(8,128)S(1)}) fusion(bf16[8,2,8,128,128]{4,3,2,1,0:T(8,128)(2,1)} %get-tuple-element.44, s32[]{:T(128)S(6)} %select_n.249, bf16[2,8,32,128]{3,2,1,0:T(8,128)(2,1)S(1)} %bitcast.329, pred[2,2,128]{2,1,0:T(4,128)(4,1)S(1)} %broadcast_compare_fusion.1), kind=kOutput, calls=%fused_computation.479 | convolution fusion | flops 33947136 | bytes 1706500 | tf_op jit(solution)/shard_map/rjgxd,rjgpd->rjgxp/dot_general | solution.py:46
  132.1 2.5 %collective-permute-done.11 = bf16[4,2,8192]{2,1,0:T(2,128)(2,1)S(1)} collective-permute-done((bf16[4,2,8192]{2,1,0:T(2,128)(2,1)S(1)}, bf16[4,2,8192]{2,1,0:T(2,128)(2,1)S(1)}, u32[]{:S(2)}, u32[]{:S(2)}) %collective-permute-start.11) | collective-permute-done | bytes 131104 | tf_op jit(solution)/shard_map/ppermute | solution.py:165
  135.7 2.0 %fusion.253 = (f32[2,8,32]{2,1,0:T(8,128)S(1)}, f32[2,2,8,32,128]{4,3,2,1,0:T(8,128)S(1)}) fusion(bf16[8,2,8,128,128]{4,3,2,1,0:T(8,128)(2,1)} %get-tuple-element.44, s32[]{:T(128)S(6)} %select_n.252, bf16[2,8,32,128]{3,2,1,0:T(8,128)(2,1)S(1)} %bitcast.322, pred[2,2,128]{2,1,0:T(4,128)(4,1)S(1)} %broadcast_compare_fusion), kind=kOutput, calls=%fused_computation.481 | convolution fusion | flops 33947136 | bytes 1706500 | tf_op jit(solution)/shard_map/rjgxd,rjgpd->rjgxp/dot_general | solution.py:46
  (265 shorter events, 60.1 us)
Async XLA Ops:
  0.6 8.8 %copy-start = (s32[1,8]{1,0:T(1,128)S(1)}, s32[1,8]{1,0:T(1,128)}, u32[]{:S(2)}) copy-start(s32[1,8]{1,0:T(1,128)} %param.10) | copy-start | bytes 100
  9.4 4.7 %copy-start.2 = (f32[1,8192]{1,0:T(1,128)S(1)}, f32[1,8192]{1,0:T(1,128)}, u32[]{:S(2)}) copy-start(f32[1,8192]{1,0:T(1,128)} %param.13) | copy-start | bytes 98308
  9.4 4.7 %copy-start.3 = (bf16[1,4,8,8192]{3,2,1,0:T(8,128)(2,1)S(1)}, bf16[1,4,8,8192]{3,2,1,0:T(8,128)(2,1)}, u32[]{:S(2)}) copy-start(bf16[1,4,8,8192]{3,2,1,0:T(8,128)(2,1)} %param.7) | copy-start | bytes 1572868
  9.5 5.6 %copy-start.7 = (s32[1,2]{1,0:T(1,128)S(1)}, s32[1,2]{1,0:T(1,128)}, u32[]{:S(2)}) copy-start(s32[1,2]{1,0:T(1,128)} %param.11) | copy-start | bytes 28
  14.3 5.8 %collective-permute-start = (bf16[4,2,8192]{2,1,0:T(2,128)(2,1)S(1)}, bf16[4,2,8192]{2,1,0:T(2,128)(2,1)S(1)}, u32[]{:S(2)}, u32[]{:S(2)}) collective-permute-start(bf16[4,2,8192]{2,1,0:T(2,128)(2,1)S(1)} %get-tuple-element.97), channel_id=1, source_target_pairs={{0,1},{8,9},{16,17},{24,25}} | collective-permute-start | bytes 393224 | tf_op jit(solution)/shard_map/ppermute | solution.py:165
  15.7 4.9 %copy-start.1 = (f32[1,8192]{1,0:T(1,128)S(1)}, f32[1,8192]{1,0:T(1,128)}, u32[]{:S(2)}) copy-start(f32[1,8192]{1,0:T(1,128)} %param.12) | copy-start | bytes 98308
  15.7 5.7 %collective-permute-start.6 = (s32[2]{0:T(128)S(1)}, s32[2]{0:T(128)S(1)}, u32[]{:S(2)}, u32[]{:S(2)}) collective-permute-start(s32[2]{0:T(128)S(1)} %gather_fusion.1), channel_id=1, source_target_pairs={{0,8},{8,0},{1,9},{9,1},{2,10},{10,2},{3,11},{11,3},{4,12},{12,4},... | collective-permute-start | bytes 32 | tf_op jit(solution)/shard_map/ppermute | solution.py:20
  26.0 5.1 %collective-permute-start.1 = (bf16[4,2,8192]{2,1,0:T(2,128)(2,1)S(1)}, bf16[4,2,8192]{2,1,0:T(2,128)(2,1)S(1)}, u32[]{:S(2)}, u32[]{:S(2)}) collective-permute-start(bf16[4,2,8192]{2,1,0:T(2,128)(2,1)S(1)} %get-tuple-element.93), channel_id=1, source_target_pairs={{0,1},{1,2},{8,9},{9,10},{16,17},{17,18},{24,25},{25,26}} | collective-permute-start | bytes 393224 | tf_op jit(solution)/shard_map/ppermute | solution.py:165
  32.2 5.4 %copy-start.6 = (s32[1,8,2]{1,2,0:T(2,128)S(1)}, s32[1,8,2]{1,2,0:T(2,128)}, u32[]{:S(2)}) copy-start(s32[1,8,2]{1,2,0:T(2,128)} %param.9) | copy-start | bytes 196
  37.0 5.8 %collective-permute-start.2 = (bf16[4,2,8192]{2,1,0:T(2,128)(2,1)S(1)}, bf16[4,2,8192]{2,1,0:T(2,128)(2,1)S(1)}, u32[]{:S(2)}, u32[]{:S(2)}) collective-permute-start(bf16[4,2,8192]{2,1,0:T(2,128)(2,1)S(1)} %get-tuple-element.89), channel_id=1, source_target_pairs={{0,1},{1,2},{2,3},{8,9},{9,10},{10,11},{16,17},{17,18},{18,19},{24... | collective-permute-start | bytes 393224 | tf_op jit(solution)/shard_map/ppermute | solution.py:165
  48.5 0.9 collective-permute-start.3
  55.1 1.2 copy-start.4
  56.3 6.8 %collective-permute-start.4 = (bf16[4,2,8192]{2,1,0:T(2,128)(2,1)S(1)}, bf16[4,2,8192]{2,1,0:T(2,128)(2,1)S(1)}, u32[]{:S(2)}, u32[]{:S(2)}) collective-permute-start(bf16[4,2,8192]{2,1,0:T(2,128)(2,1)S(1)} %get-tuple-element.83), channel_id=1, source_target_pairs={{1,2},{2,3},{3,4},{4,5},{9,10},{10,11},{11,12},{12,13},{17,18},{18... | collective-permute-start | bytes 393224 | tf_op jit(solution)/shard_map/ppermute | solution.py:165
  62.6 8.1 %collective-permute-start.7 = (bf16[2,2,2,8,128,128]{5,4,3,2,1,0:T(8,128)(2,1)}, bf16[2,2,2,8,128,128]{5,4,3,2,1,0:T(8,128)(2,1)S(1)}, u32[]{:S(2)}, u32[]{:S(2)}) collective-permute-start(bf16[2,2,2,8,128,128]{5,4,3,2,1,0:T(8,128)(2,1)} %bitcast.317), channel_id=1, source_target_pairs={{0,8},{8,0},{1,9},{9,1},{2,10},{10,2},{3,11},{11,3},{4,12},{12,4},... | collective-permute-start | bytes 6291464 | tf_op jit(solution)/shard_map/ppermute | solution.py:20
  69.4 13.7 %collective-permute-start.5 = (bf16[4,2,8192]{2,1,0:T(2,128)(2,1)S(1)}, bf16[4,2,8192]{2,1,0:T(2,128)(2,1)S(1)}, u32[]{:S(2)}, u32[]{:S(2)}) collective-permute-start(bf16[4,2,8192]{2,1,0:T(2,128)(2,1)S(1)} %get-tuple-element.81), channel_id=1, source_target_pairs={{2,3},{3,4},{4,5},{5,6},{10,11},{11,12},{12,13},{13,14},{18,19},{1... | collective-permute-start | bytes 393224 | tf_op jit(solution)/shard_map/ppermute | solution.py:165
  83.8 4.8 %copy-start.5 = (bf16[11,4,2,8192]{3,2,1,0:T(2,128)(2,1)S(1)}, bf16[11,4,2,8192]{3,2,1,0:T(2,128)(2,1)}, u32[]{:S(2)}) copy-start(bf16[11,4,2,8192]{3,2,1,0:T(2,128)(2,1)} %get-tuple-element.80) | copy-start | bytes 4325380
  88.9 9.3 %collective-permute-start.8 = (bf16[4,2,8192]{2,1,0:T(2,128)(2,1)S(1)}, bf16[4,2,8192]{2,1,0:T(2,128)(2,1)S(1)}, u32[]{:S(2)}, u32[]{:S(2)}) collective-permute-start(bf16[4,2,8192]{2,1,0:T(2,128)(2,1)S(1)} %get-tuple-element.79), channel_id=1, source_target_pairs={{3,4},{4,5},{5,6},{6,7},{11,12},{12,13},{13,14},{14,15},{19,20},{2... | collective-permute-start | bytes 393224 | tf_op jit(solution)/shard_map/ppermute | solution.py:165
  103.9 7.8 %collective-permute-start.9 = (bf16[4,2,8192]{2,1,0:T(2,128)(2,1)S(1)}, bf16[4,2,8192]{2,1,0:T(2,128)(2,1)S(1)}, u32[]{:S(2)}, u32[]{:S(2)}) collective-permute-start(bf16[4,2,8192]{2,1,0:T(2,128)(2,1)S(1)} %get-tuple-element.77), channel_id=1, source_target_pairs={{4,5},{5,6},{6,7},{12,13},{13,14},{14,15},{20,21},{21,22},{22,23},... | collective-permute-start | bytes 393224 | tf_op jit(solution)/shard_map/ppermute | solution.py:165
  117.3 7.8 %collective-permute-start.10 = (bf16[4,2,8192]{2,1,0:T(2,128)(2,1)S(1)}, bf16[4,2,8192]{2,1,0:T(2,128)(2,1)S(1)}, u32[]{:S(2)}, u32[]{:S(2)}) collective-permute-start(bf16[4,2,8192]{2,1,0:T(2,128)(2,1)S(1)} %get-tuple-element.75), channel_id=1, source_target_pairs={{5,6},{6,7},{13,14},{14,15},{21,22},{22,23},{29,30},{30,31}} | collective-permute-start | bytes 393224 | tf_op jit(solution)/shard_map/ppermute | solution.py:165
  130.8 3.8 %collective-permute-start.11 = (bf16[4,2,8192]{2,1,0:T(2,128)(2,1)S(1)}, bf16[4,2,8192]{2,1,0:T(2,128)(2,1)S(1)}, u32[]{:S(2)}, u32[]{:S(2)}) collective-permute-start(bf16[4,2,8192]{2,1,0:T(2,128)(2,1)S(1)} %get-tuple-element.73), channel_id=1, source_target_pairs={{6,7},{14,15},{22,23},{30,31}} | collective-permute-start | bytes 393224 | tf_op jit(solution)/shard_map/ppermute | solution.py:165
  142.2 1.4 collective-permute-start.12

commit v13 on v12

--- a/solution.py
+++ b/solution.py
@@ -155,6 +155,10 @@
             rows = jnp.where(section == 0, first, incoming)
         else:
             rows = incoming
+        if k == 0:
+            start = 0
+        elif k == chunks + count - 2:
+            start = (chunks - 1) * block
         part_keys = lax.dynamic_slice_in_dim(keys, start, block, 0)
         part_values = lax.dynamic_slice_in_dim(values, start, block, 0)
         part_lens = lax.dynamic_slice_in_dim(lens_used, start, block, 0)

time: 148 us -> 152 us (1.027)
  local copies, waits for them, and re-layouts: 18.1 us -> 21.3 us
  other arithmetic: 17.5 us -> 20.5 us
  matrix products: 43.7 us -> 41.2 us
    unnamed x10, other arithmetic: 2.7 us -> 5.27 us
    dot_general x11, matrix products: 17.3 us -> 14.8 us  [layer(): jnp.einsum('rjgxp,rjgpd->rjgxd', cache_w, values, preferred_element_type=...]
    dynamic_slice x0 -> x1, local copies, waits for them, and re-layouts: none -> 1.68 us  [per_device(): part_values = lax.dynamic_slice_in_dim(values, start, block, 0)]
    unnamed x18 -> x16, local copies, waits for them, and re-layouts: 3.07 us -> 3.06 us
where the time goes in v13:
time: 152 us; the launch traced here: 149 us
  matrix products  41.2 us (27%)
  waiting for transfers between devices  33.7 us (22%)
  local copies, waits for them, and re-layouts  21.3 us (14%)
  other arithmetic  20.5 us (13%)
  Pallas kernels  17.8 us (12%)
  starting transfers between devices  12.6 us (8%)
  between operations  2.12 us (1%)
    ppermute x10, waiting for transfers between devices, per_device(): incoming = lax.ppermute(result, 'section', pairs)  32.3 us
    dot_general x11, matrix products, layer(): jnp.einsum('rjgxd,rjgpd->rjgxp', wide_query, keys, preferred_element_type...  21.6 us
    pallas_call x4, Pallas kernels, gather_chunk(): pl.pallas_call(copy_kernel, grid_spec=grid_spec, out_shape=[half, half],...  17.8 us
    dot_general x11, matrix products, layer(): jnp.einsum('rjgxp,rjgpd->rjgxd', cache_w, values, preferred_element_type=...  14.8 us
    ppermute x10, starting transfers between devices, per_device(): incoming = lax.ppermute(result, 'section', pairs)  12 us
    gather x1, local copies, waits for them, and re-layouts, per_device(): received = partner(pool[chosen], 'inst', 0)  5.51 us
    unnamed x10, other arithmetic  5.27 us
    reduce_sum x11, other arithmetic, layer(): jnp.mean(wide * wide, axis=-1, keepdims=True) + 1e-05  4.06 us
  transfers between devices with their start and end apart: 13, of which 6 were waited for; matrix products, arithmetic and copies ran while one was open for 11% of the time, Pallas kernels for 9%

profile of v13, /device:TPU:26, one launch (start us, length us, event | category | flops | bytes accessed | tf_op | source)
XLA Modules:
  0.0 149.3 jit_solution(13910777269876138471)
XLA Ops:
  5.6 4.5 %shard_map.86 = (bf16[8,2,8,128,128]{4,3,2,1,0:T(8,128)(2,1)}, bf16[8,2,8,128,128]{4,3,2,1,0:T(8,128)(2,1)}) custom-call(s32[16]{0:T(128)} %reshape_squeeze.2.table_ref, bf16[16,2,8,128,128]{4,3,2,1,0:T(8,128)(2,1)} %bitcast.288), custom_call_target="tpu_custom_call" | custom-call | tf_op jit(solution)/shard_map/pallas_call | solution.py:108
  10.4 2.0 %fusion.230 = (f32[2,8,32]{2,1,0:T(8,128)S(1)}, f32[2,2,8,32,128]{4,3,2,1,0:T(8,128)S(1)}) fusion(bf16[8,2,8,128,128]{4,3,2,1,0:T(8,128)(2,1)} %get-tuple-element.30.refs_0_, bf16[2,8,32,128]{3,2,1,0:T(8,128)(2,1)S(1)} %bitcast.330, pred[2,2,128]{2,1,0:T(4,128)(4,1)S(1)} %broadcast_compare_fusion.11), kind=kOutput, calls=%fused_computation.456 | convolution fusion | flops 33947136 | bytes 1706496 | tf_op jit(solution)/shard_map/rjgxd,rjgpd->rjgxp/dot_general | solution.py:46
  16.3 4.5 %shard_map.87 = (bf16[8,2,8,128,128]{4,3,2,1,0:T(8,128)(2,1)}, bf16[8,2,8,128,128]{4,3,2,1,0:T(8,128)(2,1)}) custom-call(s32[16]{0:T(128)} %reshape_squeeze.2.table_ref, bf16[16,2,8,128,128]{4,3,2,1,0:T(8,128)(2,1)} %bitcast.289, bf16[8,2,8,128,128]{4,3,2,1,0:T(8,128)(2,1)} %get-tuple-element.30.refs_0_, ...), custom_call_target="tpu_custom_call", output_to_operand_aliasing={{0}: (2, {}), {1}: (3, {})} | custom-call | tf_op jit(solution)/shard_map/pallas_call | solution.py:108
  22.0 2.0 %fusion.232 = (f32[2,8,32]{2,1,0:T(8,128)S(1)}, f32[2,2,8,32,128]{4,3,2,1,0:T(8,128)S(1)}) fusion(bf16[8,2,8,128,128]{4,3,2,1,0:T(8,128)(2,1)} %get-tuple-element.34.refs_0_, s32[]{:T(128)S(6)} %select_n.208, bf16[2,8,32,128]{3,2,1,0:T(8,128)(2,1)S(1)} %bitcast.321, pred[2,2,128]{2,1,0:T(4,128)(4,1)S(1)} %get-tuple-element.123), kind=kOutput, calls=%fused_computation.458 | convolution fusion | flops 33947136 | bytes 1706500 | tf_op jit(solution)/shard_map/rjgxd,rjgpd->rjgxp/dot_general | solution.py:46
  27.3 4.5 %shard_map.88 = (bf16[8,2,8,128,128]{4,3,2,1,0:T(8,128)(2,1)}, bf16[8,2,8,128,128]{4,3,2,1,0:T(8,128)(2,1)}) custom-call(s32[16]{0:T(128)} %reshape_squeeze.2.table_ref, bf16[16,2,8,128,128]{4,3,2,1,0:T(8,128)(2,1)} %bitcast.290, bf16[8,2,8,128,128]{4,3,2,1,0:T(8,128)(2,1)} %get-tuple-element.34.refs_0_, ...), custom_call_target="tpu_custom_call", output_to_operand_aliasing={{0}: (2, {}), {1}: (3, {})} | custom-call | tf_op jit(solution)/shard_map/pallas_call | solution.py:108
  33.0 2.0 %fusion.234 = (f32[2,8,32]{2,1,0:T(8,128)S(1)}, f32[2,2,8,32,128]{4,3,2,1,0:T(8,128)S(1)}) fusion(bf16[8,2,8,128,128]{4,3,2,1,0:T(8,128)(2,1)} %get-tuple-element.38.refs_0_, s32[]{:T(128)S(6)} %select_n.212, bf16[2,8,32,128]{3,2,1,0:T(8,128)(2,1)S(1)} %bitcast.328, pred[2,2,128]{2,1,0:T(4,128)(4,1)S(1)} %broadcast_compare_fusion.9), kind=kOutput, calls=%fused_computation.460 | convolution fusion | flops 33947136 | bytes 1706500 | tf_op jit(solution)/shard_map/rjgxd,rjgpd->rjgxp/dot_general | solution.py:46
  38.9 4.5 %shard_map.89 = (bf16[8,2,8,128,128]{4,3,2,1,0:T(8,128)(2,1)}, bf16[8,2,8,128,128]{4,3,2,1,0:T(8,128)(2,1)}) custom-call(s32[16]{0:T(128)} %reshape_squeeze.2.table_ref, bf16[16,2,8,128,128]{4,3,2,1,0:T(8,128)(2,1)} %bitcast.291, bf16[8,2,8,128,128]{4,3,2,1,0:T(8,128)(2,1)} %get-tuple-element.38.refs_0_, ...), custom_call_target="tpu_custom_call", output_to_operand_aliasing={{0}: (2, {}), {1}: (3, {})} | custom-call | tf_op jit(solution)/shard_map/pallas_call | solution.py:108
  44.6 2.0 %fusion.236 = (f32[2,8,32]{2,1,0:T(8,128)S(1)}, f32[2,2,8,32,128]{4,3,2,1,0:T(8,128)S(1)}) fusion(bf16[8,2,8,128,128]{4,3,2,1,0:T(8,128)(2,1)} %get-tuple-element.42, s32[]{:T(128)S(6)} %select_n.217, bf16[2,8,32,128]{3,2,1,0:T(8,128)(2,1)S(1)} %bitcast.329, pred[2,2,128]{2,1,0:T(4,128)(4,1)S(1)} %broadcast_compare_fusion.8), kind=kOutput, calls=%fused_computation.462 | convolution fusion | flops 33947136 | bytes 1706500 | tf_op jit(solution)/shard_map/rjgxd,rjgpd->rjgxp/dot_general | solution.py:46
  51.1 2.0 %fusion.238 = (f32[2,8,32]{2,1,0:T(8,128)S(1)}, f32[2,2,8,32,128]{4,3,2,1,0:T(8,128)S(1)}) fusion(bf16[8,2,8,128,128]{4,3,2,1,0:T(8,128)(2,1)} %get-tuple-element.42, s32[]{:T(128)S(6)} %select_n.221, bf16[2,8,32,128]{3,2,1,0:T(8,128)(2,1)S(1)} %bitcast.322, pred[2,2,128]{2,1,0:T(4,128)(4,1)S(1)} %broadcast_compare_fusion.7), kind=kOutput, calls=%fused_computation.464 | convolution fusion | flops 33947136 | bytes 1706500 | tf_op jit(solution)/shard_map/rjgxd,rjgpd->rjgxp/dot_general | solution.py:46
  57.7 5.5 %gather_fusion.2 = bf16[4,2,8,128,128]{4,3,2,1,0:T(8,128)(2,1)} fusion(bf16[16,2,8,128,128]{4,3,2,1,0:T(8,128)(2,1)} %bitcast.292, s32[1024]{0:T(1024)S(1)} %pad_clamp_fusion), kind=kCustom, calls=%fused_computation.2 | custom fusion | bytes 4194320 | tf_op jit(solution)/shard_map/gather | solution.py:142
  64.8 2.0 %fusion.240 = (f32[2,8,32]{2,1,0:T(8,128)S(1)}, f32[2,2,8,32,128]{4,3,2,1,0:T(8,128)S(1)}) fusion(bf16[8,2,8,128,128]{4,3,2,1,0:T(8,128)(2,1)} %get-tuple-element.42, s32[]{:T(128)S(6)} %select_n.224, bf16[2,8,32,128]{3,2,1,0:T(8,128)(2,1)S(1)} %bitcast.323, pred[2,2,128]{2,1,0:T(4,128)(4,1)S(1)} %broadcast_compare_fusion.6), kind=kOutput, calls=%fused_computation.466 | convolution fusion | flops 33947136 | bytes 1706500 | tf_op jit(solution)/shard_map/rjgxd,rjgpd->rjgxp/dot_general | solution.py:46
  72.9 10.8 %collective-permute-done.5 = bf16[4,2,8192]{2,1,0:T(2,128)(2,1)S(1)} collective-permute-done((bf16[4,2,8192]{2,1,0:T(2,128)(2,1)S(1)}, bf16[4,2,8192]{2,1,0:T(2,128)(2,1)S(1)}, u32[]{:S(2)}, u32[]{:S(2)}) %collective-permute-start.5) | collective-permute-done | bytes 131104 | tf_op jit(solution)/shard_map/ppermute | solution.py:169
  84.9 2.0 %fusion.242 = (f32[2,8,32]{2,1,0:T(8,128)S(1)}, f32[2,2,8,32,128]{4,3,2,1,0:T(8,128)S(1)}) fusion(bf16[8,2,8,128,128]{4,3,2,1,0:T(8,128)(2,1)} %get-tuple-element.42, s32[]{:T(128)S(6)} %select_n.229, bf16[2,8,32,128]{3,2,1,0:T(8,128)(2,1)S(1)} %bitcast.324, pred[2,2,128]{2,1,0:T(4,128)(4,1)S(1)} %broadcast_compare_fusion.4), kind=kOutput, calls=%fused_computation.468 | convolution fusion | flops 33947136 | bytes 1706500 | tf_op jit(solution)/shard_map/rjgxd,rjgpd->rjgxp/dot_general | solution.py:46
  90.0 1.9 %collective-permute-start.8 = (bf16[4,2,8192]{2,1,0:T(2,128)(2,1)S(1)}, bf16[4,2,8192]{2,1,0:T(2,128)(2,1)S(1)}, u32[]{:S(2)}, u32[]{:S(2)}) collective-permute-start(bf16[4,2,8192]{2,1,0:T(2,128)(2,1)S(1)} %get-tuple-element.75), channel_id=1, source_target_pairs={{3,4},{4,5},{5,6},{6,7},{11,12},{12,13},{13,14},{14,15},{19,20},{2... | collective-permute-start | bytes 393224 | tf_op jit(solution)/shard_map/ppermute | solution.py:169
  92.0 7.4 %collective-permute-done.8 = bf16[4,2,8192]{2,1,0:T(2,128)(2,1)S(1)} collective-permute-done((bf16[4,2,8192]{2,1,0:T(2,128)(2,1)S(1)}, bf16[4,2,8192]{2,1,0:T(2,128)(2,1)S(1)}, u32[]{:S(2)}, u32[]{:S(2)}) %collective-permute-start.8) | collective-permute-done | bytes 131104 | tf_op jit(solution)/shard_map/ppermute | solution.py:169
  100.5 2.0 %fusion.244 = (f32[2,8,32]{2,1,0:T(8,128)S(1)}, f32[2,2,8,32,128]{4,3,2,1,0:T(8,128)S(1)}) fusion(bf16[8,2,8,128,128]{4,3,2,1,0:T(8,128)(2,1)} %get-tuple-element.42, s32[]{:T(128)S(6)} %select_n.232, bf16[2,8,32,128]{3,2,1,0:T(8,128)(2,1)S(1)} %bitcast.325, pred[2,2,128]{2,1,0:T(4,128)(4,1)S(1)} %broadcast_compare_fusion.3), kind=kOutput, calls=%fused_computation.470 | convolution fusion | flops 33947136 | bytes 1706500 | tf_op jit(solution)/shard_map/rjgxd,rjgpd->rjgxp/dot_general | solution.py:46
  105.7 1.9 %collective-permute-start.9 = (bf16[4,2,8192]{2,1,0:T(2,128)(2,1)S(1)}, bf16[4,2,8192]{2,1,0:T(2,128)(2,1)S(1)}, u32[]{:S(2)}, u32[]{:S(2)}) collective-permute-start(bf16[4,2,8192]{2,1,0:T(2,128)(2,1)S(1)} %get-tuple-element.73), channel_id=1, source_target_pairs={{4,5},{5,6},{6,7},{12,13},{13,14},{14,15},{20,21},{21,22},{22,23},... | collective-permute-start | bytes 393224 | tf_op jit(solution)/shard_map/ppermute | solution.py:169
  107.6 5.8 %collective-permute-done.9 = bf16[4,2,8192]{2,1,0:T(2,128)(2,1)S(1)} collective-permute-done((bf16[4,2,8192]{2,1,0:T(2,128)(2,1)S(1)}, bf16[4,2,8192]{2,1,0:T(2,128)(2,1)S(1)}, u32[]{:S(2)}, u32[]{:S(2)}) %collective-permute-start.9) | collective-permute-done | bytes 131104 | tf_op jit(solution)/shard_map/ppermute | solution.py:169
  114.5 2.0 %fusion.246 = (f32[2,8,32]{2,1,0:T(8,128)S(1)}, f32[2,2,8,32,128]{4,3,2,1,0:T(8,128)S(1)}) fusion(bf16[8,2,8,128,128]{4,3,2,1,0:T(8,128)(2,1)} %get-tuple-element.42, s32[]{:T(128)S(6)} %select_n.235, bf16[2,8,32,128]{3,2,1,0:T(8,128)(2,1)S(1)} %bitcast.326, pred[2,2,128]{2,1,0:T(4,128)(4,1)S(1)} %broadcast_compare_fusion.2), kind=kOutput, calls=%fused_computation.472 | convolution fusion | flops 33947136 | bytes 1706500 | tf_op jit(solution)/shard_map/rjgxd,rjgpd->rjgxp/dot_general | solution.py:46
  119.7 2.1 %collective-permute-start.10 = (bf16[4,2,8192]{2,1,0:T(2,128)(2,1)S(1)}, bf16[4,2,8192]{2,1,0:T(2,128)(2,1)S(1)}, u32[]{:S(2)}, u32[]{:S(2)}) collective-permute-start(bf16[4,2,8192]{2,1,0:T(2,128)(2,1)S(1)} %get-tuple-element.71), channel_id=1, source_target_pairs={{5,6},{6,7},{13,14},{14,15},{21,22},{22,23},{29,30},{30,31}} | collective-permute-start | bytes 393224 | tf_op jit(solution)/shard_map/ppermute | solution.py:169
  121.9 5.8 %collective-permute-done.10 = bf16[4,2,8192]{2,1,0:T(2,128)(2,1)S(1)} collective-permute-done((bf16[4,2,8192]{2,1,0:T(2,128)(2,1)S(1)}, bf16[4,2,8192]{2,1,0:T(2,128)(2,1)S(1)}, u32[]{:S(2)}, u32[]{:S(2)}) %collective-permute-start.10) | collective-permute-done | bytes 131104 | tf_op jit(solution)/shard_map/ppermute | solution.py:169
  130.5 2.0 %fusion.248 = (f32[2,8,32]{2,1,0:T(8,128)S(1)}, f32[2,2,8,32,128]{4,3,2,1,0:T(8,128)S(1)}) fusion(bf16[8,2,8,128,128]{4,3,2,1,0:T(8,128)(2,1)} %get-tuple-element.42, s32[]{:T(128)S(6)} %select_n.238, bf16[2,8,32,128]{3,2,1,0:T(8,128)(2,1)S(1)} %bitcast.327, pred[2,2,128]{2,1,0:T(4,128)(4,1)S(1)} %broadcast_compare_fusion.1), kind=kOutput, calls=%fused_computation.474 | convolution fusion | flops 33947136 | bytes 1706500 | tf_op jit(solution)/shard_map/rjgxd,rjgpd->rjgxp/dot_general | solution.py:46
  135.7 2.5 %collective-permute-done.11 = bf16[4,2,8192]{2,1,0:T(2,128)(2,1)S(1)} collective-permute-done((bf16[4,2,8192]{2,1,0:T(2,128)(2,1)S(1)}, bf16[4,2,8192]{2,1,0:T(2,128)(2,1)S(1)}, u32[]{:S(2)}, u32[]{:S(2)}) %collective-permute-start.11) | collective-permute-done | bytes 131104 | tf_op jit(solution)/shard_map/ppermute | solution.py:169
  139.2 2.0 %fusion.250 = (f32[2,8,32]{2,1,0:T(8,128)S(1)}, f32[2,2,8,32,128]{4,3,2,1,0:T(8,128)S(1)}) fusion(bf16[8,2,8,128,128]{4,3,2,1,0:T(8,128)(2,1)} %get-tuple-element.42, bf16[2,8,32,128]{3,2,1,0:T(8,128)(2,1)S(1)} %bitcast.331, pred[2,2,128]{2,1,0:T(4,128)(4,1)S(1)} %get-tuple-element.122), kind=kOutput, calls=%fused_computation.476 | convolution fusion | flops 33947136 | bytes 1706496 | tf_op jit(solution)/shard_map/rjgxd,rjgpd->rjgxp/dot_general | solution.py:46
  (262 shorter events, 63.9 us)
Async XLA Ops:
  10.1 4.6 %copy-start.2 = (f32[1,8192]{1,0:T(1,128)S(1)}, f32[1,8192]{1,0:T(1,128)}, u32[]{:S(2)}) copy-start(f32[1,8192]{1,0:T(1,128)} %param.13) | copy-start | bytes 98308
  10.1 4.6 %copy-start.3 = (bf16[1,4,8,8192]{3,2,1,0:T(8,128)(2,1)S(1)}, bf16[1,4,8,8192]{3,2,1,0:T(8,128)(2,1)}, u32[]{:S(2)}) copy-start(bf16[1,4,8,8192]{3,2,1,0:T(8,128)(2,1)} %param.7) | copy-start | bytes 1572868
  10.4 5.2 %copy-start.6 = (s32[1,2]{1,0:T(1,128)S(1)}, s32[1,2]{1,0:T(1,128)}, u32[]{:S(2)}) copy-start(s32[1,2]{1,0:T(1,128)} %param.11) | copy-start | bytes 28
  10.4 5.3 %copy-start = (s32[1,8]{1,0:T(1,128)S(1)}, s32[1,8]{1,0:T(1,128)}, u32[]{:S(2)}) copy-start(s32[1,8]{1,0:T(1,128)} %param.10) | copy-start | bytes 100
  14.9 5.8 %collective-permute-start = (bf16[4,2,8192]{2,1,0:T(2,128)(2,1)S(1)}, bf16[4,2,8192]{2,1,0:T(2,128)(2,1)S(1)}, u32[]{:S(2)}, u32[]{:S(2)}) collective-permute-start(bf16[4,2,8192]{2,1,0:T(2,128)(2,1)S(1)} %get-tuple-element.93), channel_id=1, source_target_pairs={{0,1},{8,9},{16,17},{24,25}} | collective-permute-start | bytes 393224 | tf_op jit(solution)/shard_map/ppermute | solution.py:169
  16.3 4.9 %copy-start.1 = (f32[1,8192]{1,0:T(1,128)S(1)}, f32[1,8192]{1,0:T(1,128)}, u32[]{:S(2)}) copy-start(f32[1,8192]{1,0:T(1,128)} %param.12) | copy-start | bytes 98308
  16.3 5.7 %collective-permute-start.6 = (s32[2]{0:T(128)S(1)}, s32[2]{0:T(128)S(1)}, u32[]{:S(2)}, u32[]{:S(2)}) collective-permute-start(s32[2]{0:T(128)S(1)} %gather_fusion.1), channel_id=1, source_target_pairs={{0,8},{8,0},{1,9},{9,1},{2,10},{10,2},{3,11},{11,3},{4,12},{12,4},... | collective-permute-start | bytes 32 | tf_op jit(solution)/shard_map/ppermute | solution.py:20
  26.6 5.1 %collective-permute-start.1 = (bf16[4,2,8192]{2,1,0:T(2,128)(2,1)S(1)}, bf16[4,2,8192]{2,1,0:T(2,128)(2,1)S(1)}, u32[]{:S(2)}, u32[]{:S(2)}) collective-permute-start(bf16[4,2,8192]{2,1,0:T(2,128)(2,1)S(1)} %get-tuple-element.89), channel_id=1, source_target_pairs={{0,1},{1,2},{8,9},{9,10},{16,17},{17,18},{24,25},{25,26}} | collective-permute-start | bytes 393224 | tf_op jit(solution)/shard_map/ppermute | solution.py:169
  32.8 5.4 %copy-start.5 = (s32[1,8,2]{1,2,0:T(2,128)S(1)}, s32[1,8,2]{1,2,0:T(2,128)}, u32[]{:S(2)}) copy-start(s32[1,8,2]{1,2,0:T(2,128)} %param.9) | copy-start | bytes 196
  37.5 5.8 %collective-permute-start.2 = (bf16[4,2,8192]{2,1,0:T(2,128)(2,1)S(1)}, bf16[4,2,8192]{2,1,0:T(2,128)(2,1)S(1)}, u32[]{:S(2)}, u32[]{:S(2)}) collective-permute-start(bf16[4,2,8192]{2,1,0:T(2,128)(2,1)S(1)} %get-tuple-element.85), channel_id=1, source_target_pairs={{0,1},{1,2},{2,3},{8,9},{9,10},{10,11},{16,17},{17,18},{18,19},{24... | collective-permute-start | bytes 393224 | tf_op jit(solution)/shard_map/ppermute | solution.py:169
  49.1 0.9 collective-permute-start.3
  55.7 1.2 copy-start.4
  56.9 6.8 %collective-permute-start.4 = (bf16[4,2,8192]{2,1,0:T(2,128)(2,1)S(1)}, bf16[4,2,8192]{2,1,0:T(2,128)(2,1)S(1)}, u32[]{:S(2)}, u32[]{:S(2)}) collective-permute-start(bf16[4,2,8192]{2,1,0:T(2,128)(2,1)S(1)} %get-tuple-element.79), channel_id=1, source_target_pairs={{1,2},{2,3},{3,4},{4,5},{9,10},{10,11},{11,12},{12,13},{17,18},{18... | collective-permute-start | bytes 393224 | tf_op jit(solution)/shard_map/ppermute | solution.py:169
  63.2 8.1 %collective-permute-start.7 = (bf16[2,2,2,8,128,128]{5,4,3,2,1,0:T(8,128)(2,1)}, bf16[2,2,2,8,128,128]{5,4,3,2,1,0:T(8,128)(2,1)S(1)}, u32[]{:S(2)}, u32[]{:S(2)}) collective-permute-start(bf16[2,2,2,8,128,128]{5,4,3,2,1,0:T(8,128)(2,1)} %bitcast.317), channel_id=1, source_target_pairs={{0,8},{8,0},{1,9},{9,1},{2,10},{10,2},{3,11},{11,3},{4,12},{12,4},... | collective-permute-start | bytes 6291464 | tf_op jit(solution)/shard_map/ppermute | solution.py:20
  70.0 13.7 %collective-permute-start.5 = (bf16[4,2,8192]{2,1,0:T(2,128)(2,1)S(1)}, bf16[4,2,8192]{2,1,0:T(2,128)(2,1)S(1)}, u32[]{:S(2)}, u32[]{:S(2)}) collective-permute-start(bf16[4,2,8192]{2,1,0:T(2,128)(2,1)S(1)} %get-tuple-element.77), channel_id=1, source_target_pairs={{2,3},{3,4},{4,5},{5,6},{10,11},{11,12},{12,13},{13,14},{18,19},{1... | collective-permute-start | bytes 393224 | tf_op jit(solution)/shard_map/ppermute | solution.py:169
  90.0 9.3 %collective-permute-start.8 = (bf16[4,2,8192]{2,1,0:T(2,128)(2,1)S(1)}, bf16[4,2,8192]{2,1,0:T(2,128)(2,1)S(1)}, u32[]{:S(2)}, u32[]{:S(2)}) collective-permute-start(bf16[4,2,8192]{2,1,0:T(2,128)(2,1)S(1)} %get-tuple-element.75), channel_id=1, source_target_pairs={{3,4},{4,5},{5,6},{6,7},{11,12},{12,13},{13,14},{14,15},{19,20},{2... | collective-permute-start | bytes 393224 | tf_op jit(solution)/shard_map/ppermute | solution.py:169
  105.7 7.7 %collective-permute-start.9 = (bf16[4,2,8192]{2,1,0:T(2,128)(2,1)S(1)}, bf16[4,2,8192]{2,1,0:T(2,128)(2,1)S(1)}, u32[]{:S(2)}, u32[]{:S(2)}) collective-permute-start(bf16[4,2,8192]{2,1,0:T(2,128)(2,1)S(1)} %get-tuple-element.73), channel_id=1, source_target_pairs={{4,5},{5,6},{6,7},{12,13},{13,14},{14,15},{20,21},{21,22},{22,23},... | collective-permute-start | bytes 393224 | tf_op jit(solution)/shard_map/ppermute | solution.py:169
  119.7 8.0 %collective-permute-start.10 = (bf16[4,2,8192]{2,1,0:T(2,128)(2,1)S(1)}, bf16[4,2,8192]{2,1,0:T(2,128)(2,1)S(1)}, u32[]{:S(2)}, u32[]{:S(2)}) collective-permute-start(bf16[4,2,8192]{2,1,0:T(2,128)(2,1)S(1)} %get-tuple-element.71), channel_id=1, source_target_pairs={{5,6},{6,7},{13,14},{14,15},{21,22},{22,23},{29,30},{30,31}} | collective-permute-start | bytes 393224 | tf_op jit(solution)/shard_map/ppermute | solution.py:169
  134.5 3.8 %collective-permute-start.11 = (bf16[4,2,8192]{2,1,0:T(2,128)(2,1)S(1)}, bf16[4,2,8192]{2,1,0:T(2,128)(2,1)S(1)}, u32[]{:S(2)}, u32[]{:S(2)}) collective-permute-start(bf16[4,2,8192]{2,1,0:T(2,128)(2,1)S(1)} %get-tuple-element.69), channel_id=1, source_target_pairs={{6,7},{14,15},{22,23},{30,31}} | collective-permute-start | bytes 393224 | tf_op jit(solution)/shard_map/ppermute | solution.py:169
  146.1 1.4 collective-permute-start.12

commit v14 on v12

--- a/solution.py
+++ b/solution.py
@@ -137,14 +137,14 @@
             keys, values = gather_chunk(pool, table, k, block, previous)
         item = k - section
         start = jnp.clip(item, 0, chunks - 1) * block
-        if k == 3:
+        if k == 1:
             start, incoming, chosen = lax.optimization_barrier((start, incoming, chosen))
             received = partner(pool[chosen], "inst", 0)
             keep = spots[None, :, :] < arrived_lens[:, None, None]
             arrived = jnp.where(
                 keep[:, :, None, None, :, None], received, jnp.zeros((), jnp.bfloat16)
             )
-        elif k == 6:
+        elif k == 4:
             start, incoming, arrived = lax.optimization_barrier((start, incoming, arrived))
         elif k > 0:
             start, incoming = lax.optimization_barrier((start, incoming))

time: 148 us -> 154 us (1.041)
  waiting for transfers between devices: 33.5 us -> 38.4 us
  other arithmetic: 17.5 us -> 19.4 us
    ppermute x10, waiting for transfers between devices: 32.1 us -> 37 us  [per_device(): incoming = lax.ppermute(result, 'section', pairs)]
    unnamed x10, other arithmetic: 2.7 us -> 4.6 us
where the time goes in v14:
time: 154 us; the launch traced here: 151 us
  matrix products  43.7 us (28%)
  waiting for transfers between devices  38.4 us (25%)
  other arithmetic  19.4 us (13%)
  Pallas kernels  17.8 us (12%)
  local copies, waits for them, and re-layouts  16.9 us (11%)
  starting transfers between devices  12.7 us (8%)
  between operations  2.12 us (1%)
    ppermute x10, waiting for transfers between devices, per_device(): incoming = lax.ppermute(result, 'section', pairs)  37 us
    dot_general x11, matrix products, layer(): jnp.einsum('rjgxd,rjgpd->rjgxp', wide_query, keys, preferred_element_type...  21.6 us
    pallas_call x4, Pallas kernels, gather_chunk(): pl.pallas_call(copy_kernel, grid_spec=grid_spec, out_shape=[half, half],...  17.8 us
    dot_general x11, matrix products, layer(): jnp.einsum('rjgxp,rjgpd->rjgxd', cache_w, values, preferred_element_type=...  17.3 us
    ppermute x10, starting transfers between devices, per_device(): incoming = lax.ppermute(result, 'section', pairs)  12 us
    gather x1, local copies, waits for them, and re-layouts, per_device(): received = partner(pool[chosen], 'inst', 0)  5.51 us
    unnamed x10, other arithmetic  4.6 us
    reduce_sum x11, other arithmetic, layer(): jnp.mean(wide * wide, axis=-1, keepdims=True) + 1e-05  4.06 us
  transfers between devices with their start and end apart: 13, of which 6 were waited for; matrix products, arithmetic and copies ran while one was open for 11% of the time, Pallas kernels for 9%

profile of v14, /device:TPU:26, one launch (start us, length us, event | category | flops | bytes accessed | tf_op | source)
XLA Modules:
  0.0 150.9 jit_solution(3608594794791840766)
XLA Ops:
  5.0 4.5 %shard_map.86 = (bf16[8,2,8,128,128]{4,3,2,1,0:T(8,128)(2,1)}, bf16[8,2,8,128,128]{4,3,2,1,0:T(8,128)(2,1)}) custom-call(s32[16]{0:T(128)} %reshape_squeeze.2.table_ref, bf16[16,2,8,128,128]{4,3,2,1,0:T(8,128)(2,1)} %bitcast.288), custom_call_target="tpu_custom_call" | custom-call | tf_op jit(solution)/shard_map/pallas_call | solution.py:108
  9.8 2.0 %fusion.233 = (f32[2,8,32]{2,1,0:T(8,128)S(1)}, f32[2,2,8,32,128]{4,3,2,1,0:T(8,128)S(1)}) fusion(bf16[8,2,8,128,128]{4,3,2,1,0:T(8,128)(2,1)} %get-tuple-element.32.refs_0_, s32[]{:T(128)S(6)} %select_n.214, bf16[2,8,32,128]{3,2,1,0:T(8,128)(2,1)S(1)} %bitcast.321, pred[2,2,128]{2,1,0:T(4,128)(4,1)S(1)} %broadcast_compare_fusion.11), kind=kOutput, calls=%fused_computation.461 | convolution fusion | flops 33947136 | bytes 1706500 | tf_op jit(solution)/shard_map/rjgxd,rjgpd->rjgxp/dot_general | solution.py:46
  16.4 4.5 %shard_map.87 = (bf16[8,2,8,128,128]{4,3,2,1,0:T(8,128)(2,1)}, bf16[8,2,8,128,128]{4,3,2,1,0:T(8,128)(2,1)}) custom-call(s32[16]{0:T(128)} %reshape_squeeze.2.table_ref, bf16[16,2,8,128,128]{4,3,2,1,0:T(8,128)(2,1)} %bitcast.289, bf16[8,2,8,128,128]{4,3,2,1,0:T(8,128)(2,1)} %get-tuple-element.32.refs_0_, ...), custom_call_target="tpu_custom_call", output_to_operand_aliasing={{0}: (2, {}), {1}: (3, {})} | custom-call | tf_op jit(solution)/shard_map/pallas_call | solution.py:108
  22.8 2.0 %fusion.235 = (f32[2,8,32]{2,1,0:T(8,128)S(1)}, f32[2,2,8,32,128]{4,3,2,1,0:T(8,128)S(1)}) fusion(bf16[8,2,8,128,128]{4,3,2,1,0:T(8,128)(2,1)} %get-tuple-element.36.refs_0_, s32[]{:T(128)S(6)} %select_n.220, bf16[2,8,32,128]{3,2,1,0:T(8,128)(2,1)S(1)} %bitcast.323, pred[2,2,128]{2,1,0:T(4,128)(4,1)S(1)} %get-tuple-element.125), kind=kOutput, calls=%fused_computation.463 | convolution fusion | flops 33947136 | bytes 1706500 | tf_op jit(solution)/shard_map/rjgxd,rjgpd->rjgxp/dot_general | solution.py:46
  28.6 4.5 %shard_map.88 = (bf16[8,2,8,128,128]{4,3,2,1,0:T(8,128)(2,1)}, bf16[8,2,8,128,128]{4,3,2,1,0:T(8,128)(2,1)}) custom-call(s32[16]{0:T(128)} %reshape_squeeze.2.table_ref, bf16[16,2,8,128,128]{4,3,2,1,0:T(8,128)(2,1)} %bitcast.290, bf16[8,2,8,128,128]{4,3,2,1,0:T(8,128)(2,1)} %get-tuple-element.36.refs_0_, ...), custom_call_target="tpu_custom_call", output_to_operand_aliasing={{0}: (2, {}), {1}: (3, {})} | custom-call | tf_op jit(solution)/shard_map/pallas_call | solution.py:108
  34.3 2.0 %fusion.237 = (f32[2,8,32]{2,1,0:T(8,128)S(1)}, f32[2,2,8,32,128]{4,3,2,1,0:T(8,128)S(1)}) fusion(bf16[8,2,8,128,128]{4,3,2,1,0:T(8,128)(2,1)} %get-tuple-element.40.refs_0_, s32[]{:T(128)S(6)} %select_n.224, bf16[2,8,32,128]{3,2,1,0:T(8,128)(2,1)S(1)} %bitcast.330, pred[2,2,128]{2,1,0:T(4,128)(4,1)S(1)} %broadcast_compare_fusion.9), kind=kOutput, calls=%fused_computation.465 | convolution fusion | flops 33947136 | bytes 1706500 | tf_op jit(solution)/shard_map/rjgxd,rjgpd->rjgxp/dot_general | solution.py:46
  40.3 5.5 %gather_fusion.2 = bf16[4,2,8,128,128]{4,3,2,1,0:T(8,128)(2,1)} fusion(bf16[16,2,8,128,128]{4,3,2,1,0:T(8,128)(2,1)} %bitcast.291, s32[1024]{0:T(1024)S(1)} %pad_clamp_fusion), kind=kCustom, calls=%fused_computation.2 | custom fusion | bytes 4194320 | tf_op jit(solution)/shard_map/gather | solution.py:142
  46.3 4.5 %shard_map.89 = (bf16[8,2,8,128,128]{4,3,2,1,0:T(8,128)(2,1)}, bf16[8,2,8,128,128]{4,3,2,1,0:T(8,128)(2,1)}) custom-call(s32[16]{0:T(128)} %reshape_squeeze.2.table_ref, bf16[16,2,8,128,128]{4,3,2,1,0:T(8,128)(2,1)} %bitcast.292, bf16[8,2,8,128,128]{4,3,2,1,0:T(8,128)(2,1)} %get-tuple-element.40.refs_0_, ...), custom_call_target="tpu_custom_call", output_to_operand_aliasing={{0}: (2, {}), {1}: (3, {})} | custom-call | tf_op jit(solution)/shard_map/pallas_call | solution.py:108
  52.0 2.0 %fusion.239 = (f32[2,8,32]{2,1,0:T(8,128)S(1)}, f32[2,2,8,32,128]{4,3,2,1,0:T(8,128)S(1)}) fusion(bf16[8,2,8,128,128]{4,3,2,1,0:T(8,128)(2,1)} %get-tuple-element.44, s32[]{:T(128)S(6)} %select_n.228, bf16[2,8,32,128]{3,2,1,0:T(8,128)(2,1)S(1)} %bitcast.331, pred[2,2,128]{2,1,0:T(4,128)(4,1)S(1)} %broadcast_compare_fusion.8), kind=kOutput, calls=%fused_computation.467 | convolution fusion | flops 33947136 | bytes 1706500 | tf_op jit(solution)/shard_map/rjgxd,rjgpd->rjgxp/dot_general | solution.py:46
  60.8 2.0 %fusion.241 = (f32[2,8,32]{2,1,0:T(8,128)S(1)}, f32[2,2,8,32,128]{4,3,2,1,0:T(8,128)S(1)}) fusion(bf16[8,2,8,128,128]{4,3,2,1,0:T(8,128)(2,1)} %get-tuple-element.44, s32[]{:T(128)S(6)} %select_n.234, bf16[2,8,32,128]{3,2,1,0:T(8,128)(2,1)S(1)} %bitcast.324, pred[2,2,128]{2,1,0:T(4,128)(4,1)S(1)} %broadcast_compare_fusion.6), kind=kOutput, calls=%fused_computation.469 | convolution fusion | flops 33947136 | bytes 1706500 | tf_op jit(solution)/shard_map/rjgxd,rjgpd->rjgxp/dot_general | solution.py:46
  67.2 2.0 %fusion.243 = (f32[2,8,32]{2,1,0:T(8,128)S(1)}, f32[2,2,8,32,128]{4,3,2,1,0:T(8,128)S(1)}) fusion(bf16[8,2,8,128,128]{4,3,2,1,0:T(8,128)(2,1)} %get-tuple-element.44, s32[]{:T(128)S(6)} %select_n.237, bf16[2,8,32,128]{3,2,1,0:T(8,128)(2,1)S(1)} %bitcast.325, pred[2,2,128]{2,1,0:T(4,128)(4,1)S(1)} %broadcast_compare_fusion.5), kind=kOutput, calls=%fused_computation.471 | convolution fusion | flops 33947136 | bytes 1706500 | tf_op jit(solution)/shard_map/rjgxd,rjgpd->rjgxp/dot_general | solution.py:46
  73.0 15.4 %collective-permute-done.7 = bf16[4,2,8192]{2,1,0:T(2,128)(2,1)S(1)} collective-permute-done((bf16[4,2,8192]{2,1,0:T(2,128)(2,1)S(1)}, bf16[4,2,8192]{2,1,0:T(2,128)(2,1)S(1)}, u32[]{:S(2)}, u32[]{:S(2)}) %collective-permute-start.7) | collective-permute-done | bytes 131104 | tf_op jit(solution)/shard_map/ppermute | solution.py:165
  89.5 2.0 %fusion.245 = (f32[2,8,32]{2,1,0:T(8,128)S(1)}, f32[2,2,8,32,128]{4,3,2,1,0:T(8,128)S(1)}) fusion(bf16[8,2,8,128,128]{4,3,2,1,0:T(8,128)(2,1)} %get-tuple-element.44, s32[]{:T(128)S(6)} %select_n.240, bf16[2,8,32,128]{3,2,1,0:T(8,128)(2,1)S(1)} %bitcast.326, pred[2,2,128]{2,1,0:T(4,128)(4,1)S(1)} %broadcast_compare_fusion.4), kind=kOutput, calls=%fused_computation.473 | convolution fusion | flops 33947136 | bytes 1706500 | tf_op jit(solution)/shard_map/rjgxd,rjgpd->rjgxp/dot_general | solution.py:46
  94.1 1.9 %collective-permute-start.8 = (bf16[4,2,8192]{2,1,0:T(2,128)(2,1)S(1)}, bf16[4,2,8192]{2,1,0:T(2,128)(2,1)S(1)}, u32[]{:S(2)}, u32[]{:S(2)}) collective-permute-start(bf16[4,2,8192]{2,1,0:T(2,128)(2,1)S(1)} %get-tuple-element.79), channel_id=1, source_target_pairs={{3,4},{4,5},{5,6},{6,7},{11,12},{12,13},{13,14},{14,15},{19,20},{2... | collective-permute-start | bytes 393224 | tf_op jit(solution)/shard_map/ppermute | solution.py:165
  96.0 7.7 %collective-permute-done.8 = bf16[4,2,8192]{2,1,0:T(2,128)(2,1)S(1)} collective-permute-done((bf16[4,2,8192]{2,1,0:T(2,128)(2,1)S(1)}, bf16[4,2,8192]{2,1,0:T(2,128)(2,1)S(1)}, u32[]{:S(2)}, u32[]{:S(2)}) %collective-permute-start.8) | collective-permute-done | bytes 131104 | tf_op jit(solution)/shard_map/ppermute | solution.py:165
  104.9 2.0 %fusion.247 = (f32[2,8,32]{2,1,0:T(8,128)S(1)}, f32[2,2,8,32,128]{4,3,2,1,0:T(8,128)S(1)}) fusion(bf16[8,2,8,128,128]{4,3,2,1,0:T(8,128)(2,1)} %get-tuple-element.44, s32[]{:T(128)S(6)} %select_n.243, bf16[2,8,32,128]{3,2,1,0:T(8,128)(2,1)S(1)} %bitcast.327, pred[2,2,128]{2,1,0:T(4,128)(4,1)S(1)} %broadcast_compare_fusion.3), kind=kOutput, calls=%fused_computation.475 | convolution fusion | flops 33947136 | bytes 1706500 | tf_op jit(solution)/shard_map/rjgxd,rjgpd->rjgxp/dot_general | solution.py:46
  109.4 1.9 %collective-permute-start.9 = (bf16[4,2,8192]{2,1,0:T(2,128)(2,1)S(1)}, bf16[4,2,8192]{2,1,0:T(2,128)(2,1)S(1)}, u32[]{:S(2)}, u32[]{:S(2)}) collective-permute-start(bf16[4,2,8192]{2,1,0:T(2,128)(2,1)S(1)} %get-tuple-element.77), channel_id=1, source_target_pairs={{4,5},{5,6},{6,7},{12,13},{13,14},{14,15},{20,21},{21,22},{22,23},... | collective-permute-start | bytes 393224 | tf_op jit(solution)/shard_map/ppermute | solution.py:165
  111.4 5.8 %collective-permute-done.9 = bf16[4,2,8192]{2,1,0:T(2,128)(2,1)S(1)} collective-permute-done((bf16[4,2,8192]{2,1,0:T(2,128)(2,1)S(1)}, bf16[4,2,8192]{2,1,0:T(2,128)(2,1)S(1)}, u32[]{:S(2)}, u32[]{:S(2)}) %collective-permute-start.9) | collective-permute-done | bytes 131104 | tf_op jit(solution)/shard_map/ppermute | solution.py:165
  118.4 2.0 %fusion.249 = (f32[2,8,32]{2,1,0:T(8,128)S(1)}, f32[2,2,8,32,128]{4,3,2,1,0:T(8,128)S(1)}) fusion(bf16[8,2,8,128,128]{4,3,2,1,0:T(8,128)(2,1)} %get-tuple-element.44, s32[]{:T(128)S(6)} %select_n.246, bf16[2,8,32,128]{3,2,1,0:T(8,128)(2,1)S(1)} %bitcast.328, pred[2,2,128]{2,1,0:T(4,128)(4,1)S(1)} %broadcast_compare_fusion.2), kind=kOutput, calls=%fused_computation.477 | convolution fusion | flops 33947136 | bytes 1706500 | tf_op jit(solution)/shard_map/rjgxd,rjgpd->rjgxp/dot_general | solution.py:46
  122.9 2.1 %collective-permute-start.10 = (bf16[4,2,8192]{2,1,0:T(2,128)(2,1)S(1)}, bf16[4,2,8192]{2,1,0:T(2,128)(2,1)S(1)}, u32[]{:S(2)}, u32[]{:S(2)}) collective-permute-start(bf16[4,2,8192]{2,1,0:T(2,128)(2,1)S(1)} %get-tuple-element.75), channel_id=1, source_target_pairs={{5,6},{6,7},{13,14},{14,15},{21,22},{22,23},{29,30},{30,31}} | collective-permute-start | bytes 393224 | tf_op jit(solution)/shard_map/ppermute | solution.py:165
  125.1 5.6 %collective-permute-done.10 = bf16[4,2,8192]{2,1,0:T(2,128)(2,1)S(1)} collective-permute-done((bf16[4,2,8192]{2,1,0:T(2,128)(2,1)S(1)}, bf16[4,2,8192]{2,1,0:T(2,128)(2,1)S(1)}, u32[]{:S(2)}, u32[]{:S(2)}) %collective-permute-start.10) | collective-permute-done | bytes 131104 | tf_op jit(solution)/shard_map/ppermute | solution.py:165
  131.8 2.0 %fusion.251 = (f32[2,8,32]{2,1,0:T(8,128)S(1)}, f32[2,2,8,32,128]{4,3,2,1,0:T(8,128)S(1)}) fusion(bf16[8,2,8,128,128]{4,3,2,1,0:T(8,128)(2,1)} %get-tuple-element.44, s32[]{:T(128)S(6)} %select_n.249, bf16[2,8,32,128]{3,2,1,0:T(8,128)(2,1)S(1)} %bitcast.329, pred[2,2,128]{2,1,0:T(4,128)(4,1)S(1)} %broadcast_compare_fusion.1), kind=kOutput, calls=%fused_computation.479 | convolution fusion | flops 33947136 | bytes 1706500 | tf_op jit(solution)/shard_map/rjgxd,rjgpd->rjgxp/dot_general | solution.py:46
  137.7 2.5 %collective-permute-done.11 = bf16[4,2,8192]{2,1,0:T(2,128)(2,1)S(1)} collective-permute-done((bf16[4,2,8192]{2,1,0:T(2,128)(2,1)S(1)}, bf16[4,2,8192]{2,1,0:T(2,128)(2,1)S(1)}, u32[]{:S(2)}, u32[]{:S(2)}) %collective-permute-start.11) | collective-permute-done | bytes 131104 | tf_op jit(solution)/shard_map/ppermute | solution.py:165
  141.3 2.0 %fusion.253 = (f32[2,8,32]{2,1,0:T(8,128)S(1)}, f32[2,2,8,32,128]{4,3,2,1,0:T(8,128)S(1)}) fusion(bf16[8,2,8,128,128]{4,3,2,1,0:T(8,128)(2,1)} %get-tuple-element.44, s32[]{:T(128)S(6)} %select_n.252, bf16[2,8,32,128]{3,2,1,0:T(8,128)(2,1)S(1)} %bitcast.322, pred[2,2,128]{2,1,0:T(4,128)(4,1)S(1)} %broadcast_compare_fusion), kind=kOutput, calls=%fused_computation.481 | convolution fusion | flops 33947136 | bytes 1706500 | tf_op jit(solution)/shard_map/rjgxd,rjgpd->rjgxp/dot_general | solution.py:46
  (263 shorter events, 60.8 us)
Async XLA Ops:
  0.6 8.8 %copy-start = (s32[1,8]{1,0:T(1,128)S(1)}, s32[1,8]{1,0:T(1,128)}, u32[]{:S(2)}) copy-start(s32[1,8]{1,0:T(1,128)} %param.10) | copy-start | bytes 100
  9.4 4.7 %copy-start.2 = (f32[1,8192]{1,0:T(1,128)S(1)}, f32[1,8192]{1,0:T(1,128)}, u32[]{:S(2)}) copy-start(f32[1,8192]{1,0:T(1,128)} %param.13) | copy-start | bytes 98308
  9.4 4.7 %copy-start.3 = (bf16[1,4,8,8192]{3,2,1,0:T(8,128)(2,1)S(1)}, bf16[1,4,8,8192]{3,2,1,0:T(8,128)(2,1)}, u32[]{:S(2)}) copy-start(bf16[1,4,8,8192]{3,2,1,0:T(8,128)(2,1)} %param.7) | copy-start | bytes 1572868
  9.5 6.2 %copy-start.6 = (s32[1,2]{1,0:T(1,128)S(1)}, s32[1,2]{1,0:T(1,128)}, u32[]{:S(2)}) copy-start(s32[1,2]{1,0:T(1,128)} %param.11) | copy-start | bytes 28
  15.0 6.5 %collective-permute-start = (bf16[4,2,8192]{2,1,0:T(2,128)(2,1)S(1)}, bf16[4,2,8192]{2,1,0:T(2,128)(2,1)S(1)}, u32[]{:S(2)}, u32[]{:S(2)}) collective-permute-start(bf16[4,2,8192]{2,1,0:T(2,128)(2,1)S(1)} %get-tuple-element.97), channel_id=1, source_target_pairs={{0,1},{8,9},{16,17},{24,25}} | collective-permute-start | bytes 393224 | tf_op jit(solution)/shard_map/ppermute | solution.py:165
  16.3 4.5 %copy-start.5 = (s32[1,8,2]{1,2,0:T(2,128)S(1)}, s32[1,8,2]{1,2,0:T(2,128)}, u32[]{:S(2)}) copy-start(s32[1,8,2]{1,2,0:T(2,128)} %param.9) | copy-start | bytes 196
  16.3 5.6 %copy-start.1 = (f32[1,8192]{1,0:T(1,128)S(1)}, f32[1,8192]{1,0:T(1,128)}, u32[]{:S(2)}) copy-start(f32[1,8192]{1,0:T(1,128)} %param.12) | copy-start | bytes 98308
  16.3 6.4 %collective-permute-start.4 = (s32[2]{0:T(128)S(1)}, s32[2]{0:T(128)S(1)}, u32[]{:S(2)}, u32[]{:S(2)}) collective-permute-start(s32[2]{0:T(128)S(1)} %gather_fusion.1), channel_id=1, source_target_pairs={{0,8},{8,0},{1,9},{9,1},{2,10},{10,2},{3,11},{11,3},{4,12},{12,4},... | collective-permute-start | bytes 32 | tf_op jit(solution)/shard_map/ppermute | solution.py:20
  27.9 5.1 %collective-permute-start.1 = (bf16[4,2,8192]{2,1,0:T(2,128)(2,1)S(1)}, bf16[4,2,8192]{2,1,0:T(2,128)(2,1)S(1)}, u32[]{:S(2)}, u32[]{:S(2)}) collective-permute-start(bf16[4,2,8192]{2,1,0:T(2,128)(2,1)S(1)} %get-tuple-element.93), channel_id=1, source_target_pairs={{0,1},{1,2},{8,9},{9,10},{16,17},{17,18},{24,25},{25,26}} | collective-permute-start | bytes 393224 | tf_op jit(solution)/shard_map/ppermute | solution.py:165
  39.5 11.2 %collective-permute-start.2 = (bf16[4,2,8192]{2,1,0:T(2,128)(2,1)S(1)}, bf16[4,2,8192]{2,1,0:T(2,128)(2,1)S(1)}, u32[]{:S(2)}, u32[]{:S(2)}) collective-permute-start(bf16[4,2,8192]{2,1,0:T(2,128)(2,1)S(1)} %get-tuple-element.89), channel_id=1, source_target_pairs={{0,1},{1,2},{2,3},{8,9},{9,10},{10,11},{16,17},{17,18},{18,19},{24... | collective-permute-start | bytes 393224 | tf_op jit(solution)/shard_map/ppermute | solution.py:165
  45.8 12.2 %collective-permute-start.5 = (bf16[2,2,2,8,128,128]{5,4,3,2,1,0:T(8,128)(2,1)}, bf16[2,2,2,8,128,128]{5,4,3,2,1,0:T(8,128)(2,1)S(1)}, u32[]{:S(2)}, u32[]{:S(2)}) collective-permute-start(bf16[2,2,2,8,128,128]{5,4,3,2,1,0:T(8,128)(2,1)} %bitcast.317), channel_id=1, source_target_pairs={{0,8},{8,0},{1,9},{9,1},{2,10},{10,2},{3,11},{11,3},{4,12},{12,4},... | collective-permute-start | bytes 6291464 | tf_op jit(solution)/shard_map/ppermute | solution.py:20
  57.2 2.5 %collective-permute-start.3 = (bf16[4,2,8192]{2,1,0:T(2,128)(2,1)S(1)}, bf16[4,2,8192]{2,1,0:T(2,128)(2,1)S(1)}, u32[]{:S(2)}, u32[]{:S(2)}) collective-permute-start(bf16[4,2,8192]{2,1,0:T(2,128)(2,1)S(1)} %get-tuple-element.85), channel_id=1, source_target_pairs={{0,1},{1,2},{2,3},{3,4},{8,9},{9,10},{10,11},{11,12},{16,17},{17,1... | collective-permute-start | bytes 393224 | tf_op jit(solution)/shard_map/ppermute | solution.py:165
  60.3 4.8 %copy-start.4 = (bf16[11,4,2,8192]{3,2,1,0:T(2,128)(2,1)S(1)}, bf16[11,4,2,8192]{3,2,1,0:T(2,128)(2,1)}, u32[]{:S(2)}) copy-start(bf16[11,4,2,8192]{3,2,1,0:T(2,128)(2,1)} %get-tuple-element.84) | copy-start | bytes 4325380
  65.3 0.7 collective-permute-start.6
  71.7 16.7 %collective-permute-start.7 = (bf16[4,2,8192]{2,1,0:T(2,128)(2,1)S(1)}, bf16[4,2,8192]{2,1,0:T(2,128)(2,1)S(1)}, u32[]{:S(2)}, u32[]{:S(2)}) collective-permute-start(bf16[4,2,8192]{2,1,0:T(2,128)(2,1)S(1)} %get-tuple-element.81), channel_id=1, source_target_pairs={{2,3},{3,4},{4,5},{5,6},{10,11},{11,12},{12,13},{13,14},{18,19},{1... | collective-permute-start | bytes 393224 | tf_op jit(solution)/shard_map/ppermute | solution.py:165
  94.1 9.7 %collective-permute-start.8 = (bf16[4,2,8192]{2,1,0:T(2,128)(2,1)S(1)}, bf16[4,2,8192]{2,1,0:T(2,128)(2,1)S(1)}, u32[]{:S(2)}, u32[]{:S(2)}) collective-permute-start(bf16[4,2,8192]{2,1,0:T(2,128)(2,1)S(1)} %get-tuple-element.79), channel_id=1, source_target_pairs={{3,4},{4,5},{5,6},{6,7},{11,12},{12,13},{13,14},{14,15},{19,20},{2... | collective-permute-start | bytes 393224 | tf_op jit(solution)/shard_map/ppermute | solution.py:165
  109.4 7.8 %collective-permute-start.9 = (bf16[4,2,8192]{2,1,0:T(2,128)(2,1)S(1)}, bf16[4,2,8192]{2,1,0:T(2,128)(2,1)S(1)}, u32[]{:S(2)}, u32[]{:S(2)}) collective-permute-start(bf16[4,2,8192]{2,1,0:T(2,128)(2,1)S(1)} %get-tuple-element.77), channel_id=1, source_target_pairs={{4,5},{5,6},{6,7},{12,13},{13,14},{14,15},{20,21},{21,22},{22,23},... | collective-permute-start | bytes 393224 | tf_op jit(solution)/shard_map/ppermute | solution.py:165
  122.9 7.8 %collective-permute-start.10 = (bf16[4,2,8192]{2,1,0:T(2,128)(2,1)S(1)}, bf16[4,2,8192]{2,1,0:T(2,128)(2,1)S(1)}, u32[]{:S(2)}, u32[]{:S(2)}) collective-permute-start(bf16[4,2,8192]{2,1,0:T(2,128)(2,1)S(1)} %get-tuple-element.75), channel_id=1, source_target_pairs={{5,6},{6,7},{13,14},{14,15},{21,22},{22,23},{29,30},{30,31}} | collective-permute-start | bytes 393224 | tf_op jit(solution)/shard_map/ppermute | solution.py:165
  136.4 3.8 %collective-permute-start.11 = (bf16[4,2,8192]{2,1,0:T(2,128)(2,1)S(1)}, bf16[4,2,8192]{2,1,0:T(2,128)(2,1)S(1)}, u32[]{:S(2)}, u32[]{:S(2)}) collective-permute-start(bf16[4,2,8192]{2,1,0:T(2,128)(2,1)S(1)} %get-tuple-element.73), channel_id=1, source_target_pairs={{6,7},{14,15},{22,23},{30,31}} | collective-permute-start | bytes 393224 | tf_op jit(solution)/shard_map/ppermute | solution.py:165
  147.8 1.4 collective-permute-start.12

commit v15 on v12

--- a/solution.py
+++ b/solution.py
@@ -144,8 +144,6 @@
             arrived = jnp.where(
                 keep[:, :, None, None, :, None], received, jnp.zeros((), jnp.bfloat16)
             )
-        elif k == 6:
-            start, incoming, arrived = lax.optimization_barrier((start, incoming, arrived))
         elif k > 0:
             start, incoming = lax.optimization_barrier((start, incoming))
         if k == 0:

time: 148 us -> 152 us (1.027)
  waiting for transfers between devices: 33.5 us -> 36.8 us
    ppermute x10, waiting for transfers between devices: 32.1 us -> 35.8 us  [per_device(): incoming = lax.ppermute(result, 'section', pairs)]
    select_n x1 -> x0, other arithmetic: 1.59 us -> none  [per_device(): jnp.where(keep[:, :, None, None, :, None], received, jnp.zeros((), jnp.bf...]
    broadcast_in_dim x0 -> x1, other arithmetic: none -> 1.59 us  [per_device(): return (finished[None, None], arrived[None, None])]
    unnamed x18 -> x16, local copies, waits for them, and re-layouts: 3.07 us -> 3.06 us
  transfers between devices with their start and end apart: 13 -> 13, of which waited for: 6 -> 5; matrix products, arithmetic and copies ran while one was open for 11% -> 13% of each run, Pallas kernels for 9% -> 9%
where the time goes in v15:
time: 152 us; the launch traced here: 150 us
  matrix products  43.7 us (29%)
  waiting for transfers between devices  36.8 us (24%)
  local copies, waits for them, and re-layouts  19.1 us (13%)
  Pallas kernels  17.8 us (12%)
  other arithmetic  17.5 us (12%)
  starting transfers between devices  12.7 us (8%)
  between operations  2.13 us (1%)
    ppermute x10, waiting for transfers between devices, per_device(): incoming = lax.ppermute(result, 'section', pairs)  35.8 us
    dot_general x11, matrix products, layer(): jnp.einsum('rjgxd,rjgpd->rjgxp', wide_query, keys, preferred_element_type...  21.6 us
    pallas_call x4, Pallas kernels, gather_chunk(): pl.pallas_call(copy_kernel, grid_spec=grid_spec, out_shape=[half, half],...  17.8 us
    dot_general x11, matrix products, layer(): jnp.einsum('rjgxp,rjgpd->rjgxd', cache_w, values, preferred_element_type=...  17.3 us
    ppermute x10, starting transfers between devices, per_device(): incoming = lax.ppermute(result, 'section', pairs)  12.1 us
    gather x1, local copies, waits for them, and re-layouts, per_device(): received = partner(pool[chosen], 'inst', 0)  5.51 us
    reduce_sum x11, other arithmetic, layer(): jnp.mean(wide * wide, axis=-1, keepdims=True) + 1e-05  4.06 us
    unnamed x16, local copies, waits for them, and re-layouts  3.06 us
  transfers between devices with their start and end apart: 13, of which 5 were waited for; matrix products, arithmetic and copies ran while one was open for 13% of the time, Pallas kernels for 9%

profile of v15, /device:TPU:26, one launch (start us, length us, event | category | flops | bytes accessed | tf_op | source)
XLA Modules:
  0.0 149.7 jit_solution(3477998836776490424)
XLA Ops:
  5.0 4.5 %shard_map.86 = (bf16[8,2,8,128,128]{4,3,2,1,0:T(8,128)(2,1)}, bf16[8,2,8,128,128]{4,3,2,1,0:T(8,128)(2,1)}) custom-call(s32[16]{0:T(128)} %reshape_squeeze.2.table_ref, bf16[16,2,8,128,128]{4,3,2,1,0:T(8,128)(2,1)} %bitcast.289), custom_call_target="tpu_custom_call" | custom-call | tf_op jit(solution)/shard_map/pallas_call | solution.py:108
  9.8 2.0 %fusion.233 = (f32[2,8,32]{2,1,0:T(8,128)S(1)}, f32[2,2,8,32,128]{4,3,2,1,0:T(8,128)S(1)}) fusion(bf16[8,2,8,128,128]{4,3,2,1,0:T(8,128)(2,1)} %get-tuple-element.31.refs_0_, s32[]{:T(128)S(6)} %select_n.214, bf16[2,8,32,128]{3,2,1,0:T(8,128)(2,1)S(1)} %bitcast.321, pred[2,2,128]{2,1,0:T(4,128)(4,1)S(1)} %broadcast_compare_fusion.11), kind=kOutput, calls=%fused_computation.461 | convolution fusion | flops 33947136 | bytes 1706500 | tf_op jit(solution)/shard_map/rjgxd,rjgpd->rjgxp/dot_general | solution.py:46
  15.7 4.5 %shard_map.87 = (bf16[8,2,8,128,128]{4,3,2,1,0:T(8,128)(2,1)}, bf16[8,2,8,128,128]{4,3,2,1,0:T(8,128)(2,1)}) custom-call(s32[16]{0:T(128)} %reshape_squeeze.2.table_ref, bf16[16,2,8,128,128]{4,3,2,1,0:T(8,128)(2,1)} %bitcast.290, bf16[8,2,8,128,128]{4,3,2,1,0:T(8,128)(2,1)} %get-tuple-element.31.refs_0_, ...), custom_call_target="tpu_custom_call", output_to_operand_aliasing={{0}: (2, {}), {1}: (3, {})} | custom-call | tf_op jit(solution)/shard_map/pallas_call | solution.py:108
  21.4 2.0 %fusion.235 = (f32[2,8,32]{2,1,0:T(8,128)S(1)}, f32[2,2,8,32,128]{4,3,2,1,0:T(8,128)S(1)}) fusion(bf16[8,2,8,128,128]{4,3,2,1,0:T(8,128)(2,1)} %get-tuple-element.35.refs_0_, s32[]{:T(128)S(6)} %select_n.219, bf16[2,8,32,128]{3,2,1,0:T(8,128)(2,1)S(1)} %bitcast.323, pred[2,2,128]{2,1,0:T(4,128)(4,1)S(1)} %get-tuple-element.123), kind=kOutput, calls=%fused_computation.463 | convolution fusion | flops 33947136 | bytes 1706500 | tf_op jit(solution)/shard_map/rjgxd,rjgpd->rjgxp/dot_general | solution.py:46
  26.7 4.5 %shard_map.88 = (bf16[8,2,8,128,128]{4,3,2,1,0:T(8,128)(2,1)}, bf16[8,2,8,128,128]{4,3,2,1,0:T(8,128)(2,1)}) custom-call(s32[16]{0:T(128)} %reshape_squeeze.2.table_ref, bf16[16,2,8,128,128]{4,3,2,1,0:T(8,128)(2,1)} %bitcast.291, bf16[8,2,8,128,128]{4,3,2,1,0:T(8,128)(2,1)} %get-tuple-element.35.refs_0_, ...), custom_call_target="tpu_custom_call", output_to_operand_aliasing={{0}: (2, {}), {1}: (3, {})} | custom-call | tf_op jit(solution)/shard_map/pallas_call | solution.py:108
  32.4 2.0 %fusion.237 = (f32[2,8,32]{2,1,0:T(8,128)S(1)}, f32[2,2,8,32,128]{4,3,2,1,0:T(8,128)S(1)}) fusion(bf16[8,2,8,128,128]{4,3,2,1,0:T(8,128)(2,1)} %get-tuple-element.39.refs_0_, s32[]{:T(128)S(6)} %select_n.223, bf16[2,8,32,128]{3,2,1,0:T(8,128)(2,1)S(1)} %bitcast.330, pred[2,2,128]{2,1,0:T(4,128)(4,1)S(1)} %broadcast_compare_fusion.9), kind=kOutput, calls=%fused_computation.465 | convolution fusion | flops 33947136 | bytes 1706500 | tf_op jit(solution)/shard_map/rjgxd,rjgpd->rjgxp/dot_general | solution.py:46
  38.3 4.5 %shard_map.89 = (bf16[8,2,8,128,128]{4,3,2,1,0:T(8,128)(2,1)}, bf16[8,2,8,128,128]{4,3,2,1,0:T(8,128)(2,1)}) custom-call(s32[16]{0:T(128)} %reshape_squeeze.2.table_ref, bf16[16,2,8,128,128]{4,3,2,1,0:T(8,128)(2,1)} %bitcast.292, bf16[8,2,8,128,128]{4,3,2,1,0:T(8,128)(2,1)} %get-tuple-element.39.refs_0_, ...), custom_call_target="tpu_custom_call", output_to_operand_aliasing={{0}: (2, {}), {1}: (3, {})} | custom-call | tf_op jit(solution)/shard_map/pallas_call | solution.py:108
  44.0 2.0 %fusion.239 = (f32[2,8,32]{2,1,0:T(8,128)S(1)}, f32[2,2,8,32,128]{4,3,2,1,0:T(8,128)S(1)}) fusion(bf16[8,2,8,128,128]{4,3,2,1,0:T(8,128)(2,1)} %get-tuple-element.43, s32[]{:T(128)S(6)} %select_n.228, bf16[2,8,32,128]{3,2,1,0:T(8,128)(2,1)S(1)} %bitcast.331, pred[2,2,128]{2,1,0:T(4,128)(4,1)S(1)} %broadcast_compare_fusion.8), kind=kOutput, calls=%fused_computation.467 | convolution fusion | flops 33947136 | bytes 1706500 | tf_op jit(solution)/shard_map/rjgxd,rjgpd->rjgxp/dot_general | solution.py:46
  50.6 2.0 %fusion.241 = (f32[2,8,32]{2,1,0:T(8,128)S(1)}, f32[2,2,8,32,128]{4,3,2,1,0:T(8,128)S(1)}) fusion(bf16[8,2,8,128,128]{4,3,2,1,0:T(8,128)(2,1)} %get-tuple-element.43, s32[]{:T(128)S(6)} %select_n.232, bf16[2,8,32,128]{3,2,1,0:T(8,128)(2,1)S(1)} %bitcast.324, pred[2,2,128]{2,1,0:T(4,128)(4,1)S(1)} %broadcast_compare_fusion.7), kind=kOutput, calls=%fused_computation.469 | convolution fusion | flops 33947136 | bytes 1706500 | tf_op jit(solution)/shard_map/rjgxd,rjgpd->rjgxp/dot_general | solution.py:46
  57.0 2.0 %fusion.243 = (f32[2,8,32]{2,1,0:T(8,128)S(1)}, f32[2,2,8,32,128]{4,3,2,1,0:T(8,128)S(1)}) fusion(bf16[8,2,8,128,128]{4,3,2,1,0:T(8,128)(2,1)} %get-tuple-element.43, s32[]{:T(128)S(6)} %select_n.235, bf16[2,8,32,128]{3,2,1,0:T(8,128)(2,1)S(1)} %bitcast.325, pred[2,2,128]{2,1,0:T(4,128)(4,1)S(1)} %broadcast_compare_fusion.6), kind=kOutput, calls=%fused_computation.471 | convolution fusion | flops 33947136 | bytes 1706500 | tf_op jit(solution)/shard_map/rjgxd,rjgpd->rjgxp/dot_general | solution.py:46
  62.8 18.5 %collective-permute-done.5 = bf16[4,2,8192]{2,1,0:T(2,128)(2,1)S(1)} collective-permute-done((bf16[4,2,8192]{2,1,0:T(2,128)(2,1)S(1)}, bf16[4,2,8192]{2,1,0:T(2,128)(2,1)S(1)}, u32[]{:S(2)}, u32[]{:S(2)}) %collective-permute-start.5) | collective-permute-done | bytes 131104 | tf_op jit(solution)/shard_map/ppermute | solution.py:163
  82.5 2.0 %fusion.245 = (f32[2,8,32]{2,1,0:T(8,128)S(1)}, f32[2,2,8,32,128]{4,3,2,1,0:T(8,128)S(1)}) fusion(bf16[8,2,8,128,128]{4,3,2,1,0:T(8,128)(2,1)} %get-tuple-element.43, s32[]{:T(128)S(6)} %select_n.238, bf16[2,8,32,128]{3,2,1,0:T(8,128)(2,1)S(1)} %bitcast.326, pred[2,2,128]{2,1,0:T(4,128)(4,1)S(1)} %broadcast_compare_fusion.5), kind=kOutput, calls=%fused_computation.473 | convolution fusion | flops 33947136 | bytes 1706500 | tf_op jit(solution)/shard_map/rjgxd,rjgpd->rjgxp/dot_general | solution.py:46
  87.0 1.9 %collective-permute-start.6 = (bf16[4,2,8192]{2,1,0:T(2,128)(2,1)S(1)}, bf16[4,2,8192]{2,1,0:T(2,128)(2,1)S(1)}, u32[]{:S(2)}, u32[]{:S(2)}) collective-permute-start(bf16[4,2,8192]{2,1,0:T(2,128)(2,1)S(1)} %get-tuple-element.77), channel_id=1, source_target_pairs={{3,4},{4,5},{5,6},{6,7},{11,12},{12,13},{13,14},{14,15},{19,20},{2... | collective-permute-start | bytes 393224 | tf_op jit(solution)/shard_map/ppermute | solution.py:163
  89.0 5.8 %collective-permute-done.6 = bf16[4,2,8192]{2,1,0:T(2,128)(2,1)S(1)} collective-permute-done((bf16[4,2,8192]{2,1,0:T(2,128)(2,1)S(1)}, bf16[4,2,8192]{2,1,0:T(2,128)(2,1)S(1)}, u32[]{:S(2)}, u32[]{:S(2)}) %collective-permute-start.6) | collective-permute-done | bytes 131104 | tf_op jit(solution)/shard_map/ppermute | solution.py:163
  95.9 2.0 %fusion.247 = (f32[2,8,32]{2,1,0:T(8,128)S(1)}, f32[2,2,8,32,128]{4,3,2,1,0:T(8,128)S(1)}) fusion(bf16[8,2,8,128,128]{4,3,2,1,0:T(8,128)(2,1)} %get-tuple-element.43, s32[]{:T(128)S(6)} %select_n.241, bf16[2,8,32,128]{3,2,1,0:T(8,128)(2,1)S(1)} %bitcast.327, pred[2,2,128]{2,1,0:T(4,128)(4,1)S(1)} %broadcast_compare_fusion.4), kind=kOutput, calls=%fused_computation.475 | convolution fusion | flops 33947136 | bytes 1706500 | tf_op jit(solution)/shard_map/rjgxd,rjgpd->rjgxp/dot_general | solution.py:46
  100.5 1.9 %collective-permute-start.7 = (bf16[4,2,8192]{2,1,0:T(2,128)(2,1)S(1)}, bf16[4,2,8192]{2,1,0:T(2,128)(2,1)S(1)}, u32[]{:S(2)}, u32[]{:S(2)}) collective-permute-start(bf16[4,2,8192]{2,1,0:T(2,128)(2,1)S(1)} %get-tuple-element.75), channel_id=1, source_target_pairs={{4,5},{5,6},{6,7},{12,13},{13,14},{14,15},{20,21},{21,22},{22,23},... | collective-permute-start | bytes 393224 | tf_op jit(solution)/shard_map/ppermute | solution.py:163
  102.4 5.8 %collective-permute-done.7 = bf16[4,2,8192]{2,1,0:T(2,128)(2,1)S(1)} collective-permute-done((bf16[4,2,8192]{2,1,0:T(2,128)(2,1)S(1)}, bf16[4,2,8192]{2,1,0:T(2,128)(2,1)S(1)}, u32[]{:S(2)}, u32[]{:S(2)}) %collective-permute-start.7) | collective-permute-done | bytes 131104 | tf_op jit(solution)/shard_map/ppermute | solution.py:163
  109.4 2.0 %fusion.249 = (f32[2,8,32]{2,1,0:T(8,128)S(1)}, f32[2,2,8,32,128]{4,3,2,1,0:T(8,128)S(1)}) fusion(bf16[8,2,8,128,128]{4,3,2,1,0:T(8,128)(2,1)} %get-tuple-element.43, s32[]{:T(128)S(6)} %select_n.244, bf16[2,8,32,128]{3,2,1,0:T(8,128)(2,1)S(1)} %bitcast.328, pred[2,2,128]{2,1,0:T(4,128)(4,1)S(1)} %broadcast_compare_fusion.3), kind=kOutput, calls=%fused_computation.477 | convolution fusion | flops 33947136 | bytes 1706500 | tf_op jit(solution)/shard_map/rjgxd,rjgpd->rjgxp/dot_general | solution.py:46
  114.0 2.1 %collective-permute-start.8 = (bf16[4,2,8192]{2,1,0:T(2,128)(2,1)S(1)}, bf16[4,2,8192]{2,1,0:T(2,128)(2,1)S(1)}, u32[]{:S(2)}, u32[]{:S(2)}) collective-permute-start(bf16[4,2,8192]{2,1,0:T(2,128)(2,1)S(1)} %get-tuple-element.73), channel_id=1, source_target_pairs={{5,6},{6,7},{13,14},{14,15},{21,22},{22,23},{29,30},{30,31}} | collective-permute-start | bytes 393224 | tf_op jit(solution)/shard_map/ppermute | solution.py:163
  116.1 5.6 %collective-permute-done.8 = bf16[4,2,8192]{2,1,0:T(2,128)(2,1)S(1)} collective-permute-done((bf16[4,2,8192]{2,1,0:T(2,128)(2,1)S(1)}, bf16[4,2,8192]{2,1,0:T(2,128)(2,1)S(1)}, u32[]{:S(2)}, u32[]{:S(2)}) %collective-permute-start.8) | collective-permute-done | bytes 131104 | tf_op jit(solution)/shard_map/ppermute | solution.py:163
  122.9 2.0 %fusion.251 = (f32[2,8,32]{2,1,0:T(8,128)S(1)}, f32[2,2,8,32,128]{4,3,2,1,0:T(8,128)S(1)}) fusion(bf16[8,2,8,128,128]{4,3,2,1,0:T(8,128)(2,1)} %get-tuple-element.43, s32[]{:T(128)S(6)} %select_n.247, bf16[2,8,32,128]{3,2,1,0:T(8,128)(2,1)S(1)} %bitcast.329, pred[2,2,128]{2,1,0:T(4,128)(4,1)S(1)} %broadcast_compare_fusion.2), kind=kOutput, calls=%fused_computation.479 | convolution fusion | flops 33947136 | bytes 1706500 | tf_op jit(solution)/shard_map/rjgxd,rjgpd->rjgxp/dot_general | solution.py:46
  130.0 5.5 %gather_fusion.3 = bf16[4,2,8,128,128]{4,3,2,1,0:T(8,128)(2,1)} fusion(bf16[16,2,8,128,128]{4,3,2,1,0:T(8,128)(2,1)} %bitcast.293, s32[1024]{0:T(1024)S(1)} %pad_clamp_fusion), kind=kCustom, calls=%fused_computation.3 | custom fusion | bytes 4194320 | tf_op jit(solution)/shard_map/gather | solution.py:142
  136.7 2.0 %fusion.253 = (f32[2,8,32]{2,1,0:T(8,128)S(1)}, f32[2,2,8,32,128]{4,3,2,1,0:T(8,128)S(1)}) fusion(bf16[8,2,8,128,128]{4,3,2,1,0:T(8,128)(2,1)} %get-tuple-element.43, s32[]{:T(128)S(6)} %select_n.250, bf16[2,8,32,128]{3,2,1,0:T(8,128)(2,1)S(1)} %bitcast.322, pred[2,2,128]{2,1,0:T(4,128)(4,1)S(1)} %broadcast_compare_fusion.1), kind=kOutput, calls=%fused_computation.481 | convolution fusion | flops 33947136 | bytes 1706500 | tf_op jit(solution)/shard_map/rjgxd,rjgpd->rjgxp/dot_general | solution.py:46
  148.1 1.6 %select_bitcast_fusion = bf16[1,1,2,2,2,8,128,128]{7,6,5,4,3,2,1,0:T(8,128)(2,1)} fusion(bf16[2,2,2,8,128,128]{5,4,3,2,1,0:T(8,128)(2,1)S(1)} %collective-permute-done.12, pred[2,2,128]{2,1,0:T(4,128)(4,1)S(1)} %get-tuple-element.122), kind=kLoop, calls=%fused_computation.5 | loop fusion | flops 1048576 | bytes 4194816 | tf_op jit(solution)/shard_map/broadcast_in_dim | solution.py:170
  (263 shorter events, 59.2 us)
Async XLA Ops:
  0.6 8.8 %copy-start = (s32[1,8]{1,0:T(1,128)S(1)}, s32[1,8]{1,0:T(1,128)}, u32[]{:S(2)}) copy-start(s32[1,8]{1,0:T(1,128)} %param.10) | copy-start | bytes 100
  9.4 4.7 %copy-start.2 = (f32[1,8192]{1,0:T(1,128)S(1)}, f32[1,8192]{1,0:T(1,128)}, u32[]{:S(2)}) copy-start(f32[1,8192]{1,0:T(1,128)} %param.13) | copy-start | bytes 98308
  9.4 4.7 %copy-start.3 = (bf16[1,4,8,8192]{3,2,1,0:T(8,128)(2,1)S(1)}, bf16[1,4,8,8192]{3,2,1,0:T(8,128)(2,1)}, u32[]{:S(2)}) copy-start(bf16[1,4,8,8192]{3,2,1,0:T(8,128)(2,1)} %param.7) | copy-start | bytes 1572868
  9.5 5.6 %copy-start.6 = (s32[1,2]{1,0:T(1,128)S(1)}, s32[1,2]{1,0:T(1,128)}, u32[]{:S(2)}) copy-start(s32[1,2]{1,0:T(1,128)} %param.11) | copy-start | bytes 28
  14.3 5.8 %collective-permute-start = (bf16[4,2,8192]{2,1,0:T(2,128)(2,1)S(1)}, bf16[4,2,8192]{2,1,0:T(2,128)(2,1)S(1)}, u32[]{:S(2)}, u32[]{:S(2)}) collective-permute-start(bf16[4,2,8192]{2,1,0:T(2,128)(2,1)S(1)} %get-tuple-element.95), channel_id=1, source_target_pairs={{0,1},{8,9},{16,17},{24,25}} | collective-permute-start | bytes 393224 | tf_op jit(solution)/shard_map/ppermute | solution.py:163
  15.7 4.9 %copy-start.1 = (f32[1,8192]{1,0:T(1,128)S(1)}, f32[1,8192]{1,0:T(1,128)}, u32[]{:S(2)}) copy-start(f32[1,8192]{1,0:T(1,128)} %param.12) | copy-start | bytes 98308
  15.7 5.7 %collective-permute-start.11 = (s32[2]{0:T(128)S(1)}, s32[2]{0:T(128)S(1)}, u32[]{:S(2)}, u32[]{:S(2)}) collective-permute-start(s32[2]{0:T(128)S(1)} %gather_fusion.2), channel_id=1, source_target_pairs={{0,8},{8,0},{1,9},{9,1},{2,10},{10,2},{3,11},{11,3},{4,12},{12,4},... | collective-permute-start | bytes 32 | tf_op jit(solution)/shard_map/ppermute | solution.py:20
  26.0 5.1 %collective-permute-start.1 = (bf16[4,2,8192]{2,1,0:T(2,128)(2,1)S(1)}, bf16[4,2,8192]{2,1,0:T(2,128)(2,1)S(1)}, u32[]{:S(2)}, u32[]{:S(2)}) collective-permute-start(bf16[4,2,8192]{2,1,0:T(2,128)(2,1)S(1)} %get-tuple-element.91), channel_id=1, source_target_pairs={{0,1},{1,2},{8,9},{9,10},{16,17},{17,18},{24,25},{25,26}} | collective-permute-start | bytes 393224 | tf_op jit(solution)/shard_map/ppermute | solution.py:163
  32.2 5.4 %copy-start.5 = (s32[1,8,2]{1,2,0:T(2,128)S(1)}, s32[1,8,2]{1,2,0:T(2,128)}, u32[]{:S(2)}) copy-start(s32[1,8,2]{1,2,0:T(2,128)} %param.9) | copy-start | bytes 196
  37.0 5.8 %collective-permute-start.2 = (bf16[4,2,8192]{2,1,0:T(2,128)(2,1)S(1)}, bf16[4,2,8192]{2,1,0:T(2,128)(2,1)S(1)}, u32[]{:S(2)}, u32[]{:S(2)}) collective-permute-start(bf16[4,2,8192]{2,1,0:T(2,128)(2,1)S(1)} %get-tuple-element.87), channel_id=1, source_target_pairs={{0,1},{1,2},{2,3},{8,9},{9,10},{10,11},{16,17},{17,18},{18,19},{24... | collective-permute-start | bytes 393224 | tf_op jit(solution)/shard_map/ppermute | solution.py:163
  48.5 0.9 collective-permute-start.3
  55.1 0.7 collective-permute-start.4
  61.5 19.8 %collective-permute-start.5 = (bf16[4,2,8192]{2,1,0:T(2,128)(2,1)S(1)}, bf16[4,2,8192]{2,1,0:T(2,128)(2,1)S(1)}, u32[]{:S(2)}, u32[]{:S(2)}) collective-permute-start(bf16[4,2,8192]{2,1,0:T(2,128)(2,1)S(1)} %get-tuple-element.79), channel_id=1, source_target_pairs={{2,3},{3,4},{4,5},{5,6},{10,11},{11,12},{12,13},{13,14},{18,19},{1... | collective-permute-start | bytes 393224 | tf_op jit(solution)/shard_map/ppermute | solution.py:163
  87.0 7.8 %collective-permute-start.6 = (bf16[4,2,8192]{2,1,0:T(2,128)(2,1)S(1)}, bf16[4,2,8192]{2,1,0:T(2,128)(2,1)S(1)}, u32[]{:S(2)}, u32[]{:S(2)}) collective-permute-start(bf16[4,2,8192]{2,1,0:T(2,128)(2,1)S(1)} %get-tuple-element.77), channel_id=1, source_target_pairs={{3,4},{4,5},{5,6},{6,7},{11,12},{12,13},{13,14},{14,15},{19,20},{2... | collective-permute-start | bytes 393224 | tf_op jit(solution)/shard_map/ppermute | solution.py:163
  100.5 7.8 %collective-permute-start.7 = (bf16[4,2,8192]{2,1,0:T(2,128)(2,1)S(1)}, bf16[4,2,8192]{2,1,0:T(2,128)(2,1)S(1)}, u32[]{:S(2)}, u32[]{:S(2)}) collective-permute-start(bf16[4,2,8192]{2,1,0:T(2,128)(2,1)S(1)} %get-tuple-element.75), channel_id=1, source_target_pairs={{4,5},{5,6},{6,7},{12,13},{13,14},{14,15},{20,21},{21,22},{22,23},... | collective-permute-start | bytes 393224 | tf_op jit(solution)/shard_map/ppermute | solution.py:163
  114.0 7.8 %collective-permute-start.8 = (bf16[4,2,8192]{2,1,0:T(2,128)(2,1)S(1)}, bf16[4,2,8192]{2,1,0:T(2,128)(2,1)S(1)}, u32[]{:S(2)}, u32[]{:S(2)}) collective-permute-start(bf16[4,2,8192]{2,1,0:T(2,128)(2,1)S(1)} %get-tuple-element.73), channel_id=1, source_target_pairs={{5,6},{6,7},{13,14},{14,15},{21,22},{22,23},{29,30},{30,31}} | collective-permute-start | bytes 393224 | tf_op jit(solution)/shard_map/ppermute | solution.py:163
  127.4 1.2 copy-start.4
  128.6 6.9 %collective-permute-start.9 = (bf16[4,2,8192]{2,1,0:T(2,128)(2,1)S(1)}, bf16[4,2,8192]{2,1,0:T(2,128)(2,1)S(1)}, u32[]{:S(2)}, u32[]{:S(2)}) collective-permute-start(bf16[4,2,8192]{2,1,0:T(2,128)(2,1)S(1)} %get-tuple-element.71), channel_id=1, source_target_pairs={{6,7},{14,15},{22,23},{30,31}} | collective-permute-start | bytes 393224 | tf_op jit(solution)/shard_map/ppermute | solution.py:163
  135.5 12.6 %collective-permute-start.12 = (bf16[2,2,2,8,128,128]{5,4,3,2,1,0:T(8,128)(2,1)}, bf16[2,2,2,8,128,128]{5,4,3,2,1,0:T(8,128)(2,1)S(1)}, u32[]{:S(2)}, u32[]{:S(2)}) collective-permute-start(bf16[2,2,2,8,128,128]{5,4,3,2,1,0:T(8,128)(2,1)} %bitcast.317), channel_id=1, source_target_pairs={{0,8},{8,0},{1,9},{9,1},{2,10},{10,2},{3,11},{11,3},{4,12},{12,4},... | collective-permute-start | bytes 6291464 | tf_op jit(solution)/shard_map/ppermute | solution.py:20
  144.8 1.6 %collective-permute-start.10 = (bf16[4,2,8192]{2,0,1:T(4,128)(2,1)S(1)}, bf16[4,2,8192]{2,0,1:T(4,128)(2,1)S(1)}, u32[]{:S(2)}, u32[]{:S(2)}) collective-permute-start(bf16[4,2,8192]{2,0,1:T(4,128)(2,1)S(1)} %bitcast.333), channel_id=1, source_target_pairs={{0,8},{8,0},{1,9},{9,1},{2,10},{10,2},{3,11},{11,3},{4,12},{12,4},... | collective-permute-start | bytes 393224 | tf_op jit(solution)/shard_map/ppermute | solution.py:20
